TPU v7x, 32 devices: a whole 2x2x4 slice. The times are simulated.
32 devices in a mesh: own: 4 (over z), rep: 8 (over y, x, core).
Axes of the slice: x: 2, y: 2, z: 4, core: 2. Of those that a mesh axis runs over, the one named last changes fastest.
Arguments:
- amplitudes: bfloat16 [1024, 16384], P('own', 'rep'), may hold values from -6 to 6
- integrals: bfloat16 [2048, 128, 128], P(('own', 'rep')), may hold values from -0.125 to 0.125
- ab_list: int32 [32, 32, 2], P(('own', 'rep')), may hold values from 0 to 15, as said below
- cd_list: int32 [32, 32, 2], P(('own', 'rep')), may hold values from 0 to 15
- live_count: int32 [32, 32], P(('own', 'rep')), may hold values from 0 to 2, as said below
Outputs:
- ladder: float32 [1024, 8192], P('rep', 'own')
Inputs may be any that keep to these rules, and one draw needn't show every extreme that they name: live_count[d, s] is how many of the 2 slots from source s to destination d hold a tile; the rest are ignored; every device fills all its slots to itself. For one destination d, no two slots (of any sources) have the same pair (ab_list[d, s, k], cd_list[d, s, k]).
All inputs are finite; a program needn't handle non-finite values.
Results may differ from a plain program's by a relative error of at most 0.0003.
Values may be sent and summed in bfloat16 or wider, within the bound.
No kernel may reach another device: no remote copies, remote signals or barrier semaphores. Data moves between devices by JAX's collectives and lax.ppermute only.
A program may use at most 128 MiB of HBM per device.

v0:
```python
import jax
import jax.numpy as jnp
from jax import lax
from jax.sharding import PartitionSpec as P

AB_DEV = 16


def on_device(amplitudes, integrals, ab_list, cd_list, live_count):
    tile_len = integrals.shape[-1]
    gathered = lax.all_gather(amplitudes, "own", axis=0, tiled=True)
    cd_count = gathered.shape[1] // tile_len
    own_count = lax.axis_size("own")
    rep_count = lax.axis_size("rep")
    peer_count = own_count * rep_count
    slot_count = integrals.shape[0] // peer_count
    received = lax.all_to_all(integrals, ("own", "rep"), split_axis=0, concat_axis=0, tiled=True)
    ab_ids = ab_list.reshape(-1)
    cd_ids = cd_list.reshape(-1)
    live_mask = (
        jnp.arange(slot_count, dtype=jnp.int32)[None, :] < live_count.reshape(peer_count, 1)
    ).reshape(-1)
    masked = jnp.where(live_mask[:, None, None], received, jnp.zeros_like(received))
    cell_ids = ab_ids * cd_count + cd_ids
    grid = (
        jnp.zeros((AB_DEV * cd_count, tile_len, tile_len), received.dtype).at[cell_ids].set(masked)
    )
    weight = (
        grid.reshape(AB_DEV, cd_count, tile_len, tile_len)
        .transpose(1, 2, 0, 3)
        .reshape(cd_count * tile_len, AB_DEV * tile_len)
    )
    flattened = jnp.dot(gathered, weight, preferred_element_type=jnp.float32)
    return lax.psum_scatter(flattened, "rep", scatter_dimension=0, tiled=True)


def solution(mesh):
    return jax.shard_map(
        on_device,
        mesh=mesh,
        in_specs=(
            P("own", "rep"),
            P(("own", "rep"), None, None),
            P(("own", "rep"), None, None),
            P(("own", "rep"), None, None),
            P(("own", "rep"), None),
        ),
        out_specs=P("rep", "own"),
        check_vma=False,
    )
```

profile of v0, /device:TPU:0, one launch (start us, length us, event | category | flops | bytes accessed | tf_op | source)
XLA Modules:
  0.0 239.2 jit_solution(12314872404377372005)
XLA Ops:
  6.5 0.0 copy-start.2
  6.5 0.0 copy-start.1
  6.5 0.0 copy-start
  6.5 0.0 all-gather.2.cloned.1.call-start
  6.5 0.7 all-gather.2.cloned.1.call-update
  7.3 7.4 %all-to-all-start = ((bf16[64,128,128]{2,1,0:T(8,128)(2,1)}), bf16[64,128,128]{2,1,0:T(8,128)(2,1)}, u32[]{:S(2)}, u32[]{:S(2)}) async-start(bf16[64,128,128]{2,1,0:T(8,128)(2,1)} %param.6), calls=%async_computation | async-start | bytes 4194304 | tf_op jit(solution)/shard_map/all_to_all | solution.py:17
  14.7 0.0 reduce-scatter.2.cloned.1.call-start
  14.8 0.0 copy-done.2
  14.8 0.1 iota_compare_fusion
  14.8 0.1 lt.41
  15.0 0.0 copy-done.1
  15.0 0.0 copy-done
  15.0 0.1 copy.8
  15.1 0.1 add.29
  15.2 98.1 %all-to-all-done = bf16[64,128,128]{2,1,0:T(8,128)(2,1)} async-done(((bf16[64,128,128]{2,1,0:T(8,128)(2,1)}), bf16[64,128,128]{2,1,0:T(8,128)(2,1)}, u32[]{:S(2)}, u32[]{:S(2)}) %all-to-all-start) | async-done | bytes 2097184 | tf_op jit(solution)/shard_map/all_to_all | solution.py:17
  113.2 1.8 broadcast_select_fusion
  115.0 5.4 %broadcast_in_dim.16 = bf16[256,128,128]{2,1,0:T(8,128)(2,1)} broadcast(bf16[]{:T(256)} %constant.4.clone.1), dimensions={} | broadcast | bytes 8388610 | tf_op jit(solution)/shard_map/broadcast_in_dim | solution.py:26
  120.4 8.7 %scatter_fusion = bf16[256,128,128]{2,1,0:T(8,128)(2,1)} fusion(bf16[256,128,128]{2,1,0:T(8,128)(2,1)} %broadcast_in_dim.16, s32[64]{0:T(128)S(1)} %fusion.6, bf16[64,128,128]{2,1,0:T(8,128)(2,1)S(1)} %broadcast_select_fusion), kind=kCustom, calls=%fused_computation | custom fusion | bytes 6291712 | tf_op jit(solution)/shard_map/scatter | solution.py:26
  129.1 13.7 %copy.9 = bf16[16,16,128,128]{3,0,2,1:T(8,128)(2,1)} copy(bf16[16,16,128,128]{3,2,1,0:T(8,128)(2,1)} %bitcast.15) | data formatting | bytes 16777216 | tf_op jit(solution)/shard_map/reshape | solution.py:29
  142.8 0.0 all-gather.2.cloned.1.call-done
  142.8 14.5 %fusion.3 = f32[1024,2048]{0,1:T(8,128)} fusion(bf16[1024,2048]{1,0:T(8,128)(2,1)} %all-gather.2.cloned.1.call-done, bf16[256,8,16,128]{3,2,1,0:T(8,128)(2,1)} %bitcast.16), kind=kOutput, calls=%fused_computation.4 | convolution fusion | flops 8589934592 | bytes 20971520 | tf_op jit(solution)/shard_map/dot_general | solution.py:33
  157.3 0.0 reduce-scatter.2.cloned.1.call-update
  157.3 72.5 %reduce-scatter.2.cloned.1.call-done = f32[128,2048]{0,1:T(8,128)} async-done(((f32[1024,2048]{0,1:T(8,128)}), f32[128,2048]{0,1:T(8,128)}) %reduce-scatter.2.cloned.1.call-update) | async-done | bytes 1048592 | tf_op jit(solution)/shard_map/reduce_scatter | solution.py:34
  229.8 2.5 %copy.10 = f32[128,2048]{1,0:T(8,128)} copy(f32[128,2048]{0,1:T(8,128)} %reduce-scatter.2.cloned.1.call-done) | data formatting | bytes 2097152 | tf_op jit(solution)/shard_map/reduce_scatter | solution.py:34
  (2 shorter events, 0.0 us)
Async XLA Ops:
  6.5 8.2 %copy-start.2 = (s32[1,32]{1,0:T(1,128)S(1)}, s32[1,32]{1,0:T(1,128)}, u32[]{:S(2)}) copy-start(s32[1,32]{1,0:T(1,128)} %param.9) | copy-start | bytes 388
  6.5 8.4 %copy-start.1 = (s32[1,32,2]{1,2,0:T(2,128)S(1)}, s32[1,32,2]{1,2,0:T(2,128)}, u32[]{:S(2)}) copy-start(s32[1,32,2]{1,2,0:T(2,128)} %param.7) | copy-start | bytes 772
  6.5 8.4 %copy-start = (s32[1,32,2]{1,2,0:T(2,128)S(1)}, s32[1,32,2]{1,2,0:T(2,128)}, u32[]{:S(2)}) copy-start(s32[1,32,2]{1,2,0:T(2,128)} %param.8) | copy-start | bytes 772
  6.5 136.2 %all-gather.2.cloned.1.call-start = ((), (), s32[]{:S(2)}) async-start(), calls=%async_computation.2 | async-start | bytes 5242880 | tf_op jit(solution)/shard_map/all_gather | solution.py:11
  7.3 106.0 %all-to-all-start = ((bf16[64,128,128]{2,1,0:T(8,128)(2,1)}), bf16[64,128,128]{2,1,0:T(8,128)(2,1)}, u32[]{:S(2)}, u32[]{:S(2)}) async-start(bf16[64,128,128]{2,1,0:T(8,128)(2,1)} %param.6), calls=%async_computation | async-start | bytes 4194304 | tf_op jit(solution)/shard_map/all_to_all | solution.py:17
  14.7 215.1 %reduce-scatter.2.cloned.1.call-start = ((), (), s32[]{:S(2)}) async-start(), calls=%async_computation.3 | async-start | bytes 9437184 | tf_op jit(solution)/shard_map/reduce_scatter | solution.py:34
Sparse Core Ops, SparseCore 0:
  8.9 122.0 all-gather.1
  157.5 72.3 reduce-scatter.1
where the time goes:
time: 240 us; the launch traced here: 239 us
  waiting for transfers between devices  171 us (71%)
  local copies, waits for them, and re-layouts  30.6 us (13%)
  matrix products  14.5 us (6%)
  between operations  13.5 us (6%)
  starting transfers between devices  7.48 us (3%)
    all_to_all x1, waiting for transfers between devices, on_device(): lax.all_to_all(integrals, ('own', 'rep'), split_axis=0, concat_axis=0, ti...  98.1 us
    reduce_scatter x1, waiting for transfers between devices, on_device(): return lax.psum_scatter(flattened, 'rep', scatter_dimension=0, tiled=True)  72.5 us
    dot_general x1, matrix products, on_device(): flattened = jnp.dot(gathered, weight, preferred_element_type=jnp.float32)  14.5 us
    reshape x1, local copies, waits for them, and re-layouts, on_device(): grid.reshape(AB_DEV, cd_count, tile_len, tile_len).transpose(1, 2, 0, 3)  13.7 us
    scatter x1, local copies, waits for them, and re-layouts, on_device(): jnp.zeros((AB_DEV * cd_count, tile_len, tile_len), received.dtype)  8.7 us
    all_to_all x1, starting transfers between devices, on_device(): lax.all_to_all(integrals, ('own', 'rep'), split_axis=0, concat_axis=0, ti...  7.43 us
    broadcast_in_dim x1, local copies, waits for them, and re-layouts, on_device(): jnp.zeros((AB_DEV * cd_count, tile_len, tile_len), received.dtype)  5.35 us
  transfers between devices with their start and end apart: 3, of which 2 were waited for; matrix products, arithmetic and copies ran while one was open for 13% of the time, Pallas kernels for 0%

commit v1 on v0

v1 whole, which is shorter than its diff:
```python
import functools

import jax
import jax.numpy as jnp
from jax import lax
from jax.experimental import pallas as pl
from jax.experimental.pallas import tpu as pltpu
from jax.sharding import PartitionSpec as P

AB_DEV = 16


def _slot_order(ab_ids, live_mask, ab_count):
    n = ab_ids.shape[0]
    key = jnp.where(live_mask, ab_ids, ab_count)
    idx = jnp.arange(n, dtype=jnp.int32)
    earlier = (key[None, :] < key[:, None]) | ((key[None, :] == key[:, None]) & (idx[None, :] < idx[:, None]))
    rank = jnp.sum(earlier.astype(jnp.int32), axis=1)
    order = jnp.sum(jnp.where(rank[None, :] == idx[:, None], idx[None, :], 0), axis=1).astype(jnp.int32)
    bounds = jnp.arange(ab_count + 1, dtype=jnp.int32)
    starts = jnp.sum((key[None, :] < bounds[:, None]).astype(jnp.int32), axis=1).astype(jnp.int32)
    return order, starts


def _ladder_kernel(order_ref, starts_ref, cd_ref, amp_ref, tiles_ref, out_ref):
    j = pl.program_id(0)
    tile = tiles_ref.shape[-1]
    out_ref[...] = jnp.zeros(out_ref.shape, jnp.float32)

    def body(t, carry):
        i = order_ref[t]
        col = pl.multiple_of(cd_ref[i] * tile, tile)
        out_ref[...] += jnp.dot(
            amp_ref[:, pl.ds(col, tile)], tiles_ref[i], preferred_element_type=jnp.float32
        )
        return carry

    lax.fori_loop(starts_ref[j], starts_ref[j + 1], body, 0)


def _ladder_products(amp, tiles, order, starts, cd_ids, ab_count):
    rows, width = amp.shape
    n, tile, _ = tiles.shape
    cost = pl.CostEstimate(
        flops=2 * rows * tile * tile * n,
        transcendentals=0,
        bytes_accessed=amp.size * 2 + tiles.size * 2 + rows * ab_count * tile * 4,
    )
    grid_spec = pltpu.PrefetchScalarGridSpec(
        num_scalar_prefetch=3,
        grid=(ab_count,),
        in_specs=[
            pl.BlockSpec((rows, width), lambda j, *_: (0, 0)),
            pl.BlockSpec((n, tile, tile), lambda j, *_: (0, 0, 0)),
        ],
        out_specs=pl.BlockSpec((rows, tile), lambda j, *_: (0, j)),
    )
    return pl.pallas_call(
        _ladder_kernel,
        grid_spec=grid_spec,
        out_shape=jax.ShapeDtypeStruct((rows, ab_count * tile), jnp.float32),
        cost_estimate=cost,
    )(order, starts, cd_ids, amp, tiles)


def on_device(amplitudes, integrals, ab_list, cd_list, live_count):
    gathered = lax.all_gather(amplitudes, "own", axis=0, tiled=True)
    own_count = lax.axis_size("own")
    rep_count = lax.axis_size("rep")
    peer_count = own_count * rep_count
    slot_count = integrals.shape[0] // peer_count
    received = lax.all_to_all(integrals, ("own", "rep"), split_axis=0, concat_axis=0, tiled=True)
    ab_ids = ab_list.reshape(-1)
    cd_ids = cd_list.reshape(-1)
    live_mask = (
        jnp.arange(slot_count, dtype=jnp.int32)[None, :] < live_count.reshape(peer_count, 1)
    ).reshape(-1)
    order, starts = _slot_order(ab_ids, live_mask, AB_DEV)
    flattened = _ladder_products(gathered, received, order, starts, cd_ids, AB_DEV)
    return lax.psum_scatter(flattened, "rep", scatter_dimension=0, tiled=True)


def solution(mesh):
    return jax.shard_map(
        on_device,
        mesh=mesh,
        in_specs=(
            P("own", "rep"),
            P(("own", "rep"), None, None),
            P(("own", "rep"), None, None),
            P(("own", "rep"), None, None),
            P(("own", "rep"), None),
        ),
        out_specs=P("rep", "own"),
        check_vma=False,
    )
```

time: 240 us -> 225 us (0.938)
  local copies, waits for them, and re-layouts: 30.6 us -> 1.04 us
  Pallas kernels: 0 us -> 15.4 us
  waiting for transfers between devices: 171 us -> 186 us
  matrix products: 14.5 us -> 0 us
    all_gather x1, waiting for transfers between devices: 0.01 us -> 17.9 us  [on_device(): gathered = lax.all_gather(amplitudes, 'own', axis=0, tiled=True)]
    pallas_call x0 -> x1, Pallas kernels: none -> 15.4 us  [_ladder_products(): pl.pallas_call(_ladder_kernel, grid_spec=grid_spec, out_shape=jax.ShapeDt...]
    dot_general x1 -> x0, matrix products: 14.5 us -> none  [on_device(): flattened = jnp.dot(gathered, weight, preferred_element_type=jnp.float32)]
    reshape x1 -> x2, local copies, waits for them, and re-layouts: 13.7 us -> 0.73 us  [the longest x1 0.63 us: on_device(): cd_ids = cd_list.reshape(-1)]
    scatter x1 -> x0, local copies, waits for them, and re-layouts: 8.7 us -> none  [on_device(): jnp.zeros((AB_DEV * cd_count, tile_len, tile_len), received.dtype)]
    broadcast_in_dim x1 -> x0, local copies, waits for them, and re-layouts: 5.35 us -> none  [on_device(): jnp.zeros((AB_DEV * cd_count, tile_len, tile_len), received.dtype)]
    reduce_scatter x1 -> x0, local copies, waits for them, and re-layouts: 2.53 us -> none  [on_device(): return lax.psum_scatter(flattened, 'rep', scatter_dimension=0, tiled=True)]
  transfers between devices with their start and end apart: 3 -> 3, of which waited for: 2 -> 3; matrix products, arithmetic and copies ran while one was open for 13% -> 1% of each run, Pallas kernels for 0% -> 0%
where the time goes in v1:
time: 225 us
  waiting for transfers between devices  186 us (83%)
  Pallas kernels  15.4 us (7%)
  between operations  13.4 us (6%)
  starting transfers between devices  7.35 us (3%)
    all_to_all x1, waiting for transfers between devices, on_device(): lax.all_to_all(integrals, ('own', 'rep'), split_axis=0, concat_axis=0, ti...  95.9 us
    reduce_scatter x1, waiting for transfers between devices, on_device(): return lax.psum_scatter(flattened, 'rep', scatter_dimension=0, tiled=True)  71.8 us
    all_gather x1, waiting for transfers between devices, on_device(): gathered = lax.all_gather(amplitudes, 'own', axis=0, tiled=True)  17.9 us
    pallas_call x1, Pallas kernels, _ladder_products(): pl.pallas_call(_ladder_kernel, grid_spec=grid_spec, out_shape=jax.ShapeDt...  15.4 us
    all_to_all x1, starting transfers between devices, on_device(): lax.all_to_all(integrals, ('own', 'rep'), split_axis=0, concat_axis=0, ti...  7.3 us
  transfers between devices with their start and end apart: 3, of which 3 were waited for; matrix products, arithmetic and copies ran while one was open for 1% of the time, Pallas kernels for 0%

profile of v1, /device:TPU:0, one launch (start us, length us, event | category | flops | bytes accessed | tf_op | source)
XLA Modules:
  0.0 225.1 jit_solution(11711515490092315196)
XLA Ops:
  6.5 0.0 copy-start.3
  6.5 0.0 copy-start.1
  6.5 0.0 copy-start.2
  6.5 0.0 all-gather.2.cloned.1.call-start
  6.5 0.7 all-gather.2.cloned.1.call-update
  7.3 7.3 %all-to-all-start = ((bf16[64,128,128]{2,1,0:T(8,128)(2,1)}), bf16[64,128,128]{2,1,0:T(8,128)(2,1)S(1)}, u32[]{:S(2)}, u32[]{:S(2)}) async-start(bf16[64,128,128]{2,1,0:T(8,128)(2,1)} %param.6), calls=%async_computation | async-start | bytes 4194304 | tf_op jit(solution)/shard_map/all_to_all | solution.py:72
  14.6 0.0 reduce-scatter.2.cloned.1.call-start
  14.6 0.0 copy-done.3
  14.6 0.1 iota_compare_fusion.2
  14.7 0.1 lt.74
  14.8 0.0 copy-done.1
  14.8 0.1 copy.10
  14.9 0.1 reshape.41
  15.0 0.0 copy-done.2
  15.0 0.1 copy.11
  15.1 0.6 reshape.42.cd_ref
  15.8 0.7 convert_reduce_fusion.1.starts_ref
  16.5 0.2 convert_reduce_fusion
  16.6 0.6 select_reduce_fusion.order_ref
  17.3 95.9 %all-to-all-done.tiles_ref = bf16[64,128,128]{2,1,0:T(8,128)(2,1)S(1)} async-done(((bf16[64,128,128]{2,1,0:T(8,128)(2,1)}), bf16[64,128,128]{2,1,0:T(8,128)(2,1)S(1)}, u32[]{:S(2)}, u32[]{:S(2)}) %all-to-all-start) | async-done | bytes 2097184 | tf_op jit(solution)/shard_map/all_to_all | solution.py:72
  113.1 0.0 copy-start
  113.1 17.9 %all-gather.2.cloned.1.call-done.amp_ref = bf16[1024,2048]{1,0:T(8,128)(2,1)} async-done(((bf16[256,2048]{1,0:T(8,128)(2,1)}), bf16[1024,2048]{1,0:T(8,128)(2,1)}) %all-gather.2.cloned.1.call-update) | async-done | bytes 4194320 | tf_op jit(solution)/shard_map/all_gather | solution.py:67
  131.1 0.0 copy-done
  131.1 15.4 %shard_map.55 = f32[1024,2048]{1,0:T(8,128)} custom-call(s32[64]{0:T(128)} %select_reduce_fusion.order_ref, s32[17]{0:T(128)} %convert_reduce_fusion.1.starts_ref, s32[64]{0:T(128)} %reshape.42.cd_ref, bf16[1024,2048]{1,0:T(8,128)(2,1)} %all-gather.2.cloned.1.call-done.amp_ref, bf16[64,128,128]{2,1,0:T(8,128)(2,1)} %copy-done), custom_call_target="tpu_custom_call" | custom-call | flops 2147483648 | bytes 14680064 | tf_op jit(solution)/shard_map/pallas_call | solution.py:58
  146.4 0.0 reduce-scatter.2.cloned.1.call-update
  146.4 71.8 %reduce-scatter.2.cloned.1.call-done = f32[128,2048]{1,0:T(8,128)} async-done(((f32[1024,2048]{1,0:T(8,128)}), f32[128,2048]{1,0:T(8,128)}) %reduce-scatter.2.cloned.1.call-update) | async-done | bytes 1048592 | tf_op jit(solution)/shard_map/reduce_scatter | solution.py:80
  (1 shorter events, 0.0 us)
Async XLA Ops:
  6.5 8.1 %copy-start.3 = (s32[1,32]{1,0:T(1,128)S(1)}, s32[1,32]{1,0:T(1,128)}, u32[]{:S(2)}) copy-start(s32[1,32]{1,0:T(1,128)} %param.9) | copy-start | bytes 388
  6.5 8.3 %copy-start.1 = (s32[1,32,2]{1,2,0:T(2,128)S(1)}, s32[1,32,2]{1,2,0:T(2,128)}, u32[]{:S(2)}) copy-start(s32[1,32,2]{1,2,0:T(2,128)} %param.7) | copy-start | bytes 772
  6.5 8.5 %copy-start.2 = (s32[1,32,2]{1,2,0:T(2,128)S(1)}, s32[1,32,2]{1,2,0:T(2,128)}, u32[]{:S(2)}) copy-start(s32[1,32,2]{1,2,0:T(2,128)} %param.8) | copy-start | bytes 772
  6.5 124.5 %all-gather.2.cloned.1.call-start = ((), (), s32[]{:S(2)}) async-start(), calls=%async_computation.2 | async-start | bytes 5242880 | tf_op jit(solution)/shard_map/all_gather | solution.py:67
  7.3 105.9 %all-to-all-start = ((bf16[64,128,128]{2,1,0:T(8,128)(2,1)}), bf16[64,128,128]{2,1,0:T(8,128)(2,1)S(1)}, u32[]{:S(2)}, u32[]{:S(2)}) async-start(bf16[64,128,128]{2,1,0:T(8,128)(2,1)} %param.6), calls=%async_computation | async-start | bytes 4194304 | tf_op jit(solution)/shard_map/all_to_all | solution.py:72
  14.6 203.7 %reduce-scatter.2.cloned.1.call-start = ((), (), s32[]{:S(2)}) async-start(), calls=%async_computation.3 | async-start | bytes 9437184 | tf_op jit(solution)/shard_map/reduce_scatter | solution.py:80
  113.1 17.9 %copy-start = (bf16[64,128,128]{2,1,0:T(8,128)(2,1)}, bf16[64,128,128]{2,1,0:T(8,128)(2,1)S(1)}, u32[]{:S(2)}) copy-start(bf16[64,128,128]{2,1,0:T(8,128)(2,1)S(1)} %all-to-all-done.tiles_ref) | copy-start | bytes 6291460
Sparse Core Ops, SparseCore 0:
  8.9 122.0 all-gather.1
  146.6 71.6 reduce-scatter.1

commit v2 on v1

--- a/solution.py
+++ b/solution.py
@@ -8,6 +8,7 @@
 from jax.sharding import PartitionSpec as P
 
 AB_DEV = 16
+N_CHUNK = 2
 
 
 def _slot_order(ab_ids, live_mask, ab_count):
@@ -25,32 +26,33 @@
 def _ladder_kernel(order_ref, starts_ref, cd_ref, amp_ref, tiles_ref, out_ref):
     j = pl.program_id(0)
     tile = tiles_ref.shape[-1]
+    groups, part, _ = amp_ref.shape
     out_ref[...] = jnp.zeros(out_ref.shape, jnp.float32)
 
     def body(t, carry):
         i = order_ref[t]
         col = pl.multiple_of(cd_ref[i] * tile, tile)
-        out_ref[...] += jnp.dot(
-            amp_ref[:, pl.ds(col, tile)], tiles_ref[i], preferred_element_type=jnp.float32
-        )
+        lhs = amp_ref[:, :, pl.ds(col, tile)].reshape(groups * part, tile)
+        out_ref[...] += jnp.dot(lhs, tiles_ref[i], preferred_element_type=jnp.float32)
         return carry
 
     lax.fori_loop(starts_ref[j], starts_ref[j + 1], body, 0)
 
 
-def _ladder_products(amp, tiles, order, starts, cd_ids, ab_count):
-    rows, width = amp.shape
+def _ladder_products(amp4, chunk, tiles, order, starts, cd_ids, ab_count):
+    groups, _, part, width = amp4.shape
+    rows = groups * part
     n, tile, _ = tiles.shape
     cost = pl.CostEstimate(
         flops=2 * rows * tile * tile * n,
         transcendentals=0,
-        bytes_accessed=amp.size * 2 + tiles.size * 2 + rows * ab_count * tile * 4,
+        bytes_accessed=rows * width * 2 + tiles.size * 2 + rows * ab_count * tile * 4,
     )
     grid_spec = pltpu.PrefetchScalarGridSpec(
         num_scalar_prefetch=3,
         grid=(ab_count,),
         in_specs=[
-            pl.BlockSpec((rows, width), lambda j, *_: (0, 0)),
+            pl.BlockSpec((groups, None, part, width), lambda j, *_: (0, chunk, 0, 0)),
             pl.BlockSpec((n, tile, tile), lambda j, *_: (0, 0, 0)),
         ],
         out_specs=pl.BlockSpec((rows, tile), lambda j, *_: (0, j)),
@@ -60,7 +62,24 @@
         grid_spec=grid_spec,
         out_shape=jax.ShapeDtypeStruct((rows, ab_count * tile), jnp.float32),
         cost_estimate=cost,
-    )(order, starts, cd_ids, amp, tiles)
+    )(order, starts, cd_ids, amp4, tiles)
+
+
+def _halving_scatter(partial, bit_order, rep_index, rep_count):
+    levels = rep_count.bit_length() - 1
+    width = partial.shape[-1]
+    part = partial.shape[0] // rep_count
+    x = partial.reshape((2,) * levels + (part, width))
+    axis_bits = list(range(levels - 1, -1, -1))
+    for bit in bit_order:
+        ax = axis_bits.index(bit)
+        mine = (rep_index >> bit) & 1
+        keep = lax.dynamic_index_in_dim(x, mine, ax, keepdims=False)
+        send = lax.dynamic_index_in_dim(x, 1 - mine, ax, keepdims=False)
+        pairs = [(i, i ^ (1 << bit)) for i in range(rep_count)]
+        x = keep + lax.ppermute(send, "rep", perm=pairs)
+        axis_bits.pop(ax)
+    return x.reshape(part, width)
 
 
 def on_device(amplitudes, integrals, ab_list, cd_list, live_count):
@@ -76,8 +95,22 @@
         jnp.arange(slot_count, dtype=jnp.int32)[None, :] < live_count.reshape(peer_count, 1)
     ).reshape(-1)
     order, starts = _slot_order(ab_ids, live_mask, AB_DEV)
-    flattened = _ladder_products(gathered, received, order, starts, cd_ids, AB_DEV)
-    return lax.psum_scatter(flattened, "rep", scatter_dimension=0, tiled=True)
+    rows, width = gathered.shape
+    part = rows // (rep_count * N_CHUNK)
+    amp4 = gathered.reshape(rep_count, N_CHUNK, part, width)
+    rep_index = lax.axis_index("rep")
+    levels = rep_count.bit_length() - 1
+    orders = (list(range(levels)), [0] + list(range(levels - 1, 0, -1)))
+    pieces = []
+    for chunk in range(N_CHUNK):
+        partial = _ladder_products(amp4, chunk, received, order, starts, cd_ids, AB_DEV)
+        half = partial.shape[1] // 2
+        sides = [
+            _halving_scatter(partial[:, h * half:(h + 1) * half], orders[h], rep_index, rep_count)
+            for h in range(2)
+        ]
+        pieces.append(jnp.concatenate(sides, axis=1))
+    return jnp.concatenate(pieces, axis=0)
 
 
 def solution(mesh):

time: 225 us -> 219 us (0.973)
  waiting for transfers between devices: 186 us -> 144 us
  starting transfers between devices: 7.35 us -> 18.9 us
  local copies, waits for them, and re-layouts: 1.04 us -> 11.6 us
  Pallas kernels: 15.4 us -> 22.9 us
  other arithmetic: 1.6 us -> 7.4 us
    reduce_scatter x1 -> x0, waiting for transfers between devices: 71.8 us -> none  [on_device(): return lax.psum_scatter(flattened, 'rep', scatter_dimension=0, tiled=True)]
    ppermute x0 -> x12, waiting for transfers between devices: none -> 29.4 us  [_halving_scatter(): x = keep + lax.ppermute(send, 'rep', perm=pairs)]
    ppermute x0 -> x12, starting transfers between devices: none -> 11.6 us  [_halving_scatter(): x = keep + lax.ppermute(send, 'rep', perm=pairs)]
    pallas_call x1 -> x2, Pallas kernels: 15.4 us -> 22.9 us  [_ladder_products(): pl.pallas_call(_ladder_kernel, grid_spec=grid_spec, out_shape=jax.ShapeDt...]
    slice x0 -> x2, local copies, waits for them, and re-layouts: none -> 5.06 us  [on_device(): partial[:, h * half:(h + 1) * half]]
    add x0 -> x12, other arithmetic: none -> 4.7 us  [_halving_scatter(): x = keep + lax.ppermute(send, 'rep', perm=pairs)]
    squeeze x0 -> x12, local copies, waits for them, and re-layouts: none -> 2.73 us  [_halving_scatter(): send = lax.dynamic_index_in_dim(x, 1 - mine, ax, keepdims=False)]
    unnamed x10 -> x22, local copies, waits for them, and re-layouts: 0.19 us -> 2.92 us
  transfers between devices with their start and end apart: 3 -> 14, of which waited for: 3 -> 8; matrix products, arithmetic and copies ran while one was open for 1% -> 5% of each run, Pallas kernels for 0% -> 5%
where the time goes in v2:
time: 219 us; the launch traced here: 218 us
  waiting for transfers between devices  144 us (66%)
  Pallas kernels  22.9 us (10%)
  starting transfers between devices  18.9 us (9%)
  between operations  13.7 us (6%)
  local copies, waits for them, and re-layouts  11.6 us (5%)
  other arithmetic  7.4 us (3%)
    all_to_all x1, waiting for transfers between devices, on_device(): lax.all_to_all(integrals, ('own', 'rep'), split_axis=0, concat_axis=0, ti...  95.9 us
    ppermute x12, waiting for transfers between devices, _halving_scatter(): x = keep + lax.ppermute(send, 'rep', perm=pairs)  29.4 us
    pallas_call x2, Pallas kernels, _ladder_products(): pl.pallas_call(_ladder_kernel, grid_spec=grid_spec, out_shape=jax.ShapeDt...  22.9 us
    all_gather x1, waiting for transfers between devices, on_device(): gathered = lax.all_gather(amplitudes, 'own', axis=0, tiled=True)  17.9 us
    ppermute x12, starting transfers between devices, _halving_scatter(): x = keep + lax.ppermute(send, 'rep', perm=pairs)  11.6 us
    all_to_all x1, starting transfers between devices, on_device(): lax.all_to_all(integrals, ('own', 'rep'), split_axis=0, concat_axis=0, ti...  7.3 us
    slice x2, local copies, waits for them, and re-layouts, on_device(): partial[:, h * half:(h + 1) * half]  5.06 us
    add x12, other arithmetic, _halving_scatter(): x = keep + lax.ppermute(send, 'rep', perm=pairs)  4.7 us
  transfers between devices with their start and end apart: 14, of which 8 were waited for; matrix products, arithmetic and copies ran while one was open for 5% of the time, Pallas kernels for 5%

profile of v2, /device:TPU:0, one launch (start us, length us, event | category | flops | bytes accessed | tf_op | source)
XLA Modules:
  0.0 218.3 jit_solution(9815960599308635952)
XLA Ops:
  6.5 0.7 all-gather.2.cloned.1.call-update
  7.3 7.3 %all-to-all-start = ((bf16[64,128,128]{2,1,0:T(8,128)(2,1)}), bf16[64,128,128]{2,1,0:T(8,128)(2,1)S(1)}, u32[]{:S(2)}, u32[]{:S(2)}) async-start(bf16[64,128,128]{2,1,0:T(8,128)(2,1)} %param.6), calls=%async_computation | async-start | bytes 4194304 | tf_op jit(solution)/shard_map/all_to_all | solution.py:91
  15.7 0.7 convert_reduce_fusion.1.starts_ref
  16.6 0.7 select_reduce_fusion.order_ref
  17.3 95.9 %all-to-all-done.tiles_ref = bf16[64,128,128]{2,1,0:T(8,128)(2,1)S(1)} async-done(((bf16[64,128,128]{2,1,0:T(8,128)(2,1)}), bf16[64,128,128]{2,1,0:T(8,128)(2,1)S(1)}, u32[]{:S(2)}, u32[]{:S(2)}) %all-to-all-start) | async-done | bytes 2097184 | tf_op jit(solution)/shard_map/all_to_all | solution.py:91
  113.2 17.9 %all-gather.2.cloned.1.call-done = bf16[1024,2048]{1,0:T(8,128)(2,1)} async-done(((bf16[256,2048]{1,0:T(8,128)(2,1)}), bf16[1024,2048]{1,0:T(8,128)(2,1)}) %all-gather.2.cloned.1.call-update) | async-done | bytes 4194320 | tf_op jit(solution)/shard_map/all_gather | solution.py:86
  131.1 11.5 %shard_map.56 = f32[512,2048]{1,0:T(8,128)} custom-call(s32[64]{0:T(128)} %select_reduce_fusion.order_ref, s32[17]{0:T(128)} %convert_reduce_fusion.1.starts_ref, s32[64]{0:T(128)} %reshape.57.cd_ref, bf16[8,2,64,2048]{3,2,1,0:T(8,128)(2,1)} %bitcast.54, bf16[64,128,128]{2,1,0:T(8,128)(2,1)} %copy-done), custom_call_target="tpu_custom_call" | custom-call | flops 1073741824 | bytes 8388608 | tf_op jit(solution)/shard_map/pallas_call | solution.py:60
  142.5 2.5 %fusion.3 = (f32[512,1024]{1,0:T(8,128)S(1)}, f32[512,1024]{1,0:T(8,128)S(1)}) fusion(f32[512,2048]{1,0:T(8,128)} %shard_map.56), kind=kLoop, calls=%fused_computation.36 | loop fusion | bytes 8388608 | tf_op jit(solution)/shard_map/slice | solution.py:109
  145.1 1.2 dynamic-slice_bitcast_fusion
  146.3 1.7 collective-permute-start.9
  148.1 1.0 collective-permute-start.6
  149.1 11.4 %shard_map.55 = f32[512,2048]{1,0:T(8,128)} custom-call(s32[64]{0:T(128)} %select_reduce_fusion.order_ref, s32[17]{0:T(128)} %convert_reduce_fusion.1.starts_ref, s32[64]{0:T(128)} %reshape.57.cd_ref, bf16[8,2,64,2048]{3,2,1,0:T(8,128)(2,1)} %bitcast.55, bf16[64,128,128]{2,1,0:T(8,128)(2,1)} %copy-done), custom_call_target="tpu_custom_call" | custom-call | flops 1073741824 | bytes 8388608 | tf_op jit(solution)/shard_map/pallas_call | solution.py:60
  160.5 2.5 %fusion.2 = (f32[512,1024]{1,0:T(8,128)S(1)}, f32[512,1024]{1,0:T(8,128)S(1)}) fusion(f32[512,2048]{1,0:T(8,128)} %shard_map.55), kind=kLoop, calls=%fused_computation.35 | loop fusion | bytes 8388608 | tf_op jit(solution)/shard_map/slice | solution.py:109
  163.1 1.3 copy-done.3
  164.4 1.1 dynamic-slice_bitcast_fusion.2
  165.5 1.7 collective-permute-start.3
  167.4 1.4 copy-done.6
  168.8 1.4 bitcast_add_fusion
  170.2 2.6 %collective-permute-start.10 = (f32[2,64,1024]{2,1,0:T(8,128)S(1)}, f32[2,64,1024]{2,1,0:T(8,128)S(1)}, u32[]{:S(2)}, u32[]{:S(2)}) collective-permute-start(f32[2,64,1024]{2,1,0:T(8,128)S(1)} %dynamic-slice_bitcast_fusion.4), channel_id=1, source_target_pairs={{0,4},{1,5},{2,6},{3,7},{4,0},{5,1},{6,2},{7,3},{8,12},{9,13},{10,... | collective-permute-start | bytes 1572872 | tf_op jit(solution)/shard_map/ppermute | solution.py:80
  172.8 1.4 bitcast_add_fusion.1
  174.3 1.4 bitcast_add_fusion.2
  175.8 0.8 collective-permute-start.4
  176.8 1.5 collective-permute-start.1
  178.3 7.2 %collective-permute-done.10 = f32[2,64,1024]{2,1,0:T(8,128)S(1)} collective-permute-done((f32[2,64,1024]{2,1,0:T(8,128)S(1)}, f32[2,64,1024]{2,1,0:T(8,128)S(1)}, u32[]{:S(2)}, u32[]{:S(2)}) %collective-permute-start.10) | collective-permute-done | bytes 524320 | tf_op jit(solution)/shard_map/ppermute | solution.py:80
  185.7 0.9 collective-permute-start.11
  186.5 2.6 %collective-permute-done.7 = f32[2,64,1024]{2,1,0:T(8,128)S(1)} collective-permute-done((f32[2,64,1024]{2,1,0:T(8,128)S(1)}, f32[2,64,1024]{2,1,0:T(8,128)S(1)}, u32[]{:S(2)}, u32[]{:S(2)}) %collective-permute-start.7) | collective-permute-done | bytes 524320 | tf_op jit(solution)/shard_map/ppermute | solution.py:80
  189.4 7.3 %collective-permute-done.4 = f32[2,64,1024]{2,1,0:T(8,128)S(1)} collective-permute-done((f32[2,64,1024]{2,1,0:T(8,128)S(1)}, f32[2,64,1024]{2,1,0:T(8,128)S(1)}, u32[]{:S(2)}, u32[]{:S(2)}) %collective-permute-start.4) | collective-permute-done | bytes 524320 | tf_op jit(solution)/shard_map/ppermute | solution.py:80
  196.9 0.9 collective-permute-start.5
  197.8 2.6 %collective-permute-done.1 = f32[2,64,1024]{2,1,0:T(8,128)S(1)} collective-permute-done((f32[2,64,1024]{2,1,0:T(8,128)S(1)}, f32[2,64,1024]{2,1,0:T(8,128)S(1)}, u32[]{:S(2)}, u32[]{:S(2)}) %collective-permute-start.1) | collective-permute-done | bytes 524320 | tf_op jit(solution)/shard_map/ppermute | solution.py:80
  200.7 5.3 %collective-permute-done.11 = f32[64,1024]{1,0:T(8,128)S(1)} collective-permute-done((f32[64,1024]{1,0:T(8,128)S(1)}, f32[64,1024]{1,0:T(8,128)S(1)}, u32[]{:S(2)}, u32[]{:S(2)}) %collective-permute-start.11) | collective-permute-done | bytes 262176 | tf_op jit(solution)/shard_map/ppermute | solution.py:80
  206.1 4.3 %collective-permute-done.5 = f32[64,1024]{1,0:T(8,128)S(1)} collective-permute-done((f32[64,1024]{1,0:T(8,128)S(1)}, f32[64,1024]{1,0:T(8,128)S(1)}, u32[]{:S(2)}, u32[]{:S(2)}) %collective-permute-start.5) | collective-permute-done | bytes 262176 | tf_op jit(solution)/shard_map/ppermute | solution.py:80
  210.4 1.0 maximum_maximum_fusion
  (56 shorter events, 3.0 us)
Async XLA Ops:
  6.5 124.6 %all-gather.2.cloned.1.call-start = ((), (), s32[]{:S(2)}) async-start(), calls=%async_computation.1 | async-start | bytes 5242880 | tf_op jit(solution)/shard_map/all_gather | solution.py:86
  7.3 7.3 %copy-start.9 = (s32[1,32]{1,0:T(1,128)S(1)}, s32[1,32]{1,0:T(1,128)}, u32[]{:S(2)}) copy-start(s32[1,32]{1,0:T(1,128)} %param.9) | copy-start | bytes 388
  7.3 7.5 %copy-start.7 = (s32[1,32,2]{1,2,0:T(2,128)S(1)}, s32[1,32,2]{1,2,0:T(2,128)}, u32[]{:S(2)}) copy-start(s32[1,32,2]{1,2,0:T(2,128)} %param.7) | copy-start | bytes 772
  7.3 7.7 %copy-start.8 = (s32[1,32,2]{1,2,0:T(2,128)S(1)}, s32[1,32,2]{1,2,0:T(2,128)}, u32[]{:S(2)}) copy-start(s32[1,32,2]{1,2,0:T(2,128)} %param.8) | copy-start | bytes 772
  7.3 105.9 %all-to-all-start = ((bf16[64,128,128]{2,1,0:T(8,128)(2,1)}), bf16[64,128,128]{2,1,0:T(8,128)(2,1)S(1)}, u32[]{:S(2)}, u32[]{:S(2)}) async-start(bf16[64,128,128]{2,1,0:T(8,128)(2,1)} %param.6), calls=%async_computation | async-start | bytes 4194304 | tf_op jit(solution)/shard_map/all_to_all | solution.py:91
  113.2 17.9 %copy-start = (bf16[64,128,128]{2,1,0:T(8,128)(2,1)}, bf16[64,128,128]{2,1,0:T(8,128)(2,1)S(1)}, u32[]{:S(2)}) copy-start(bf16[64,128,128]{2,1,0:T(8,128)(2,1)S(1)} %all-to-all-done.tiles_ref) | copy-start | bytes 6291460
  145.1 3.0 %copy-start.1 = (f32[512,1024]{1,0:T(8,128)}, f32[512,1024]{1,0:T(8,128)S(1)}, u32[]{:S(2)}) copy-start(f32[512,1024]{1,0:T(8,128)S(1)} %get-tuple-element.7) | copy-start | bytes 6291460
  145.1 3.0 %copy-start.5 = (f32[512,1024]{1,0:T(8,128)}, f32[512,1024]{1,0:T(8,128)S(1)}, u32[]{:S(2)}) copy-start(f32[512,1024]{1,0:T(8,128)S(1)} %get-tuple-element.8) | copy-start | bytes 6291460
  146.3 21.1 %collective-permute-start.9 = (f32[2,2,64,1024]{3,2,1,0:T(8,128)}, f32[2,2,64,1024]{3,2,1,0:T(8,128)}, u32[]{:S(2)}, u32[]{:S(2)}) collective-permute-start(f32[2,2,64,1024]{3,2,1,0:T(8,128)} %dynamic-slice_bitcast_fusion), channel_id=1, source_target_pairs={{0,1},{1,0},{2,3},{3,2},{4,5},{5,4},{6,7},{7,6},{8,9},{9,8},{10,11... | collective-permute-start | bytes 3145736 | tf_op jit(solution)/shard_map/ppermute | solution.py:80
  148.1 24.7 %collective-permute-start.6 = (f32[2,2,64,1024]{3,2,1,0:T(8,128)S(1)}, f32[2,2,64,1024]{3,2,1,0:T(8,128)}, u32[]{:S(2)}, u32[]{:S(2)}) collective-permute-start(f32[2,2,64,1024]{3,2,1,0:T(8,128)S(1)} %dynamic-slice_bitcast_fusion.1), channel_id=1, source_target_pairs={{0,1},{1,0},{2,3},{3,2},{4,5},{5,4},{6,7},{7,6},{8,9},{9,8},{10,11... | collective-permute-start | bytes 3145736 | tf_op jit(solution)/shard_map/ppermute | solution.py:80
  163.1 1.3 copy-start.3
  165.5 8.8 %collective-permute-start.3 = (f32[2,2,64,1024]{3,2,1,0:T(8,128)}, f32[2,2,64,1024]{3,2,1,0:T(8,128)}, u32[]{:S(2)}, u32[]{:S(2)}) collective-permute-start(f32[2,2,64,1024]{3,2,1,0:T(8,128)} %dynamic-slice_bitcast_fusion.2), channel_id=1, source_target_pairs={{0,1},{1,0},{2,3},{3,2},{4,5},{5,4},{6,7},{7,6},{8,9},{9,8},{10,11... | collective-permute-start | bytes 3145736 | tf_op jit(solution)/shard_map/ppermute | solution.py:80
  167.2 1.6 copy-start.6
  167.3 5.5 %copy-start.2 = (f32[512,1024]{1,0:T(8,128)S(1)}, f32[512,1024]{1,0:T(8,128)}, u32[]{:S(2)}) copy-start(f32[512,1024]{1,0:T(8,128)} %copy-done.1) | copy-start | bytes 6291460
  167.3 9.3 %collective-permute-start = (f32[2,2,64,1024]{3,2,1,0:T(8,128)S(1)}, f32[2,2,64,1024]{3,2,1,0:T(8,128)S(1)}, u32[]{:S(2)}, u32[]{:S(2)}) collective-permute-start(f32[2,2,64,1024]{3,2,1,0:T(8,128)S(1)} %dynamic-slice_bitcast_fusion.3), channel_id=1, source_target_pairs={{0,1},{1,0},{2,3},{3,2},{4,5},{5,4},{6,7},{7,6},{8,9},{9,8},{10,11... | collective-permute-start | bytes 3145736 | tf_op jit(solution)/shard_map/ppermute | solution.py:80
  170.2 4.1 %copy-start.4 = (f32[512,1024]{1,0:T(8,128)S(1)}, f32[512,1024]{1,0:T(8,128)}, u32[]{:S(2)}) copy-start(f32[512,1024]{1,0:T(8,128)} %copy-done.3) | copy-start | bytes 6291460
  170.2 15.3 %collective-permute-start.10 = (f32[2,64,1024]{2,1,0:T(8,128)S(1)}, f32[2,64,1024]{2,1,0:T(8,128)S(1)}, u32[]{:S(2)}, u32[]{:S(2)}) collective-permute-start(f32[2,64,1024]{2,1,0:T(8,128)S(1)} %dynamic-slice_bitcast_fusion.4), channel_id=1, source_target_pairs={{0,4},{1,5},{2,6},{3,7},{4,0},{5,1},{6,2},{7,3},{8,12},{9,13},{10,... | collective-permute-start | bytes 1572872 | tf_op jit(solution)/shard_map/ppermute | solution.py:80
  174.2 14.9 %collective-permute-start.7 = (f32[2,64,1024]{2,1,0:T(8,128)S(1)}, f32[2,64,1024]{2,1,0:T(8,128)S(1)}, u32[]{:S(2)}, u32[]{:S(2)}) collective-permute-start(f32[2,64,1024]{2,1,0:T(8,128)S(1)} %dynamic-slice_bitcast_fusion.5), channel_id=1, source_target_pairs={{0,2},{1,3},{2,0},{3,1},{4,6},{5,7},{6,4},{7,5},{8,10},{9,11},{10,... | collective-permute-start | bytes 1572872 | tf_op jit(solution)/shard_map/ppermute | solution.py:80
  175.8 21.0 %collective-permute-start.4 = (f32[2,64,1024]{2,1,0:T(8,128)S(1)}, f32[2,64,1024]{2,1,0:T(8,128)S(1)}, u32[]{:S(2)}, u32[]{:S(2)}) collective-permute-start(f32[2,64,1024]{2,1,0:T(8,128)S(1)} %dynamic-slice_bitcast_fusion.6), channel_id=1, source_target_pairs={{0,4},{1,5},{2,6},{3,7},{4,0},{5,1},{6,2},{7,3},{8,12},{9,13},{10,... | collective-permute-start | bytes 1572872 | tf_op jit(solution)/shard_map/ppermute | solution.py:80
  176.8 23.5 %collective-permute-start.1 = (f32[2,64,1024]{2,1,0:T(8,128)S(1)}, f32[2,64,1024]{2,1,0:T(8,128)S(1)}, u32[]{:S(2)}, u32[]{:S(2)}) collective-permute-start(f32[2,64,1024]{2,1,0:T(8,128)S(1)} %dynamic-slice_bitcast_fusion.7), channel_id=1, source_target_pairs={{0,2},{1,3},{2,0},{3,1},{4,6},{5,7},{6,4},{7,5},{8,10},{9,11},{10,... | collective-permute-start | bytes 1572872 | tf_op jit(solution)/shard_map/ppermute | solution.py:80
  185.7 20.3 %collective-permute-start.11 = (f32[64,1024]{1,0:T(8,128)S(1)}, f32[64,1024]{1,0:T(8,128)S(1)}, u32[]{:S(2)}, u32[]{:S(2)}) collective-permute-start(f32[64,1024]{1,0:T(8,128)S(1)} %dynamic-slice_bitcast_fusion.8), channel_id=1, source_target_pairs={{0,2},{1,3},{2,0},{3,1},{4,6},{5,7},{6,4},{7,5},{8,10},{9,11},{10,... | collective-permute-start | bytes 786440 | tf_op jit(solution)/shard_map/ppermute | solution.py:80
  189.2 16.8 %collective-permute-start.8 = (f32[64,1024]{1,0:T(8,128)S(1)}, f32[64,1024]{1,0:T(8,128)S(1)}, u32[]{:S(2)}, u32[]{:S(2)}) collective-permute-start(f32[64,1024]{1,0:T(8,128)S(1)} %dynamic-slice_bitcast_fusion.9), channel_id=1, source_target_pairs={{0,4},{1,5},{2,6},{3,7},{4,0},{5,1},{6,2},{7,3},{8,12},{9,13},{10,... | collective-permute-start | bytes 786440 | tf_op jit(solution)/shard_map/ppermute | solution.py:80
  196.9 13.4 %collective-permute-start.5 = (f32[64,1024]{1,0:T(8,128)S(1)}, f32[64,1024]{1,0:T(8,128)S(1)}, u32[]{:S(2)}, u32[]{:S(2)}) collective-permute-start(f32[64,1024]{1,0:T(8,128)S(1)} %dynamic-slice_bitcast_fusion.10), channel_id=1, source_target_pairs={{0,2},{1,3},{2,0},{3,1},{4,6},{5,7},{6,4},{7,5},{8,10},{9,11},{10,... | collective-permute-start | bytes 786440 | tf_op jit(solution)/shard_map/ppermute | solution.py:80
  200.5 9.9 %collective-permute-start.2 = (f32[64,1024]{1,0:T(8,128)S(1)}, f32[64,1024]{1,0:T(8,128)S(1)}, u32[]{:S(2)}, u32[]{:S(2)}) collective-permute-start(f32[64,1024]{1,0:T(8,128)S(1)} %dynamic-slice_bitcast_fusion.11), channel_id=1, source_target_pairs={{0,4},{1,5},{2,6},{3,7},{4,0},{5,1},{6,2},{7,3},{8,12},{9,13},{10,... | collective-permute-start | bytes 786440 | tf_op jit(solution)/shard_map/ppermute | solution.py:80
Sparse Core Ops, SparseCore 0:
  8.9 122.1 all-gather.1

commit v3 on v2

--- a/solution.py
+++ b/solution.py
@@ -8,7 +8,7 @@
 from jax.sharding import PartitionSpec as P
 
 AB_DEV = 16
-N_CHUNK = 2
+N_CHUNK = 4
 
 
 def _slot_order(ab_ids, live_mask, ab_count):
@@ -24,25 +24,31 @@
 
 
 def _ladder_kernel(order_ref, starts_ref, cd_ref, amp_ref, tiles_ref, out_ref):
-    j = pl.program_id(0)
+    step = pl.program_id(0)
     tile = tiles_ref.shape[-1]
     groups, part, _ = amp_ref.shape
+    per_step = out_ref.shape[1] // tile
     out_ref[...] = jnp.zeros(out_ref.shape, jnp.float32)
+    for sub in range(per_step):
+        ab = step * per_step + sub
 
-    def body(t, carry):
-        i = order_ref[t]
-        col = pl.multiple_of(cd_ref[i] * tile, tile)
-        lhs = amp_ref[:, :, pl.ds(col, tile)].reshape(groups * part, tile)
-        out_ref[...] += jnp.dot(lhs, tiles_ref[i], preferred_element_type=jnp.float32)
-        return carry
+        def body(t, carry, sub=sub):
+            i = order_ref[t]
+            col = pl.multiple_of(cd_ref[i] * tile, tile)
+            lhs = amp_ref[:, :, pl.ds(col, tile)].reshape(groups * part, tile)
+            out_ref[:, sub * tile:(sub + 1) * tile] += jnp.dot(
+                lhs, tiles_ref[i], preferred_element_type=jnp.float32
+            )
+            return carry
 
-    lax.fori_loop(starts_ref[j], starts_ref[j + 1], body, 0)
+        lax.fori_loop(starts_ref[ab], starts_ref[ab + 1], body, 0)
 
 
-def _ladder_products(amp4, chunk, tiles, order, starts, cd_ids, ab_count):
-    groups, _, part, width = amp4.shape
+def _ladder_products(amp3, tiles, order, starts, cd_ids, ab_count):
+    groups, part, width = amp3.shape
     rows = groups * part
     n, tile, _ = tiles.shape
+    per_step = 4 if ab_count % 4 == 0 else 1
     cost = pl.CostEstimate(
         flops=2 * rows * tile * tile * n,
         transcendentals=0,
@@ -50,19 +56,19 @@
     )
     grid_spec = pltpu.PrefetchScalarGridSpec(
         num_scalar_prefetch=3,
-        grid=(ab_count,),
+        grid=(ab_count // per_step,),
         in_specs=[
-            pl.BlockSpec((groups, None, part, width), lambda j, *_: (0, chunk, 0, 0)),
+            pl.BlockSpec((groups, part, width), lambda j, *_: (0, 0, 0)),
             pl.BlockSpec((n, tile, tile), lambda j, *_: (0, 0, 0)),
         ],
-        out_specs=pl.BlockSpec((rows, tile), lambda j, *_: (0, j)),
+        out_specs=pl.BlockSpec((rows, per_step * tile), lambda j, *_: (0, j)),
     )
     return pl.pallas_call(
         _ladder_kernel,
         grid_spec=grid_spec,
         out_shape=jax.ShapeDtypeStruct((rows, ab_count * tile), jnp.float32),
         cost_estimate=cost,
-    )(order, starts, cd_ids, amp4, tiles)
+    )(order, starts, cd_ids, amp3, tiles)
 
 
 def _halving_scatter(partial, bit_order, rep_index, rep_count):
@@ -83,27 +89,31 @@
 
 
 def on_device(amplitudes, integrals, ab_list, cd_list, live_count):
-    gathered = lax.all_gather(amplitudes, "own", axis=0, tiled=True)
     own_count = lax.axis_size("own")
     rep_count = lax.axis_size("rep")
     peer_count = own_count * rep_count
     slot_count = integrals.shape[0] // peer_count
     received = lax.all_to_all(integrals, ("own", "rep"), split_axis=0, concat_axis=0, tiled=True)
+    amplitudes, received = lax.optimization_barrier((amplitudes, received))
     ab_ids = ab_list.reshape(-1)
     cd_ids = cd_list.reshape(-1)
     live_mask = (
         jnp.arange(slot_count, dtype=jnp.int32)[None, :] < live_count.reshape(peer_count, 1)
     ).reshape(-1)
     order, starts = _slot_order(ab_ids, live_mask, AB_DEV)
-    rows, width = gathered.shape
-    part = rows // (rep_count * N_CHUNK)
-    amp4 = gathered.reshape(rep_count, N_CHUNK, part, width)
+    local_rows, width = amplitudes.shape
+    subs = rep_count // own_count
+    part = local_rows // (subs * N_CHUNK)
+    local4 = amplitudes.reshape(subs, N_CHUNK, part, width)
     rep_index = lax.axis_index("rep")
     levels = rep_count.bit_length() - 1
     orders = (list(range(levels)), [0] + list(range(levels - 1, 0, -1)))
     pieces = []
     for chunk in range(N_CHUNK):
-        partial = _ladder_products(amp4, chunk, received, order, starts, cd_ids, AB_DEV)
+        amp3 = lax.all_gather(local4[:, chunk], "own", axis=0, tiled=True)
+        if pieces:
+            amp3, pieces[-1] = lax.optimization_barrier((amp3, pieces[-1]))
+        partial = _ladder_products(amp3, received, order, starts, cd_ids, AB_DEV)
         half = partial.shape[1] // 2
         sides = [
             _halving_scatter(partial[:, h * half:(h + 1) * half], orders[h], rep_index, rep_count)

time: 219 us -> 251 us (1.15)
  blocking collectives: 0 us -> 56.1 us
  waiting for transfers between devices: 144 us -> 109 us
  Pallas kernels: 22.9 us -> 38 us
  other arithmetic: 7.4 us -> 4.68 us
  local copies, waits for them, and re-layouts: 11.6 us -> 14.3 us
    all_to_all x1 -> x0, waiting for transfers between devices: 95.9 us -> none  [on_device(): lax.all_to_all(integrals, ('own', 'rep'), split_axis=0, concat_axis=0, ti...]
    all_to_all x0 -> x1, blocking collectives: none -> 56.1 us  [on_device(): lax.all_to_all(integrals, ('own', 'rep'), split_axis=0, concat_axis=0, ti...]
    all_gather x1 -> x4, waiting for transfers between devices: 17.9 us -> 57.6 us  [on_device(): amp3 = lax.all_gather(local4[:, chunk], 'own', axis=0, tiled=True)]
    ppermute x12 -> x24, waiting for transfers between devices: 29.4 us -> 51.2 us  [_halving_scatter(): x = keep + lax.ppermute(send, 'rep', perm=pairs)]
    pallas_call x2 -> x4, Pallas kernels: 22.9 us -> 38 us  [_ladder_products(): pl.pallas_call(_ladder_kernel, grid_spec=grid_spec, out_shape=jax.ShapeDt...]
    all_to_all x1 -> x0, starting transfers between devices: 7.3 us -> none  [on_device(): lax.all_to_all(integrals, ('own', 'rep'), split_axis=0, concat_axis=0, ti...]
    ppermute x12 -> x24, starting transfers between devices: 11.6 us -> 16.4 us  [_halving_scatter(): x = keep + lax.ppermute(send, 'rep', perm=pairs)]
    squeeze x12 -> x24, local copies, waits for them, and re-layouts: 2.73 us -> 5.48 us  [_halving_scatter(): send = lax.dynamic_index_in_dim(x, 1 - mine, ax, keepdims=False)]
  transfers between devices with their start and end apart: 14 -> 28, of which waited for: 8 -> 24; matrix products, arithmetic and copies ran while one was open for 5% -> 3% of each run, Pallas kernels for 5% -> 0%
where the time goes in v3:
time: 251 us; the launch traced here: 252 us
  waiting for transfers between devices  109 us (43%)
  blocking collectives  56.1 us (22%)
  Pallas kernels  38 us (15%)
  starting transfers between devices  16.5 us (7%)
  local copies, waits for them, and re-layouts  14.3 us (6%)
  between operations  13.5 us (5%)
  other arithmetic  4.68 us (2%)
    all_gather x4, waiting for transfers between devices, on_device(): amp3 = lax.all_gather(local4[:, chunk], 'own', axis=0, tiled=True)  57.6 us
    all_to_all x1, blocking collectives, on_device(): lax.all_to_all(integrals, ('own', 'rep'), split_axis=0, concat_axis=0, ti...  56.1 us
    ppermute x24, waiting for transfers between devices, _halving_scatter(): x = keep + lax.ppermute(send, 'rep', perm=pairs)  51.2 us
    pallas_call x4, Pallas kernels, _ladder_products(): pl.pallas_call(_ladder_kernel, grid_spec=grid_spec, out_shape=jax.ShapeDt...  38 us
    ppermute x24, starting transfers between devices, _halving_scatter(): x = keep + lax.ppermute(send, 'rep', perm=pairs)  16.4 us
    slice x4, local copies, waits for them, and re-layouts, on_device(): partial[:, h * half:(h + 1) * half]  6.71 us
    squeeze x24, local copies, waits for them, and re-layouts, _halving_scatter(): send = lax.dynamic_index_in_dim(x, 1 - mine, ax, keepdims=False)  5.48 us
  transfers between devices with their start and end apart: 28, of which 24 were waited for; matrix products, arithmetic and copies ran while one was open for 3% of the time, Pallas kernels for 0%

profile of v3, /device:TPU:0, one launch (start us, length us, event | category | flops | bytes accessed | tf_op | source)
XLA Modules:
  0.0 251.9 jit_solution(12837235518345262845)
XLA Ops:
  6.5 56.1 %all_to_all.5.tiles_ref = bf16[64,128,128]{2,1,0:T(8,128)(2,1)} all-to-all(bf16[64,128,128]{2,1,0:T(8,128)(2,1)} %param.6), channel_id=1, replica_groups=mesh['own'=4,'rep'=8] {'own','rep'}, dimensions={0} | all-to-all | bytes 4194304 | tf_op jit(solution)/shard_map/all_to_all | solution.py:96
  66.4 24.4 %all-gather.11.cloned.1.call-done = bf16[8,1,32,2048]{3,2,1,0:T(8,128)(2,1)} async-done(((bf16[2,1,32,2048]{3,2,1,0:T(8,128)(2,1)}), bf16[8,1,32,2048]{3,2,1,0:T(8,128)(2,1)}) %all-gather.11.cloned.1.call-update) | async-done | bytes 1048592 | tf_op jit(solution)/shard_map/all_gather | solution.py:113
  90.8 9.5 %shard_map.55 = f32[256,2048]{1,0:T(8,128)} custom-call(s32[64]{0:T(128)} %select_reduce_fusion.order_ref, s32[17]{0:T(128)} %convert_reduce_fusion.1.starts_ref, s32[64]{0:T(128)} %reshape.70.cd_ref, bf16[8,32,2048]{2,1,0:T(8,128)(2,1)} %bitcast.130, bf16[64,128,128]{2,1,0:T(8,128)(2,1)} %all_to_all.5.tiles_ref), custom_call_target="tpu_custom_call" | custom-call | flops 536870912 | bytes 5242880 | tf_op jit(solution)/shard_map/pallas_call | solution.py:66
  100.3 1.7 fusion.5
  105.1 2.2 collective-permute-start.1
  107.6 6.5 %collective-permute-done.1 = f32[2,32,1024]{2,1,0:T(8,128)S(1)} collective-permute-done((f32[2,32,1024]{2,1,0:T(8,128)S(1)}, f32[2,32,1024]{2,1,0:T(8,128)S(1)}, u32[]{:S(2)}, u32[]{:S(2)}) %collective-permute-start.1) | collective-permute-done | bytes 262176 | tf_op jit(solution)/shard_map/ppermute | solution.py:86
  114.4 1.3 collective-permute-done.4
  116.9 2.5 collective-permute-done.2
  119.4 1.4 collective-permute-done.5
  120.9 11.4 %all-gather.9.cloned.1.call-done = bf16[8,1,32,2048]{3,2,1,0:T(8,128)(2,1)} async-done(((bf16[2,1,32,2048]{3,2,1,0:T(8,128)(2,1)}), bf16[8,1,32,2048]{3,2,1,0:T(8,128)(2,1)}) %all-gather.9.cloned.1.call-update) | async-done | bytes 1048592 | tf_op jit(solution)/shard_map/all_gather | solution.py:113
  132.3 9.5 %shard_map.56 = f32[256,2048]{1,0:T(8,128)} custom-call(s32[64]{0:T(128)} %select_reduce_fusion.order_ref, s32[17]{0:T(128)} %convert_reduce_fusion.1.starts_ref, s32[64]{0:T(128)} %reshape.70.cd_ref, bf16[8,32,2048]{2,1,0:T(8,128)(2,1)} %bitcast.128, bf16[64,128,128]{2,1,0:T(8,128)(2,1)} %all_to_all.5.tiles_ref), custom_call_target="tpu_custom_call" | custom-call | flops 536870912 | bytes 5242880 | tf_op jit(solution)/shard_map/pallas_call | solution.py:66
  141.8 1.7 fusion.4
  146.6 2.2 collective-permute-start.7
  149.1 6.5 %collective-permute-done.7 = f32[2,32,1024]{2,1,0:T(8,128)S(1)} collective-permute-done((f32[2,32,1024]{2,1,0:T(8,128)S(1)}, f32[2,32,1024]{2,1,0:T(8,128)S(1)}, u32[]{:S(2)}, u32[]{:S(2)}) %collective-permute-start.7) | collective-permute-done | bytes 262176 | tf_op jit(solution)/shard_map/ppermute | solution.py:86
  155.8 1.3 collective-permute-done.10
  158.4 2.5 collective-permute-done.8
  160.9 1.4 collective-permute-done.11
  162.3 11.4 %all-gather.13.cloned.1.call-done = bf16[8,1,32,2048]{3,2,1,0:T(8,128)(2,1)} async-done(((bf16[2,1,32,2048]{3,2,1,0:T(8,128)(2,1)}), bf16[8,1,32,2048]{3,2,1,0:T(8,128)(2,1)}) %all-gather.13.cloned.1.call-update) | async-done | bytes 1048592 | tf_op jit(solution)/shard_map/all_gather | solution.py:113
  173.8 9.5 %shard_map.57 = f32[256,2048]{1,0:T(8,128)} custom-call(s32[64]{0:T(128)} %select_reduce_fusion.order_ref, s32[17]{0:T(128)} %convert_reduce_fusion.1.starts_ref, s32[64]{0:T(128)} %reshape.70.cd_ref, bf16[8,32,2048]{2,1,0:T(8,128)(2,1)} %bitcast.129, bf16[64,128,128]{2,1,0:T(8,128)(2,1)} %all_to_all.5.tiles_ref), custom_call_target="tpu_custom_call" | custom-call | flops 536870912 | bytes 5242880 | tf_op jit(solution)/shard_map/pallas_call | solution.py:66
  183.2 1.7 fusion.3
  189.2 2.2 collective-permute-start.13
  191.7 6.5 %collective-permute-done.13 = f32[2,32,1024]{2,1,0:T(8,128)S(1)} collective-permute-done((f32[2,32,1024]{2,1,0:T(8,128)S(1)}, f32[2,32,1024]{2,1,0:T(8,128)S(1)}, u32[]{:S(2)}, u32[]{:S(2)}) %collective-permute-start.13) | collective-permute-done | bytes 262176 | tf_op jit(solution)/shard_map/ppermute | solution.py:86
  200.3 3.1 %collective-permute-done.14 = f32[32,1024]{1,0:T(8,128)S(1)} collective-permute-done((f32[32,1024]{1,0:T(8,128)S(1)}, f32[32,1024]{1,0:T(8,128)S(1)}, u32[]{:S(2)}, u32[]{:S(2)}) %collective-permute-start.14) | collective-permute-done | bytes 131104 | tf_op jit(solution)/shard_map/ppermute | solution.py:86
  203.5 1.4 collective-permute-done.17
  204.9 10.3 %all-gather.15.cloned.1.call-done = bf16[8,1,32,2048]{3,2,1,0:T(8,128)(2,1)} async-done(((bf16[2,1,32,2048]{3,2,1,0:T(8,128)(2,1)}), bf16[8,1,32,2048]{3,2,1,0:T(8,128)(2,1)}) %all-gather.15.cloned.1.call-update) | async-done | bytes 1048592 | tf_op jit(solution)/shard_map/all_gather | solution.py:113
  215.2 9.5 %shard_map.58 = f32[256,2048]{1,0:T(8,128)} custom-call(s32[64]{0:T(128)} %select_reduce_fusion.order_ref, s32[17]{0:T(128)} %convert_reduce_fusion.1.starts_ref, s32[64]{0:T(128)} %reshape.70.cd_ref, bf16[8,32,2048]{2,1,0:T(8,128)(2,1)} %bitcast.127, bf16[64,128,128]{2,1,0:T(8,128)(2,1)} %all_to_all.5.tiles_ref), custom_call_target="tpu_custom_call" | custom-call | flops 536870912 | bytes 5242880 | tf_op jit(solution)/shard_map/pallas_call | solution.py:66
  224.7 1.7 fusion.2
  228.5 2.2 collective-permute-start.19
  231.0 6.5 %collective-permute-done.19 = f32[2,32,1024]{2,1,0:T(8,128)S(1)} collective-permute-done((f32[2,32,1024]{2,1,0:T(8,128)S(1)}, f32[2,32,1024]{2,1,0:T(8,128)S(1)}, u32[]{:S(2)}, u32[]{:S(2)}) %collective-permute-start.19) | collective-permute-done | bytes 262176 | tf_op jit(solution)/shard_map/ppermute | solution.py:86
  237.8 1.3 collective-permute-done.22
  240.1 2.7 %collective-permute-done.20 = f32[32,1024]{1,0:T(8,128)S(1)} collective-permute-done((f32[32,1024]{1,0:T(8,128)S(1)}, f32[32,1024]{1,0:T(8,128)S(1)}, u32[]{:S(2)}, u32[]{:S(2)}) %collective-permute-start.20) | collective-permute-done | bytes 131104 | tf_op jit(solution)/shard_map/ppermute | solution.py:86
  242.9 1.4 collective-permute-done.23
  (108 shorter events, 25.1 us)
Async XLA Ops:
  6.5 56.1 %copy-start = (bf16[256,2048]{1,0:T(8,128)(2,1)S(1)}, bf16[256,2048]{1,0:T(8,128)(2,1)}, u32[]{:S(2)}) copy-start(bf16[256,2048]{1,0:T(8,128)(2,1)} %param.5) | copy-start | bytes 3145732
  6.5 84.3 %all-gather.11.cloned.1.call-start = ((), (), s32[]{:S(2)}) async-start(), calls=%async_computation.2 | async-start | bytes 1310720 | tf_op jit(solution)/shard_map/all_gather | solution.py:113
  62.7 1.1 copy-start.1
  62.7 1.3 copy-start.3
  62.7 1.5 copy-start.2
  63.7 68.6 %all-gather.9.cloned.1.call-start = ((), (), s32[]{:S(2)}) async-start(), calls=%async_computation.1 | async-start | bytes 1310720 | tf_op jit(solution)/shard_map/all_gather | solution.py:113
  102.8 2.1 collective-permute-start
  103.7 3.6 %collective-permute-start.3 = (f32[2,2,32,1024]{3,2,1,0:T(8,128)}, f32[2,2,32,1024]{3,2,1,0:T(8,128)S(1)}, u32[]{:S(2)}, u32[]{:S(2)}) collective-permute-start(f32[2,2,32,1024]{3,2,1,0:T(8,128)} %dynamic-slice_bitcast_fusion.6), channel_id=1, source_target_pairs={{0,1},{1,0},{2,3},{3,2},{4,5},{5,4},{6,7},{7,6},{8,9},{9,8},{10,11... | collective-permute-start | bytes 1572872 | tf_op jit(solution)/shard_map/ppermute | solution.py:86
  104.2 69.5 %all-gather.13.cloned.1.call-start = ((), (), s32[]{:S(2)}) async-start(), calls=%async_computation.3 | async-start | bytes 1310720 | tf_op jit(solution)/shard_map/all_gather | solution.py:113
  105.1 9.0 %collective-permute-start.1 = (f32[2,32,1024]{2,1,0:T(8,128)S(1)}, f32[2,32,1024]{2,1,0:T(8,128)S(1)}, u32[]{:S(2)}, u32[]{:S(2)}) collective-permute-start(f32[2,32,1024]{2,1,0:T(8,128)S(1)} %dynamic-slice_bitcast_fusion.15), channel_id=1, source_target_pairs={{0,2},{1,3},{2,0},{3,1},{4,6},{5,7},{6,4},{7,5},{8,10},{9,11},{10,... | collective-permute-start | bytes 786440 | tf_op jit(solution)/shard_map/ppermute | solution.py:86
  107.4 8.4 %collective-permute-start.4 = (f32[2,32,1024]{2,1,0:T(8,128)S(1)}, f32[2,32,1024]{2,1,0:T(8,128)S(1)}, u32[]{:S(2)}, u32[]{:S(2)}) collective-permute-start(f32[2,32,1024]{2,1,0:T(8,128)S(1)} %dynamic-slice_bitcast_fusion.14), channel_id=1, source_target_pairs={{0,4},{1,5},{2,6},{3,7},{4,0},{5,1},{6,2},{7,3},{8,12},{9,13},{10,... | collective-permute-start | bytes 786440 | tf_op jit(solution)/shard_map/ppermute | solution.py:86
  114.1 5.3 %collective-permute-start.2 = (f32[32,1024]{1,0:T(8,128)S(1)}, f32[32,1024]{1,0:T(8,128)S(1)}, u32[]{:S(2)}, u32[]{:S(2)}) collective-permute-start(f32[32,1024]{1,0:T(8,128)S(1)} %dynamic-slice_bitcast_fusion.23), channel_id=1, source_target_pairs={{0,4},{1,5},{2,6},{3,7},{4,0},{5,1},{6,2},{7,3},{8,12},{9,13},{10,... | collective-permute-start | bytes 393224 | tf_op jit(solution)/shard_map/ppermute | solution.py:86
  115.8 5.0 %collective-permute-start.5 = (f32[32,1024]{1,0:T(8,128)S(1)}, f32[32,1024]{1,0:T(8,128)S(1)}, u32[]{:S(2)}, u32[]{:S(2)}) collective-permute-start(f32[32,1024]{1,0:T(8,128)S(1)} %dynamic-slice_bitcast_fusion.22), channel_id=1, source_target_pairs={{0,2},{1,3},{2,0},{3,1},{4,6},{5,7},{6,4},{7,5},{8,10},{9,11},{10,... | collective-permute-start | bytes 393224 | tf_op jit(solution)/shard_map/ppermute | solution.py:86
  144.3 2.1 collective-permute-start.6
  145.1 3.6 %collective-permute-start.9 = (f32[2,2,32,1024]{3,2,1,0:T(8,128)}, f32[2,2,32,1024]{3,2,1,0:T(8,128)S(1)}, u32[]{:S(2)}, u32[]{:S(2)}) collective-permute-start(f32[2,2,32,1024]{3,2,1,0:T(8,128)} %dynamic-slice_bitcast_fusion.4), channel_id=1, source_target_pairs={{0,1},{1,0},{2,3},{3,2},{4,5},{5,4},{6,7},{7,6},{8,9},{9,8},{10,11... | collective-permute-start | bytes 1572872 | tf_op jit(solution)/shard_map/ppermute | solution.py:86
  145.7 69.5 %all-gather.15.cloned.1.call-start = ((), (), s32[]{:S(2)}) async-start(), calls=%async_computation.4 | async-start | bytes 1310720 | tf_op jit(solution)/shard_map/all_gather | solution.py:113
  146.6 9.0 %collective-permute-start.7 = (f32[2,32,1024]{2,1,0:T(8,128)S(1)}, f32[2,32,1024]{2,1,0:T(8,128)S(1)}, u32[]{:S(2)}, u32[]{:S(2)}) collective-permute-start(f32[2,32,1024]{2,1,0:T(8,128)S(1)} %dynamic-slice_bitcast_fusion.13), channel_id=1, source_target_pairs={{0,2},{1,3},{2,0},{3,1},{4,6},{5,7},{6,4},{7,5},{8,10},{9,11},{10,... | collective-permute-start | bytes 786440 | tf_op jit(solution)/shard_map/ppermute | solution.py:86
  148.8 8.4 %collective-permute-start.10 = (f32[2,32,1024]{2,1,0:T(8,128)S(1)}, f32[2,32,1024]{2,1,0:T(8,128)S(1)}, u32[]{:S(2)}, u32[]{:S(2)}) collective-permute-start(f32[2,32,1024]{2,1,0:T(8,128)S(1)} %dynamic-slice_bitcast_fusion.12), channel_id=1, source_target_pairs={{0,4},{1,5},{2,6},{3,7},{4,0},{5,1},{6,2},{7,3},{8,12},{9,13},{10,... | collective-permute-start | bytes 786440 | tf_op jit(solution)/shard_map/ppermute | solution.py:86
  155.6 5.3 %collective-permute-start.8 = (f32[32,1024]{1,0:T(8,128)S(1)}, f32[32,1024]{1,0:T(8,128)S(1)}, u32[]{:S(2)}, u32[]{:S(2)}) collective-permute-start(f32[32,1024]{1,0:T(8,128)S(1)} %dynamic-slice_bitcast_fusion.21), channel_id=1, source_target_pairs={{0,4},{1,5},{2,6},{3,7},{4,0},{5,1},{6,2},{7,3},{8,12},{9,13},{10,... | collective-permute-start | bytes 393224 | tf_op jit(solution)/shard_map/ppermute | solution.py:86
  157.2 5.0 %collective-permute-start.11 = (f32[32,1024]{1,0:T(8,128)S(1)}, f32[32,1024]{1,0:T(8,128)S(1)}, u32[]{:S(2)}, u32[]{:S(2)}) collective-permute-start(f32[32,1024]{1,0:T(8,128)S(1)} %dynamic-slice_bitcast_fusion.20), channel_id=1, source_target_pairs={{0,2},{1,3},{2,0},{3,1},{4,6},{5,7},{6,4},{7,5},{8,10},{9,11},{10,... | collective-permute-start | bytes 393224 | tf_op jit(solution)/shard_map/ppermute | solution.py:86
  185.8 2.3 collective-permute-start.12
  186.6 4.7 %collective-permute-start.15 = (f32[2,2,32,1024]{3,2,1,0:T(8,128)}, f32[2,2,32,1024]{3,2,1,0:T(8,128)S(1)}, u32[]{:S(2)}, u32[]{:S(2)}) collective-permute-start(f32[2,2,32,1024]{3,2,1,0:T(8,128)} %dynamic-slice_bitcast_fusion.2), channel_id=1, source_target_pairs={{0,1},{1,0},{2,3},{3,2},{4,5},{5,4},{6,7},{7,6},{8,9},{9,8},{10,11... | collective-permute-start | bytes 1572872 | tf_op jit(solution)/shard_map/ppermute | solution.py:86
  189.2 9.0 %collective-permute-start.13 = (f32[2,32,1024]{2,1,0:T(8,128)S(1)}, f32[2,32,1024]{2,1,0:T(8,128)S(1)}, u32[]{:S(2)}, u32[]{:S(2)}) collective-permute-start(f32[2,32,1024]{2,1,0:T(8,128)S(1)} %dynamic-slice_bitcast_fusion.11), channel_id=1, source_target_pairs={{0,2},{1,3},{2,0},{3,1},{4,6},{5,7},{6,4},{7,5},{8,10},{9,11},{10,... | collective-permute-start | bytes 786440 | tf_op jit(solution)/shard_map/ppermute | solution.py:86
  191.4 8.4 %collective-permute-start.16 = (f32[2,32,1024]{2,1,0:T(8,128)S(1)}, f32[2,32,1024]{2,1,0:T(8,128)S(1)}, u32[]{:S(2)}, u32[]{:S(2)}) collective-permute-start(f32[2,32,1024]{2,1,0:T(8,128)S(1)} %dynamic-slice_bitcast_fusion.10), channel_id=1, source_target_pairs={{0,4},{1,5},{2,6},{3,7},{4,0},{5,1},{6,2},{7,3},{8,12},{9,13},{10,... | collective-permute-start | bytes 786440 | tf_op jit(solution)/shard_map/ppermute | solution.py:86
  198.2 5.3 %collective-permute-start.14 = (f32[32,1024]{1,0:T(8,128)S(1)}, f32[32,1024]{1,0:T(8,128)S(1)}, u32[]{:S(2)}, u32[]{:S(2)}) collective-permute-start(f32[32,1024]{1,0:T(8,128)S(1)} %dynamic-slice_bitcast_fusion.19), channel_id=1, source_target_pairs={{0,4},{1,5},{2,6},{3,7},{4,0},{5,1},{6,2},{7,3},{8,12},{9,13},{10,... | collective-permute-start | bytes 393224 | tf_op jit(solution)/shard_map/ppermute | solution.py:86
  199.9 5.0 %collective-permute-start.17 = (f32[32,1024]{1,0:T(8,128)S(1)}, f32[32,1024]{1,0:T(8,128)S(1)}, u32[]{:S(2)}, u32[]{:S(2)}) collective-permute-start(f32[32,1024]{1,0:T(8,128)S(1)} %dynamic-slice_bitcast_fusion.18), channel_id=1, source_target_pairs={{0,2},{1,3},{2,0},{3,1},{4,6},{5,7},{6,4},{7,5},{8,10},{9,11},{10,... | collective-permute-start | bytes 393224 | tf_op jit(solution)/shard_map/ppermute | solution.py:86
  226.4 2.0 collective-permute-start.18
  226.6 4.1 %collective-permute-start.21 = (f32[2,2,32,1024]{3,2,1,0:T(8,128)S(1)}, f32[2,2,32,1024]{3,2,1,0:T(8,128)S(1)}, u32[]{:S(2)}, u32[]{:S(2)}) collective-permute-start(f32[2,2,32,1024]{3,2,1,0:T(8,128)S(1)} %dynamic-slice_bitcast_fusion), channel_id=1, source_target_pairs={{0,1},{1,0},{2,3},{3,2},{4,5},{5,4},{6,7},{7,6},{8,9},{9,8},{10,11... | collective-permute-start | bytes 1572872 | tf_op jit(solution)/shard_map/ppermute | solution.py:86
  228.5 9.0 %collective-permute-start.19 = (f32[2,32,1024]{2,1,0:T(8,128)S(1)}, f32[2,32,1024]{2,1,0:T(8,128)S(1)}, u32[]{:S(2)}, u32[]{:S(2)}) collective-permute-start(f32[2,32,1024]{2,1,0:T(8,128)S(1)} %dynamic-slice_bitcast_fusion.9), channel_id=1, source_target_pairs={{0,2},{1,3},{2,0},{3,1},{4,6},{5,7},{6,4},{7,5},{8,10},{9,11},{10,... | collective-permute-start | bytes 786440 | tf_op jit(solution)/shard_map/ppermute | solution.py:86
  230.8 8.4 %collective-permute-start.22 = (f32[2,32,1024]{2,1,0:T(8,128)S(1)}, f32[2,32,1024]{2,1,0:T(8,128)S(1)}, u32[]{:S(2)}, u32[]{:S(2)}) collective-permute-start(f32[2,32,1024]{2,1,0:T(8,128)S(1)} %dynamic-slice_bitcast_fusion.8), channel_id=1, source_target_pairs={{0,4},{1,5},{2,6},{3,7},{4,0},{5,1},{6,2},{7,3},{8,12},{9,13},{10,... | collective-permute-start | bytes 786440 | tf_op jit(solution)/shard_map/ppermute | solution.py:86
  237.6 5.3 %collective-permute-start.20 = (f32[32,1024]{1,0:T(8,128)S(1)}, f32[32,1024]{1,0:T(8,128)S(1)}, u32[]{:S(2)}, u32[]{:S(2)}) collective-permute-start(f32[32,1024]{1,0:T(8,128)S(1)} %dynamic-slice_bitcast_fusion.17), channel_id=1, source_target_pairs={{0,4},{1,5},{2,6},{3,7},{4,0},{5,1},{6,2},{7,3},{8,12},{9,13},{10,... | collective-permute-start | bytes 393224 | tf_op jit(solution)/shard_map/ppermute | solution.py:86
  239.2 5.0 %collective-permute-start.23 = (f32[32,1024]{1,0:T(8,128)S(1)}, f32[32,1024]{1,0:T(8,128)S(1)}, u32[]{:S(2)}, u32[]{:S(2)}) collective-permute-start(f32[32,1024]{1,0:T(8,128)S(1)} %dynamic-slice_bitcast_fusion.16), channel_id=1, source_target_pairs={{0,2},{1,3},{2,0},{3,1},{4,6},{5,7},{6,4},{7,5},{8,10},{9,11},{10,... | collective-permute-start | bytes 393224 | tf_op jit(solution)/shard_map/ppermute | solution.py:86
Sparse Core Ops, SparseCore 0:
  63.8 26.9 all-gather.10
  104.3 27.9 all-gather.8
  145.8 27.9 all-gather.12
  187.3 27.9 all-gather.14

commit v4 on v1

v4 whole, which is shorter than its diff:
```python
import functools

import jax
import jax.numpy as jnp
from jax import lax
from jax.experimental import pallas as pl
from jax.experimental.pallas import tpu as pltpu
from jax.sharding import PartitionSpec as P

AB_DEV = 16
N_CHUNK = 4


def _slot_order(ab_ids, live_mask, ab_count):
    n = ab_ids.shape[0]
    key = jnp.where(live_mask, ab_ids, ab_count)
    idx = jnp.arange(n, dtype=jnp.int32)
    earlier = (key[None, :] < key[:, None]) | ((key[None, :] == key[:, None]) & (idx[None, :] < idx[:, None]))
    rank = jnp.sum(earlier.astype(jnp.int32), axis=1)
    order = jnp.sum(jnp.where(rank[None, :] == idx[:, None], idx[None, :], 0), axis=1).astype(jnp.int32)
    bounds = jnp.arange(ab_count + 1, dtype=jnp.int32)
    starts = jnp.sum((key[None, :] < bounds[:, None]).astype(jnp.int32), axis=1).astype(jnp.int32)
    return order, starts


def _ladder_kernel(order_ref, starts_ref, ab_ref, cd_ref, amp_ref, tiles_ref, out_ref, weight_ref):
    step = pl.program_id(0)
    tile = tiles_ref.shape[-1]
    groups, part, width = amp_ref.shape
    per_step = out_ref.shape[1] // tile
    weight_ref[...] = jnp.zeros(weight_ref.shape, weight_ref.dtype)
    first = step * per_step

    def place(t, carry):
        i = order_ref[t]
        row = pl.multiple_of(cd_ref[i] * tile, tile)
        col = pl.multiple_of((ab_ref[i] - first) * tile, tile)
        weight_ref[pl.ds(row, tile), pl.ds(col, tile)] = tiles_ref[i]
        return carry

    lax.fori_loop(starts_ref[first], starts_ref[first + per_step], place, 0)
    lhs = amp_ref[...].reshape(groups * part, width)
    out_ref[...] = jnp.dot(lhs, weight_ref[...], preferred_element_type=jnp.float32)


def _ladder_products(amp3, tiles, order, starts, ab_ids, cd_ids, ab_count):
    groups, part, width = amp3.shape
    rows = groups * part
    n, tile, _ = tiles.shape
    per_step = 2 if ab_count % 2 == 0 else 1
    cost = pl.CostEstimate(
        flops=2 * rows * width * ab_count * tile,
        transcendentals=0,
        bytes_accessed=rows * width * 2 + tiles.size * 2 + rows * ab_count * tile * 4,
    )
    grid_spec = pltpu.PrefetchScalarGridSpec(
        num_scalar_prefetch=4,
        grid=(ab_count // per_step,),
        in_specs=[
            pl.BlockSpec((groups, part, width), lambda j, *_: (0, 0, 0)),
            pl.BlockSpec((n, tile, tile), lambda j, *_: (0, 0, 0)),
        ],
        out_specs=pl.BlockSpec((rows, per_step * tile), lambda j, *_: (0, j)),
        scratch_shapes=[pltpu.VMEM((width, per_step * tile), tiles.dtype)],
    )
    return pl.pallas_call(
        _ladder_kernel,
        grid_spec=grid_spec,
        out_shape=jax.ShapeDtypeStruct((rows, ab_count * tile), jnp.float32),
        cost_estimate=cost,
    )(order, starts, ab_ids, cd_ids, amp3, tiles)


class _Halving:
    def __init__(self, partial, bit_order, rep_count):
        self.levels = rep_count.bit_length() - 1
        self.part = partial.shape[0] // rep_count
        self.width = partial.shape[-1]
        self.x = partial.reshape((2,) * self.levels + (self.part, self.width))
        self.axis_bits = list(range(self.levels - 1, -1, -1))
        self.todo = list(bit_order)
        self.rep_count = rep_count

    def advance(self, rep_index):
        if not self.todo:
            return
        bit = self.todo.pop(0)
        ax = self.axis_bits.index(bit)
        mine = (rep_index >> bit) & 1
        keep = lax.dynamic_index_in_dim(self.x, mine, ax, keepdims=False)
        send = lax.dynamic_index_in_dim(self.x, 1 - mine, ax, keepdims=False)
        pairs = [(i, i ^ (1 << bit)) for i in range(self.rep_count)]
        self.x = keep + lax.ppermute(send, "rep", perm=pairs)
        self.axis_bits.pop(ax)

    def result(self):
        return self.x.reshape(self.part, self.width)


def on_device(amplitudes, integrals, ab_list, cd_list, live_count):
    own_count = lax.axis_size("own")
    rep_count = lax.axis_size("rep")
    peer_count = own_count * rep_count
    slot_count = integrals.shape[0] // peer_count
    received = lax.all_to_all(integrals, ("own", "rep"), split_axis=0, concat_axis=0, tiled=True)
    ab_ids = ab_list.reshape(-1)
    cd_ids = cd_list.reshape(-1)
    live_mask = (
        jnp.arange(slot_count, dtype=jnp.int32)[None, :] < live_count.reshape(peer_count, 1)
    ).reshape(-1)
    order, starts = _slot_order(ab_ids, live_mask, AB_DEV)
    local_rows, width = amplitudes.shape
    subs = rep_count // own_count
    part = local_rows // (subs * N_CHUNK)
    local4 = amplitudes.reshape(subs, N_CHUNK, part, width)
    rep_index = lax.axis_index("rep")
    levels = rep_count.bit_length() - 1
    orders = (list(range(levels)), [0] + list(range(levels - 1, 0, -1)))
    gathered = [lax.all_gather(local4[:, c], "own", axis=0, tiled=True) for c in range(N_CHUNK)]
    flows = []
    for chunk in range(N_CHUNK):
        for flow in flows:
            flow.advance(rep_index)
        if flows:
            amp3, held = lax.optimization_barrier((gathered[chunk], [f.x for f in flows]))
            for flow, x in zip(flows, held):
                flow.x = x
        else:
            amp3 = gathered[chunk]
        partial = _ladder_products(amp3, received, order, starts, ab_ids, cd_ids, AB_DEV)
        half = partial.shape[1] // 2
        flows.extend(
            _Halving(partial[:, h * half:(h + 1) * half], orders[h], rep_count) for h in range(2)
        )
    while any(flow.todo for flow in flows):
        for flow in flows:
            flow.advance(rep_index)
    pieces = [
        jnp.concatenate([flows[2 * c].result(), flows[2 * c + 1].result()], axis=1)
        for c in range(N_CHUNK)
    ]
    return jnp.concatenate(pieces, axis=0)


def solution(mesh):
    return jax.shard_map(
        on_device,
        mesh=mesh,
        in_specs=(
            P("own", "rep"),
            P(("own", "rep"), None, None),
            P(("own", "rep"), None, None),
            P(("own", "rep"), None, None),
            P(("own", "rep"), None),
        ),
        out_specs=P("rep", "own"),
        check_vma=False,
    )
```

time: 225 us -> 201 us (0.89)
  waiting for transfers between devices: 186 us -> 109 us
  starting transfers between devices: 7.35 us -> 26.9 us
  Pallas kernels: 15.4 us -> 34.2 us
  local copies, waits for them, and re-layouts: 1.04 us -> 11.7 us
  other arithmetic: 1.6 us -> 4.69 us
    all_to_all x1, waiting for transfers between devices: 95.9 us -> 8.25 us  [on_device(): lax.all_to_all(integrals, ('own', 'rep'), split_axis=0, concat_axis=0, ti...]
    reduce_scatter x1 -> x0, waiting for transfers between devices: 71.8 us -> none  [on_device(): return lax.psum_scatter(flattened, 'rep', scatter_dimension=0, tiled=True)]
    all_gather x1 -> x4, waiting for transfers between devices: 17.9 us -> 68.9 us  [on_device(): lax.all_gather(local4[:, c], 'own', axis=0, tiled=True)]
    ppermute x0 -> x24, waiting for transfers between devices: none -> 30.7 us  [advance(): self.x = keep + lax.ppermute(send, 'rep', perm=pairs)]
    ppermute x0 -> x24, starting transfers between devices: none -> 19.5 us  [advance(): self.x = keep + lax.ppermute(send, 'rep', perm=pairs)]
    pallas_call x1 -> x4, Pallas kernels: 15.4 us -> 34.2 us  [_ladder_products(): pl.pallas_call(_ladder_kernel, grid_spec=grid_spec, out_shape=jax.ShapeDt...]
    slice x0 -> x5, local copies, waits for them, and re-layouts: none -> 7.85 us  [the longest x4 6.87 us: on_device(): partial[:, h * half:(h + 1) * half]]
  transfers between devices with their start and end apart: 3 -> 29, of which waited for: 3 -> 16; matrix products, arithmetic and copies ran while one was open for 1% -> 7% of each run, Pallas kernels for 0% -> 17%
where the time goes in v4:
time: 201 us; the launch traced here: 200 us
  waiting for transfers between devices  109 us (54%)
  Pallas kernels  34.2 us (17%)
  starting transfers between devices  26.9 us (13%)
  between operations  13.6 us (7%)
  local copies, waits for them, and re-layouts  11.7 us (6%)
  other arithmetic  4.69 us (2%)
    all_gather x4, waiting for transfers between devices, on_device(): lax.all_gather(local4[:, c], 'own', axis=0, tiled=True)  68.9 us
    pallas_call x4, Pallas kernels, _ladder_products(): pl.pallas_call(_ladder_kernel, grid_spec=grid_spec, out_shape=jax.ShapeDt...  34.2 us
    ppermute x24, waiting for transfers between devices, advance(): self.x = keep + lax.ppermute(send, 'rep', perm=pairs)  30.7 us
    ppermute x24, starting transfers between devices, advance(): self.x = keep + lax.ppermute(send, 'rep', perm=pairs)  19.5 us
    all_to_all x1, waiting for transfers between devices, on_device(): lax.all_to_all(integrals, ('own', 'rep'), split_axis=0, concat_axis=0, ti...  8.25 us
    all_to_all x1, starting transfers between devices, on_device(): lax.all_to_all(integrals, ('own', 'rep'), split_axis=0, concat_axis=0, ti...  7.3 us
    slice x4, local copies, waits for them, and re-layouts, on_device(): partial[:, h * half:(h + 1) * half]  6.87 us
  transfers between devices with their start and end apart: 29, of which 16 were waited for; matrix products, arithmetic and copies ran while one was open for 7% of the time, Pallas kernels for 17%

profile of v4, /device:TPU:0, one launch (start us, length us, event | category | flops | bytes accessed | tf_op | source)
XLA Modules:
  0.0 200.4 jit_solution(11404019473947716508)
XLA Ops:
  6.5 7.3 %all-to-all-start = ((bf16[64,128,128]{2,1,0:T(8,128)(2,1)}), bf16[64,128,128]{2,1,0:T(8,128)(2,1)S(1)}, u32[]{:S(2)}, u32[]{:S(2)}) async-start(bf16[64,128,128]{2,1,0:T(8,128)(2,1)} %param.6), calls=%async_computation | async-start | bytes 4194304 | tf_op jit(solution)/shard_map/all_to_all | solution.py:105
  19.2 52.0 %all-gather.15.cloned.1.call-done = bf16[8,1,32,2048]{3,2,1,0:T(8,128)(2,1)} async-done(((bf16[2,1,32,2048]{3,2,1,0:T(8,128)(2,1)}), bf16[8,1,32,2048]{3,2,1,0:T(8,128)(2,1)}) %all-gather.15.cloned.1.call-update) | async-done | bytes 1048592 | tf_op jit(solution)/shard_map/all_gather | solution.py:119
  71.2 8.2 %all-to-all-done.tiles_ref = bf16[64,128,128]{2,1,0:T(8,128)(2,1)S(1)} async-done(((bf16[64,128,128]{2,1,0:T(8,128)(2,1)}), bf16[64,128,128]{2,1,0:T(8,128)(2,1)S(1)}, u32[]{:S(2)}, u32[]{:S(2)}) %all-to-all-start) | async-done | bytes 2097184 | tf_op jit(solution)/shard_map/all_to_all | solution.py:105
  79.4 1.4 copy-done
  80.8 8.6 %shard_map.55 = f32[256,2048]{1,0:T(8,128)} custom-call(s32[64]{0:T(128)} %select_reduce_fusion.order_ref, s32[17]{0:T(128)} %convert_reduce_fusion.1.starts_ref, s32[64]{0:T(128)} %copy-done.5, s32[64]{0:T(128)} %reshape.70.cd_ref, bf16[8,32,2048]{2,1,0:T(8,128)(2,1)} %bitcast.131, bf16[64,128,128]{2,1,0:T(8,128)(2,1)} %copy-done), custom_call_target="tpu_custom_call" | custom-call | flops 2147483648 | bytes 5242880 | tf_op jit(solution)/shard_map/pallas_call | solution.py:66
  89.3 1.7 fusion.5
  94.4 4.0 %all-gather.13.cloned.1.call-done = bf16[8,1,32,2048]{3,2,1,0:T(8,128)(2,1)} async-done(((bf16[2,1,32,2048]{3,2,1,0:T(8,128)(2,1)}), bf16[8,1,32,2048]{3,2,1,0:T(8,128)(2,1)}) %all-gather.13.cloned.1.call-update) | async-done | bytes 1048592 | tf_op jit(solution)/shard_map/all_gather | solution.py:119
  98.4 8.5 %shard_map.56 = f32[256,2048]{1,0:T(8,128)} custom-call(s32[64]{0:T(128)} %select_reduce_fusion.order_ref, s32[17]{0:T(128)} %convert_reduce_fusion.1.starts_ref, s32[64]{0:T(128)} %copy-done.5, s32[64]{0:T(128)} %reshape.70.cd_ref, bf16[8,32,2048]{2,1,0:T(8,128)(2,1)} %bitcast.130, bf16[64,128,128]{2,1,0:T(8,128)(2,1)} %copy-done), custom_call_target="tpu_custom_call" | custom-call | flops 2147483648 | bytes 5242880 | tf_op jit(solution)/shard_map/pallas_call | solution.py:66
  107.0 1.8 fusion.4
  108.8 1.4 collective-permute-start.3
  110.3 1.5 collective-permute-start.2
  112.2 4.4 %collective-permute-done.3 = f32[2,32,1024]{2,1,0:T(8,128)S(1)} collective-permute-done((f32[2,32,1024]{2,1,0:T(8,128)S(1)}, f32[2,32,1024]{2,1,0:T(8,128)S(1)}, u32[]{:S(2)}, u32[]{:S(2)}) %collective-permute-start.3) | collective-permute-done | bytes 262176 | tf_op jit(solution)/shard_map/ppermute | solution.py:93
  116.6 2.5 %collective-permute-done.2 = f32[2,32,1024]{2,1,0:T(8,128)S(1)} collective-permute-done((f32[2,32,1024]{2,1,0:T(8,128)S(1)}, f32[2,32,1024]{2,1,0:T(8,128)S(1)}, u32[]{:S(2)}, u32[]{:S(2)}) %collective-permute-start.2) | collective-permute-done | bytes 262176 | tf_op jit(solution)/shard_map/ppermute | solution.py:93
  119.3 8.1 %all-gather.11.cloned.1.call-done = bf16[8,1,32,2048]{3,2,1,0:T(8,128)(2,1)} async-done(((bf16[2,1,32,2048]{3,2,1,0:T(8,128)(2,1)}), bf16[8,1,32,2048]{3,2,1,0:T(8,128)(2,1)}) %all-gather.11.cloned.1.call-update) | async-done | bytes 1048592 | tf_op jit(solution)/shard_map/all_gather | solution.py:119
  127.5 8.5 %shard_map.57 = f32[256,2048]{1,0:T(8,128)} custom-call(s32[64]{0:T(128)} %select_reduce_fusion.order_ref, s32[17]{0:T(128)} %convert_reduce_fusion.1.starts_ref, s32[64]{0:T(128)} %copy-done.5, s32[64]{0:T(128)} %reshape.70.cd_ref, bf16[8,32,2048]{2,1,0:T(8,128)(2,1)} %bitcast.129, bf16[64,128,128]{2,1,0:T(8,128)(2,1)} %copy-done), custom_call_target="tpu_custom_call" | custom-call | flops 2147483648 | bytes 5242880 | tf_op jit(solution)/shard_map/pallas_call | solution.py:66
  136.0 1.7 fusion.3
  138.5 1.5 collective-permute-start.9
  140.0 1.6 collective-permute-start.7
  142.2 4.3 %collective-permute-done.7 = f32[32,1024]{1,0:T(8,128)S(1)} collective-permute-done((f32[32,1024]{1,0:T(8,128)S(1)}, f32[32,1024]{1,0:T(8,128)S(1)}, u32[]{:S(2)}, u32[]{:S(2)}) %collective-permute-start.7) | collective-permute-done | bytes 131104 | tf_op jit(solution)/shard_map/ppermute | solution.py:93
  147.1 4.3 %collective-permute-done.6 = f32[32,1024]{1,0:T(8,128)S(1)} collective-permute-done((f32[32,1024]{1,0:T(8,128)S(1)}, f32[32,1024]{1,0:T(8,128)S(1)}, u32[]{:S(2)}, u32[]{:S(2)}) %collective-permute-start.6) | collective-permute-done | bytes 131104 | tf_op jit(solution)/shard_map/ppermute | solution.py:93
  151.7 4.7 %all-gather.9.cloned.1.call-done = bf16[8,1,32,2048]{3,2,1,0:T(8,128)(2,1)} async-done(((bf16[2,1,32,2048]{3,2,1,0:T(8,128)(2,1)}), bf16[8,1,32,2048]{3,2,1,0:T(8,128)(2,1)}) %all-gather.9.cloned.1.call-update) | async-done | bytes 1048592 | tf_op jit(solution)/shard_map/all_gather | solution.py:119
  156.5 1.6 collective-permute-start.12
  158.1 1.4 collective-permute-start.13
  160.8 8.5 %shard_map.58 = f32[256,2048]{1,0:T(8,128)} custom-call(s32[64]{0:T(128)} %select_reduce_fusion.order_ref, s32[17]{0:T(128)} %convert_reduce_fusion.1.starts_ref, s32[64]{0:T(128)} %copy-done.5, s32[64]{0:T(128)} %reshape.70.cd_ref, bf16[8,32,2048]{2,1,0:T(8,128)(2,1)} %bitcast.128, bf16[64,128,128]{2,1,0:T(8,128)(2,1)} %copy-done), custom_call_target="tpu_custom_call" | custom-call | flops 2147483648 | bytes 5242880 | tf_op jit(solution)/shard_map/pallas_call | solution.py:66
  169.4 1.7 fusion.2
  171.9 1.5 collective-permute-start.15
  173.5 1.4 collective-permute-start.17
  174.9 2.5 %collective-permute-done.15 = f32[32,1024]{1,0:T(8,128)S(1)} collective-permute-done((f32[32,1024]{1,0:T(8,128)S(1)}, f32[32,1024]{1,0:T(8,128)S(1)}, u32[]{:S(2)}, u32[]{:S(2)}) %collective-permute-start.15) | collective-permute-done | bytes 131104 | tf_op jit(solution)/shard_map/ppermute | solution.py:93
  178.9 1.4 collective-permute-start.19
  181.0 5.0 %collective-permute-done.19 = f32[2,32,1024]{2,1,0:T(8,128)S(1)} collective-permute-done((f32[2,32,1024]{2,1,0:T(8,128)S(1)}, f32[2,32,1024]{2,1,0:T(8,128)S(1)}, u32[]{:S(2)}, u32[]{:S(2)}) %collective-permute-start.19) | collective-permute-done | bytes 262176 | tf_op jit(solution)/shard_map/ppermute | solution.py:93
  188.1 3.0 %collective-permute-done.20 = f32[32,1024]{1,0:T(8,128)S(1)} collective-permute-done((f32[32,1024]{1,0:T(8,128)S(1)}, f32[32,1024]{1,0:T(8,128)S(1)}, u32[]{:S(2)}, u32[]{:S(2)}) %collective-permute-start.20) | collective-permute-done | bytes 131104 | tf_op jit(solution)/shard_map/ppermute | solution.py:93
  191.1 1.7 collective-permute-done.23
  (110 shorter events, 19.0 us)
Async XLA Ops:
  6.5 7.4 %copy-start.1 = (bf16[256,2048]{1,0:T(8,128)(2,1)S(1)}, bf16[256,2048]{1,0:T(8,128)(2,1)}, u32[]{:S(2)}) copy-start(bf16[256,2048]{1,0:T(8,128)(2,1)} %param.5) | copy-start | bytes 3145732
  6.5 72.9 %all-to-all-start = ((bf16[64,128,128]{2,1,0:T(8,128)(2,1)}), bf16[64,128,128]{2,1,0:T(8,128)(2,1)S(1)}, u32[]{:S(2)}, u32[]{:S(2)}) async-start(bf16[64,128,128]{2,1,0:T(8,128)(2,1)} %param.6), calls=%async_computation | async-start | bytes 4194304 | tf_op jit(solution)/shard_map/all_to_all | solution.py:105
  13.9 3.0 %copy-start.3 = (s32[1,32,2]{1,2,0:T(2,128)S(1)}, s32[1,32,2]{1,2,0:T(2,128)}, u32[]{:S(2)}) copy-start(s32[1,32,2]{1,2,0:T(2,128)} %param.8) | copy-start | bytes 772
  13.9 57.3 %all-gather.15.cloned.1.call-start = ((), (), s32[]{:S(2)}) async-start(), calls=%async_computation.4 | async-start | bytes 1310720 | tf_op jit(solution)/shard_map/all_gather | solution.py:119
  14.9 83.5 %all-gather.13.cloned.1.call-start = ((), (), s32[]{:S(2)}) async-start(), calls=%async_computation.3 | async-start | bytes 1310720 | tf_op jit(solution)/shard_map/all_gather | solution.py:119
  15.7 111.8 %all-gather.11.cloned.1.call-start = ((), (), s32[]{:S(2)}) async-start(), calls=%async_computation.2 | async-start | bytes 1310720 | tf_op jit(solution)/shard_map/all_gather | solution.py:119
  16.4 140.0 %all-gather.9.cloned.1.call-start = ((), (), s32[]{:S(2)}) async-start(), calls=%async_computation.1 | async-start | bytes 1310720 | tf_op jit(solution)/shard_map/all_gather | solution.py:119
  16.7 62.7 %copy-start.5 = (s32[64]{0:T(128)}, s32[64]{0:T(128)S(1)}, u32[]{:S(2)}) copy-start(s32[64]{0:T(128)S(1)} %reshape.69.ab_ref) | copy-start | bytes 772
  91.1 2.1 %collective-permute-start.1 = (f32[2,2,32,1024]{3,2,1,0:T(8,128)S(1)}, f32[2,2,32,1024]{3,2,1,0:T(8,128)}, u32[]{:S(2)}, u32[]{:S(2)}) collective-permute-start(f32[2,2,32,1024]{3,2,1,0:T(8,128)S(1)} %dynamic-slice_bitcast_fusion.6), channel_id=1, source_target_pairs={{0,1},{1,0},{2,3},{3,2},{4,5},{5,4},{6,7},{7,6},{8,9},{9,8},{10,11... | collective-permute-start | bytes 1572872 | tf_op jit(solution)/shard_map/ppermute | solution.py:93
  92.0 2.3 %collective-permute-start = (f32[2,2,32,1024]{3,2,1,0:T(8,128)}, f32[2,2,32,1024]{3,2,1,0:T(8,128)S(1)}, u32[]{:S(2)}, u32[]{:S(2)}) collective-permute-start(f32[2,2,32,1024]{3,2,1,0:T(8,128)} %dynamic-slice_bitcast_fusion.7), channel_id=1, source_target_pairs={{0,1},{1,0},{2,3},{3,2},{4,5},{5,4},{6,7},{7,6},{8,9},{9,8},{10,11... | collective-permute-start | bytes 1572872 | tf_op jit(solution)/shard_map/ppermute | solution.py:93
  108.8 7.8 %collective-permute-start.3 = (f32[2,32,1024]{2,1,0:T(8,128)S(1)}, f32[2,32,1024]{2,1,0:T(8,128)S(1)}, u32[]{:S(2)}, u32[]{:S(2)}) collective-permute-start(f32[2,32,1024]{2,1,0:T(8,128)S(1)} %dynamic-slice_bitcast_fusion.14), channel_id=1, source_target_pairs={{0,4},{1,5},{2,6},{3,7},{4,0},{5,1},{6,2},{7,3},{8,12},{9,13},{10,... | collective-permute-start | bytes 786440 | tf_op jit(solution)/shard_map/ppermute | solution.py:93
  110.2 8.9 %collective-permute-start.5 = (f32[2,2,32,1024]{3,2,1,0:T(8,128)S(1)}, f32[2,2,32,1024]{3,2,1,0:T(8,128)S(1)}, u32[]{:S(2)}, u32[]{:S(2)}) collective-permute-start(f32[2,2,32,1024]{3,2,1,0:T(8,128)S(1)} %dynamic-slice_bitcast_fusion.4), channel_id=1, source_target_pairs={{0,1},{1,0},{2,3},{3,2},{4,5},{5,4},{6,7},{7,6},{8,9},{9,8},{10,11... | collective-permute-start | bytes 1572872 | tf_op jit(solution)/shard_map/ppermute | solution.py:93
  110.3 8.8 %collective-permute-start.2 = (f32[2,32,1024]{2,1,0:T(8,128)S(1)}, f32[2,32,1024]{2,1,0:T(8,128)S(1)}, u32[]{:S(2)}, u32[]{:S(2)}) collective-permute-start(f32[2,32,1024]{2,1,0:T(8,128)S(1)} %dynamic-slice_bitcast_fusion.15), channel_id=1, source_target_pairs={{0,2},{1,3},{2,0},{3,1},{4,6},{5,7},{6,4},{7,5},{8,10},{9,11},{10,... | collective-permute-start | bytes 786440 | tf_op jit(solution)/shard_map/ppermute | solution.py:93
  111.9 7.3 %collective-permute-start.4 = (f32[2,2,32,1024]{3,2,1,0:T(8,128)S(1)}, f32[2,2,32,1024]{3,2,1,0:T(8,128)S(1)}, u32[]{:S(2)}, u32[]{:S(2)}) collective-permute-start(f32[2,2,32,1024]{3,2,1,0:T(8,128)S(1)} %dynamic-slice_bitcast_fusion.5), channel_id=1, source_target_pairs={{0,1},{1,0},{2,3},{3,2},{4,5},{5,4},{6,7},{7,6},{8,9},{9,8},{10,11... | collective-permute-start | bytes 1572872 | tf_op jit(solution)/shard_map/ppermute | solution.py:93
  137.8 13.7 %collective-permute-start.11 = (f32[2,2,32,1024]{3,2,1,0:T(8,128)S(1)}, f32[2,2,32,1024]{3,2,1,0:T(8,128)S(1)}, u32[]{:S(2)}, u32[]{:S(2)}) collective-permute-start(f32[2,2,32,1024]{3,2,1,0:T(8,128)S(1)} %dynamic-slice_bitcast_fusion.2), channel_id=1, source_target_pairs={{0,1},{1,0},{2,3},{3,2},{4,5},{5,4},{6,7},{7,6},{8,9},{9,8},{10,11... | collective-permute-start | bytes 1572872 | tf_op jit(solution)/shard_map/ppermute | solution.py:93
  137.9 13.7 %collective-permute-start.10 = (f32[2,2,32,1024]{3,2,1,0:T(8,128)S(1)}, f32[2,2,32,1024]{3,2,1,0:T(8,128)S(1)}, u32[]{:S(2)}, u32[]{:S(2)}) collective-permute-start(f32[2,2,32,1024]{3,2,1,0:T(8,128)S(1)} %dynamic-slice_bitcast_fusion.3), channel_id=1, source_target_pairs={{0,1},{1,0},{2,3},{3,2},{4,5},{5,4},{6,7},{7,6},{8,9},{9,8},{10,11... | collective-permute-start | bytes 1572872 | tf_op jit(solution)/shard_map/ppermute | solution.py:93
  138.5 12.9 %collective-permute-start.9 = (f32[2,32,1024]{2,1,0:T(8,128)S(1)}, f32[2,32,1024]{2,1,0:T(8,128)S(1)}, u32[]{:S(2)}, u32[]{:S(2)}) collective-permute-start(f32[2,32,1024]{2,1,0:T(8,128)S(1)} %dynamic-slice_bitcast_fusion.12), channel_id=1, source_target_pairs={{0,4},{1,5},{2,6},{3,7},{4,0},{5,1},{6,2},{7,3},{8,12},{9,13},{10,... | collective-permute-start | bytes 786440 | tf_op jit(solution)/shard_map/ppermute | solution.py:93
  140.0 6.5 %collective-permute-start.7 = (f32[32,1024]{1,0:T(8,128)S(1)}, f32[32,1024]{1,0:T(8,128)S(1)}, u32[]{:S(2)}, u32[]{:S(2)}) collective-permute-start(f32[32,1024]{1,0:T(8,128)S(1)} %dynamic-slice_bitcast_fusion.22), channel_id=1, source_target_pairs={{0,2},{1,3},{2,0},{3,1},{4,6},{5,7},{6,4},{7,5},{8,10},{9,11},{10,... | collective-permute-start | bytes 393224 | tf_op jit(solution)/shard_map/ppermute | solution.py:93
  141.6 9.9 %collective-permute-start.8 = (f32[2,32,1024]{2,1,0:T(8,128)S(1)}, f32[2,32,1024]{2,1,0:T(8,128)S(1)}, u32[]{:S(2)}, u32[]{:S(2)}) collective-permute-start(f32[2,32,1024]{2,1,0:T(8,128)S(1)} %dynamic-slice_bitcast_fusion.13), channel_id=1, source_target_pairs={{0,2},{1,3},{2,0},{3,1},{4,6},{5,7},{6,4},{7,5},{8,10},{9,11},{10,... | collective-permute-start | bytes 786440 | tf_op jit(solution)/shard_map/ppermute | solution.py:93
  146.5 5.0 %collective-permute-start.6 = (f32[32,1024]{1,0:T(8,128)S(1)}, f32[32,1024]{1,0:T(8,128)S(1)}, u32[]{:S(2)}, u32[]{:S(2)}) collective-permute-start(f32[32,1024]{1,0:T(8,128)S(1)} %dynamic-slice_bitcast_fusion.23), channel_id=1, source_target_pairs={{0,4},{1,5},{2,6},{3,7},{4,0},{5,1},{6,2},{7,3},{8,12},{9,13},{10,... | collective-permute-start | bytes 393224 | tf_op jit(solution)/shard_map/ppermute | solution.py:93
  156.5 14.8 %collective-permute-start.12 = (f32[32,1024]{1,0:T(8,128)S(1)}, f32[32,1024]{1,0:T(8,128)S(1)}, u32[]{:S(2)}, u32[]{:S(2)}) collective-permute-start(f32[32,1024]{1,0:T(8,128)S(1)} %dynamic-slice_bitcast_fusion.21), channel_id=1, source_target_pairs={{0,4},{1,5},{2,6},{3,7},{4,0},{5,1},{6,2},{7,3},{8,12},{9,13},{10,... | collective-permute-start | bytes 393224 | tf_op jit(solution)/shard_map/ppermute | solution.py:93
  158.1 13.7 %collective-permute-start.13 = (f32[32,1024]{1,0:T(8,128)S(1)}, f32[32,1024]{1,0:T(8,128)S(1)}, u32[]{:S(2)}, u32[]{:S(2)}) collective-permute-start(f32[32,1024]{1,0:T(8,128)S(1)} %dynamic-slice_bitcast_fusion.20), channel_id=1, source_target_pairs={{0,2},{1,3},{2,0},{3,1},{4,6},{5,7},{6,4},{7,5},{8,10},{9,11},{10,... | collective-permute-start | bytes 393224 | tf_op jit(solution)/shard_map/ppermute | solution.py:93
  159.5 12.4 %collective-permute-start.14 = (f32[2,32,1024]{2,1,0:T(8,128)S(1)}, f32[2,32,1024]{2,1,0:T(8,128)S(1)}, u32[]{:S(2)}, u32[]{:S(2)}) collective-permute-start(f32[2,32,1024]{2,1,0:T(8,128)S(1)} %dynamic-slice_bitcast_fusion.11), channel_id=1, source_target_pairs={{0,2},{1,3},{2,0},{3,1},{4,6},{5,7},{6,4},{7,5},{8,10},{9,11},{10,... | collective-permute-start | bytes 786440 | tf_op jit(solution)/shard_map/ppermute | solution.py:93
  160.3 13.2 %collective-permute-start.16 = (f32[2,32,1024]{2,1,0:T(8,128)S(1)}, f32[2,32,1024]{2,1,0:T(8,128)S(1)}, u32[]{:S(2)}, u32[]{:S(2)}) collective-permute-start(f32[2,32,1024]{2,1,0:T(8,128)S(1)} %dynamic-slice_bitcast_fusion.10), channel_id=1, source_target_pairs={{0,4},{1,5},{2,6},{3,7},{4,0},{5,1},{6,2},{7,3},{8,12},{9,13},{10,... | collective-permute-start | bytes 786440 | tf_op jit(solution)/shard_map/ppermute | solution.py:93
  171.1 7.7 %collective-permute-start.18 = (f32[2,2,32,1024]{3,2,1,0:T(8,128)S(1)}, f32[2,2,32,1024]{3,2,1,0:T(8,128)S(1)}, u32[]{:S(2)}, u32[]{:S(2)}) collective-permute-start(f32[2,2,32,1024]{3,2,1,0:T(8,128)S(1)} %dynamic-slice_bitcast_fusion.1), channel_id=1, source_target_pairs={{0,1},{1,0},{2,3},{3,2},{4,5},{5,4},{6,7},{7,6},{8,9},{9,8},{10,11... | collective-permute-start | bytes 1572872 | tf_op jit(solution)/shard_map/ppermute | solution.py:93
  171.2 9.0 %collective-permute-start.21 = (f32[2,2,32,1024]{3,2,1,0:T(8,128)S(1)}, f32[2,2,32,1024]{3,2,1,0:T(8,128)S(1)}, u32[]{:S(2)}, u32[]{:S(2)}) collective-permute-start(f32[2,2,32,1024]{3,2,1,0:T(8,128)S(1)} %dynamic-slice_bitcast_fusion), channel_id=1, source_target_pairs={{0,1},{1,0},{2,3},{3,2},{4,5},{5,4},{6,7},{7,6},{8,9},{9,8},{10,11... | collective-permute-start | bytes 1572872 | tf_op jit(solution)/shard_map/ppermute | solution.py:93
  171.9 5.5 %collective-permute-start.15 = (f32[32,1024]{1,0:T(8,128)S(1)}, f32[32,1024]{1,0:T(8,128)S(1)}, u32[]{:S(2)}, u32[]{:S(2)}) collective-permute-start(f32[32,1024]{1,0:T(8,128)S(1)} %dynamic-slice_bitcast_fusion.19), channel_id=1, source_target_pairs={{0,4},{1,5},{2,6},{3,7},{4,0},{5,1},{6,2},{7,3},{8,12},{9,13},{10,... | collective-permute-start | bytes 393224 | tf_op jit(solution)/shard_map/ppermute | solution.py:93
  173.5 5.2 %collective-permute-start.17 = (f32[32,1024]{1,0:T(8,128)S(1)}, f32[32,1024]{1,0:T(8,128)S(1)}, u32[]{:S(2)}, u32[]{:S(2)}) collective-permute-start(f32[32,1024]{1,0:T(8,128)S(1)} %dynamic-slice_bitcast_fusion.18), channel_id=1, source_target_pairs={{0,2},{1,3},{2,0},{3,1},{4,6},{5,7},{6,4},{7,5},{8,10},{9,11},{10,... | collective-permute-start | bytes 393224 | tf_op jit(solution)/shard_map/ppermute | solution.py:93
  178.9 7.1 %collective-permute-start.19 = (f32[2,32,1024]{2,1,0:T(8,128)S(1)}, f32[2,32,1024]{2,1,0:T(8,128)S(1)}, u32[]{:S(2)}, u32[]{:S(2)}) collective-permute-start(f32[2,32,1024]{2,1,0:T(8,128)S(1)} %dynamic-slice_bitcast_fusion.9), channel_id=1, source_target_pairs={{0,2},{1,3},{2,0},{3,1},{4,6},{5,7},{6,4},{7,5},{8,10},{9,11},{10,... | collective-permute-start | bytes 786440 | tf_op jit(solution)/shard_map/ppermute | solution.py:93
  180.4 7.3 %collective-permute-start.22 = (f32[2,32,1024]{2,1,0:T(8,128)S(1)}, f32[2,32,1024]{2,1,0:T(8,128)S(1)}, u32[]{:S(2)}, u32[]{:S(2)}) collective-permute-start(f32[2,32,1024]{2,1,0:T(8,128)S(1)} %dynamic-slice_bitcast_fusion.8), channel_id=1, source_target_pairs={{0,4},{1,5},{2,6},{3,7},{4,0},{5,1},{6,2},{7,3},{8,12},{9,13},{10,... | collective-permute-start | bytes 786440 | tf_op jit(solution)/shard_map/ppermute | solution.py:93
  186.1 5.0 %collective-permute-start.20 = (f32[32,1024]{1,0:T(8,128)S(1)}, f32[32,1024]{1,0:T(8,128)S(1)}, u32[]{:S(2)}, u32[]{:S(2)}) collective-permute-start(f32[32,1024]{1,0:T(8,128)S(1)} %dynamic-slice_bitcast_fusion.17), channel_id=1, source_target_pairs={{0,4},{1,5},{2,6},{3,7},{4,0},{5,1},{6,2},{7,3},{8,12},{9,13},{10,... | collective-permute-start | bytes 393224 | tf_op jit(solution)/shard_map/ppermute | solution.py:93
  187.8 5.0 %collective-permute-start.23 = (f32[32,1024]{1,0:T(8,128)S(1)}, f32[32,1024]{1,0:T(8,128)S(1)}, u32[]{:S(2)}, u32[]{:S(2)}) collective-permute-start(f32[32,1024]{1,0:T(8,128)S(1)} %dynamic-slice_bitcast_fusion.16), channel_id=1, source_target_pairs={{0,2},{1,3},{2,0},{3,1},{4,6},{5,7},{6,4},{7,5},{8,10},{9,11},{10,... | collective-permute-start | bytes 393224 | tf_op jit(solution)/shard_map/ppermute | solution.py:93
  (3 other events, 6.8 us)
Sparse Core Ops, SparseCore 0:
  16.3 54.8 all-gather.14
  72.7 25.6 all-gather.12
  100.0 27.4 all-gather.10
  128.9 27.5 all-gather.8

commit v5 on v4

v5 whole, which is shorter than its diff:
```python
import functools

import jax
import jax.numpy as jnp
from jax import lax
from jax.experimental import pallas as pl
from jax.experimental.pallas import tpu as pltpu
from jax.sharding import PartitionSpec as P

AB_DEV = 16
CHUNKS = (2, 1, 1)


def _slot_order(ab_ids, live_mask, ab_count):
    n = ab_ids.shape[0]
    key = jnp.where(live_mask, ab_ids, ab_count)
    idx = jnp.arange(n, dtype=jnp.int32)
    earlier = (key[None, :] < key[:, None]) | ((key[None, :] == key[:, None]) & (idx[None, :] < idx[:, None]))
    rank = jnp.sum(earlier.astype(jnp.int32), axis=1)
    order = jnp.sum(jnp.where(rank[None, :] == idx[:, None], idx[None, :], 0), axis=1).astype(jnp.int32)
    bounds = jnp.arange(ab_count + 1, dtype=jnp.int32)
    starts = jnp.sum((key[None, :] < bounds[:, None]).astype(jnp.int32), axis=1).astype(jnp.int32)
    return order, starts


def _weight_kernel(order_ref, starts_ref, cd_ref, tiles_ref, out_ref):
    ab = pl.program_id(0)
    tile = tiles_ref.shape[-1]
    out_ref[...] = jnp.zeros(out_ref.shape, out_ref.dtype)

    def place(t, carry):
        i = order_ref[t]
        row = pl.multiple_of(cd_ref[i] * tile, tile)
        out_ref[pl.ds(row, tile), :] = tiles_ref[i]
        return carry

    lax.fori_loop(starts_ref[ab], starts_ref[ab + 1], place, 0)


def _dense_weight(tiles, order, starts, cd_ids, cd_count, ab_count):
    n, tile, _ = tiles.shape
    width = cd_count * tile
    grid_spec = pltpu.PrefetchScalarGridSpec(
        num_scalar_prefetch=3,
        grid=(ab_count,),
        in_specs=[pl.BlockSpec((n, tile, tile), lambda j, *_: (0, 0, 0))],
        out_specs=pl.BlockSpec((width, tile), lambda j, *_: (0, j)),
    )
    return pl.pallas_call(
        _weight_kernel,
        grid_spec=grid_spec,
        out_shape=jax.ShapeDtypeStruct((width, ab_count * tile), tiles.dtype),
        cost_estimate=pl.CostEstimate(
            flops=0, transcendentals=0, bytes_accessed=tiles.size * 2 + width * ab_count * tile * 2
        ),
    )(order, starts, cd_ids, tiles)


class _Halving:
    def __init__(self, partial, bit_order, rep_count):
        self.levels = rep_count.bit_length() - 1
        self.part = partial.shape[0] // rep_count
        self.width = partial.shape[-1]
        self.x = partial.reshape((2,) * self.levels + (self.part, self.width))
        self.axis_bits = list(range(self.levels - 1, -1, -1))
        self.todo = list(bit_order)
        self.rep_count = rep_count

    def advance(self, rep_index):
        if not self.todo:
            return
        bit = self.todo.pop(0)
        ax = self.axis_bits.index(bit)
        mine = (rep_index >> bit) & 1
        keep = lax.dynamic_index_in_dim(self.x, mine, ax, keepdims=False)
        send = lax.dynamic_index_in_dim(self.x, 1 - mine, ax, keepdims=False)
        pairs = [(i, i ^ (1 << bit)) for i in range(self.rep_count)]
        self.x = keep + lax.ppermute(send, "rep", perm=pairs)
        self.axis_bits.pop(ax)

    def result(self):
        return self.x.reshape(self.part, self.width)


def on_device(amplitudes, integrals, ab_list, cd_list, live_count):
    own_count = lax.axis_size("own")
    rep_count = lax.axis_size("rep")
    peer_count = own_count * rep_count
    slot_count = integrals.shape[0] // peer_count
    received = lax.all_to_all(integrals, ("own", "rep"), split_axis=0, concat_axis=0, tiled=True)
    ab_ids = ab_list.reshape(-1)
    cd_ids = cd_list.reshape(-1)
    live_mask = (
        jnp.arange(slot_count, dtype=jnp.int32)[None, :] < live_count.reshape(peer_count, 1)
    ).reshape(-1)
    order, starts = _slot_order(ab_ids, live_mask, AB_DEV)
    local_rows, width = amplitudes.shape
    tile = integrals.shape[-1]
    weight = _dense_weight(received, order, starts, cd_ids, width // tile, AB_DEV)
    subs = rep_count // own_count
    units = sum(CHUNKS)
    part = local_rows // (subs * units)
    local4 = amplitudes.reshape(subs, units, part, width)
    rep_index = lax.axis_index("rep")
    levels = rep_count.bit_length() - 1
    orders = (list(range(levels)), [0] + list(range(levels - 1, 0, -1)))
    bounds = [sum(CHUNKS[:c]) for c in range(len(CHUNKS) + 1)]
    gathered = [
        lax.all_gather(local4[:, bounds[c]:bounds[c + 1]], "own", axis=0, tiled=True)
        for c in range(len(CHUNKS))
    ]
    half = weight.shape[1] // 2
    flows = []
    for chunk in range(len(CHUNKS)):
        for flow in flows:
            flow.advance(rep_index)
        if flows:
            amp4, held = lax.optimization_barrier((gathered[chunk], [f.x for f in flows]))
            for flow, x in zip(flows, held):
                flow.x = x
        else:
            amp4 = gathered[chunk]
        lhs = amp4.reshape(-1, width)
        for h in range(2):
            partial = jnp.dot(lhs, weight[:, h * half:(h + 1) * half], preferred_element_type=jnp.float32)
            flows.append(_Halving(partial, orders[h], rep_count))
    while any(flow.todo for flow in flows):
        for flow in flows:
            flow.advance(rep_index)
    pieces = []
    for chunk in range(len(CHUNKS)):
        size = CHUNKS[chunk]
        sides = [flows[2 * chunk + h].result().reshape(size, part, half) for h in range(2)]
        pieces.append(jnp.concatenate(sides, axis=2))
    return jnp.concatenate(pieces, axis=0).reshape(units * part, 2 * half)


def solution(mesh):
    return jax.shard_map(
        on_device,
        mesh=mesh,
        in_specs=(
            P("own", "rep"),
            P(("own", "rep"), None, None),
            P(("own", "rep"), None, None),
            P(("own", "rep"), None, None),
            P(("own", "rep"), None),
        ),
        out_specs=P("rep", "own"),
        check_vma=False,
    )
```

time: 201 us -> 204 us (1.015)
  Pallas kernels: 34.2 us -> 10.1 us
  matrix products: 0 us -> 22.3 us
  waiting for transfers between devices: 109 us -> 114 us
  other arithmetic: 4.69 us -> 9.45 us
  starting transfers between devices: 26.9 us -> 23.9 us
    all_to_all x1, waiting for transfers between devices: 8.25 us -> 77.9 us  [on_device(): lax.all_to_all(integrals, ('own', 'rep'), split_axis=0, concat_axis=0, ti...]
    all_gather x4 -> x3, waiting for transfers between devices: 68.9 us -> 3.81 us  [on_device(): lax.all_gather(local4[:, bounds[c]:bounds[c + 1]], 'own', axis=0, tiled=T...]
    pallas_call x4 -> x1, Pallas kernels: 34.2 us -> 10.1 us  [_dense_weight(): pl.pallas_call(_weight_kernel, grid_spec=grid_spec, out_shape=jax.ShapeDt...]
    dot_general x0 -> x6, matrix products: none -> 22.3 us  [on_device(): jnp.dot(lhs, weight[:, h * half:(h + 1) * half], preferred_element_type=j...]
    slice x5 -> x2, local copies, waits for them, and re-layouts: 7.85 us -> 1.69 us  [on_device(): local4[:, bounds[c]:bounds[c + 1]]]
    add x24 -> x14, other arithmetic: 2.08 us -> 6.75 us  [advance(): self.x = keep + lax.ppermute(send, 'rep', perm=pairs)]
    unnamed x14 -> x28, local copies, waits for them, and re-layouts: 1.56 us -> 5.22 us
    ppermute x24 -> x18, starting transfers between devices: 19.5 us -> 16.5 us  [advance(): self.x = keep + lax.ppermute(send, 'rep', perm=pairs)]
  transfers between devices with their start and end apart: 29 -> 22, of which waited for: 16 -> 12; matrix products, arithmetic and copies ran while one was open for 7% -> 14% of each run, Pallas kernels for 17% -> 5%
where the time goes in v5:
time: 204 us
  waiting for transfers between devices  114 us (56%)
  starting transfers between devices  23.9 us (12%)
  matrix products  22.3 us (11%)
  between operations  13.5 us (7%)
  local copies, waits for them, and re-layouts  10.2 us (5%)
  Pallas kernels  10.1 us (5%)
  other arithmetic  9.45 us (5%)
    all_to_all x1, waiting for transfers between devices, on_device(): lax.all_to_all(integrals, ('own', 'rep'), split_axis=0, concat_axis=0, ti...  77.9 us
    ppermute x18, waiting for transfers between devices, advance(): self.x = keep + lax.ppermute(send, 'rep', perm=pairs)  32.6 us
    dot_general x6, matrix products, on_device(): jnp.dot(lhs, weight[:, h * half:(h + 1) * half], preferred_element_type=j...  22.3 us
    ppermute x18, starting transfers between devices, advance(): self.x = keep + lax.ppermute(send, 'rep', perm=pairs)  16.5 us
    pallas_call x1, Pallas kernels, _dense_weight(): pl.pallas_call(_weight_kernel, grid_spec=grid_spec, out_shape=jax.ShapeDt...  10.1 us
    all_to_all x1, starting transfers between devices, on_device(): lax.all_to_all(integrals, ('own', 'rep'), split_axis=0, concat_axis=0, ti...  7.3 us
    add x14, other arithmetic, advance(): self.x = keep + lax.ppermute(send, 'rep', perm=pairs)  6.75 us
    unnamed x28, local copies, waits for them, and re-layouts  5.22 us
  transfers between devices with their start and end apart: 22, of which 12 were waited for; matrix products, arithmetic and copies ran while one was open for 14% of the time, Pallas kernels for 5%

profile of v5, /device:TPU:0, one launch (start us, length us, event | category | flops | bytes accessed | tf_op | source)
XLA Modules:
  0.0 203.8 jit_solution(12788394957328887746)
XLA Ops:
  6.5 7.3 %all-to-all-start = ((bf16[64,128,128]{2,1,0:T(8,128)(2,1)}), bf16[64,128,128]{2,1,0:T(8,128)(2,1)S(1)}, u32[]{:S(2)}, u32[]{:S(2)}) async-start(bf16[64,128,128]{2,1,0:T(8,128)(2,1)} %param.6), calls=%async_computation | async-start | bytes 4194304 | tf_op jit(solution)/shard_map/all_to_all | solution.py:90
  18.4 77.9 %all-to-all-done.tiles_ref = bf16[64,128,128]{2,1,0:T(8,128)(2,1)S(1)} async-done(((bf16[64,128,128]{2,1,0:T(8,128)(2,1)}), bf16[64,128,128]{2,1,0:T(8,128)(2,1)S(1)}, u32[]{:S(2)}, u32[]{:S(2)}) %all-to-all-start) | async-done | bytes 2097184 | tf_op jit(solution)/shard_map/all_to_all | solution.py:90
  96.3 1.4 copy-done.1
  97.6 10.1 %shard_map.55 = bf16[2048,2048]{1,0:T(8,128)(2,1)} custom-call(s32[64]{0:T(128)} %select_reduce_fusion.order_ref, s32[17]{0:T(128)} %convert_reduce_fusion.1.starts_ref, s32[64]{0:T(128)} %reshape.90.cd_ref, bf16[64,128,128]{2,1,0:T(8,128)(2,1)} %copy-done.1), custom_call_target="tpu_custom_call" | custom-call | bytes 10485760 | tf_op jit(solution)/shard_map/pallas_call | solution.py:49
  107.8 5.3 %fusion.10 = f32[1024,512]{0,1:T(8,128)S(1)} fusion(bf16[512,2048]{1,0:T(8,128)(2,1)} %bitcast.131, bf16[2048,2048]{1,0:T(8,128)(2,1)} %shard_map.55), kind=kOutput, calls=%fused_computation.10 | convolution fusion | flops 2147483648 | bytes 8388608 | tf_op jit(solution)/shard_map/dot_general | solution.py:125
  113.6 2.3 %fusion.14 = f32[1024,512]{0,1:T(8,128)S(1)} fusion(bf16[512,2048]{1,0:T(8,128)(2,1)S(1)} %bitcast.132, bf16[2048,2048]{1,0:T(8,128)(2,1)S(1)} %copy-done), kind=kOutput, calls=%fused_computation.14 | convolution fusion | flops 2147483648 | bytes 8388608 | tf_op jit(solution)/shard_map/dot_general | solution.py:125
  116.0 1.4 copy-done.2
  118.6 1.4 bitcast_add_fusion
  120.0 1.5 collective-permute-done
  121.4 1.7 bitcast_add_fusion.1
  123.9 3.8 %fusion.2 = f32[2,2,2,32,1024]{4,3,2,1,0:T(8,128)S(1)} fusion(bf16[2,2,2,32,2048]{4,3,2,1,0:T(8,128)(2,1)} %bitcast.135, bf16[2048,2048]{1,0:T(8,128)(2,1)} %shard_map.55), kind=kOutput, calls=%fused_computation.2 | convolution fusion | flops 1073741824 | bytes 6291456 | tf_op jit(solution)/shard_map/dot_general | solution.py:125
  128.7 3.5 %fusion.6 = f32[2,2,2,32,1024]{4,3,2,1,0:T(8,128)S(1)} fusion(bf16[2,2,2,32,2048]{4,3,2,1,0:T(8,128)(2,1)S(1)} %bitcast.136, bf16[2048,2048]{1,0:T(8,128)(2,1)} %shard_map.55), kind=kOutput, calls=%fused_computation.6 | convolution fusion | flops 1073741824 | bytes 6291456 | tf_op jit(solution)/shard_map/dot_general | solution.py:125
  134.6 1.5 collective-permute-start.3
  136.2 1.5 collective-permute-start.2
  138.8 2.1 %bitcast_add_fusion.5 = f32[2,2,32,1024]{3,2,1,0:T(8,128)} fusion(f32[2,2,32,1024]{3,2,1,0:T(8,128)} %collective-permute-done.4, f32[2,2,2,32,1024]{4,3,2,1,0:T(8,128)} %copy-done.5, s32[]{:T(128)S(6)} %select_n.74), kind=kLoop, calls=%fused_computation.24 | loop fusion | flops 131072 | bytes 1572868 | tf_op jit(solution)/shard_map/add | solution.py:78
  140.9 7.6 %collective-permute-done.3 = f32[2,64,1024]{2,1,0:T(8,128)S(1)} collective-permute-done((f32[2,64,1024]{2,1,0:T(8,128)S(1)}, f32[2,64,1024]{2,1,0:T(8,128)S(1)}, u32[]{:S(2)}, u32[]{:S(2)}) %collective-permute-start.3) | collective-permute-done | bytes 524320 | tf_op jit(solution)/shard_map/ppermute | solution.py:78
  148.6 1.2 collective-permute-done.2
  149.9 3.0 %all-gather.4.cloned.1.call-done = bf16[8,1,32,2048]{3,2,1,0:T(8,128)(2,1)} async-done(((bf16[2,1,32,2048]{3,2,1,0:T(8,128)(2,1)}), bf16[8,1,32,2048]{3,2,1,0:T(8,128)(2,1)}) %all-gather.4.cloned.1.call-update) | async-done | bytes 1048592 | tf_op jit(solution)/shard_map/all_gather | solution.py:109
  152.9 3.8 %fusion.4 = f32[2,2,2,32,1024]{4,3,2,1,0:T(8,128)S(1)} fusion(bf16[2,2,2,32,2048]{4,3,2,1,0:T(8,128)(2,1)} %bitcast.133, bf16[2048,2048]{1,0:T(8,128)(2,1)} %shard_map.55), kind=kOutput, calls=%fused_computation.4 | convolution fusion | flops 1073741824 | bytes 6291456 | tf_op jit(solution)/shard_map/dot_general | solution.py:125
  156.8 3.5 %fusion = f32[2,2,2,32,1024]{4,3,2,1,0:T(8,128)S(1)} fusion(bf16[2,2,2,32,2048]{4,3,2,1,0:T(8,128)(2,1)S(1)} %bitcast.134, bf16[2048,2048]{1,0:T(8,128)(2,1)} %shard_map.55), kind=kOutput, calls=%fused_computation | convolution fusion | flops 1073741824 | bytes 6291456 | tf_op jit(solution)/shard_map/dot_general | solution.py:125
  160.3 1.5 collective-permute-start.6
  161.9 1.5 collective-permute-start.7
  164.9 10.3 %collective-permute-done.8 = f32[2,32,1024]{2,1,0:T(8,128)S(1)} collective-permute-done((f32[2,32,1024]{2,1,0:T(8,128)S(1)}, f32[2,32,1024]{2,1,0:T(8,128)S(1)}, u32[]{:S(2)}, u32[]{:S(2)}) %collective-permute-start.8) | collective-permute-done | bytes 262176 | tf_op jit(solution)/shard_map/ppermute | solution.py:78
  176.0 1.5 collective-permute-start.11
  177.6 3.7 %collective-permute-done.9 = f32[32,1024]{1,0:T(8,128)S(1)} collective-permute-done((f32[32,1024]{1,0:T(8,128)S(1)}, f32[32,1024]{1,0:T(8,128)S(1)}, u32[]{:S(2)}, u32[]{:S(2)}) %collective-permute-start.9) | collective-permute-done | bytes 131104 | tf_op jit(solution)/shard_map/ppermute | solution.py:78
  181.8 1.5 collective-permute-start.13
  183.5 1.5 collective-permute-start.16
  185.0 4.5 %collective-permute-done.13 = f32[2,32,1024]{2,1,0:T(8,128)S(1)} collective-permute-done((f32[2,32,1024]{2,1,0:T(8,128)S(1)}, f32[2,32,1024]{2,1,0:T(8,128)S(1)}, u32[]{:S(2)}, u32[]{:S(2)}) %collective-permute-start.13) | collective-permute-done | bytes 262176 | tf_op jit(solution)/shard_map/ppermute | solution.py:78
  189.5 1.5 collective-permute-start.14
  191.2 1.5 collective-permute-start.17
  192.7 1.9 collective-permute-done.14
  194.6 1.6 collective-permute-done.17
  (97 shorter events, 15.8 us)
Async XLA Ops:
  6.5 7.4 %copy-start.4 = (bf16[256,2048]{1,0:T(8,128)(2,1)S(1)}, bf16[256,2048]{1,0:T(8,128)(2,1)}, u32[]{:S(2)}) copy-start(bf16[256,2048]{1,0:T(8,128)(2,1)} %param.5) | copy-start | bytes 3145732
  6.5 9.2 %copy-start.7 = (s32[1,32,2]{1,2,0:T(2,128)S(1)}, s32[1,32,2]{1,2,0:T(2,128)}, u32[]{:S(2)}) copy-start(s32[1,32,2]{1,2,0:T(2,128)} %param.7) | copy-start | bytes 772
  6.5 9.4 %copy-start.9 = (s32[1,32]{1,0:T(1,128)S(1)}, s32[1,32]{1,0:T(1,128)}, u32[]{:S(2)}) copy-start(s32[1,32]{1,0:T(1,128)} %param.9) | copy-start | bytes 388
  6.5 9.6 %copy-start.8 = (s32[1,32,2]{1,2,0:T(2,128)S(1)}, s32[1,32,2]{1,2,0:T(2,128)}, u32[]{:S(2)}) copy-start(s32[1,32,2]{1,2,0:T(2,128)} %param.8) | copy-start | bytes 772
  6.5 89.7 %all-to-all-start = ((bf16[64,128,128]{2,1,0:T(8,128)(2,1)}), bf16[64,128,128]{2,1,0:T(8,128)(2,1)S(1)}, u32[]{:S(2)}, u32[]{:S(2)}) async-start(bf16[64,128,128]{2,1,0:T(8,128)(2,1)} %param.6), calls=%async_computation | async-start | bytes 4194304 | tf_op jit(solution)/shard_map/all_to_all | solution.py:90
  13.8 93.9 %all-gather.8.cloned.1.call-start = ((), (), s32[]{:S(2)}) async-start(), calls=%async_computation.3 | async-start | bytes 2621440 | tf_op jit(solution)/shard_map/all_gather | solution.py:109
  14.8 109.1 %all-gather.6.cloned.1.call-start = ((), (), s32[]{:S(2)}) async-start(), calls=%async_computation.2 | async-start | bytes 1310720 | tf_op jit(solution)/shard_map/all_gather | solution.py:109
  15.7 137.2 %all-gather.4.cloned.1.call-start = ((), (), s32[]{:S(2)}) async-start(), calls=%async_computation.1 | async-start | bytes 1310720 | tf_op jit(solution)/shard_map/all_gather | solution.py:109
  107.8 5.5 %copy-start = (bf16[2048,2048]{1,0:T(8,128)(2,1)S(1)}, bf16[2048,2048]{1,0:T(8,128)(2,1)}, u32[]{:S(2)}) copy-start(bf16[2048,2048]{1,0:T(8,128)(2,1)} %shard_map.55) | copy-start | bytes 25165828
  107.8 5.9 %copy-start.10 = (bf16[8,2,32,2048]{3,2,1,0:T(8,128)(2,1)S(1)}, bf16[8,2,32,2048]{3,2,1,0:T(8,128)(2,1)}, u32[]{:S(2)}) copy-start(bf16[8,2,32,2048]{3,2,1,0:T(8,128)(2,1)} %all-gather.8.cloned.1.call-done) | copy-start | bytes 6291460
  113.2 5.4 %collective-permute-start.1 = (f32[2,2,64,1024]{3,2,1,0:T(8,128)S(1)}, f32[2,2,64,1024]{3,2,1,0:T(8,128)}, u32[]{:S(2)}, u32[]{:S(2)}) collective-permute-start(f32[2,2,64,1024]{3,2,1,0:T(8,128)S(1)} %dynamic-slice_bitcast_fusion), channel_id=1, source_target_pairs={{0,1},{1,0},{2,3},{3,2},{4,5},{5,4},{6,7},{7,6},{8,9},{9,8},{10,11... | collective-permute-start | bytes 3145736 | tf_op jit(solution)/shard_map/ppermute | solution.py:78
  116.0 1.4 copy-start.2
  118.4 3.0 %collective-permute-start = (f32[2,2,64,1024]{3,2,1,0:T(8,128)}, f32[2,2,64,1024]{3,2,1,0:T(8,128)}, u32[]{:S(2)}, u32[]{:S(2)}) collective-permute-start(f32[2,2,64,1024]{3,2,1,0:T(8,128)} %dynamic-slice_bitcast_fusion.1), channel_id=1, source_target_pairs={{0,1},{1,0},{2,3},{3,2},{4,5},{5,4},{6,7},{7,6},{8,9},{9,8},{10,11... | collective-permute-start | bytes 3145736 | tf_op jit(solution)/shard_map/ppermute | solution.py:78
  123.9 4.8 %copy-start.12 = (bf16[8,1,32,2048]{3,2,1,0:T(8,128)(2,1)S(1)}, bf16[8,1,32,2048]{3,2,1,0:T(8,128)(2,1)}, u32[]{:S(2)}) copy-start(bf16[8,1,32,2048]{3,2,1,0:T(8,128)(2,1)} %all-gather.6.cloned.1.call-done) | copy-start | bytes 3145732
  128.7 9.0 %collective-permute-start.5 = (f32[2,2,32,1024]{3,2,1,0:T(8,128)S(1)}, f32[2,2,32,1024]{3,2,1,0:T(8,128)S(1)}, u32[]{:S(2)}, u32[]{:S(2)}) collective-permute-start(f32[2,2,32,1024]{3,2,1,0:T(8,128)S(1)} %dynamic-slice_bitcast_fusion.4), channel_id=1, source_target_pairs={{0,1},{1,0},{2,3},{3,2},{4,5},{5,4},{6,7},{7,6},{8,9},{9,8},{10,11... | collective-permute-start | bytes 1572872 | tf_op jit(solution)/shard_map/ppermute | solution.py:78
  134.1 4.8 %collective-permute-start.4 = (f32[2,2,32,1024]{3,2,1,0:T(8,128)}, f32[2,2,32,1024]{3,2,1,0:T(8,128)}, u32[]{:S(2)}, u32[]{:S(2)}) collective-permute-start(f32[2,2,32,1024]{3,2,1,0:T(8,128)} %dynamic-slice_bitcast_fusion.5), channel_id=1, source_target_pairs={{0,1},{1,0},{2,3},{3,2},{4,5},{5,4},{6,7},{7,6},{8,9},{9,8},{10,11... | collective-permute-start | bytes 1572872 | tf_op jit(solution)/shard_map/ppermute | solution.py:78
  134.6 13.9 %collective-permute-start.3 = (f32[2,64,1024]{2,1,0:T(8,128)S(1)}, f32[2,64,1024]{2,1,0:T(8,128)S(1)}, u32[]{:S(2)}, u32[]{:S(2)}) collective-permute-start(f32[2,64,1024]{2,1,0:T(8,128)S(1)} %dynamic-slice_bitcast_fusion.6), channel_id=1, source_target_pairs={{0,4},{1,5},{2,6},{3,7},{4,0},{5,1},{6,2},{7,3},{8,12},{9,13},{10,... | collective-permute-start | bytes 1572872 | tf_op jit(solution)/shard_map/ppermute | solution.py:78
  136.2 13.6 %collective-permute-start.2 = (f32[2,64,1024]{2,1,0:T(8,128)S(1)}, f32[2,64,1024]{2,1,0:T(8,128)S(1)}, u32[]{:S(2)}, u32[]{:S(2)}) collective-permute-start(f32[2,64,1024]{2,1,0:T(8,128)S(1)} %dynamic-slice_bitcast_fusion.7), channel_id=1, source_target_pairs={{0,2},{1,3},{2,0},{3,1},{4,6},{5,7},{6,4},{7,5},{8,10},{9,11},{10,... | collective-permute-start | bytes 1572872 | tf_op jit(solution)/shard_map/ppermute | solution.py:78
  152.9 3.8 %copy-start.11 = (bf16[8,1,32,2048]{3,2,1,0:T(8,128)(2,1)S(1)}, bf16[8,1,32,2048]{3,2,1,0:T(8,128)(2,1)}, u32[]{:S(2)}) copy-start(bf16[8,1,32,2048]{3,2,1,0:T(8,128)(2,1)} %all-gather.4.cloned.1.call-done) | copy-start | bytes 3145732
  156.8 6.6 %copy-start.3 = (f32[2,2,32,1024]{3,2,1,0:T(8,128)S(1)}, f32[2,2,32,1024]{3,2,1,0:T(8,128)}, u32[]{:S(2)}) copy-start(f32[2,2,32,1024]{3,2,1,0:T(8,128)} %bitcast_add_fusion.5) | copy-start | bytes 1572868
  160.3 15.6 %collective-permute-start.6 = (f32[64,1024]{1,0:T(8,128)S(1)}, f32[64,1024]{1,0:T(8,128)S(1)}, u32[]{:S(2)}, u32[]{:S(2)}) collective-permute-start(f32[64,1024]{1,0:T(8,128)S(1)} %dynamic-slice_bitcast_fusion.13), channel_id=1, source_target_pairs={{0,4},{1,5},{2,6},{3,7},{4,0},{5,1},{6,2},{7,3},{8,12},{9,13},{10,... | collective-permute-start | bytes 786440 | tf_op jit(solution)/shard_map/ppermute | solution.py:78
  161.9 15.7 %collective-permute-start.7 = (f32[64,1024]{1,0:T(8,128)S(1)}, f32[64,1024]{1,0:T(8,128)S(1)}, u32[]{:S(2)}, u32[]{:S(2)}) collective-permute-start(f32[64,1024]{1,0:T(8,128)S(1)} %dynamic-slice_bitcast_fusion.12), channel_id=1, source_target_pairs={{0,2},{1,3},{2,0},{3,1},{4,6},{5,7},{6,4},{7,5},{8,10},{9,11},{10,... | collective-permute-start | bytes 786440 | tf_op jit(solution)/shard_map/ppermute | solution.py:78
  163.4 11.8 %collective-permute-start.8 = (f32[2,32,1024]{2,1,0:T(8,128)S(1)}, f32[2,32,1024]{2,1,0:T(8,128)S(1)}, u32[]{:S(2)}, u32[]{:S(2)}) collective-permute-start(f32[2,32,1024]{2,1,0:T(8,128)S(1)} %dynamic-slice_bitcast_fusion.11), channel_id=1, source_target_pairs={{0,2},{1,3},{2,0},{3,1},{4,6},{5,7},{6,4},{7,5},{8,10},{9,11},{10,... | collective-permute-start | bytes 786440 | tf_op jit(solution)/shard_map/ppermute | solution.py:78
  164.1 11.2 %collective-permute-start.10 = (f32[2,32,1024]{2,1,0:T(8,128)S(1)}, f32[2,32,1024]{2,1,0:T(8,128)S(1)}, u32[]{:S(2)}, u32[]{:S(2)}) collective-permute-start(f32[2,32,1024]{2,1,0:T(8,128)S(1)} %dynamic-slice_bitcast_fusion.10), channel_id=1, source_target_pairs={{0,4},{1,5},{2,6},{3,7},{4,0},{5,1},{6,2},{7,3},{8,12},{9,13},{10,... | collective-permute-start | bytes 786440 | tf_op jit(solution)/shard_map/ppermute | solution.py:78
  164.7 16.9 %collective-permute-start.12 = (f32[2,2,32,1024]{3,2,1,0:T(8,128)S(1)}, f32[2,2,32,1024]{3,2,1,0:T(8,128)S(1)}, u32[]{:S(2)}, u32[]{:S(2)}) collective-permute-start(f32[2,2,32,1024]{3,2,1,0:T(8,128)S(1)} %dynamic-slice_bitcast_fusion.3), channel_id=1, source_target_pairs={{0,1},{1,0},{2,3},{3,2},{4,5},{5,4},{6,7},{7,6},{8,9},{9,8},{10,11... | collective-permute-start | bytes 1572872 | tf_op jit(solution)/shard_map/ppermute | solution.py:78
  175.2 8.2 %collective-permute-start.15 = (f32[2,2,32,1024]{3,2,1,0:T(8,128)S(1)}, f32[2,2,32,1024]{3,2,1,0:T(8,128)S(1)}, u32[]{:S(2)}, u32[]{:S(2)}) collective-permute-start(f32[2,2,32,1024]{3,2,1,0:T(8,128)S(1)} %dynamic-slice_bitcast_fusion.2), channel_id=1, source_target_pairs={{0,1},{1,0},{2,3},{3,2},{4,5},{5,4},{6,7},{7,6},{8,9},{9,8},{10,11... | collective-permute-start | bytes 1572872 | tf_op jit(solution)/shard_map/ppermute | solution.py:78
  175.3 6.0 %collective-permute-start.9 = (f32[32,1024]{1,0:T(8,128)S(1)}, f32[32,1024]{1,0:T(8,128)S(1)}, u32[]{:S(2)}, u32[]{:S(2)}) collective-permute-start(f32[32,1024]{1,0:T(8,128)S(1)} %dynamic-slice_bitcast_fusion.17), channel_id=1, source_target_pairs={{0,4},{1,5},{2,6},{3,7},{4,0},{5,1},{6,2},{7,3},{8,12},{9,13},{10,... | collective-permute-start | bytes 393224 | tf_op jit(solution)/shard_map/ppermute | solution.py:78
  176.0 5.7 %collective-permute-start.11 = (f32[32,1024]{1,0:T(8,128)S(1)}, f32[32,1024]{1,0:T(8,128)S(1)}, u32[]{:S(2)}, u32[]{:S(2)}) collective-permute-start(f32[32,1024]{1,0:T(8,128)S(1)} %dynamic-slice_bitcast_fusion.16), channel_id=1, source_target_pairs={{0,2},{1,3},{2,0},{3,1},{4,6},{5,7},{6,4},{7,5},{8,10},{9,11},{10,... | collective-permute-start | bytes 393224 | tf_op jit(solution)/shard_map/ppermute | solution.py:78
  181.8 7.7 %collective-permute-start.13 = (f32[2,32,1024]{2,1,0:T(8,128)S(1)}, f32[2,32,1024]{2,1,0:T(8,128)S(1)}, u32[]{:S(2)}, u32[]{:S(2)}) collective-permute-start(f32[2,32,1024]{2,1,0:T(8,128)S(1)} %dynamic-slice_bitcast_fusion.9), channel_id=1, source_target_pairs={{0,2},{1,3},{2,0},{3,1},{4,6},{5,7},{6,4},{7,5},{8,10},{9,11},{10,... | collective-permute-start | bytes 786440 | tf_op jit(solution)/shard_map/ppermute | solution.py:78
  183.5 7.6 %collective-permute-start.16 = (f32[2,32,1024]{2,1,0:T(8,128)S(1)}, f32[2,32,1024]{2,1,0:T(8,128)S(1)}, u32[]{:S(2)}, u32[]{:S(2)}) collective-permute-start(f32[2,32,1024]{2,1,0:T(8,128)S(1)} %dynamic-slice_bitcast_fusion.8), channel_id=1, source_target_pairs={{0,4},{1,5},{2,6},{3,7},{4,0},{5,1},{6,2},{7,3},{8,12},{9,13},{10,... | collective-permute-start | bytes 786440 | tf_op jit(solution)/shard_map/ppermute | solution.py:78
  189.5 5.0 %collective-permute-start.14 = (f32[32,1024]{1,0:T(8,128)S(1)}, f32[32,1024]{1,0:T(8,128)S(1)}, u32[]{:S(2)}, u32[]{:S(2)}) collective-permute-start(f32[32,1024]{1,0:T(8,128)S(1)} %dynamic-slice_bitcast_fusion.15), channel_id=1, source_target_pairs={{0,4},{1,5},{2,6},{3,7},{4,0},{5,1},{6,2},{7,3},{8,12},{9,13},{10,... | collective-permute-start | bytes 393224 | tf_op jit(solution)/shard_map/ppermute | solution.py:78
  191.2 5.0 %collective-permute-start.17 = (f32[32,1024]{1,0:T(8,128)S(1)}, f32[32,1024]{1,0:T(8,128)S(1)}, u32[]{:S(2)}, u32[]{:S(2)}) collective-permute-start(f32[32,1024]{1,0:T(8,128)S(1)} %dynamic-slice_bitcast_fusion.14), channel_id=1, source_target_pairs={{0,2},{1,3},{2,0},{3,1},{4,6},{5,7},{6,4},{7,5},{8,10},{9,11},{10,... | collective-permute-start | bytes 393224 | tf_op jit(solution)/shard_map/ppermute | solution.py:78
  (3 other events, 3.4 us)
Sparse Core Ops, SparseCore 0:
  16.3 80.0 all-gather.7
  97.9 25.9 all-gather.5
  125.5 27.4 all-gather.3

commit v6 on v5

--- a/solution.py
+++ b/solution.py
@@ -8,7 +8,7 @@
 from jax.sharding import PartitionSpec as P
 
 AB_DEV = 16
-CHUNKS = (2, 1, 1)
+CHUNKS = (4, 2, 1, 1)
 
 
 def _slot_order(ab_ids, live_mask, ab_count):

time: 204 us -> 233 us (1.14)
  blocking collectives: 0 us -> 32.9 us
  waiting for transfers between devices: 114 us -> 108 us
  starting transfers between devices: 23.9 us -> 28.2 us
    all_gather x0 -> x2, blocking collectives: none -> 32.9 us  [on_device(): lax.all_gather(local4[:, bounds[c]:bounds[c + 1]], 'own', axis=0, tiled=T...]
    ppermute x18 -> x24, starting transfers between devices: 16.5 us -> 20.8 us  [advance(): self.x = keep + lax.ppermute(send, 'rep', perm=pairs)]
    all_gather x3 -> x2, waiting for transfers between devices: 3.81 us -> 0.02 us  [on_device(): lax.all_gather(local4[:, bounds[c]:bounds[c + 1]], 'own', axis=0, tiled=T...]
    ppermute x18 -> x24, waiting for transfers between devices: 32.6 us -> 29.5 us  [advance(): self.x = keep + lax.ppermute(send, 'rep', perm=pairs)]
    dot_general x6 -> x8, matrix products: 22.3 us -> 20.6 us  [on_device(): jnp.dot(lhs, weight[:, h * half:(h + 1) * half], preferred_element_type=j...]
    unnamed x28 -> x32, local copies, waits for them, and re-layouts: 5.22 us -> 3.66 us
    add x14 -> x20, other arithmetic: 6.75 us -> 5.96 us  [advance(): self.x = keep + lax.ppermute(send, 'rep', perm=pairs)]
  transfers between devices with their start and end apart: 22 -> 27, of which waited for: 12 -> 14; matrix products, arithmetic and copies ran while one was open for 14% -> 9% of each run, Pallas kernels for 5% -> 4%
where the time goes in v6:
time: 233 us; the launch traced here: 232 us
  waiting for transfers between devices  108 us (46%)
  blocking collectives  32.9 us (14%)
  starting transfers between devices  28.2 us (12%)
  matrix products  20.6 us (9%)
  between operations  13.9 us (6%)
  local copies, waits for them, and re-layouts  10.4 us (4%)
  Pallas kernels  10.2 us (4%)
  other arithmetic  8.71 us (4%)
    all_to_all x1, waiting for transfers between devices, on_device(): lax.all_to_all(integrals, ('own', 'rep'), split_axis=0, concat_axis=0, ti...  78 us
    all_gather x2, blocking collectives, on_device(): lax.all_gather(local4[:, bounds[c]:bounds[c + 1]], 'own', axis=0, tiled=T...  32.9 us
    ppermute x24, waiting for transfers between devices, advance(): self.x = keep + lax.ppermute(send, 'rep', perm=pairs)  29.5 us
    ppermute x24, starting transfers between devices, advance(): self.x = keep + lax.ppermute(send, 'rep', perm=pairs)  20.8 us
    dot_general x8, matrix products, on_device(): jnp.dot(lhs, weight[:, h * half:(h + 1) * half], preferred_element_type=j...  20.6 us
    pallas_call x1, Pallas kernels, _dense_weight(): pl.pallas_call(_weight_kernel, grid_spec=grid_spec, out_shape=jax.ShapeDt...  10.2 us
    all_to_all x1, starting transfers between devices, on_device(): lax.all_to_all(integrals, ('own', 'rep'), split_axis=0, concat_axis=0, ti...  7.3 us
    add x20, other arithmetic, advance(): self.x = keep + lax.ppermute(send, 'rep', perm=pairs)  5.96 us
  transfers between devices with their start and end apart: 27, of which 14 were waited for; matrix products, arithmetic and copies ran while one was open for 9% of the time, Pallas kernels for 4%

profile of v6, /device:TPU:0, one launch (start us, length us, event | category | flops | bytes accessed | tf_op | source)
XLA Modules:
  0.0 232.4 jit_solution(8702710532417730520)
XLA Ops:
  6.5 7.3 %all-to-all-start = ((bf16[64,128,128]{2,1,0:T(8,128)(2,1)}), bf16[64,128,128]{2,1,0:T(8,128)(2,1)S(1)}, u32[]{:S(2)}, u32[]{:S(2)}) async-start(bf16[64,128,128]{2,1,0:T(8,128)(2,1)} %param.6), calls=%async_computation | async-start | bytes 4194304 | tf_op jit(solution)/shard_map/all_to_all | solution.py:90
  18.3 78.0 %all-to-all-done.tiles_ref = bf16[64,128,128]{2,1,0:T(8,128)(2,1)S(1)} async-done(((bf16[64,128,128]{2,1,0:T(8,128)(2,1)}), bf16[64,128,128]{2,1,0:T(8,128)(2,1)S(1)}, u32[]{:S(2)}, u32[]{:S(2)}) %all-to-all-start) | async-done | bytes 2097184 | tf_op jit(solution)/shard_map/all_to_all | solution.py:90
  96.3 1.4 copy-done.1
  97.6 10.2 %shard_map.55 = bf16[2048,2048]{1,0:T(8,128)(2,1)} custom-call(s32[64]{0:T(128)} %select_reduce_fusion.order_ref, s32[17]{0:T(128)} %convert_reduce_fusion.1.starts_ref, s32[64]{0:T(128)} %reshape.103.cd_ref, bf16[64,128,128]{2,1,0:T(8,128)(2,1)} %copy-done.1), custom_call_target="tpu_custom_call" | custom-call | bytes 10485760 | tf_op jit(solution)/shard_map/pallas_call | solution.py:49
  107.8 5.3 %fusion.15 = f32[1024,512]{0,1:T(8,128)S(1)} fusion(bf16[512,2048]{1,0:T(8,128)(2,1)} %bitcast.173, bf16[2048,2048]{1,0:T(8,128)(2,1)} %shard_map.55), kind=kOutput, calls=%fused_computation.15 | convolution fusion | flops 2147483648 | bytes 8388608 | tf_op jit(solution)/shard_map/dot_general | solution.py:125
  113.7 2.3 %fusion.20 = f32[1024,512]{0,1:T(8,128)S(1)} fusion(bf16[512,2048]{1,0:T(8,128)(2,1)S(1)} %bitcast.174, bf16[2048,2048]{1,0:T(8,128)(2,1)S(1)} %copy-done), kind=kOutput, calls=%fused_computation.20 | convolution fusion | flops 2147483648 | bytes 8388608 | tf_op jit(solution)/shard_map/dot_general | solution.py:125
  116.1 1.4 copy-done.2
  119.7 16.6 %all_gather.13 = bf16[8,1,16,2048]{3,2,1,0:T(8,128)(2,1)} all-gather(bf16[2,1,16,2048]{3,2,1,0:T(8,128)(2,1)S(1)} %get-tuple-element.35), channel_id=1, replica_groups=mesh['own'=4,'rep'=8] {'own'}, dimensions={0}, use_global_device_ids=true | all-gather | bytes 655360 | tf_op jit(solution)/shard_map/all_gather | solution.py:109
  136.3 1.4 bitcast_add_fusion
  137.7 1.4 bitcast_add_fusion.1
  139.1 3.8 %fusion.4 = f32[2,2,2,32,1024]{4,3,2,1,0:T(8,128)S(1)} fusion(bf16[2,2,2,32,2048]{4,3,2,1,0:T(8,128)(2,1)} %bitcast.175, bf16[2048,2048]{1,0:T(8,128)(2,1)} %shard_map.55), kind=kOutput, calls=%fused_computation.4 | convolution fusion | flops 1073741824 | bytes 6291456 | tf_op jit(solution)/shard_map/dot_general | solution.py:125
  143.0 3.8 %fusion.10 = f32[2,2,2,32,1024]{4,3,2,1,0:T(8,128)S(1)} fusion(bf16[2,2,2,32,2048]{4,3,2,1,0:T(8,128)(2,1)S(1)} %bitcast.176, bf16[2048,2048]{1,0:T(8,128)(2,1)} %shard_map.55), kind=kOutput, calls=%fused_computation.10 | convolution fusion | flops 1073741824 | bytes 6291456 | tf_op jit(solution)/shard_map/dot_general | solution.py:125
  149.1 16.3 %all_gather.12 = bf16[8,1,16,2048]{3,2,1,0:T(8,128)(2,1)} all-gather(bf16[2,1,16,2048]{3,2,1,0:T(8,128)(2,1)S(1)} %get-tuple-element.36), channel_id=1, replica_groups=mesh['own'=4,'rep'=8] {'own'}, dimensions={0}, use_global_device_ids=true | all-gather | bytes 655360 | tf_op jit(solution)/shard_map/all_gather | solution.py:109
  165.4 2.4 %collective-permute-start.3 = (f32[2,64,1024]{2,1,0:T(8,128)S(1)}, f32[2,64,1024]{2,1,0:T(8,128)S(1)}, u32[]{:S(2)}, u32[]{:S(2)}) collective-permute-start(f32[2,64,1024]{2,1,0:T(8,128)S(1)} %dynamic-slice_bitcast_fusion.4), channel_id=1, source_target_pairs={{0,4},{1,5},{2,6},{3,7},{4,0},{5,1},{6,2},{7,3},{8,12},{9,13},{10,... | collective-permute-start | bytes 1572872 | tf_op jit(solution)/shard_map/ppermute | solution.py:78
  168.7 1.4 bitcast_add_fusion.2
  170.1 1.3 bitcast_add_fusion.3
  171.4 5.0 %collective-permute-done.3 = f32[2,64,1024]{2,1,0:T(8,128)S(1)} collective-permute-done((f32[2,64,1024]{2,1,0:T(8,128)S(1)}, f32[2,64,1024]{2,1,0:T(8,128)S(1)}, u32[]{:S(2)}, u32[]{:S(2)}) %collective-permute-start.3) | collective-permute-done | bytes 524320 | tf_op jit(solution)/shard_map/ppermute | solution.py:78
  176.4 1.5 collective-permute-done.2
  178.0 3.1 %fusion.2 = f32[2,2,2,16,1024]{4,3,2,1,0:T(8,128)S(1)} fusion(bf16[2,2,2,16,2048]{4,3,2,1,0:T(8,128)(2,1)S(1)} %bitcast.168, bf16[2048,2048]{1,0:T(8,128)(2,1)} %shard_map.55), kind=kOutput, calls=%fused_computation.2 | convolution fusion | flops 536870912 | bytes 5242880 | tf_op jit(solution)/shard_map/dot_general | solution.py:125
  183.4 1.8 collective-permute-start.8
  185.6 1.7 collective-permute-start.6
  187.4 4.8 %collective-permute-done.9 = f32[2,32,1024]{2,1,0:T(8,128)S(1)} collective-permute-done((f32[2,32,1024]{2,1,0:T(8,128)S(1)}, f32[2,32,1024]{2,1,0:T(8,128)S(1)}, u32[]{:S(2)}, u32[]{:S(2)}) %collective-permute-start.9) | collective-permute-done | bytes 262176 | tf_op jit(solution)/shard_map/ppermute | solution.py:78
  192.7 4.3 %collective-permute-done.7 = f32[64,1024]{1,0:T(8,128)S(1)} collective-permute-done((f32[64,1024]{1,0:T(8,128)S(1)}, f32[64,1024]{1,0:T(8,128)S(1)}, u32[]{:S(2)}, u32[]{:S(2)}) %collective-permute-start.7) | collective-permute-done | bytes 262176 | tf_op jit(solution)/shard_map/ppermute | solution.py:78
  198.7 1.7 collective-permute-start.12
  200.4 1.4 collective-permute-start.13
  203.2 4.0 %collective-permute-done.14 = f32[2,16,1024]{2,1,0:T(8,128)S(1)} collective-permute-done((f32[2,16,1024]{2,1,0:T(8,128)S(1)}, f32[2,16,1024]{2,1,0:T(8,128)S(1)}, u32[]{:S(2)}, u32[]{:S(2)}) %collective-permute-start.14) | collective-permute-done | bytes 131104 | tf_op jit(solution)/shard_map/ppermute | solution.py:78
  208.1 1.8 collective-permute-start.17
  209.9 1.9 collective-permute-done.15
  212.5 1.8 collective-permute-start.19
  215.6 1.9 collective-permute-done.19
  217.5 1.7 collective-permute-start.20
  221.9 2.6 %collective-permute-done.23 = f32[16,1024]{1,0:T(8,128)S(1)} collective-permute-done((f32[16,1024]{1,0:T(8,128)S(1)}, f32[16,1024]{1,0:T(8,128)S(1)}, u32[]{:S(2)}, u32[]{:S(2)}) %collective-permute-start.23) | collective-permute-done | bytes 65568 | tf_op jit(solution)/shard_map/ppermute | solution.py:78
  (128 shorter events, 23.4 us)
Async XLA Ops:
  6.5 9.4 %copy-start.9 = (s32[1,32,2]{1,2,0:T(2,128)S(1)}, s32[1,32,2]{1,2,0:T(2,128)}, u32[]{:S(2)}) copy-start(s32[1,32,2]{1,2,0:T(2,128)} %param.8) | copy-start | bytes 772
  6.5 89.7 %all-to-all-start = ((bf16[64,128,128]{2,1,0:T(8,128)(2,1)}), bf16[64,128,128]{2,1,0:T(8,128)(2,1)S(1)}, u32[]{:S(2)}, u32[]{:S(2)}) async-start(bf16[64,128,128]{2,1,0:T(8,128)(2,1)} %param.6), calls=%async_computation | async-start | bytes 4194304 | tf_op jit(solution)/shard_map/all_to_all | solution.py:90
  13.8 94.0 %all-gather.5.cloned.1.call-start = ((), (), s32[]{:S(2)}) async-start(), calls=%async_computation.2 | async-start | bytes 2621440 | tf_op jit(solution)/shard_map/all_gather | solution.py:109
  14.8 124.4 %all-gather.3.cloned.1.call-start = ((), (), s32[]{:S(2)}) async-start(), calls=%async_computation.1 | async-start | bytes 1310720 | tf_op jit(solution)/shard_map/all_gather | solution.py:109
  113.3 23.1 %collective-permute-start.1 = (f32[2,2,64,1024]{3,2,1,0:T(8,128)S(1)}, f32[2,2,64,1024]{3,2,1,0:T(8,128)}, u32[]{:S(2)}, u32[]{:S(2)}) collective-permute-start(f32[2,2,64,1024]{3,2,1,0:T(8,128)S(1)} %dynamic-slice_bitcast_fusion), channel_id=1, source_target_pairs={{0,1},{1,0},{2,3},{3,2},{4,5},{5,4},{6,7},{7,6},{8,9},{9,8},{10,11... | collective-permute-start | bytes 3145736 | tf_op jit(solution)/shard_map/ppermute | solution.py:78
  118.5 19.3 %collective-permute-start = (f32[2,2,64,1024]{3,2,1,0:T(8,128)}, f32[2,2,64,1024]{3,2,1,0:T(8,128)}, u32[]{:S(2)}, u32[]{:S(2)}) collective-permute-start(f32[2,2,64,1024]{3,2,1,0:T(8,128)} %dynamic-slice_bitcast_fusion.1), channel_id=1, source_target_pairs={{0,1},{1,0},{2,3},{3,2},{4,5},{5,4},{6,7},{7,6},{8,9},{9,8},{10,11... | collective-permute-start | bytes 3145736 | tf_op jit(solution)/shard_map/ppermute | solution.py:78
  118.6 19.1 %copy-start.3 = (f32[1024,512]{0,1:T(8,128)S(1)}, f32[1024,512]{0,1:T(8,128)}, u32[]{:S(2)}) copy-start(f32[1024,512]{0,1:T(8,128)} %copy-done.2) | copy-start | bytes 6291460
  147.7 21.0 %collective-permute-start.5 = (f32[2,2,32,1024]{3,2,1,0:T(8,128)}, f32[2,2,32,1024]{3,2,1,0:T(8,128)}, u32[]{:S(2)}, u32[]{:S(2)}) collective-permute-start(f32[2,2,32,1024]{3,2,1,0:T(8,128)} %dynamic-slice_bitcast_fusion.2), channel_id=1, source_target_pairs={{0,1},{1,0},{2,3},{3,2},{4,5},{5,4},{6,7},{7,6},{8,9},{9,8},{10,11... | collective-permute-start | bytes 1572872 | tf_op jit(solution)/shard_map/ppermute | solution.py:78
  148.6 21.5 %collective-permute-start.4 = (f32[2,2,32,1024]{3,2,1,0:T(8,128)}, f32[2,2,32,1024]{3,2,1,0:T(8,128)}, u32[]{:S(2)}, u32[]{:S(2)}) collective-permute-start(f32[2,2,32,1024]{3,2,1,0:T(8,128)} %dynamic-slice_bitcast_fusion.3), channel_id=1, source_target_pairs={{0,1},{1,0},{2,3},{3,2},{4,5},{5,4},{6,7},{7,6},{8,9},{9,8},{10,11... | collective-permute-start | bytes 1572872 | tf_op jit(solution)/shard_map/ppermute | solution.py:78
  165.3 12.7 %copy-start.7 = (bf16[8,1,16,2048]{3,2,1,0:T(8,128)(2,1)S(1)}, bf16[8,1,16,2048]{3,2,1,0:T(8,128)(2,1)}, u32[]{:S(2)}) copy-start(bf16[8,1,16,2048]{3,2,1,0:T(8,128)(2,1)} %all_gather.13) | copy-start | bytes 1572868
  165.4 11.0 %collective-permute-start.3 = (f32[2,64,1024]{2,1,0:T(8,128)S(1)}, f32[2,64,1024]{2,1,0:T(8,128)S(1)}, u32[]{:S(2)}, u32[]{:S(2)}) collective-permute-start(f32[2,64,1024]{2,1,0:T(8,128)S(1)} %dynamic-slice_bitcast_fusion.4), channel_id=1, source_target_pairs={{0,4},{1,5},{2,6},{3,7},{4,0},{5,1},{6,2},{7,3},{8,12},{9,13},{10,... | collective-permute-start | bytes 1572872 | tf_op jit(solution)/shard_map/ppermute | solution.py:78
  167.8 10.1 %collective-permute-start.2 = (f32[2,64,1024]{2,1,0:T(8,128)S(1)}, f32[2,64,1024]{2,1,0:T(8,128)S(1)}, u32[]{:S(2)}, u32[]{:S(2)}) collective-permute-start(f32[2,64,1024]{2,1,0:T(8,128)S(1)} %dynamic-slice_bitcast_fusion.5), channel_id=1, source_target_pairs={{0,2},{1,3},{2,0},{3,1},{4,6},{5,7},{6,4},{7,5},{8,10},{9,11},{10,... | collective-permute-start | bytes 1572872 | tf_op jit(solution)/shard_map/ppermute | solution.py:78
  168.7 12.4 %slice-start = ((s8[8388608]{0:T(1024)(128)(4,1)}), s8[4194304]{0:T(1024)(128)(4,1)S(1)}, s32[]{:S(2)}) async-start(s8[8388608]{0:T(1024)(128)(4,1)} %bitcast.155), calls=%async_computation.3 | async-start | bytes 8388608
  182.2 15.0 %copy-start.6 = (bf16[8,1,16,2048]{3,2,1,0:T(8,128)(2,1)S(1)}, bf16[8,1,16,2048]{3,2,1,0:T(8,128)(2,1)}, u32[]{:S(2)}) copy-start(bf16[8,1,16,2048]{3,2,1,0:T(8,128)(2,1)} %all_gather.12) | copy-start | bytes 1572868
  182.2 3.4 %collective-permute-start.11 = (f32[2,2,16,1024]{3,2,1,0:T(8,128)S(1)}, f32[2,2,16,1024]{3,2,1,0:T(8,128)S(1)}, u32[]{:S(2)}, u32[]{:S(2)}) collective-permute-start(f32[2,2,16,1024]{3,2,1,0:T(8,128)S(1)} %dynamic-slice_bitcast_fusion.8), channel_id=1, source_target_pairs={{0,1},{1,0},{2,3},{3,2},{4,5},{5,4},{6,7},{7,6},{8,9},{9,8},{10,11... | collective-permute-start | bytes 786440 | tf_op jit(solution)/shard_map/ppermute | solution.py:78
  182.4 5.0 %collective-permute-start.10 = (f32[2,2,16,1024]{3,2,1,0:T(8,128)S(1)}, f32[2,2,16,1024]{3,2,1,0:T(8,128)S(1)}, u32[]{:S(2)}, u32[]{:S(2)}) collective-permute-start(f32[2,2,16,1024]{3,2,1,0:T(8,128)S(1)} %dynamic-slice_bitcast_fusion.9), channel_id=1, source_target_pairs={{0,1},{1,0},{2,3},{3,2},{4,5},{5,4},{6,7},{7,6},{8,9},{9,8},{10,11... | collective-permute-start | bytes 786440 | tf_op jit(solution)/shard_map/ppermute | solution.py:78
  182.9 9.2 %collective-permute-start.9 = (f32[2,32,1024]{2,1,0:T(8,128)S(1)}, f32[2,32,1024]{2,1,0:T(8,128)S(1)}, u32[]{:S(2)}, u32[]{:S(2)}) collective-permute-start(f32[2,32,1024]{2,1,0:T(8,128)S(1)} %dynamic-slice_bitcast_fusion.10), channel_id=1, source_target_pairs={{0,4},{1,5},{2,6},{3,7},{4,0},{5,1},{6,2},{7,3},{8,12},{9,13},{10,... | collective-permute-start | bytes 786440 | tf_op jit(solution)/shard_map/ppermute | solution.py:78
  183.4 9.3 %collective-permute-start.8 = (f32[2,32,1024]{2,1,0:T(8,128)S(1)}, f32[2,32,1024]{2,1,0:T(8,128)S(1)}, u32[]{:S(2)}, u32[]{:S(2)}) collective-permute-start(f32[2,32,1024]{2,1,0:T(8,128)S(1)} %dynamic-slice_bitcast_fusion.11), channel_id=1, source_target_pairs={{0,2},{1,3},{2,0},{3,1},{4,6},{5,7},{6,4},{7,5},{8,10},{9,11},{10,... | collective-permute-start | bytes 786440 | tf_op jit(solution)/shard_map/ppermute | solution.py:78
  185.3 11.8 %collective-permute-start.7 = (f32[64,1024]{1,0:T(8,128)S(1)}, f32[64,1024]{1,0:T(8,128)S(1)}, u32[]{:S(2)}, u32[]{:S(2)}) collective-permute-start(f32[64,1024]{1,0:T(8,128)S(1)} %dynamic-slice_bitcast_fusion.12), channel_id=1, source_target_pairs={{0,2},{1,3},{2,0},{3,1},{4,6},{5,7},{6,4},{7,5},{8,10},{9,11},{10,... | collective-permute-start | bytes 786440 | tf_op jit(solution)/shard_map/ppermute | solution.py:78
  185.6 11.5 %collective-permute-start.6 = (f32[64,1024]{1,0:T(8,128)S(1)}, f32[64,1024]{1,0:T(8,128)S(1)}, u32[]{:S(2)}, u32[]{:S(2)}) collective-permute-start(f32[64,1024]{1,0:T(8,128)S(1)} %dynamic-slice_bitcast_fusion.13), channel_id=1, source_target_pairs={{0,4},{1,5},{2,6},{3,7},{4,0},{5,1},{6,2},{7,3},{8,12},{9,13},{10,... | collective-permute-start | bytes 786440 | tf_op jit(solution)/shard_map/ppermute | solution.py:78
  198.7 9.4 %collective-permute-start.12 = (f32[32,1024]{1,0:T(8,128)S(1)}, f32[32,1024]{1,0:T(8,128)S(1)}, u32[]{:S(2)}, u32[]{:S(2)}) collective-permute-start(f32[32,1024]{1,0:T(8,128)S(1)} %dynamic-slice_bitcast_fusion.19), channel_id=1, source_target_pairs={{0,4},{1,5},{2,6},{3,7},{4,0},{5,1},{6,2},{7,3},{8,12},{9,13},{10,... | collective-permute-start | bytes 393224 | tf_op jit(solution)/shard_map/ppermute | solution.py:78
  200.4 9.5 %collective-permute-start.13 = (f32[32,1024]{1,0:T(8,128)S(1)}, f32[32,1024]{1,0:T(8,128)S(1)}, u32[]{:S(2)}, u32[]{:S(2)}) collective-permute-start(f32[32,1024]{1,0:T(8,128)S(1)} %dynamic-slice_bitcast_fusion.18), channel_id=1, source_target_pairs={{0,2},{1,3},{2,0},{3,1},{4,6},{5,7},{6,4},{7,5},{8,10},{9,11},{10,... | collective-permute-start | bytes 393224 | tf_op jit(solution)/shard_map/ppermute | solution.py:78
  201.8 5.5 %collective-permute-start.14 = (f32[2,16,1024]{2,1,0:T(8,128)S(1)}, f32[2,16,1024]{2,1,0:T(8,128)S(1)}, u32[]{:S(2)}, u32[]{:S(2)}) collective-permute-start(f32[2,16,1024]{2,1,0:T(8,128)S(1)} %dynamic-slice_bitcast_fusion.17), channel_id=1, source_target_pairs={{0,2},{1,3},{2,0},{3,1},{4,6},{5,7},{6,4},{7,5},{8,10},{9,11},{10,... | collective-permute-start | bytes 393224 | tf_op jit(solution)/shard_map/ppermute | solution.py:78
  202.5 5.0 %collective-permute-start.16 = (f32[2,16,1024]{2,1,0:T(8,128)S(1)}, f32[2,16,1024]{2,1,0:T(8,128)S(1)}, u32[]{:S(2)}, u32[]{:S(2)}) collective-permute-start(f32[2,16,1024]{2,1,0:T(8,128)S(1)} %dynamic-slice_bitcast_fusion.16), channel_id=1, source_target_pairs={{0,4},{1,5},{2,6},{3,7},{4,0},{5,1},{6,2},{7,3},{8,12},{9,13},{10,... | collective-permute-start | bytes 393224 | tf_op jit(solution)/shard_map/ppermute | solution.py:78
  203.1 9.3 %collective-permute-start.18 = (f32[2,2,16,1024]{3,2,1,0:T(8,128)S(1)}, f32[2,2,16,1024]{3,2,1,0:T(8,128)S(1)}, u32[]{:S(2)}, u32[]{:S(2)}) collective-permute-start(f32[2,2,16,1024]{3,2,1,0:T(8,128)S(1)} %dynamic-slice_bitcast_fusion.7), channel_id=1, source_target_pairs={{0,1},{1,0},{2,3},{3,2},{4,5},{5,4},{6,7},{7,6},{8,9},{9,8},{10,11... | collective-permute-start | bytes 786440 | tf_op jit(solution)/shard_map/ppermute | solution.py:78
  207.2 7.1 %collective-permute-start.21 = (f32[2,2,16,1024]{3,2,1,0:T(8,128)S(1)}, f32[2,2,16,1024]{3,2,1,0:T(8,128)S(1)}, u32[]{:S(2)}, u32[]{:S(2)}) collective-permute-start(f32[2,2,16,1024]{3,2,1,0:T(8,128)S(1)} %dynamic-slice_bitcast_fusion.6), channel_id=1, source_target_pairs={{0,1},{1,0},{2,3},{3,2},{4,5},{5,4},{6,7},{7,6},{8,9},{9,8},{10,11... | collective-permute-start | bytes 786440 | tf_op jit(solution)/shard_map/ppermute | solution.py:78
  207.6 4.3 %collective-permute-start.15 = (f32[16,1024]{1,0:T(8,128)S(1)}, f32[16,1024]{1,0:T(8,128)S(1)}, u32[]{:S(2)}, u32[]{:S(2)}) collective-permute-start(f32[16,1024]{1,0:T(8,128)S(1)} %dynamic-slice_bitcast_fusion.23), channel_id=1, source_target_pairs={{0,4},{1,5},{2,6},{3,7},{4,0},{5,1},{6,2},{7,3},{8,12},{9,13},{10,... | collective-permute-start | bytes 196616 | tf_op jit(solution)/shard_map/ppermute | solution.py:78
  208.1 4.3 %collective-permute-start.17 = (f32[16,1024]{1,0:T(8,128)S(1)}, f32[16,1024]{1,0:T(8,128)S(1)}, u32[]{:S(2)}, u32[]{:S(2)}) collective-permute-start(f32[16,1024]{1,0:T(8,128)S(1)} %dynamic-slice_bitcast_fusion.22), channel_id=1, source_target_pairs={{0,2},{1,3},{2,0},{3,1},{4,6},{5,7},{6,4},{7,5},{8,10},{9,11},{10,... | collective-permute-start | bytes 196616 | tf_op jit(solution)/shard_map/ppermute | solution.py:78
  212.5 5.0 %collective-permute-start.19 = (f32[2,16,1024]{2,1,0:T(8,128)S(1)}, f32[2,16,1024]{2,1,0:T(8,128)S(1)}, u32[]{:S(2)}, u32[]{:S(2)}) collective-permute-start(f32[2,16,1024]{2,1,0:T(8,128)S(1)} %dynamic-slice_bitcast_fusion.15), channel_id=1, source_target_pairs={{0,2},{1,3},{2,0},{3,1},{4,6},{5,7},{6,4},{7,5},{8,10},{9,11},{10,... | collective-permute-start | bytes 393224 | tf_op jit(solution)/shard_map/ppermute | solution.py:78
  214.3 5.7 %collective-permute-start.22 = (f32[2,16,1024]{2,1,0:T(8,128)S(1)}, f32[2,16,1024]{2,1,0:T(8,128)S(1)}, u32[]{:S(2)}, u32[]{:S(2)}) collective-permute-start(f32[2,16,1024]{2,1,0:T(8,128)S(1)} %dynamic-slice_bitcast_fusion.14), channel_id=1, source_target_pairs={{0,4},{1,5},{2,6},{3,7},{4,0},{5,1},{6,2},{7,3},{8,12},{9,13},{10,... | collective-permute-start | bytes 393224 | tf_op jit(solution)/shard_map/ppermute | solution.py:78
  217.5 4.3 %collective-permute-start.20 = (f32[16,1024]{1,0:T(8,128)S(1)}, f32[16,1024]{1,0:T(8,128)S(1)}, u32[]{:S(2)}, u32[]{:S(2)}) collective-permute-start(f32[16,1024]{1,0:T(8,128)S(1)} %dynamic-slice_bitcast_fusion.21), channel_id=1, source_target_pairs={{0,4},{1,5},{2,6},{3,7},{4,0},{5,1},{6,2},{7,3},{8,12},{9,13},{10,... | collective-permute-start | bytes 196616 | tf_op jit(solution)/shard_map/ppermute | solution.py:78
  220.1 4.3 %collective-permute-start.23 = (f32[16,1024]{1,0:T(8,128)S(1)}, f32[16,1024]{1,0:T(8,128)S(1)}, u32[]{:S(2)}, u32[]{:S(2)}) collective-permute-start(f32[16,1024]{1,0:T(8,128)S(1)} %dynamic-slice_bitcast_fusion.20), channel_id=1, source_target_pairs={{0,2},{1,3},{2,0},{3,1},{4,6},{5,7},{6,4},{7,5},{8,10},{9,11},{10,... | collective-permute-start | bytes 196616 | tf_op jit(solution)/shard_map/ppermute | solution.py:78
  (10 other events, 51.0 us)
Sparse Core Ops, SparseCore 0:
  16.3 80.0 all-gather.4
  97.9 25.9 all-gather.2

commit v7 on v5

--- a/solution.py
+++ b/solution.py
@@ -82,6 +82,23 @@
         return self.x.reshape(self.part, self.width)
 
 
+def _line_gather(block, own_count):
+    me = lax.axis_index("own")
+    up = [block]
+    down = [block]
+    for k in range(1, own_count):
+        up.append(lax.ppermute(up[-1], "own", perm=[(i, i + 1) for i in range(k - 1, own_count - 1)]))
+        down.append(lax.ppermute(down[-1], "own", perm=[(i + 1, i) for i in range(own_count - k)]))
+    out = jnp.zeros((own_count,) + block.shape, block.dtype)
+    zero = (0,) * block.ndim
+    for k in range(own_count - 1, 0, -1):
+        out = lax.dynamic_update_slice(out, up[k][None], (me - k,) + zero)
+    for k in range(own_count - 1, 0, -1):
+        out = lax.dynamic_update_slice(out, down[k][None], (me + k,) + zero)
+    out = lax.dynamic_update_slice(out, block[None], (me,) + zero)
+    return out.reshape((own_count * block.shape[0],) + block.shape[1:])
+
+
 def on_device(amplitudes, integrals, ab_list, cd_list, live_count):
     own_count = lax.axis_size("own")
     rep_count = lax.axis_size("rep")
@@ -107,6 +124,8 @@
     bounds = [sum(CHUNKS[:c]) for c in range(len(CHUNKS) + 1)]
     gathered = [
         lax.all_gather(local4[:, bounds[c]:bounds[c + 1]], "own", axis=0, tiled=True)
+        if c == 0
+        else _line_gather(local4[:, bounds[c]:bounds[c + 1]], own_count)
         for c in range(len(CHUNKS))
     ]
     half = weight.shape[1] // 2

time: 204 us -> 236 us (1.16)
  starting transfers between devices: 23.9 us -> 41.8 us
  local copies, waits for them, and re-layouts: 10.2 us -> 22.7 us
  waiting for transfers between devices: 114 us -> 122 us
  matrix products: 22.3 us -> 17.5 us
  other arithmetic: 9.45 us -> 6.28 us
    ppermute x0 -> x12, waiting for transfers between devices: none -> 84.4 us  [the longest x6 84.4 us: _line_gather(): lax.ppermute(down[-1], 'own', perm=[(i + 1, i) for i in range(own_count -...]
    all_to_all x1, waiting for transfers between devices: 77.9 us -> 0.01 us  [on_device(): lax.all_to_all(integrals, ('own', 'rep'), split_axis=0, concat_axis=0, ti...]
    ppermute x0 -> x12, starting transfers between devices: none -> 21.3 us  [the longest x6 13.6 us: _line_gather(): lax.ppermute(up[-1], 'own', perm=[(i, i + 1) for i in range(k - 1, own_co...]
    dynamic_update_slice x0 -> x12, local copies, waits for them, and re-layouts: none -> 10.9 us  [the longest x6 6.03 us: _line_gather(): out = lax.dynamic_update_slice(out, up[k][None], (me - k,) + zero)]
    ppermute x18, waiting for transfers between devices: 32.6 us -> 37.8 us  [advance(): self.x = keep + lax.ppermute(send, 'rep', perm=pairs)]
    dot_general x6, matrix products: 22.3 us -> 17.5 us  [on_device(): jnp.dot(lhs, weight[:, h * half:(h + 1) * half], preferred_element_type=j...]
    all_gather x3 -> x1, waiting for transfers between devices: 3.81 us -> 0.01 us  [on_device(): lax.all_gather(local4[:, bounds[c]:bounds[c + 1]], 'own', axis=0, tiled=T...]
    add x14, other arithmetic: 6.75 us -> 3.57 us  [advance(): self.x = keep + lax.ppermute(send, 'rep', perm=pairs)]
  transfers between devices with their start and end apart: 22 -> 32, of which waited for: 12 -> 17; matrix products, arithmetic and copies ran while one was open for 14% -> 10% of each run, Pallas kernels for 5% -> 4%
where the time goes in v7:
time: 236 us; the launch traced here: 235 us
  waiting for transfers between devices  122 us (52%)
  starting transfers between devices  41.8 us (18%)
  local copies, waits for them, and re-layouts  22.7 us (10%)
  matrix products  17.5 us (7%)
  between operations  14 us (6%)
  Pallas kernels  10.2 us (4%)
  other arithmetic  6.28 us (3%)
    ppermute x6, waiting for transfers between devices, _line_gather(): lax.ppermute(down[-1], 'own', perm=[(i + 1, i) for i in range(own_count -...  84.4 us
    ppermute x18, waiting for transfers between devices, advance(): self.x = keep + lax.ppermute(send, 'rep', perm=pairs)  37.8 us
    dot_general x6, matrix products, on_device(): jnp.dot(lhs, weight[:, h * half:(h + 1) * half], preferred_element_type=j...  17.5 us
    ppermute x6, starting transfers between devices, _line_gather(): lax.ppermute(up[-1], 'own', perm=[(i, i + 1) for i in range(k - 1, own_co...  13.6 us
    ppermute x18, starting transfers between devices, advance(): self.x = keep + lax.ppermute(send, 'rep', perm=pairs)  13.6 us
    pallas_call x1, Pallas kernels, _dense_weight(): pl.pallas_call(_weight_kernel, grid_spec=grid_spec, out_shape=jax.ShapeDt...  10.2 us
    ppermute x6, starting transfers between devices, _line_gather(): lax.ppermute(down[-1], 'own', perm=[(i + 1, i) for i in range(own_count -...  7.72 us
    all_to_all x1, starting transfers between devices, on_device(): lax.all_to_all(integrals, ('own', 'rep'), split_axis=0, concat_axis=0, ti...  6.92 us
  transfers between devices with their start and end apart: 32, of which 17 were waited for; matrix products, arithmetic and copies ran while one was open for 10% of the time, Pallas kernels for 4%

profile of v7, /device:TPU:0, one launch (start us, length us, event | category | flops | bytes accessed | tf_op | source)
XLA Modules:
  0.0 234.8 jit_solution(12053777000193528105)
XLA Ops:
  6.5 1.9 fusion.22
  8.5 4.9 %collective-permute-start.6 = (bf16[2,1,32,2048]{3,2,1,0:T(8,128)(2,1)}, bf16[2,1,32,2048]{3,2,1,0:T(8,128)(2,1)S(1)}, u32[]{:S(2)}, u32[]{:S(2)}) collective-permute-start(bf16[2,1,32,2048]{3,2,1,0:T(8,128)(2,1)} %get-tuple-element.23), channel_id=1, source_target_pairs={{0,8},{8,16},{16,24},{1,9},{9,17},{17,25},{2,10},{10,18},{18,26},{... | collective-permute-start | bytes 786440 | tf_op jit(solution)/shard_map/ppermute | solution.py:90
  14.7 4.6 %collective-permute-start = (bf16[2,1,32,2048]{3,2,1,0:T(8,128)(2,1)}, bf16[2,1,32,2048]{3,2,1,0:T(8,128)(2,1)S(1)}, u32[]{:S(2)}, u32[]{:S(2)}) collective-permute-start(bf16[2,1,32,2048]{3,2,1,0:T(8,128)(2,1)} %get-tuple-element.24), channel_id=1, source_target_pairs={{0,8},{8,16},{16,24},{1,9},{9,17},{17,25},{2,10},{10,18},{18,26},{... | collective-permute-start | bytes 786440 | tf_op jit(solution)/shard_map/ppermute | solution.py:90
  20.6 1.9 slice.26
  22.5 6.9 %all-to-all-start = ((bf16[64,128,128]{2,1,0:T(8,128)(2,1)}), bf16[64,128,128]{2,1,0:T(8,128)(2,1)S(1)}, u32[]{:S(2)}, u32[]{:S(2)}) async-start(bf16[64,128,128]{2,1,0:T(8,128)(2,1)} %param.6), calls=%async_computation | async-start | bytes 4194304 | tf_op jit(solution)/shard_map/all_to_all | solution.py:107
  31.9 1.4 collective-permute-start.1
  34.6 1.4 collective-permute-start.8
  38.2 54.8 %collective-permute-done.10 = bf16[2,1,32,2048]{3,2,1,0:T(8,128)(2,1)} collective-permute-done((bf16[2,1,32,2048]{3,2,1,0:T(8,128)(2,1)S(1)}, bf16[2,1,32,2048]{3,2,1,0:T(8,128)(2,1)}, u32[]{:S(2)}, u32[]{:S(2)}) %collective-permute-start.10) | collective-permute-done | bytes 262176 | tf_op jit(solution)/shard_map/ppermute | solution.py:91
  94.9 12.6 %collective-permute-done.4 = bf16[2,1,32,2048]{3,2,1,0:T(8,128)(2,1)} collective-permute-done((bf16[2,1,32,2048]{3,2,1,0:T(8,128)(2,1)S(1)}, bf16[2,1,32,2048]{3,2,1,0:T(8,128)(2,1)}, u32[]{:S(2)}, u32[]{:S(2)}) %collective-permute-start.4) | collective-permute-done | bytes 262176 | tf_op jit(solution)/shard_map/ppermute | solution.py:91
  109.9 1.7 bitcast_dynamic-update-slice_fusion.6
  113.5 1.7 bitcast_dynamic-update-slice_fusion.4
  116.1 12.0 %collective-permute-done.11 = bf16[2,1,32,2048]{3,2,1,0:T(8,128)(2,1)S(1)} collective-permute-done((bf16[2,1,32,2048]{3,2,1,0:T(8,128)(2,1)}, bf16[2,1,32,2048]{3,2,1,0:T(8,128)(2,1)S(1)}, u32[]{:S(2)}, u32[]{:S(2)}) %collective-permute-start.11) | collective-permute-done | bytes 262176 | tf_op jit(solution)/shard_map/ppermute | solution.py:91
  128.1 5.0 %collective-permute-done.5 = bf16[2,1,32,2048]{3,2,1,0:T(8,128)(2,1)S(1)} collective-permute-done((bf16[2,1,32,2048]{3,2,1,0:T(8,128)(2,1)}, bf16[2,1,32,2048]{3,2,1,0:T(8,128)(2,1)S(1)}, u32[]{:S(2)}, u32[]{:S(2)}) %collective-permute-start.5) | collective-permute-done | bytes 262176 | tf_op jit(solution)/shard_map/ppermute | solution.py:91
  133.9 1.7 bitcast_dynamic-update-slice_fusion.2
  137.2 1.4 copy-done.1
  138.6 10.2 %shard_map.55 = bf16[2048,2048]{1,0:T(8,128)(2,1)} custom-call(s32[64]{0:T(128)} %select_reduce_fusion.order_ref, s32[17]{0:T(128)} %convert_reduce_fusion.1.starts_ref, s32[64]{0:T(128)} %reshape.98.cd_ref, bf16[64,128,128]{2,1,0:T(8,128)(2,1)} %copy-done.1), custom_call_target="tpu_custom_call" | custom-call | bytes 10485760 | tf_op jit(solution)/shard_map/pallas_call | solution.py:49
  148.8 5.3 %fusion.14 = f32[1024,512]{0,1:T(8,128)S(1)} fusion(bf16[512,2048]{1,0:T(8,128)(2,1)} %bitcast.166, bf16[2048,2048]{1,0:T(8,128)(2,1)} %shard_map.55), kind=kOutput, calls=%fused_computation.14 | convolution fusion | flops 2147483648 | bytes 8388608 | tf_op jit(solution)/shard_map/dot_general | solution.py:144
  154.6 2.3 fusion.10
  161.5 2.5 %fusion.6 = f32[2,2,2,32,1024]{4,3,2,1,0:T(8,128)S(1)} fusion(bf16[2,2,2,32,2048]{4,3,2,1,0:T(8,128)(2,1)} %bitcast.33, bf16[2048,2048]{1,0:T(8,128)(2,1)S(1)} %copy-done), kind=kOutput, calls=%fused_computation.6 | convolution fusion | flops 1073741824 | bytes 6291456 | tf_op jit(solution)/shard_map/dot_general | solution.py:144
  165.3 2.5 %fusion.2 = f32[2,2,2,32,1024]{4,3,2,1,0:T(8,128)S(1)} fusion(bf16[2,2,2,32,2048]{4,3,2,1,0:T(8,128)(2,1)} %bitcast.33, bf16[2048,2048]{1,0:T(8,128)(2,1)S(1)} %copy-done), kind=kOutput, calls=%fused_computation.2 | convolution fusion | flops 1073741824 | bytes 6291456 | tf_op jit(solution)/shard_map/dot_general | solution.py:144
  171.4 2.0 collective-permute-start.15
  174.7 1.4 bitcast_add_fusion.4
  176.2 7.9 %collective-permute-done.14 = f32[2,64,1024]{2,1,0:T(8,128)S(1)} collective-permute-done((f32[2,64,1024]{2,1,0:T(8,128)S(1)}, f32[2,64,1024]{2,1,0:T(8,128)S(1)}, u32[]{:S(2)}, u32[]{:S(2)}) %collective-permute-start.14) | collective-permute-done | bytes 524320 | tf_op jit(solution)/shard_map/ppermute | solution.py:78
  185.5 3.6 %fusion = f32[2,2,2,32,1024]{4,3,2,1,0:T(8,128)S(1)} fusion(bf16[2,2,2,32,2048]{4,3,2,1,0:T(8,128)(2,1)S(1)} %bitcast.161, bf16[2048,2048]{1,0:T(8,128)(2,1)} %shard_map.55), kind=kOutput, calls=%fused_computation | convolution fusion | flops 1073741824 | bytes 6291456 | tf_op jit(solution)/shard_map/dot_general | solution.py:144
  191.2 1.8 collective-permute-start.22
  193.6 1.6 collective-permute-start.19
  195.2 4.3 %collective-permute-done.22 = f32[2,32,1024]{2,1,0:T(8,128)S(1)} collective-permute-done((f32[2,32,1024]{2,1,0:T(8,128)S(1)}, f32[2,32,1024]{2,1,0:T(8,128)S(1)}, u32[]{:S(2)}, u32[]{:S(2)}) %collective-permute-start.22) | collective-permute-done | bytes 262176 | tf_op jit(solution)/shard_map/ppermute | solution.py:78
  199.5 1.7 collective-permute-start.18
  202.8 5.1 %collective-permute-done.19 = f32[64,1024]{1,0:T(8,128)S(1)} collective-permute-done((f32[64,1024]{1,0:T(8,128)S(1)}, f32[64,1024]{1,0:T(8,128)S(1)}, u32[]{:S(2)}, u32[]{:S(2)}) %collective-permute-start.19) | collective-permute-done | bytes 262176 | tf_op jit(solution)/shard_map/ppermute | solution.py:78
  209.5 3.9 %collective-permute-done.21 = f32[32,1024]{1,0:T(8,128)S(1)} collective-permute-done((f32[32,1024]{1,0:T(8,128)S(1)}, f32[32,1024]{1,0:T(8,128)S(1)}, u32[]{:S(2)}, u32[]{:S(2)}) %collective-permute-start.21) | collective-permute-done | bytes 131104 | tf_op jit(solution)/shard_map/ppermute | solution.py:78
  214.6 6.7 %collective-permute-done.28 = f32[2,32,1024]{2,1,0:T(8,128)S(1)} collective-permute-done((f32[2,32,1024]{2,1,0:T(8,128)S(1)}, f32[2,32,1024]{2,1,0:T(8,128)S(1)}, u32[]{:S(2)}, u32[]{:S(2)}) %collective-permute-start.28) | collective-permute-done | bytes 262176 | tf_op jit(solution)/shard_map/ppermute | solution.py:78
  222.8 3.5 %collective-permute-done.29 = f32[32,1024]{1,0:T(8,128)S(1)} collective-permute-done((f32[32,1024]{1,0:T(8,128)S(1)}, f32[32,1024]{1,0:T(8,128)S(1)}, u32[]{:S(2)}, u32[]{:S(2)}) %collective-permute-start.29) | collective-permute-done | bytes 131104 | tf_op jit(solution)/shard_map/ppermute | solution.py:78
  (134 shorter events, 40.6 us)
Async XLA Ops:
  6.5 142.3 %all-gather.2.cloned.1.call-start = ((), (), s32[]{:S(2)}) async-start(), calls=%async_computation.1 | async-start | bytes 2621440 | tf_op jit(solution)/shard_map/all_gather | solution.py:126
  8.5 21.0 %collective-permute-start.6 = (bf16[2,1,32,2048]{3,2,1,0:T(8,128)(2,1)}, bf16[2,1,32,2048]{3,2,1,0:T(8,128)(2,1)S(1)}, u32[]{:S(2)}, u32[]{:S(2)}) collective-permute-start(bf16[2,1,32,2048]{3,2,1,0:T(8,128)(2,1)} %get-tuple-element.23), channel_id=1, source_target_pairs={{0,8},{8,16},{16,24},{1,9},{9,17},{17,25},{2,10},{10,18},{18,26},{... | collective-permute-start | bytes 786440 | tf_op jit(solution)/shard_map/ppermute | solution.py:90
  13.4 17.2 %collective-permute-start.9 = (bf16[2,1,32,2048]{3,2,1,0:T(8,128)(2,1)}, bf16[2,1,32,2048]{3,2,1,0:T(8,128)(2,1)S(1)}, u32[]{:S(2)}, u32[]{:S(2)}) collective-permute-start(bf16[2,1,32,2048]{3,2,1,0:T(8,128)(2,1)} %get-tuple-element.23), channel_id=1, source_target_pairs={{8,0},{16,8},{24,16},{9,1},{17,9},{25,17},{10,2},{18,10},{26,18},{... | collective-permute-start | bytes 786440 | tf_op jit(solution)/shard_map/ppermute | solution.py:91
  14.7 17.2 %collective-permute-start = (bf16[2,1,32,2048]{3,2,1,0:T(8,128)(2,1)}, bf16[2,1,32,2048]{3,2,1,0:T(8,128)(2,1)S(1)}, u32[]{:S(2)}, u32[]{:S(2)}) collective-permute-start(bf16[2,1,32,2048]{3,2,1,0:T(8,128)(2,1)} %get-tuple-element.24), channel_id=1, source_target_pairs={{0,8},{8,16},{16,24},{1,9},{9,17},{17,25},{2,10},{10,18},{18,26},{... | collective-permute-start | bytes 786440 | tf_op jit(solution)/shard_map/ppermute | solution.py:90
  19.3 14.0 %collective-permute-start.3 = (bf16[2,1,32,2048]{3,2,1,0:T(8,128)(2,1)}, bf16[2,1,32,2048]{3,2,1,0:T(8,128)(2,1)S(1)}, u32[]{:S(2)}, u32[]{:S(2)}) collective-permute-start(bf16[2,1,32,2048]{3,2,1,0:T(8,128)(2,1)} %get-tuple-element.24), channel_id=1, source_target_pairs={{8,0},{16,8},{24,16},{9,1},{17,9},{25,17},{10,2},{18,10},{26,18},{... | collective-permute-start | bytes 786440 | tf_op jit(solution)/shard_map/ppermute | solution.py:91
  22.5 114.7 %all-to-all-start = ((bf16[64,128,128]{2,1,0:T(8,128)(2,1)}), bf16[64,128,128]{2,1,0:T(8,128)(2,1)S(1)}, u32[]{:S(2)}, u32[]{:S(2)}) async-start(bf16[64,128,128]{2,1,0:T(8,128)(2,1)} %param.6), calls=%async_computation | async-start | bytes 4194304 | tf_op jit(solution)/shard_map/all_to_all | solution.py:107
  29.5 5.1 %collective-permute-start.7 = (bf16[2,1,32,2048]{3,2,1,0:T(8,128)(2,1)S(1)}, bf16[2,1,32,2048]{3,2,1,0:T(8,128)(2,1)S(1)}, u32[]{:S(2)}, u32[]{:S(2)}) collective-permute-start(bf16[2,1,32,2048]{3,2,1,0:T(8,128)(2,1)S(1)} %collective-permute-done.6), channel_id=1, source_target_pairs={{8,16},{16,24},{9,17},{17,25},{10,18},{18,26},{11,19},{19,27},{12,... | collective-permute-start | bytes 786440 | tf_op jit(solution)/shard_map/ppermute | solution.py:90
  30.6 62.4 %collective-permute-start.10 = (bf16[2,1,32,2048]{3,2,1,0:T(8,128)(2,1)S(1)}, bf16[2,1,32,2048]{3,2,1,0:T(8,128)(2,1)}, u32[]{:S(2)}, u32[]{:S(2)}) collective-permute-start(bf16[2,1,32,2048]{3,2,1,0:T(8,128)(2,1)S(1)} %collective-permute-done.9), channel_id=1, source_target_pairs={{8,0},{16,8},{9,1},{17,9},{10,2},{18,10},{11,3},{19,11},{12,4},{20... | collective-permute-start | bytes 786440 | tf_op jit(solution)/shard_map/ppermute | solution.py:91
  31.9 62.3 %collective-permute-start.1 = (bf16[2,1,32,2048]{3,2,1,0:T(8,128)(2,1)S(1)}, bf16[2,1,32,2048]{3,2,1,0:T(8,128)(2,1)}, u32[]{:S(2)}, u32[]{:S(2)}) collective-permute-start(bf16[2,1,32,2048]{3,2,1,0:T(8,128)(2,1)S(1)} %collective-permute-done), channel_id=1, source_target_pairs={{8,16},{16,24},{9,17},{17,25},{10,18},{18,26},{11,19},{19,27},{12,... | collective-permute-start | bytes 786440 | tf_op jit(solution)/shard_map/ppermute | solution.py:90
  33.3 74.3 %collective-permute-start.4 = (bf16[2,1,32,2048]{3,2,1,0:T(8,128)(2,1)S(1)}, bf16[2,1,32,2048]{3,2,1,0:T(8,128)(2,1)}, u32[]{:S(2)}, u32[]{:S(2)}) collective-permute-start(bf16[2,1,32,2048]{3,2,1,0:T(8,128)(2,1)S(1)} %collective-permute-done.3), channel_id=1, source_target_pairs={{8,0},{16,8},{9,1},{17,9},{10,2},{18,10},{11,3},{19,11},{12,4},{20... | collective-permute-start | bytes 786440 | tf_op jit(solution)/shard_map/ppermute | solution.py:91
  34.6 74.3 %collective-permute-start.8 = (bf16[2,1,32,2048]{3,2,1,0:T(8,128)(2,1)S(1)}, bf16[2,1,32,2048]{3,2,1,0:T(8,128)(2,1)}, u32[]{:S(2)}, u32[]{:S(2)}) collective-permute-start(bf16[2,1,32,2048]{3,2,1,0:T(8,128)(2,1)S(1)} %collective-permute-done.7), channel_id=1, source_target_pairs={{16,24},{17,25},{18,26},{19,27},{20,28},{21,29},{22,30},{23,31}} | collective-permute-start | bytes 786440 | tf_op jit(solution)/shard_map/ppermute | solution.py:90
  92.9 35.2 %collective-permute-start.11 = (bf16[2,1,32,2048]{3,2,1,0:T(8,128)(2,1)}, bf16[2,1,32,2048]{3,2,1,0:T(8,128)(2,1)S(1)}, u32[]{:S(2)}, u32[]{:S(2)}) collective-permute-start(bf16[2,1,32,2048]{3,2,1,0:T(8,128)(2,1)} %collective-permute-done.10), channel_id=1, source_target_pairs={{8,0},{9,1},{10,2},{11,3},{12,4},{13,5},{14,6},{15,7}} | collective-permute-start | bytes 786440 | tf_op jit(solution)/shard_map/ppermute | solution.py:91
  94.2 18.1 %collective-permute-start.2 = (bf16[2,1,32,2048]{3,2,1,0:T(8,128)(2,1)}, bf16[2,1,32,2048]{3,2,1,0:T(8,128)(2,1)S(1)}, u32[]{:S(2)}, u32[]{:S(2)}) collective-permute-start(bf16[2,1,32,2048]{3,2,1,0:T(8,128)(2,1)} %collective-permute-done.1), channel_id=1, source_target_pairs={{16,24},{17,25},{18,26},{19,27},{20,28},{21,29},{22,30},{23,31}} | collective-permute-start | bytes 786440 | tf_op jit(solution)/shard_map/ppermute | solution.py:90
  107.6 25.5 %collective-permute-start.5 = (bf16[2,1,32,2048]{3,2,1,0:T(8,128)(2,1)}, bf16[2,1,32,2048]{3,2,1,0:T(8,128)(2,1)S(1)}, u32[]{:S(2)}, u32[]{:S(2)}) collective-permute-start(bf16[2,1,32,2048]{3,2,1,0:T(8,128)(2,1)} %collective-permute-done.4), channel_id=1, source_target_pairs={{8,0},{9,1},{10,2},{11,3},{12,4},{13,5},{14,6},{15,7}} | collective-permute-start | bytes 786440 | tf_op jit(solution)/shard_map/ppermute | solution.py:91
  157.1 2.7 %collective-permute-start.12 = (f32[2,2,64,1024]{3,2,1,0:T(8,128)S(1)}, f32[2,2,64,1024]{3,2,1,0:T(8,128)S(1)}, u32[]{:S(2)}, u32[]{:S(2)}) collective-permute-start(f32[2,2,64,1024]{3,2,1,0:T(8,128)S(1)} %dynamic-slice_bitcast_fusion.1), channel_id=1, source_target_pairs={{0,1},{1,0},{2,3},{3,2},{4,5},{5,4},{6,7},{7,6},{8,9},{9,8},{10,11... | collective-permute-start | bytes 3145736 | tf_op jit(solution)/shard_map/ppermute | solution.py:78
  157.2 4.1 %collective-permute-start.13 = (f32[2,2,64,1024]{3,2,1,0:T(8,128)S(1)}, f32[2,2,64,1024]{3,2,1,0:T(8,128)S(1)}, u32[]{:S(2)}, u32[]{:S(2)}) collective-permute-start(f32[2,2,64,1024]{3,2,1,0:T(8,128)S(1)} %dynamic-slice_bitcast_fusion), channel_id=1, source_target_pairs={{0,1},{1,0},{2,3},{3,2},{4,5},{5,4},{6,7},{7,6},{8,9},{9,8},{10,11... | collective-permute-start | bytes 3145736 | tf_op jit(solution)/shard_map/ppermute | solution.py:78
  165.2 8.3 %collective-permute-start.16 = (f32[2,2,32,1024]{3,2,1,0:T(8,128)}, f32[2,2,32,1024]{3,2,1,0:T(8,128)}, u32[]{:S(2)}, u32[]{:S(2)}) collective-permute-start(f32[2,2,32,1024]{3,2,1,0:T(8,128)} %dynamic-slice_bitcast_fusion.5), channel_id=1, source_target_pairs={{0,1},{1,0},{2,3},{3,2},{4,5},{5,4},{6,7},{7,6},{8,9},{9,8},{10,11... | collective-permute-start | bytes 1572872 | tf_op jit(solution)/shard_map/ppermute | solution.py:78
  169.6 5.1 %collective-permute-start.17 = (f32[2,2,32,1024]{3,2,1,0:T(8,128)}, f32[2,2,32,1024]{3,2,1,0:T(8,128)}, u32[]{:S(2)}, u32[]{:S(2)}) collective-permute-start(f32[2,2,32,1024]{3,2,1,0:T(8,128)} %dynamic-slice_bitcast_fusion.4), channel_id=1, source_target_pairs={{0,1},{1,0},{2,3},{3,2},{4,5},{5,4},{6,7},{7,6},{8,9},{9,8},{10,11... | collective-permute-start | bytes 1572872 | tf_op jit(solution)/shard_map/ppermute | solution.py:78
  170.1 14.0 %collective-permute-start.14 = (f32[2,64,1024]{2,1,0:T(8,128)S(1)}, f32[2,64,1024]{2,1,0:T(8,128)S(1)}, u32[]{:S(2)}, u32[]{:S(2)}) collective-permute-start(f32[2,64,1024]{2,1,0:T(8,128)S(1)} %dynamic-slice_bitcast_fusion.7), channel_id=1, source_target_pairs={{0,2},{1,3},{2,0},{3,1},{4,6},{5,7},{6,4},{7,5},{8,10},{9,11},{10,... | collective-permute-start | bytes 1572872 | tf_op jit(solution)/shard_map/ppermute | solution.py:78
  171.4 14.0 %collective-permute-start.15 = (f32[2,64,1024]{2,1,0:T(8,128)S(1)}, f32[2,64,1024]{2,1,0:T(8,128)S(1)}, u32[]{:S(2)}, u32[]{:S(2)}) collective-permute-start(f32[2,64,1024]{2,1,0:T(8,128)S(1)} %dynamic-slice_bitcast_fusion.6), channel_id=1, source_target_pairs={{0,4},{1,5},{2,6},{3,7},{4,0},{5,1},{6,2},{7,3},{8,12},{9,13},{10,... | collective-permute-start | bytes 1572872 | tf_op jit(solution)/shard_map/ppermute | solution.py:78
  190.4 22.9 %collective-permute-start.27 = (f32[2,2,32,1024]{3,2,1,0:T(8,128)S(1)}, f32[2,2,32,1024]{3,2,1,0:T(8,128)S(1)}, u32[]{:S(2)}, u32[]{:S(2)}) collective-permute-start(f32[2,2,32,1024]{3,2,1,0:T(8,128)S(1)} %dynamic-slice_bitcast_fusion.2), channel_id=1, source_target_pairs={{0,1},{1,0},{2,3},{3,2},{4,5},{5,4},{6,7},{7,6},{8,9},{9,8},{10,11... | collective-permute-start | bytes 1572872 | tf_op jit(solution)/shard_map/ppermute | solution.py:78
  190.6 23.2 %collective-permute-start.24 = (f32[2,2,32,1024]{3,2,1,0:T(8,128)S(1)}, f32[2,2,32,1024]{3,2,1,0:T(8,128)S(1)}, u32[]{:S(2)}, u32[]{:S(2)}) collective-permute-start(f32[2,2,32,1024]{3,2,1,0:T(8,128)S(1)} %dynamic-slice_bitcast_fusion.3), channel_id=1, source_target_pairs={{0,1},{1,0},{2,3},{3,2},{4,5},{5,4},{6,7},{7,6},{8,9},{9,8},{10,11... | collective-permute-start | bytes 1572872 | tf_op jit(solution)/shard_map/ppermute | solution.py:78
  191.2 8.3 %collective-permute-start.22 = (f32[2,32,1024]{2,1,0:T(8,128)S(1)}, f32[2,32,1024]{2,1,0:T(8,128)S(1)}, u32[]{:S(2)}, u32[]{:S(2)}) collective-permute-start(f32[2,32,1024]{2,1,0:T(8,128)S(1)} %dynamic-slice_bitcast_fusion.10), channel_id=1, source_target_pairs={{0,4},{1,5},{2,6},{3,7},{4,0},{5,1},{6,2},{7,3},{8,12},{9,13},{10,... | collective-permute-start | bytes 786440 | tf_op jit(solution)/shard_map/ppermute | solution.py:78
  193.0 9.3 %collective-permute-start.20 = (f32[2,32,1024]{2,1,0:T(8,128)S(1)}, f32[2,32,1024]{2,1,0:T(8,128)S(1)}, u32[]{:S(2)}, u32[]{:S(2)}) collective-permute-start(f32[2,32,1024]{2,1,0:T(8,128)S(1)} %dynamic-slice_bitcast_fusion.11), channel_id=1, source_target_pairs={{0,2},{1,3},{2,0},{3,1},{4,6},{5,7},{6,4},{7,5},{8,10},{9,11},{10,... | collective-permute-start | bytes 786440 | tf_op jit(solution)/shard_map/ppermute | solution.py:78
  193.6 14.3 %collective-permute-start.19 = (f32[64,1024]{1,0:T(8,128)S(1)}, f32[64,1024]{1,0:T(8,128)S(1)}, u32[]{:S(2)}, u32[]{:S(2)}) collective-permute-start(f32[64,1024]{1,0:T(8,128)S(1)} %dynamic-slice_bitcast_fusion.12), channel_id=1, source_target_pairs={{0,2},{1,3},{2,0},{3,1},{4,6},{5,7},{6,4},{7,5},{8,10},{9,11},{10,... | collective-permute-start | bytes 786440 | tf_op jit(solution)/shard_map/ppermute | solution.py:78
  199.5 8.7 %collective-permute-start.18 = (f32[64,1024]{1,0:T(8,128)S(1)}, f32[64,1024]{1,0:T(8,128)S(1)}, u32[]{:S(2)}, u32[]{:S(2)}) collective-permute-start(f32[64,1024]{1,0:T(8,128)S(1)} %dynamic-slice_bitcast_fusion.13), channel_id=1, source_target_pairs={{0,4},{1,5},{2,6},{3,7},{4,0},{5,1},{6,2},{7,3},{8,12},{9,13},{10,... | collective-permute-start | bytes 786440 | tf_op jit(solution)/shard_map/ppermute | solution.py:78
  202.3 7.2 %collective-permute-start.23 = (f32[32,1024]{1,0:T(8,128)S(1)}, f32[32,1024]{1,0:T(8,128)S(1)}, u32[]{:S(2)}, u32[]{:S(2)}) collective-permute-start(f32[32,1024]{1,0:T(8,128)S(1)} %dynamic-slice_bitcast_fusion.16), channel_id=1, source_target_pairs={{0,2},{1,3},{2,0},{3,1},{4,6},{5,7},{6,4},{7,5},{8,10},{9,11},{10,... | collective-permute-start | bytes 393224 | tf_op jit(solution)/shard_map/ppermute | solution.py:78
  207.9 5.5 %collective-permute-start.21 = (f32[32,1024]{1,0:T(8,128)S(1)}, f32[32,1024]{1,0:T(8,128)S(1)}, u32[]{:S(2)}, u32[]{:S(2)}) collective-permute-start(f32[32,1024]{1,0:T(8,128)S(1)} %dynamic-slice_bitcast_fusion.17), channel_id=1, source_target_pairs={{0,4},{1,5},{2,6},{3,7},{4,0},{5,1},{6,2},{7,3},{8,12},{9,13},{10,... | collective-permute-start | bytes 393224 | tf_op jit(solution)/shard_map/ppermute | solution.py:78
  213.5 7.8 %collective-permute-start.28 = (f32[2,32,1024]{2,1,0:T(8,128)S(1)}, f32[2,32,1024]{2,1,0:T(8,128)S(1)}, u32[]{:S(2)}, u32[]{:S(2)}) collective-permute-start(f32[2,32,1024]{2,1,0:T(8,128)S(1)} %dynamic-slice_bitcast_fusion.8), channel_id=1, source_target_pairs={{0,4},{1,5},{2,6},{3,7},{4,0},{5,1},{6,2},{7,3},{8,12},{9,13},{10,... | collective-permute-start | bytes 786440 | tf_op jit(solution)/shard_map/ppermute | solution.py:78
  213.9 7.8 %collective-permute-start.25 = (f32[2,32,1024]{2,1,0:T(8,128)S(1)}, f32[2,32,1024]{2,1,0:T(8,128)S(1)}, u32[]{:S(2)}, u32[]{:S(2)}) collective-permute-start(f32[2,32,1024]{2,1,0:T(8,128)S(1)} %dynamic-slice_bitcast_fusion.9), channel_id=1, source_target_pairs={{0,2},{1,3},{2,0},{3,1},{4,6},{5,7},{6,4},{7,5},{8,10},{9,11},{10,... | collective-permute-start | bytes 786440 | tf_op jit(solution)/shard_map/ppermute | solution.py:78
  221.3 5.0 %collective-permute-start.29 = (f32[32,1024]{1,0:T(8,128)S(1)}, f32[32,1024]{1,0:T(8,128)S(1)}, u32[]{:S(2)}, u32[]{:S(2)}) collective-permute-start(f32[32,1024]{1,0:T(8,128)S(1)} %dynamic-slice_bitcast_fusion.14), channel_id=1, source_target_pairs={{0,2},{1,3},{2,0},{3,1},{4,6},{5,7},{6,4},{7,5},{8,10},{9,11},{10,... | collective-permute-start | bytes 393224 | tf_op jit(solution)/shard_map/ppermute | solution.py:78
  221.8 5.0 %collective-permute-start.26 = (f32[32,1024]{1,0:T(8,128)S(1)}, f32[32,1024]{1,0:T(8,128)S(1)}, u32[]{:S(2)}, u32[]{:S(2)}) collective-permute-start(f32[32,1024]{1,0:T(8,128)S(1)} %dynamic-slice_bitcast_fusion.15), channel_id=1, source_target_pairs={{0,4},{1,5},{2,6},{3,7},{4,0},{5,1},{6,2},{7,3},{8,12},{9,13},{10,... | collective-permute-start | bytes 393224 | tf_op jit(solution)/shard_map/ppermute | solution.py:78
  (15 other events, 380.6 us)
Sparse Core Ops, SparseCore 0:
  22.6 86.4 all-gather.1

commit v8 on v6

--- a/solution.py
+++ b/solution.py
@@ -8,7 +8,7 @@
 from jax.sharding import PartitionSpec as P
 
 AB_DEV = 16
-CHUNKS = (4, 2, 1, 1)
+CHUNKS = (3, 1)
 
 
 def _slot_order(ab_ids, live_mask, ab_count):

time: 233 us -> 222 us (0.953)
  waiting for transfers between devices: 108 us -> 143 us
  blocking collectives: 32.9 us -> 0 us
  starting transfers between devices: 28.2 us -> 18.4 us
  matrix products: 20.6 us -> 17 us
  local copies, waits for them, and re-layouts: 10.4 us -> 13.1 us
    all_gather x2 -> x0, blocking collectives: 32.9 us -> none  [on_device(): lax.all_gather(local4[:, bounds[c]:bounds[c + 1]], 'own', axis=0, tiled=T...]
    all_gather x2, waiting for transfers between devices: 0.02 us -> 24.6 us  [on_device(): lax.all_gather(local4[:, bounds[c]:bounds[c + 1]], 'own', axis=0, tiled=T...]
    all_to_all x1, waiting for transfers between devices: 78 us -> 91.4 us  [on_device(): lax.all_to_all(integrals, ('own', 'rep'), split_axis=0, concat_axis=0, ti...]
    ppermute x24 -> x12, starting transfers between devices: 20.8 us -> 11.1 us  [advance(): self.x = keep + lax.ppermute(send, 'rep', perm=pairs)]
    dot_general x8 -> x4, matrix products: 20.6 us -> 17 us  [on_device(): jnp.dot(lhs, weight[:, h * half:(h + 1) * half], preferred_element_type=j...]
    unnamed x32 -> x22, local copies, waits for them, and re-layouts: 3.66 us -> 6.56 us
    ppermute x24 -> x12, waiting for transfers between devices: 29.5 us -> 26.8 us  [advance(): self.x = keep + lax.ppermute(send, 'rep', perm=pairs)]
    add x20 -> x10, other arithmetic: 5.96 us -> 4.01 us  [advance(): self.x = keep + lax.ppermute(send, 'rep', perm=pairs)]
  transfers between devices with their start and end apart: 27 -> 15, of which waited for: 14 -> 6; matrix products, arithmetic and copies ran while one was open for 9% -> 8% of each run, Pallas kernels for 4% -> 5%
where the time goes in v8:
time: 222 us
  waiting for transfers between devices  143 us (64%)
  starting transfers between devices  18.4 us (8%)
  matrix products  17 us (8%)
  between operations  13.7 us (6%)
  local copies, waits for them, and re-layouts  13.1 us (6%)
  Pallas kernels  10.2 us (5%)
  other arithmetic  6.68 us (3%)
    all_to_all x1, waiting for transfers between devices, on_device(): lax.all_to_all(integrals, ('own', 'rep'), split_axis=0, concat_axis=0, ti...  91.4 us
    ppermute x12, waiting for transfers between devices, advance(): self.x = keep + lax.ppermute(send, 'rep', perm=pairs)  26.8 us
    all_gather x2, waiting for transfers between devices, on_device(): lax.all_gather(local4[:, bounds[c]:bounds[c + 1]], 'own', axis=0, tiled=T...  24.6 us
    dot_general x4, matrix products, on_device(): jnp.dot(lhs, weight[:, h * half:(h + 1) * half], preferred_element_type=j...  17 us
    ppermute x12, starting transfers between devices, advance(): self.x = keep + lax.ppermute(send, 'rep', perm=pairs)  11.1 us
    pallas_call x1, Pallas kernels, _dense_weight(): pl.pallas_call(_weight_kernel, grid_spec=grid_spec, out_shape=jax.ShapeDt...  10.2 us
    all_to_all x1, starting transfers between devices, on_device(): lax.all_to_all(integrals, ('own', 'rep'), split_axis=0, concat_axis=0, ti...  7.3 us
    unnamed x22, local copies, waits for them, and re-layouts  6.56 us
  transfers between devices with their start and end apart: 15, of which 6 were waited for; matrix products, arithmetic and copies ran while one was open for 8% of the time, Pallas kernels for 5%

profile of v8, /device:TPU:0, one launch (start us, length us, event | category | flops | bytes accessed | tf_op | source)
XLA Modules:
  0.0 221.8 jit_solution(11340706442573021821)
XLA Ops:
  6.5 2.1 slice.19
  8.7 7.3 %all-to-all-start = ((bf16[64,128,128]{2,1,0:T(8,128)(2,1)}), bf16[64,128,128]{2,1,0:T(8,128)(2,1)S(1)}, u32[]{:S(2)}, u32[]{:S(2)}) async-start(bf16[64,128,128]{2,1,0:T(8,128)(2,1)} %param.6), calls=%async_computation | async-start | bytes 4194304 | tf_op jit(solution)/shard_map/all_to_all | solution.py:90
  16.6 0.7 reshape.77.cd_ref
  17.3 0.7 convert_reduce_fusion.1.starts_ref
  18.1 0.6 select_reduce_fusion.order_ref
  18.8 91.4 %all-to-all-done.tiles_ref = bf16[64,128,128]{2,1,0:T(8,128)(2,1)S(1)} async-done(((bf16[64,128,128]{2,1,0:T(8,128)(2,1)}), bf16[64,128,128]{2,1,0:T(8,128)(2,1)S(1)}, u32[]{:S(2)}, u32[]{:S(2)}) %all-to-all-start) | async-done | bytes 2097184 | tf_op jit(solution)/shard_map/all_to_all | solution.py:90
  110.1 1.5 copy-done.1
  111.6 10.2 %shard_map.55 = bf16[2048,2048]{1,0:T(8,128)(2,1)} custom-call(s32[64]{0:T(128)} %select_reduce_fusion.order_ref, s32[17]{0:T(128)} %convert_reduce_fusion.1.starts_ref, s32[64]{0:T(128)} %reshape.77.cd_ref, bf16[64,128,128]{2,1,0:T(8,128)(2,1)} %copy-done.1), custom_call_target="tpu_custom_call" | custom-call | bytes 10485760 | tf_op jit(solution)/shard_map/pallas_call | solution.py:49
  121.8 6.3 %fusion.5 = f32[1024,768]{0,1:T(8,128)S(1)} fusion(bf16[768,2048]{1,0:T(8,128)(2,1)} %bitcast.92, bf16[2048,2048]{1,0:T(8,128)(2,1)} %shard_map.55), kind=kOutput, calls=%fused_computation.5 | convolution fusion | flops 3221225472 | bytes 10485760 | tf_op jit(solution)/shard_map/dot_general | solution.py:125
  128.2 1.6 copy-done.4
  129.9 1.3 copy-done.8
  131.1 3.4 %fusion.8 = f32[1024,768]{0,1:T(8,128)S(1)} fusion(bf16[768,2048]{1,0:T(8,128)(2,1)S(1)} %bitcast.93, bf16[2048,2048]{1,0:T(8,128)(2,1)S(1)} %copy-done), kind=kOutput, calls=%fused_computation.8 | convolution fusion | flops 3221225472 | bytes 10485760 | tf_op jit(solution)/shard_map/dot_general | solution.py:125
  134.6 1.7 copy-done.2
  136.3 1.3 dynamic-slice_bitcast_fusion.1
  137.6 1.7 slice.18
  139.3 1.8 bitcast_add_fusion
  141.7 1.7 bitcast_add_fusion.1
  143.3 24.6 %all-gather.3.cloned.1.call-done = bf16[8,1,32,2048]{3,2,1,0:T(8,128)(2,1)} async-done(((bf16[2,1,32,2048]{3,2,1,0:T(8,128)(2,1)}), bf16[8,1,32,2048]{3,2,1,0:T(8,128)(2,1)}) %all-gather.3.cloned.1.call-update) | async-done | bytes 1048592 | tf_op jit(solution)/shard_map/all_gather | solution.py:109
  167.9 3.8 %fusion.2 = f32[2,2,2,32,1024]{4,3,2,1,0:T(8,128)S(1)} fusion(bf16[2,2,2,32,2048]{4,3,2,1,0:T(8,128)(2,1)} %bitcast.94, bf16[2048,2048]{1,0:T(8,128)(2,1)} %shard_map.55), kind=kOutput, calls=%fused_computation.2 | convolution fusion | flops 1073741824 | bytes 6291456 | tf_op jit(solution)/shard_map/dot_general | solution.py:125
  171.9 3.5 %fusion = f32[2,2,2,32,1024]{4,3,2,1,0:T(8,128)S(1)} fusion(bf16[2,2,2,32,2048]{4,3,2,1,0:T(8,128)(2,1)S(1)} %bitcast.95, bf16[2048,2048]{1,0:T(8,128)(2,1)} %shard_map.55), kind=kOutput, calls=%fused_computation | convolution fusion | flops 1073741824 | bytes 6291456 | tf_op jit(solution)/shard_map/dot_general | solution.py:125
  176.0 1.5 collective-permute-start.2
  177.6 1.5 collective-permute-start.4
  179.2 0.6 collective-permute-start.7
  180.0 0.6 collective-permute-start.10
  180.6 15.9 %collective-permute-done.2 = f32[2,96,1024]{2,1,0:T(8,128)S(1)} collective-permute-done((f32[2,96,1024]{2,1,0:T(8,128)S(1)}, f32[2,96,1024]{2,1,0:T(8,128)S(1)}, u32[]{:S(2)}, u32[]{:S(2)}) %collective-permute-start.2) | collective-permute-done | bytes 786464 | tf_op jit(solution)/shard_map/ppermute | solution.py:78
  196.6 1.5 collective-permute-start.3
  198.3 1.5 collective-permute-start.5
  199.8 2.3 %collective-permute-done.7 = f32[2,32,1024]{2,1,0:T(8,128)S(1)} collective-permute-done((f32[2,32,1024]{2,1,0:T(8,128)S(1)}, f32[2,32,1024]{2,1,0:T(8,128)S(1)}, u32[]{:S(2)}, u32[]{:S(2)}) %collective-permute-start.7) | collective-permute-done | bytes 262176 | tf_op jit(solution)/shard_map/ppermute | solution.py:78
  202.2 1.5 collective-permute-start.8
  203.8 1.5 collective-permute-start.11
  205.3 8.4 %collective-permute-done.8 = f32[32,1024]{1,0:T(8,128)S(1)} collective-permute-done((f32[32,1024]{1,0:T(8,128)S(1)}, f32[32,1024]{1,0:T(8,128)S(1)}, u32[]{:S(2)}, u32[]{:S(2)}) %collective-permute-start.8) | collective-permute-done | bytes 131104 | tf_op jit(solution)/shard_map/ppermute | solution.py:78
  213.9 1.1 maximum_maximum_fusion
  (62 shorter events, 2.9 us)
Async XLA Ops:
  6.5 115.3 %all-gather.5.cloned.1.call-start = ((), (), s32[]{:S(2)}) async-start(), calls=%async_computation.2 | async-start | bytes 3932160 | tf_op jit(solution)/shard_map/all_gather | solution.py:109
  6.5 9.5 %copy-start.5 = (s32[1,32,2]{1,2,0:T(2,128)S(1)}, s32[1,32,2]{1,2,0:T(2,128)}, u32[]{:S(2)}) copy-start(s32[1,32,2]{1,2,0:T(2,128)} %param.7) | copy-start | bytes 772
  6.5 9.7 %copy-start.7 = (s32[1,32]{1,0:T(1,128)S(1)}, s32[1,32]{1,0:T(1,128)}, u32[]{:S(2)}) copy-start(s32[1,32]{1,0:T(1,128)} %param.9) | copy-start | bytes 388
  6.5 9.9 %copy-start.6 = (s32[1,32,2]{1,2,0:T(2,128)S(1)}, s32[1,32,2]{1,2,0:T(2,128)}, u32[]{:S(2)}) copy-start(s32[1,32,2]{1,2,0:T(2,128)} %param.8) | copy-start | bytes 772
  8.7 101.4 %all-to-all-start = ((bf16[64,128,128]{2,1,0:T(8,128)(2,1)}), bf16[64,128,128]{2,1,0:T(8,128)(2,1)S(1)}, u32[]{:S(2)}, u32[]{:S(2)}) async-start(bf16[64,128,128]{2,1,0:T(8,128)(2,1)} %param.6), calls=%async_computation | async-start | bytes 4194304 | tf_op jit(solution)/shard_map/all_to_all | solution.py:90
  16.0 151.9 %all-gather.3.cloned.1.call-start = ((), (), s32[]{:S(2)}) async-start(), calls=%async_computation.1 | async-start | bytes 1310720 | tf_op jit(solution)/shard_map/all_gather | solution.py:109
  110.1 1.5 copy-start.1
  121.8 8.1 %copy-start = (bf16[2048,2048]{1,0:T(8,128)(2,1)S(1)}, bf16[2048,2048]{1,0:T(8,128)(2,1)}, u32[]{:S(2)}) copy-start(bf16[2048,2048]{1,0:T(8,128)(2,1)} %shard_map.55) | copy-start | bytes 25165828
  128.1 1.7 copy-start.4
  128.1 3.0 %copy-start.8 = (bf16[8,3,32,2048]{3,2,1,0:T(8,128)(2,1)S(1)}, bf16[8,3,32,2048]{3,2,1,0:T(8,128)(2,1)}, u32[]{:S(2)}) copy-start(bf16[8,3,32,2048]{3,2,1,0:T(8,128)(2,1)} %all-gather.5.cloned.1.call-done) | copy-start | bytes 9437188
  129.9 9.5 %collective-permute-start.1 = (f32[2,2,96,1024]{3,2,1,0:T(8,128)S(1)}, f32[2,2,96,1024]{3,2,1,0:T(8,128)S(1)}, u32[]{:S(2)}, u32[]{:S(2)}) collective-permute-start(f32[2,2,96,1024]{3,2,1,0:T(8,128)S(1)} %dynamic-slice_bitcast_fusion), channel_id=1, source_target_pairs={{0,1},{1,0},{2,3},{3,2},{4,5},{5,4},{6,7},{7,6},{8,9},{9,8},{10,11... | collective-permute-start | bytes 4718600 | tf_op jit(solution)/shard_map/ppermute | solution.py:78
  134.6 1.7 copy-start.2
  137.6 3.8 %collective-permute-start = (f32[2,2,96,1024]{3,2,1,0:T(8,128)}, f32[2,2,96,1024]{3,2,1,0:T(8,128)}, u32[]{:S(2)}, u32[]{:S(2)}) collective-permute-start(f32[2,2,96,1024]{3,2,1,0:T(8,128)} %dynamic-slice_bitcast_fusion.1), channel_id=1, source_target_pairs={{0,1},{1,0},{2,3},{3,2},{4,5},{5,4},{6,7},{7,6},{8,9},{9,8},{10,11... | collective-permute-start | bytes 4718600 | tf_op jit(solution)/shard_map/ppermute | solution.py:78
  139.3 2.4 %copy-start.3 = (f32[1024,768]{0,1:T(8,128)S(1)}, f32[1024,768]{0,1:T(8,128)}, u32[]{:S(2)}) copy-start(f32[1024,768]{0,1:T(8,128)} %copy-done.2) | copy-start | bytes 9437188
  167.9 4.0 %copy-start.9 = (bf16[8,1,32,2048]{3,2,1,0:T(8,128)(2,1)S(1)}, bf16[8,1,32,2048]{3,2,1,0:T(8,128)(2,1)}, u32[]{:S(2)}) copy-start(bf16[8,1,32,2048]{3,2,1,0:T(8,128)(2,1)} %all-gather.3.cloned.1.call-done) | copy-start | bytes 3145732
  171.8 7.3 %collective-permute-start.6 = (f32[2,2,32,1024]{3,2,1,0:T(8,128)S(1)}, f32[2,2,32,1024]{3,2,1,0:T(8,128)S(1)}, u32[]{:S(2)}, u32[]{:S(2)}) collective-permute-start(f32[2,2,32,1024]{3,2,1,0:T(8,128)S(1)} %dynamic-slice_bitcast_fusion.5), channel_id=1, source_target_pairs={{0,1},{1,0},{2,3},{3,2},{4,5},{5,4},{6,7},{7,6},{8,9},{9,8},{10,11... | collective-permute-start | bytes 1572872 | tf_op jit(solution)/shard_map/ppermute | solution.py:78
  175.4 4.5 %collective-permute-start.9 = (f32[2,2,32,1024]{3,2,1,0:T(8,128)S(1)}, f32[2,2,32,1024]{3,2,1,0:T(8,128)S(1)}, u32[]{:S(2)}, u32[]{:S(2)}) collective-permute-start(f32[2,2,32,1024]{3,2,1,0:T(8,128)S(1)} %dynamic-slice_bitcast_fusion.4), channel_id=1, source_target_pairs={{0,1},{1,0},{2,3},{3,2},{4,5},{5,4},{6,7},{7,6},{8,9},{9,8},{10,11... | collective-permute-start | bytes 1572872 | tf_op jit(solution)/shard_map/ppermute | solution.py:78
  176.0 20.5 %collective-permute-start.2 = (f32[2,96,1024]{2,1,0:T(8,128)S(1)}, f32[2,96,1024]{2,1,0:T(8,128)S(1)}, u32[]{:S(2)}, u32[]{:S(2)}) collective-permute-start(f32[2,96,1024]{2,1,0:T(8,128)S(1)} %dynamic-slice_bitcast_fusion.3), channel_id=1, source_target_pairs={{0,2},{1,3},{2,0},{3,1},{4,6},{5,7},{6,4},{7,5},{8,10},{9,11},{10,... | collective-permute-start | bytes 2359304 | tf_op jit(solution)/shard_map/ppermute | solution.py:78
  177.6 20.6 %collective-permute-start.4 = (f32[2,96,1024]{2,1,0:T(8,128)S(1)}, f32[2,96,1024]{2,1,0:T(8,128)S(1)}, u32[]{:S(2)}, u32[]{:S(2)}) collective-permute-start(f32[2,96,1024]{2,1,0:T(8,128)S(1)} %dynamic-slice_bitcast_fusion.2), channel_id=1, source_target_pairs={{0,4},{1,5},{2,6},{3,7},{4,0},{5,1},{6,2},{7,3},{8,12},{9,13},{10,... | collective-permute-start | bytes 2359304 | tf_op jit(solution)/shard_map/ppermute | solution.py:78
  179.2 22.8 %collective-permute-start.7 = (f32[2,32,1024]{2,1,0:T(8,128)S(1)}, f32[2,32,1024]{2,1,0:T(8,128)S(1)}, u32[]{:S(2)}, u32[]{:S(2)}) collective-permute-start(f32[2,32,1024]{2,1,0:T(8,128)S(1)} %dynamic-slice_bitcast_fusion.9), channel_id=1, source_target_pairs={{0,2},{1,3},{2,0},{3,1},{4,6},{5,7},{6,4},{7,5},{8,10},{9,11},{10,... | collective-permute-start | bytes 786440 | tf_op jit(solution)/shard_map/ppermute | solution.py:78
  180.0 23.7 %collective-permute-start.10 = (f32[2,32,1024]{2,1,0:T(8,128)S(1)}, f32[2,32,1024]{2,1,0:T(8,128)S(1)}, u32[]{:S(2)}, u32[]{:S(2)}) collective-permute-start(f32[2,32,1024]{2,1,0:T(8,128)S(1)} %dynamic-slice_bitcast_fusion.8), channel_id=1, source_target_pairs={{0,4},{1,5},{2,6},{3,7},{4,0},{5,1},{6,2},{7,3},{8,12},{9,13},{10,... | collective-permute-start | bytes 786440 | tf_op jit(solution)/shard_map/ppermute | solution.py:78
  196.6 17.1 %collective-permute-start.3 = (f32[96,1024]{1,0:T(8,128)S(1)}, f32[96,1024]{1,0:T(8,128)S(1)}, u32[]{:S(2)}, u32[]{:S(2)}) collective-permute-start(f32[96,1024]{1,0:T(8,128)S(1)} %dynamic-slice_bitcast_fusion.7), channel_id=1, source_target_pairs={{0,4},{1,5},{2,6},{3,7},{4,0},{5,1},{6,2},{7,3},{8,12},{9,13},{10,... | collective-permute-start | bytes 1179656 | tf_op jit(solution)/shard_map/ppermute | solution.py:78
  198.3 15.5 %collective-permute-start.5 = (f32[96,1024]{1,0:T(8,128)S(1)}, f32[96,1024]{1,0:T(8,128)S(1)}, u32[]{:S(2)}, u32[]{:S(2)}) collective-permute-start(f32[96,1024]{1,0:T(8,128)S(1)} %dynamic-slice_bitcast_fusion.6), channel_id=1, source_target_pairs={{0,2},{1,3},{2,0},{3,1},{4,6},{5,7},{6,4},{7,5},{8,10},{9,11},{10,... | collective-permute-start | bytes 1179656 | tf_op jit(solution)/shard_map/ppermute | solution.py:78
  202.2 11.6 %collective-permute-start.8 = (f32[32,1024]{1,0:T(8,128)S(1)}, f32[32,1024]{1,0:T(8,128)S(1)}, u32[]{:S(2)}, u32[]{:S(2)}) collective-permute-start(f32[32,1024]{1,0:T(8,128)S(1)} %dynamic-slice_bitcast_fusion.11), channel_id=1, source_target_pairs={{0,4},{1,5},{2,6},{3,7},{4,0},{5,1},{6,2},{7,3},{8,12},{9,13},{10,... | collective-permute-start | bytes 393224 | tf_op jit(solution)/shard_map/ppermute | solution.py:78
  203.8 9.9 %collective-permute-start.11 = (f32[32,1024]{1,0:T(8,128)S(1)}, f32[32,1024]{1,0:T(8,128)S(1)}, u32[]{:S(2)}, u32[]{:S(2)}) collective-permute-start(f32[32,1024]{1,0:T(8,128)S(1)} %dynamic-slice_bitcast_fusion.10), channel_id=1, source_target_pairs={{0,2},{1,3},{2,0},{3,1},{4,6},{5,7},{6,4},{7,5},{8,10},{9,11},{10,... | collective-permute-start | bytes 393224 | tf_op jit(solution)/shard_map/ppermute | solution.py:78
Sparse Core Ops, SparseCore 0:
  8.9 106.6 all-gather.4
  139.4 28.4 all-gather.2

commit v9 on v7

--- a/solution.py
+++ b/solution.py
@@ -113,7 +113,6 @@
     order, starts = _slot_order(ab_ids, live_mask, AB_DEV)
     local_rows, width = amplitudes.shape
     tile = integrals.shape[-1]
-    weight = _dense_weight(received, order, starts, cd_ids, width // tile, AB_DEV)
     subs = rep_count // own_count
     units = sum(CHUNKS)
     part = local_rows // (subs * units)
@@ -122,12 +121,12 @@
     levels = rep_count.bit_length() - 1
     orders = (list(range(levels)), [0] + list(range(levels - 1, 0, -1)))
     bounds = [sum(CHUNKS[:c]) for c in range(len(CHUNKS) + 1)]
-    gathered = [
-        lax.all_gather(local4[:, bounds[c]:bounds[c + 1]], "own", axis=0, tiled=True)
-        if c == 0
-        else _line_gather(local4[:, bounds[c]:bounds[c + 1]], own_count)
-        for c in range(len(CHUNKS))
-    ]
+    gathered = [lax.all_gather(local4[:, bounds[0]:bounds[1]], "own", axis=0, tiled=True)]
+    later, received = lax.optimization_barrier((local4[:, bounds[1]:], received))
+    for c in range(1, len(CHUNKS)):
+        lo, hi = bounds[c] - bounds[1], bounds[c + 1] - bounds[1]
+        gathered.append(_line_gather(later[:, lo:hi], own_count))
+    weight = _dense_weight(received, order, starts, cd_ids, width // tile, AB_DEV)
     half = weight.shape[1] // 2
     flows = []
     for chunk in range(len(CHUNKS)):

time: 236 us -> 226 us (0.958)
  local copies, waits for them, and re-layouts: 22.7 us -> 8.9 us
  waiting for transfers between devices: 122 us -> 133 us
  starting transfers between devices: 41.8 us -> 37.4 us
    all_to_all x1, waiting for transfers between devices: 0.01 us -> 77.6 us  [on_device(): lax.all_to_all(integrals, ('own', 'rep'), split_axis=0, concat_axis=0, ti...]
    ppermute x6, waiting for transfers between devices: 84.4 us -> 20.3 us  [_line_gather(): lax.ppermute(down[-1], 'own', perm=[(i + 1, i) for i in range(own_count -...]
    dynamic_update_slice x6, local copies, waits for them, and re-layouts: 6.03 us -> 1.1 us  [_line_gather(): out = lax.dynamic_update_slice(out, up[k][None], (me - k,) + zero)]
    ppermute x6, starting transfers between devices: 13.6 us -> 9.25 us  [_line_gather(): lax.ppermute(up[-1], 'own', perm=[(i, i + 1) for i in range(k - 1, own_co...]
    dynamic_update_slice x5, local copies, waits for them, and re-layouts: 4.13 us -> 0.13 us  [_line_gather(): out = lax.dynamic_update_slice(out, down[k][None], (me + k,) + zero)]
    unnamed x32 -> x28, local copies, waits for them, and re-layouts: 3.75 us -> 0.23 us
    ppermute x18, waiting for transfers between devices: 37.8 us -> 35.1 us  [advance(): self.x = keep + lax.ppermute(send, 'rep', perm=pairs)]
  transfers between devices with their start and end apart: 32 -> 32, of which waited for: 17 -> 16; matrix products, arithmetic and copies ran while one was open for 10% -> 10% of each run, Pallas kernels for 4% -> 5%
where the time goes in v9:
time: 226 us
  waiting for transfers between devices  133 us (59%)
  starting transfers between devices  37.4 us (17%)
  matrix products  16.1 us (7%)
  between operations  14.1 us (6%)
  Pallas kernels  10.2 us (5%)
  local copies, waits for them, and re-layouts  8.9 us (4%)
  other arithmetic  6.25 us (3%)
    all_to_all x1, waiting for transfers between devices, on_device(): lax.all_to_all(integrals, ('own', 'rep'), split_axis=0, concat_axis=0, ti...  77.6 us
    ppermute x18, waiting for transfers between devices, advance(): self.x = keep + lax.ppermute(send, 'rep', perm=pairs)  35.1 us
    ppermute x6, waiting for transfers between devices, _line_gather(): lax.ppermute(down[-1], 'own', perm=[(i + 1, i) for i in range(own_count -...  20.3 us
    dot_general x6, matrix products, on_device(): jnp.dot(lhs, weight[:, h * half:(h + 1) * half], preferred_element_type=j...  16.1 us
    ppermute x18, starting transfers between devices, advance(): self.x = keep + lax.ppermute(send, 'rep', perm=pairs)  12.9 us
    pallas_call x1, Pallas kernels, _dense_weight(): pl.pallas_call(_weight_kernel, grid_spec=grid_spec, out_shape=jax.ShapeDt...  10.2 us
    ppermute x6, starting transfers between devices, _line_gather(): lax.ppermute(up[-1], 'own', perm=[(i, i + 1) for i in range(k - 1, own_co...  9.25 us
    ppermute x6, starting transfers between devices, _line_gather(): lax.ppermute(down[-1], 'own', perm=[(i + 1, i) for i in range(own_count -...  7.91 us
  transfers between devices with their start and end apart: 32, of which 16 were waited for; matrix products, arithmetic and copies ran while one was open for 10% of the time, Pallas kernels for 5%

profile of v9, /device:TPU:0, one launch (start us, length us, event | category | flops | bytes accessed | tf_op | source)
XLA Modules:
  0.0 225.9 jit_solution(12577537261425461615)
XLA Ops:
  6.5 7.3 %all-to-all-start = ((bf16[64,128,128]{2,1,0:T(8,128)(2,1)}), bf16[64,128,128]{2,1,0:T(8,128)(2,1)S(1)}, u32[]{:S(2)}, u32[]{:S(2)}) async-start(bf16[64,128,128]{2,1,0:T(8,128)(2,1)} %param.6), calls=%async_computation | async-start | bytes 4194304 | tf_op jit(solution)/shard_map/all_to_all | solution.py:107
  13.9 2.1 fusion.22
  18.7 77.6 %all-to-all-done.tiles_ref = bf16[64,128,128]{2,1,0:T(8,128)(2,1)S(1)} async-done(((bf16[64,128,128]{2,1,0:T(8,128)(2,1)}), bf16[64,128,128]{2,1,0:T(8,128)(2,1)S(1)}, u32[]{:S(2)}, u32[]{:S(2)}) %all-to-all-start) | async-done | bytes 2097184 | tf_op jit(solution)/shard_map/all_to_all | solution.py:107
  97.1 1.3 collective-permute-start.6
  98.4 1.3 collective-permute-start.9
  99.7 5.3 %collective-permute-start = (bf16[2,1,32,2048]{3,2,1,0:T(8,128)(2,1)}, bf16[2,1,32,2048]{3,2,1,0:T(8,128)(2,1)}, u32[]{:S(2)}, u32[]{:S(2)}) collective-permute-start(bf16[2,1,32,2048]{3,2,1,0:T(8,128)(2,1)} %get-tuple-element.30), channel_id=1, source_target_pairs={{0,8},{8,16},{16,24},{1,9},{9,17},{17,25},{2,10},{10,18},{18,26},{... | collective-permute-start | bytes 786440 | tf_op jit(solution)/shard_map/ppermute | solution.py:90
  106.3 10.2 %shard_map.55 = bf16[2048,2048]{1,0:T(8,128)(2,1)} custom-call(s32[64]{0:T(128)} %select_reduce_fusion.order_ref, s32[17]{0:T(128)} %convert_reduce_fusion.1.starts_ref, s32[64]{0:T(128)} %reshape.98.cd_ref, bf16[64,128,128]{2,1,0:T(8,128)(2,1)} %copy-done.1), custom_call_target="tpu_custom_call" | custom-call | bytes 10485760 | tf_op jit(solution)/shard_map/pallas_call | solution.py:49
  116.5 5.3 %fusion.14 = f32[1024,512]{0,1:T(8,128)S(1)} fusion(bf16[512,2048]{1,0:T(8,128)(2,1)} %bitcast.166, bf16[2048,2048]{1,0:T(8,128)(2,1)} %shard_map.55), kind=kOutput, calls=%fused_computation.14 | convolution fusion | flops 2147483648 | bytes 8388608 | tf_op jit(solution)/shard_map/dot_general | solution.py:143
  122.5 2.3 %fusion.10 = f32[1024,512]{0,1:T(8,128)S(1)} fusion(bf16[512,2048]{1,0:T(8,128)(2,1)S(1)} %bitcast.167, bf16[2048,2048]{1,0:T(8,128)(2,1)S(1)} %copy-done), kind=kOutput, calls=%fused_computation.10 | convolution fusion | flops 2147483648 | bytes 8388608 | tf_op jit(solution)/shard_map/dot_general | solution.py:143
  124.9 1.3 collective-permute-start.10
  126.9 1.3 collective-permute-start.4
  129.2 8.6 %collective-permute-done.10 = bf16[2,1,32,2048]{3,2,1,0:T(8,128)(2,1)S(1)} collective-permute-done((bf16[2,1,32,2048]{3,2,1,0:T(8,128)(2,1)S(1)}, bf16[2,1,32,2048]{3,2,1,0:T(8,128)(2,1)S(1)}, u32[]{:S(2)}, u32[]{:S(2)}) %collective-permute-start.10) | collective-permute-done | bytes 262176 | tf_op jit(solution)/shard_map/ppermute | solution.py:91
  139.1 4.5 %collective-permute-done.4 = bf16[2,1,32,2048]{3,2,1,0:T(8,128)(2,1)S(1)} collective-permute-done((bf16[2,1,32,2048]{3,2,1,0:T(8,128)(2,1)S(1)}, bf16[2,1,32,2048]{3,2,1,0:T(8,128)(2,1)S(1)}, u32[]{:S(2)}, u32[]{:S(2)}) %collective-permute-start.4) | collective-permute-done | bytes 262176 | tf_op jit(solution)/shard_map/ppermute | solution.py:91
  144.2 1.5 collective-permute-start.5
  147.1 2.1 collective-permute-done.11
  149.2 5.2 %collective-permute-done.5 = bf16[2,1,32,2048]{3,2,1,0:T(8,128)(2,1)S(1)} collective-permute-done((bf16[2,1,32,2048]{3,2,1,0:T(8,128)(2,1)S(1)}, bf16[2,1,32,2048]{3,2,1,0:T(8,128)(2,1)S(1)}, u32[]{:S(2)}, u32[]{:S(2)}) %collective-permute-start.5) | collective-permute-done | bytes 262176 | tf_op jit(solution)/shard_map/ppermute | solution.py:91
  155.0 1.3 fusion.6
  157.3 2.3 %fusion.2 = f32[2,2,2,32,1024]{4,3,2,1,0:T(8,128)} fusion(bf16[2,2,2,32,2048]{4,3,2,1,0:T(8,128)(2,1)S(1)} %bitcast.162, bf16[2048,2048]{1,0:T(8,128)(2,1)S(1)} %copy-done), kind=kOutput, calls=%fused_computation.2 | convolution fusion | flops 1073741824 | bytes 6291456 | tf_op jit(solution)/shard_map/dot_general | solution.py:143
  159.5 1.9 dynamic-slice_bitcast_fusion.4
  162.3 2.4 %collective-permute-start.15 = (f32[2,64,1024]{2,1,0:T(8,128)S(1)}, f32[2,64,1024]{2,1,0:T(8,128)S(1)}, u32[]{:S(2)}, u32[]{:S(2)}) collective-permute-start(f32[2,64,1024]{2,1,0:T(8,128)S(1)} %dynamic-slice_bitcast_fusion.6), channel_id=1, source_target_pairs={{0,4},{1,5},{2,6},{3,7},{4,0},{5,1},{6,2},{7,3},{8,12},{9,13},{10,... | collective-permute-start | bytes 1572872 | tf_op jit(solution)/shard_map/ppermute | solution.py:78
  166.0 1.4 bitcast_add_fusion.4
  167.4 8.5 %collective-permute-done.14 = f32[2,64,1024]{2,1,0:T(8,128)S(1)} collective-permute-done((f32[2,64,1024]{2,1,0:T(8,128)S(1)}, f32[2,64,1024]{2,1,0:T(8,128)S(1)}, u32[]{:S(2)}, u32[]{:S(2)}) %collective-permute-start.14) | collective-permute-done | bytes 524320 | tf_op jit(solution)/shard_map/ppermute | solution.py:78
  176.6 3.6 %fusion = f32[2,2,2,32,1024]{4,3,2,1,0:T(8,128)S(1)} fusion(bf16[2,2,2,32,2048]{4,3,2,1,0:T(8,128)(2,1)S(1)} %bitcast.159, bf16[2048,2048]{1,0:T(8,128)(2,1)} %shard_map.55), kind=kOutput, calls=%fused_computation | convolution fusion | flops 1073741824 | bytes 6291456 | tf_op jit(solution)/shard_map/dot_general | solution.py:143
  182.3 1.8 collective-permute-start.22
  184.5 1.8 collective-permute-start.19
  186.3 4.3 %collective-permute-done.22 = f32[2,32,1024]{2,1,0:T(8,128)S(1)} collective-permute-done((f32[2,32,1024]{2,1,0:T(8,128)S(1)}, f32[2,32,1024]{2,1,0:T(8,128)S(1)}, u32[]{:S(2)}, u32[]{:S(2)}) %collective-permute-start.22) | collective-permute-done | bytes 262176 | tf_op jit(solution)/shard_map/ppermute | solution.py:78
  190.6 1.7 collective-permute-start.18
  193.8 5.3 %collective-permute-done.19 = f32[64,1024]{1,0:T(8,128)S(1)} collective-permute-done((f32[64,1024]{1,0:T(8,128)S(1)}, f32[64,1024]{1,0:T(8,128)S(1)}, u32[]{:S(2)}, u32[]{:S(2)}) %collective-permute-start.19) | collective-permute-done | bytes 262176 | tf_op jit(solution)/shard_map/ppermute | solution.py:78
  200.6 3.9 %collective-permute-done.21 = f32[32,1024]{1,0:T(8,128)S(1)} collective-permute-done((f32[32,1024]{1,0:T(8,128)S(1)}, f32[32,1024]{1,0:T(8,128)S(1)}, u32[]{:S(2)}, u32[]{:S(2)}) %collective-permute-start.21) | collective-permute-done | bytes 131104 | tf_op jit(solution)/shard_map/ppermute | solution.py:78
  205.1 1.3 collective-permute-start.25
  206.4 6.1 %collective-permute-done.28 = f32[2,32,1024]{2,1,0:T(8,128)S(1)} collective-permute-done((f32[2,32,1024]{2,1,0:T(8,128)S(1)}, f32[2,32,1024]{2,1,0:T(8,128)S(1)}, u32[]{:S(2)}, u32[]{:S(2)}) %collective-permute-start.28) | collective-permute-done | bytes 262176 | tf_op jit(solution)/shard_map/ppermute | solution.py:78
  214.0 3.6 %collective-permute-done.29 = f32[32,1024]{1,0:T(8,128)S(1)} collective-permute-done((f32[32,1024]{1,0:T(8,128)S(1)}, f32[32,1024]{1,0:T(8,128)S(1)}, u32[]{:S(2)}, u32[]{:S(2)}) %collective-permute-start.29) | collective-permute-done | bytes 131104 | tf_op jit(solution)/shard_map/ppermute | solution.py:78
  (130 shorter events, 23.7 us)
Async XLA Ops:
  6.5 89.7 %all-to-all-start = ((bf16[64,128,128]{2,1,0:T(8,128)(2,1)}), bf16[64,128,128]{2,1,0:T(8,128)(2,1)S(1)}, u32[]{:S(2)}, u32[]{:S(2)}) async-start(bf16[64,128,128]{2,1,0:T(8,128)(2,1)} %param.6), calls=%async_computation | async-start | bytes 4194304 | tf_op jit(solution)/shard_map/all_to_all | solution.py:107
  13.8 102.6 %all-gather.2.cloned.1.call-start = ((), (), s32[]{:S(2)}) async-start(), calls=%async_computation.1 | async-start | bytes 2621440 | tf_op jit(solution)/shard_map/all_gather | solution.py:124
  97.1 24.7 %collective-permute-start.6 = (bf16[2,1,32,2048]{3,2,1,0:T(8,128)(2,1)}, bf16[2,1,32,2048]{3,2,1,0:T(8,128)(2,1)S(1)}, u32[]{:S(2)}, u32[]{:S(2)}) collective-permute-start(bf16[2,1,32,2048]{3,2,1,0:T(8,128)(2,1)} %get-tuple-element.29), channel_id=1, source_target_pairs={{0,8},{8,16},{16,24},{1,9},{9,17},{17,25},{2,10},{10,18},{18,26},{... | collective-permute-start | bytes 786440 | tf_op jit(solution)/shard_map/ppermute | solution.py:90
  98.4 26.4 %collective-permute-start.9 = (bf16[2,1,32,2048]{3,2,1,0:T(8,128)(2,1)}, bf16[2,1,32,2048]{3,2,1,0:T(8,128)(2,1)S(1)}, u32[]{:S(2)}, u32[]{:S(2)}) collective-permute-start(bf16[2,1,32,2048]{3,2,1,0:T(8,128)(2,1)} %get-tuple-element.29), channel_id=1, source_target_pairs={{8,0},{16,8},{24,16},{9,1},{17,9},{25,17},{10,2},{18,10},{26,18},{... | collective-permute-start | bytes 786440 | tf_op jit(solution)/shard_map/ppermute | solution.py:91
  99.7 26.5 %collective-permute-start = (bf16[2,1,32,2048]{3,2,1,0:T(8,128)(2,1)}, bf16[2,1,32,2048]{3,2,1,0:T(8,128)(2,1)}, u32[]{:S(2)}, u32[]{:S(2)}) collective-permute-start(bf16[2,1,32,2048]{3,2,1,0:T(8,128)(2,1)} %get-tuple-element.30), channel_id=1, source_target_pairs={{0,8},{8,16},{16,24},{1,9},{9,17},{17,25},{2,10},{10,18},{18,26},{... | collective-permute-start | bytes 786440 | tf_op jit(solution)/shard_map/ppermute | solution.py:90
  105.0 21.9 %collective-permute-start.3 = (bf16[2,1,32,2048]{3,2,1,0:T(8,128)(2,1)}, bf16[2,1,32,2048]{3,2,1,0:T(8,128)(2,1)S(1)}, u32[]{:S(2)}, u32[]{:S(2)}) collective-permute-start(bf16[2,1,32,2048]{3,2,1,0:T(8,128)(2,1)} %get-tuple-element.30), channel_id=1, source_target_pairs={{8,0},{16,8},{24,16},{9,1},{17,9},{25,17},{10,2},{18,10},{26,18},{... | collective-permute-start | bytes 786440 | tf_op jit(solution)/shard_map/ppermute | solution.py:91
  121.8 6.4 %collective-permute-start.7 = (bf16[2,1,32,2048]{3,2,1,0:T(8,128)(2,1)S(1)}, bf16[2,1,32,2048]{3,2,1,0:T(8,128)(2,1)S(1)}, u32[]{:S(2)}, u32[]{:S(2)}) collective-permute-start(bf16[2,1,32,2048]{3,2,1,0:T(8,128)(2,1)S(1)} %collective-permute-done.6), channel_id=1, source_target_pairs={{8,16},{16,24},{9,17},{17,25},{10,18},{18,26},{11,19},{19,27},{12,... | collective-permute-start | bytes 786440 | tf_op jit(solution)/shard_map/ppermute | solution.py:90
  124.9 12.9 %collective-permute-start.10 = (bf16[2,1,32,2048]{3,2,1,0:T(8,128)(2,1)S(1)}, bf16[2,1,32,2048]{3,2,1,0:T(8,128)(2,1)S(1)}, u32[]{:S(2)}, u32[]{:S(2)}) collective-permute-start(bf16[2,1,32,2048]{3,2,1,0:T(8,128)(2,1)S(1)} %collective-permute-done.9), channel_id=1, source_target_pairs={{8,0},{16,8},{9,1},{17,9},{10,2},{18,10},{11,3},{19,11},{12,4},{20... | collective-permute-start | bytes 786440 | tf_op jit(solution)/shard_map/ppermute | solution.py:91
  126.2 11.6 %collective-permute-start.1 = (bf16[2,1,32,2048]{3,2,1,0:T(8,128)(2,1)}, bf16[2,1,32,2048]{3,2,1,0:T(8,128)(2,1)S(1)}, u32[]{:S(2)}, u32[]{:S(2)}) collective-permute-start(bf16[2,1,32,2048]{3,2,1,0:T(8,128)(2,1)} %collective-permute-done), channel_id=1, source_target_pairs={{8,16},{16,24},{9,17},{17,25},{10,18},{18,26},{11,19},{19,27},{12,... | collective-permute-start | bytes 786440 | tf_op jit(solution)/shard_map/ppermute | solution.py:90
  126.9 16.6 %collective-permute-start.4 = (bf16[2,1,32,2048]{3,2,1,0:T(8,128)(2,1)S(1)}, bf16[2,1,32,2048]{3,2,1,0:T(8,128)(2,1)S(1)}, u32[]{:S(2)}, u32[]{:S(2)}) collective-permute-start(bf16[2,1,32,2048]{3,2,1,0:T(8,128)(2,1)S(1)} %collective-permute-done.3), channel_id=1, source_target_pairs={{8,0},{16,8},{9,1},{17,9},{10,2},{18,10},{11,3},{19,11},{12,4},{20... | collective-permute-start | bytes 786440 | tf_op jit(solution)/shard_map/ppermute | solution.py:91
  128.2 16.0 %collective-permute-start.8 = (bf16[2,1,32,2048]{3,2,1,0:T(8,128)(2,1)S(1)}, bf16[2,1,32,2048]{3,2,1,0:T(8,128)(2,1)S(1)}, u32[]{:S(2)}, u32[]{:S(2)}) collective-permute-start(bf16[2,1,32,2048]{3,2,1,0:T(8,128)(2,1)S(1)} %collective-permute-done.7), channel_id=1, source_target_pairs={{16,24},{17,25},{18,26},{19,27},{20,28},{21,29},{22,30},{23,31}} | collective-permute-start | bytes 786440 | tf_op jit(solution)/shard_map/ppermute | solution.py:90
  129.0 25.6 %collective-permute-start.12 = (f32[2,2,64,1024]{3,2,1,0:T(8,128)S(1)}, f32[2,2,64,1024]{3,2,1,0:T(8,128)S(1)}, u32[]{:S(2)}, u32[]{:S(2)}) collective-permute-start(f32[2,2,64,1024]{3,2,1,0:T(8,128)S(1)} %dynamic-slice_bitcast_fusion.1), channel_id=1, source_target_pairs={{0,1},{1,0},{2,3},{3,2},{4,5},{5,4},{6,7},{7,6},{8,9},{9,8},{10,11... | collective-permute-start | bytes 3145736 | tf_op jit(solution)/shard_map/ppermute | solution.py:78
  137.8 17.1 %collective-permute-start.13 = (f32[2,2,64,1024]{3,2,1,0:T(8,128)S(1)}, f32[2,2,64,1024]{3,2,1,0:T(8,128)S(1)}, u32[]{:S(2)}, u32[]{:S(2)}) collective-permute-start(f32[2,2,64,1024]{3,2,1,0:T(8,128)S(1)} %dynamic-slice_bitcast_fusion), channel_id=1, source_target_pairs={{0,1},{1,0},{2,3},{3,2},{4,5},{5,4},{6,7},{7,6},{8,9},{9,8},{10,11... | collective-permute-start | bytes 3145736 | tf_op jit(solution)/shard_map/ppermute | solution.py:78
  137.8 11.4 %collective-permute-start.11 = (bf16[2,1,32,2048]{3,2,1,0:T(8,128)(2,1)S(1)}, bf16[2,1,32,2048]{3,2,1,0:T(8,128)(2,1)S(1)}, u32[]{:S(2)}, u32[]{:S(2)}) collective-permute-start(bf16[2,1,32,2048]{3,2,1,0:T(8,128)(2,1)S(1)} %collective-permute-done.10), channel_id=1, source_target_pairs={{8,0},{9,1},{10,2},{11,3},{12,4},{13,5},{14,6},{15,7}} | collective-permute-start | bytes 786440 | tf_op jit(solution)/shard_map/ppermute | solution.py:91
  143.5 2.4 %collective-permute-start.2 = (bf16[2,1,32,2048]{3,2,1,0:T(8,128)(2,1)S(1)}, bf16[2,1,32,2048]{3,2,1,0:T(8,128)(2,1)S(1)}, u32[]{:S(2)}, u32[]{:S(2)}) collective-permute-start(bf16[2,1,32,2048]{3,2,1,0:T(8,128)(2,1)S(1)} %collective-permute-done.1), channel_id=1, source_target_pairs={{16,24},{17,25},{18,26},{19,27},{20,28},{21,29},{22,30},{23,31}} | collective-permute-start | bytes 786440 | tf_op jit(solution)/shard_map/ppermute | solution.py:90
  144.2 10.2 %collective-permute-start.5 = (bf16[2,1,32,2048]{3,2,1,0:T(8,128)(2,1)S(1)}, bf16[2,1,32,2048]{3,2,1,0:T(8,128)(2,1)S(1)}, u32[]{:S(2)}, u32[]{:S(2)}) collective-permute-start(bf16[2,1,32,2048]{3,2,1,0:T(8,128)(2,1)S(1)} %collective-permute-done.4), channel_id=1, source_target_pairs={{8,0},{9,1},{10,2},{11,3},{12,4},{13,5},{14,6},{15,7}} | collective-permute-start | bytes 786440 | tf_op jit(solution)/shard_map/ppermute | solution.py:91
  157.3 7.5 %collective-permute-start.16 = (f32[2,2,32,1024]{3,2,1,0:T(8,128)}, f32[2,2,32,1024]{3,2,1,0:T(8,128)}, u32[]{:S(2)}, u32[]{:S(2)}) collective-permute-start(f32[2,2,32,1024]{3,2,1,0:T(8,128)} %dynamic-slice_bitcast_fusion.5), channel_id=1, source_target_pairs={{0,1},{1,0},{2,3},{3,2},{4,5},{5,4},{6,7},{7,6},{8,9},{9,8},{10,11... | collective-permute-start | bytes 1572872 | tf_op jit(solution)/shard_map/ppermute | solution.py:78
  161.4 4.6 %collective-permute-start.17 = (f32[2,2,32,1024]{3,2,1,0:T(8,128)}, f32[2,2,32,1024]{3,2,1,0:T(8,128)}, u32[]{:S(2)}, u32[]{:S(2)}) collective-permute-start(f32[2,2,32,1024]{3,2,1,0:T(8,128)} %dynamic-slice_bitcast_fusion.4), channel_id=1, source_target_pairs={{0,1},{1,0},{2,3},{3,2},{4,5},{5,4},{6,7},{7,6},{8,9},{9,8},{10,11... | collective-permute-start | bytes 1572872 | tf_op jit(solution)/shard_map/ppermute | solution.py:78
  162.0 13.9 %collective-permute-start.14 = (f32[2,64,1024]{2,1,0:T(8,128)S(1)}, f32[2,64,1024]{2,1,0:T(8,128)S(1)}, u32[]{:S(2)}, u32[]{:S(2)}) collective-permute-start(f32[2,64,1024]{2,1,0:T(8,128)S(1)} %dynamic-slice_bitcast_fusion.7), channel_id=1, source_target_pairs={{0,2},{1,3},{2,0},{3,1},{4,6},{5,7},{6,4},{7,5},{8,10},{9,11},{10,... | collective-permute-start | bytes 1572872 | tf_op jit(solution)/shard_map/ppermute | solution.py:78
  162.3 14.2 %collective-permute-start.15 = (f32[2,64,1024]{2,1,0:T(8,128)S(1)}, f32[2,64,1024]{2,1,0:T(8,128)S(1)}, u32[]{:S(2)}, u32[]{:S(2)}) collective-permute-start(f32[2,64,1024]{2,1,0:T(8,128)S(1)} %dynamic-slice_bitcast_fusion.6), channel_id=1, source_target_pairs={{0,4},{1,5},{2,6},{3,7},{4,0},{5,1},{6,2},{7,3},{8,12},{9,13},{10,... | collective-permute-start | bytes 1572872 | tf_op jit(solution)/shard_map/ppermute | solution.py:78
  181.6 22.9 %collective-permute-start.27 = (f32[2,2,32,1024]{3,2,1,0:T(8,128)S(1)}, f32[2,2,32,1024]{3,2,1,0:T(8,128)S(1)}, u32[]{:S(2)}, u32[]{:S(2)}) collective-permute-start(f32[2,2,32,1024]{3,2,1,0:T(8,128)S(1)} %dynamic-slice_bitcast_fusion.2), channel_id=1, source_target_pairs={{0,1},{1,0},{2,3},{3,2},{4,5},{5,4},{6,7},{7,6},{8,9},{9,8},{10,11... | collective-permute-start | bytes 1572872 | tf_op jit(solution)/shard_map/ppermute | solution.py:78
  181.7 23.2 %collective-permute-start.24 = (f32[2,2,32,1024]{3,2,1,0:T(8,128)S(1)}, f32[2,2,32,1024]{3,2,1,0:T(8,128)S(1)}, u32[]{:S(2)}, u32[]{:S(2)}) collective-permute-start(f32[2,2,32,1024]{3,2,1,0:T(8,128)S(1)} %dynamic-slice_bitcast_fusion.3), channel_id=1, source_target_pairs={{0,1},{1,0},{2,3},{3,2},{4,5},{5,4},{6,7},{7,6},{8,9},{9,8},{10,11... | collective-permute-start | bytes 1572872 | tf_op jit(solution)/shard_map/ppermute | solution.py:78
  182.3 8.3 %collective-permute-start.22 = (f32[2,32,1024]{2,1,0:T(8,128)S(1)}, f32[2,32,1024]{2,1,0:T(8,128)S(1)}, u32[]{:S(2)}, u32[]{:S(2)}) collective-permute-start(f32[2,32,1024]{2,1,0:T(8,128)S(1)} %dynamic-slice_bitcast_fusion.10), channel_id=1, source_target_pairs={{0,4},{1,5},{2,6},{3,7},{4,0},{5,1},{6,2},{7,3},{8,12},{9,13},{10,... | collective-permute-start | bytes 786440 | tf_op jit(solution)/shard_map/ppermute | solution.py:78
  184.1 9.3 %collective-permute-start.20 = (f32[2,32,1024]{2,1,0:T(8,128)S(1)}, f32[2,32,1024]{2,1,0:T(8,128)S(1)}, u32[]{:S(2)}, u32[]{:S(2)}) collective-permute-start(f32[2,32,1024]{2,1,0:T(8,128)S(1)} %dynamic-slice_bitcast_fusion.11), channel_id=1, source_target_pairs={{0,2},{1,3},{2,0},{3,1},{4,6},{5,7},{6,4},{7,5},{8,10},{9,11},{10,... | collective-permute-start | bytes 786440 | tf_op jit(solution)/shard_map/ppermute | solution.py:78
  184.5 14.5 %collective-permute-start.19 = (f32[64,1024]{1,0:T(8,128)S(1)}, f32[64,1024]{1,0:T(8,128)S(1)}, u32[]{:S(2)}, u32[]{:S(2)}) collective-permute-start(f32[64,1024]{1,0:T(8,128)S(1)} %dynamic-slice_bitcast_fusion.12), channel_id=1, source_target_pairs={{0,2},{1,3},{2,0},{3,1},{4,6},{5,7},{6,4},{7,5},{8,10},{9,11},{10,... | collective-permute-start | bytes 786440 | tf_op jit(solution)/shard_map/ppermute | solution.py:78
  190.6 8.7 %collective-permute-start.18 = (f32[64,1024]{1,0:T(8,128)S(1)}, f32[64,1024]{1,0:T(8,128)S(1)}, u32[]{:S(2)}, u32[]{:S(2)}) collective-permute-start(f32[64,1024]{1,0:T(8,128)S(1)} %dynamic-slice_bitcast_fusion.13), channel_id=1, source_target_pairs={{0,4},{1,5},{2,6},{3,7},{4,0},{5,1},{6,2},{7,3},{8,12},{9,13},{10,... | collective-permute-start | bytes 786440 | tf_op jit(solution)/shard_map/ppermute | solution.py:78
  193.4 7.2 %collective-permute-start.23 = (f32[32,1024]{1,0:T(8,128)S(1)}, f32[32,1024]{1,0:T(8,128)S(1)}, u32[]{:S(2)}, u32[]{:S(2)}) collective-permute-start(f32[32,1024]{1,0:T(8,128)S(1)} %dynamic-slice_bitcast_fusion.16), channel_id=1, source_target_pairs={{0,2},{1,3},{2,0},{3,1},{4,6},{5,7},{6,4},{7,5},{8,10},{9,11},{10,... | collective-permute-start | bytes 393224 | tf_op jit(solution)/shard_map/ppermute | solution.py:78
  199.0 5.5 %collective-permute-start.21 = (f32[32,1024]{1,0:T(8,128)S(1)}, f32[32,1024]{1,0:T(8,128)S(1)}, u32[]{:S(2)}, u32[]{:S(2)}) collective-permute-start(f32[32,1024]{1,0:T(8,128)S(1)} %dynamic-slice_bitcast_fusion.17), channel_id=1, source_target_pairs={{0,4},{1,5},{2,6},{3,7},{4,0},{5,1},{6,2},{7,3},{8,12},{9,13},{10,... | collective-permute-start | bytes 393224 | tf_op jit(solution)/shard_map/ppermute | solution.py:78
  204.6 7.8 %collective-permute-start.28 = (f32[2,32,1024]{2,1,0:T(8,128)S(1)}, f32[2,32,1024]{2,1,0:T(8,128)S(1)}, u32[]{:S(2)}, u32[]{:S(2)}) collective-permute-start(f32[2,32,1024]{2,1,0:T(8,128)S(1)} %dynamic-slice_bitcast_fusion.8), channel_id=1, source_target_pairs={{0,4},{1,5},{2,6},{3,7},{4,0},{5,1},{6,2},{7,3},{8,12},{9,13},{10,... | collective-permute-start | bytes 786440 | tf_op jit(solution)/shard_map/ppermute | solution.py:78
  205.1 7.8 %collective-permute-start.25 = (f32[2,32,1024]{2,1,0:T(8,128)S(1)}, f32[2,32,1024]{2,1,0:T(8,128)S(1)}, u32[]{:S(2)}, u32[]{:S(2)}) collective-permute-start(f32[2,32,1024]{2,1,0:T(8,128)S(1)} %dynamic-slice_bitcast_fusion.9), channel_id=1, source_target_pairs={{0,2},{1,3},{2,0},{3,1},{4,6},{5,7},{6,4},{7,5},{8,10},{9,11},{10,... | collective-permute-start | bytes 786440 | tf_op jit(solution)/shard_map/ppermute | solution.py:78
  212.5 5.0 %collective-permute-start.29 = (f32[32,1024]{1,0:T(8,128)S(1)}, f32[32,1024]{1,0:T(8,128)S(1)}, u32[]{:S(2)}, u32[]{:S(2)}) collective-permute-start(f32[32,1024]{1,0:T(8,128)S(1)} %dynamic-slice_bitcast_fusion.14), channel_id=1, source_target_pairs={{0,2},{1,3},{2,0},{3,1},{4,6},{5,7},{6,4},{7,5},{8,10},{9,11},{10,... | collective-permute-start | bytes 393224 | tf_op jit(solution)/shard_map/ppermute | solution.py:78
  213.0 5.0 %collective-permute-start.26 = (f32[32,1024]{1,0:T(8,128)S(1)}, f32[32,1024]{1,0:T(8,128)S(1)}, u32[]{:S(2)}, u32[]{:S(2)}) collective-permute-start(f32[32,1024]{1,0:T(8,128)S(1)} %dynamic-slice_bitcast_fusion.15), channel_id=1, source_target_pairs={{0,4},{1,5},{2,6},{3,7},{4,0},{5,1},{6,2},{7,3},{8,12},{9,13},{10,... | collective-permute-start | bytes 393224 | tf_op jit(solution)/shard_map/ppermute | solution.py:78
  (13 other events, 120.1 us)
Sparse Core Ops, SparseCore 0:
  16.3 80.0 all-gather.1

commit v10 on v4

--- a/solution.py
+++ b/solution.py
@@ -97,6 +97,23 @@
         return self.x.reshape(self.part, self.width)
 
 
+def _line_gather(block, own_count):
+    me = lax.axis_index("own")
+    up = [block]
+    down = [block]
+    for k in range(1, own_count):
+        up.append(lax.ppermute(up[-1], "own", perm=[(i, i + 1) for i in range(k - 1, own_count - 1)]))
+        down.append(lax.ppermute(down[-1], "own", perm=[(i + 1, i) for i in range(own_count - k)]))
+    out = jnp.zeros((own_count,) + block.shape, block.dtype)
+    zero = (0,) * block.ndim
+    for k in range(own_count - 1, 0, -1):
+        out = lax.dynamic_update_slice(out, up[k][None], (me - k,) + zero)
+    for k in range(own_count - 1, 0, -1):
+        out = lax.dynamic_update_slice(out, down[k][None], (me + k,) + zero)
+    out = lax.dynamic_update_slice(out, block[None], (me,) + zero)
+    return out.reshape((own_count * block.shape[0],) + block.shape[1:])
+
+
 def on_device(amplitudes, integrals, ab_list, cd_list, live_count):
     own_count = lax.axis_size("own")
     rep_count = lax.axis_size("rep")
@@ -116,7 +133,12 @@
     rep_index = lax.axis_index("rep")
     levels = rep_count.bit_length() - 1
     orders = (list(range(levels)), [0] + list(range(levels - 1, 0, -1)))
-    gathered = [lax.all_gather(local4[:, c], "own", axis=0, tiled=True) for c in range(N_CHUNK)]
+    gathered = [
+        lax.all_gather(local4[:, c], "own", axis=0, tiled=True)
+        if c < N_CHUNK - 1
+        else _line_gather(local4[:, c], own_count)
+        for c in range(N_CHUNK)
+    ]
     flows = []
     for chunk in range(N_CHUNK):
         for flow in flows:

time: 201 us -> 243 us (1.21)
  waiting for transfers between devices: 109 us -> 139 us
  starting transfers between devices: 26.9 us -> 37 us
  local copies, waits for them, and re-layouts: 11.7 us -> 15.9 us
    ppermute x0 -> x6, waiting for transfers between devices: none -> 107 us  [the longest x3 55.4 us: _line_gather(): lax.ppermute(down[-1], 'own', perm=[(i + 1, i) for i in range(own_count -...]
    all_gather x4 -> x3, waiting for transfers between devices: 68.9 us -> 0.06 us  [on_device(): lax.all_gather(local4[:, c], 'own', axis=0, tiled=True)]
    ppermute x0 -> x6, starting transfers between devices: none -> 9.6 us  [the longest x3 5.74 us: _line_gather(): lax.ppermute(up[-1], 'own', perm=[(i, i + 1) for i in range(k - 1, own_co...]
    all_to_all x1, waiting for transfers between devices: 8.25 us -> 0.01 us  [on_device(): lax.all_to_all(integrals, ('own', 'rep'), split_axis=0, concat_axis=0, ti...]
    dynamic_update_slice x0 -> x7, local copies, waits for them, and re-layouts: none -> 3.96 us  [the longest x3 1.97 us: _line_gather(): out = lax.dynamic_update_slice(out, up[k][None], (me - k,) + zero)]
  transfers between devices with their start and end apart: 29 -> 34, of which waited for: 16 -> 14; matrix products, arithmetic and copies ran while one was open for 7% -> 5% of each run, Pallas kernels for 17% -> 10%
where the time goes in v10:
time: 243 us
  waiting for transfers between devices  139 us (57%)
  starting transfers between devices  37 us (15%)
  Pallas kernels  33.5 us (14%)
  local copies, waits for them, and re-layouts  15.9 us (7%)
  between operations  13.7 us (6%)
  other arithmetic  3.63 us (1%)
    ppermute x3, waiting for transfers between devices, _line_gather(): lax.ppermute(down[-1], 'own', perm=[(i + 1, i) for i in range(own_count -...  55.4 us
    ppermute x3, waiting for transfers between devices, _line_gather(): lax.ppermute(up[-1], 'own', perm=[(i, i + 1) for i in range(k - 1, own_co...  52 us
    pallas_call x4, Pallas kernels, _ladder_products(): pl.pallas_call(_ladder_kernel, grid_spec=grid_spec, out_shape=jax.ShapeDt...  33.5 us
    ppermute x24, waiting for transfers between devices, advance(): self.x = keep + lax.ppermute(send, 'rep', perm=pairs)  30.5 us
    ppermute x24, starting transfers between devices, advance(): self.x = keep + lax.ppermute(send, 'rep', perm=pairs)  20 us
    all_to_all x1, starting transfers between devices, on_device(): lax.all_to_all(integrals, ('own', 'rep'), split_axis=0, concat_axis=0, ti...  7.3 us
    slice x4, local copies, waits for them, and re-layouts, on_device(): partial[:, h * half:(h + 1) * half]  6.71 us
    ppermute x3, starting transfers between devices, _line_gather(): lax.ppermute(up[-1], 'own', perm=[(i, i + 1) for i in range(k - 1, own_co...  5.74 us
  transfers between devices with their start and end apart: 34, of which 14 were waited for; matrix products, arithmetic and copies ran while one was open for 5% of the time, Pallas kernels for 10%

profile of v10, /device:TPU:0, one launch (start us, length us, event | category | flops | bytes accessed | tf_op | source)
XLA Modules:
  0.0 242.5 jit_solution(10383040685967642956)
XLA Ops:
  6.5 2.1 fusion.6
  9.4 7.3 %all-to-all-start = ((bf16[64,128,128]{2,1,0:T(8,128)(2,1)}), bf16[64,128,128]{2,1,0:T(8,128)(2,1)S(1)}, u32[]{:S(2)}, u32[]{:S(2)}) async-start(bf16[64,128,128]{2,1,0:T(8,128)(2,1)} %param.6), calls=%async_computation | async-start | bytes 4194304 | tf_op jit(solution)/shard_map/all_to_all | solution.py:122
  16.8 3.7 %collective-permute-start = (bf16[2,32,2048]{2,1,0:T(8,128)(2,1)S(1)}, bf16[2,32,2048]{2,1,0:T(8,128)(2,1)S(1)}, u32[]{:S(2)}, u32[]{:S(2)}) collective-permute-start(bf16[2,32,2048]{2,1,0:T(8,128)(2,1)S(1)} %get-tuple-element.46), channel_id=1, source_target_pairs={{0,8},{8,16},{16,24},{1,9},{9,17},{17,25},{2,10},{10,18},{18,26},{... | collective-permute-start | bytes 786440 | tf_op jit(solution)/shard_map/ppermute | solution.py:105
  21.8 52.0 %collective-permute-done = bf16[2,32,2048]{2,1,0:T(8,128)(2,1)S(1)} collective-permute-done((bf16[2,32,2048]{2,1,0:T(8,128)(2,1)S(1)}, bf16[2,32,2048]{2,1,0:T(8,128)(2,1)S(1)}, u32[]{:S(2)}, u32[]{:S(2)}) %collective-permute-start) | collective-permute-done | bytes 262176 | tf_op jit(solution)/shard_map/ppermute | solution.py:105
  76.3 1.4 collective-permute-start.2
  79.8 41.9 %collective-permute-done.4 = bf16[2,32,2048]{2,1,0:T(8,128)(2,1)} collective-permute-done((bf16[2,32,2048]{2,1,0:T(8,128)(2,1)S(1)}, bf16[2,32,2048]{2,1,0:T(8,128)(2,1)}, u32[]{:S(2)}, u32[]{:S(2)}) %collective-permute-start.4) | collective-permute-done | bytes 262176 | tf_op jit(solution)/shard_map/ppermute | solution.py:106
  125.2 13.5 %collective-permute-done.5 = bf16[2,32,2048]{2,1,0:T(8,128)(2,1)S(1)} collective-permute-done((bf16[2,32,2048]{2,1,0:T(8,128)(2,1)}, bf16[2,32,2048]{2,1,0:T(8,128)(2,1)S(1)}, u32[]{:S(2)}, u32[]{:S(2)}) %collective-permute-start.5) | collective-permute-done | bytes 262176 | tf_op jit(solution)/shard_map/ppermute | solution.py:106
  139.8 1.3 copy-done
  141.1 8.4 %shard_map.55 = f32[256,2048]{1,0:T(8,128)} custom-call(s32[64]{0:T(128)} %select_reduce_fusion.order_ref, s32[17]{0:T(128)} %convert_reduce_fusion.1.starts_ref, s32[64]{0:T(128)} %copy-done.8, s32[64]{0:T(128)} %reshape.74.cd_ref, bf16[8,32,2048]{2,1,0:T(8,128)(2,1)} %bitcast.148, bf16[64,128,128]{2,1,0:T(8,128)(2,1)} %copy-done), custom_call_target="tpu_custom_call" | custom-call | flops 2147483648 | bytes 5242880 | tf_op jit(solution)/shard_map/pallas_call | solution.py:66
  149.5 1.7 fusion.5
  154.1 1.9 collective-permute-start.9
  155.9 8.4 %shard_map.56 = f32[256,2048]{1,0:T(8,128)} custom-call(s32[64]{0:T(128)} %select_reduce_fusion.order_ref, s32[17]{0:T(128)} %convert_reduce_fusion.1.starts_ref, s32[64]{0:T(128)} %copy-done.8, s32[64]{0:T(128)} %reshape.74.cd_ref, bf16[8,32,2048]{2,1,0:T(8,128)(2,1)} %bitcast.147, bf16[64,128,128]{2,1,0:T(8,128)(2,1)} %copy-done), custom_call_target="tpu_custom_call" | custom-call | flops 2147483648 | bytes 5242880 | tf_op jit(solution)/shard_map/pallas_call | solution.py:66
  164.3 1.7 fusion.4
  166.2 1.5 collective-permute-start.8
  168.0 6.9 %collective-permute-done.8 = f32[2,32,1024]{2,1,0:T(8,128)S(1)} collective-permute-done((f32[2,32,1024]{2,1,0:T(8,128)S(1)}, f32[2,32,1024]{2,1,0:T(8,128)S(1)}, u32[]{:S(2)}, u32[]{:S(2)}) %collective-permute-start.8) | collective-permute-done | bytes 262176 | tf_op jit(solution)/shard_map/ppermute | solution.py:93
  175.2 8.4 %shard_map.57 = f32[256,2048]{1,0:T(8,128)} custom-call(s32[64]{0:T(128)} %select_reduce_fusion.order_ref, s32[17]{0:T(128)} %convert_reduce_fusion.1.starts_ref, s32[64]{0:T(128)} %copy-done.8, s32[64]{0:T(128)} %reshape.74.cd_ref, bf16[8,32,2048]{2,1,0:T(8,128)(2,1)} %bitcast.146, bf16[64,128,128]{2,1,0:T(8,128)(2,1)} %copy-done), custom_call_target="tpu_custom_call" | custom-call | flops 2147483648 | bytes 5242880 | tf_op jit(solution)/shard_map/pallas_call | solution.py:66
  183.5 1.7 fusion.3
  188.7 4.3 %collective-permute-done.13 = f32[32,1024]{1,0:T(8,128)S(1)} collective-permute-done((f32[32,1024]{1,0:T(8,128)S(1)}, f32[32,1024]{1,0:T(8,128)S(1)}, u32[]{:S(2)}, u32[]{:S(2)}) %collective-permute-start.13) | collective-permute-done | bytes 131104 | tf_op jit(solution)/shard_map/ppermute | solution.py:93
  193.0 1.5 collective-permute-start.12
  194.6 3.4 %collective-permute-done.12 = f32[32,1024]{1,0:T(8,128)S(1)} collective-permute-done((f32[32,1024]{1,0:T(8,128)S(1)}, f32[32,1024]{1,0:T(8,128)S(1)}, u32[]{:S(2)}, u32[]{:S(2)}) %collective-permute-start.12) | collective-permute-done | bytes 131104 | tf_op jit(solution)/shard_map/ppermute | solution.py:93
  198.3 1.6 collective-permute-start.18
  199.9 1.5 collective-permute-start.19
  202.7 8.4 %shard_map.58 = f32[256,2048]{1,0:T(8,128)} custom-call(s32[64]{0:T(128)} %select_reduce_fusion.order_ref, s32[17]{0:T(128)} %convert_reduce_fusion.1.starts_ref, s32[64]{0:T(128)} %copy-done.8, s32[64]{0:T(128)} %reshape.74.cd_ref, bf16[8,32,2048]{2,1,0:T(8,128)(2,1)} %bitcast.144, bf16[64,128,128]{2,1,0:T(8,128)(2,1)} %copy-done), custom_call_target="tpu_custom_call" | custom-call | flops 2147483648 | bytes 5242880 | tf_op jit(solution)/shard_map/pallas_call | solution.py:66
  211.0 1.7 fusion.2
  213.6 1.7 collective-permute-start.21
  215.4 1.5 collective-permute-start.23
  216.9 2.2 collective-permute-done.21
  219.1 1.5 collective-permute-done.23
  220.8 1.5 collective-permute-start.25
  222.7 5.1 %collective-permute-done.25 = f32[2,32,1024]{2,1,0:T(8,128)S(1)} collective-permute-done((f32[2,32,1024]{2,1,0:T(8,128)S(1)}, f32[2,32,1024]{2,1,0:T(8,128)S(1)}, u32[]{:S(2)}, u32[]{:S(2)}) %collective-permute-start.25) | collective-permute-done | bytes 262176 | tf_op jit(solution)/shard_map/ppermute | solution.py:93
  230.1 2.9 %collective-permute-done.26 = f32[32,1024]{1,0:T(8,128)S(1)} collective-permute-done((f32[32,1024]{1,0:T(8,128)S(1)}, f32[32,1024]{1,0:T(8,128)S(1)}, u32[]{:S(2)}, u32[]{:S(2)}) %collective-permute-start.26) | collective-permute-done | bytes 131104 | tf_op jit(solution)/shard_map/ppermute | solution.py:93
  233.0 1.9 collective-permute-done.29
  (133 shorter events, 24.4 us)
Async XLA Ops:
  6.5 133.2 %all-gather.11.cloned.1.call-start = ((), (), s32[]{:S(2)}) async-start(), calls=%async_computation.3 | async-start | bytes 1310720 | tf_op jit(solution)/shard_map/all_gather | solution.py:137
  8.7 145.4 %all-gather.9.cloned.1.call-start = ((), (), s32[]{:S(2)}) async-start(), calls=%async_computation.2 | async-start | bytes 1310720 | tf_op jit(solution)/shard_map/all_gather | solution.py:137
  9.4 130.3 %all-to-all-start = ((bf16[64,128,128]{2,1,0:T(8,128)(2,1)}), bf16[64,128,128]{2,1,0:T(8,128)(2,1)S(1)}, u32[]{:S(2)}, u32[]{:S(2)}) async-start(bf16[64,128,128]{2,1,0:T(8,128)(2,1)} %param.6), calls=%async_computation | async-start | bytes 4194304 | tf_op jit(solution)/shard_map/all_to_all | solution.py:122
  16.8 158.4 %all-gather.7.cloned.1.call-start = ((), (), s32[]{:S(2)}) async-start(), calls=%async_computation.1 | async-start | bytes 1310720 | tf_op jit(solution)/shard_map/all_gather | solution.py:137
  16.8 57.1 %collective-permute-start = (bf16[2,32,2048]{2,1,0:T(8,128)(2,1)S(1)}, bf16[2,32,2048]{2,1,0:T(8,128)(2,1)S(1)}, u32[]{:S(2)}, u32[]{:S(2)}) collective-permute-start(bf16[2,32,2048]{2,1,0:T(8,128)(2,1)S(1)} %get-tuple-element.46), channel_id=1, source_target_pairs={{0,8},{8,16},{16,24},{1,9},{9,17},{17,25},{2,10},{10,18},{18,26},{... | collective-permute-start | bytes 786440 | tf_op jit(solution)/shard_map/ppermute | solution.py:105
  20.5 54.5 %collective-permute-start.3 = (bf16[2,32,2048]{2,1,0:T(8,128)(2,1)S(1)}, bf16[2,32,2048]{2,1,0:T(8,128)(2,1)S(1)}, u32[]{:S(2)}, u32[]{:S(2)}) collective-permute-start(bf16[2,32,2048]{2,1,0:T(8,128)(2,1)S(1)} %get-tuple-element.46), channel_id=1, source_target_pairs={{8,0},{16,8},{24,16},{9,1},{17,9},{25,17},{10,2},{18,10},{26,18},{... | collective-permute-start | bytes 786440 | tf_op jit(solution)/shard_map/ppermute | solution.py:106
  75.0 46.8 %collective-permute-start.4 = (bf16[2,32,2048]{2,1,0:T(8,128)(2,1)S(1)}, bf16[2,32,2048]{2,1,0:T(8,128)(2,1)}, u32[]{:S(2)}, u32[]{:S(2)}) collective-permute-start(bf16[2,32,2048]{2,1,0:T(8,128)(2,1)S(1)} %collective-permute-done.3), channel_id=1, source_target_pairs={{8,0},{16,8},{9,1},{17,9},{10,2},{18,10},{11,3},{19,11},{12,4},{20... | collective-permute-start | bytes 786440 | tf_op jit(solution)/shard_map/ppermute | solution.py:106
  76.3 46.8 %collective-permute-start.2 = (bf16[2,32,2048]{2,1,0:T(8,128)(2,1)S(1)}, bf16[2,32,2048]{2,1,0:T(8,128)(2,1)}, u32[]{:S(2)}, u32[]{:S(2)}) collective-permute-start(bf16[2,32,2048]{2,1,0:T(8,128)(2,1)S(1)} %collective-permute-done.1), channel_id=1, source_target_pairs={{16,24},{17,25},{18,26},{19,27},{20,28},{21,29},{22,30},{23,31}} | collective-permute-start | bytes 786440 | tf_op jit(solution)/shard_map/ppermute | solution.py:105
  121.8 16.9 %collective-permute-start.5 = (bf16[2,32,2048]{2,1,0:T(8,128)(2,1)}, bf16[2,32,2048]{2,1,0:T(8,128)(2,1)S(1)}, u32[]{:S(2)}, u32[]{:S(2)}) collective-permute-start(bf16[2,32,2048]{2,1,0:T(8,128)(2,1)} %collective-permute-done.4), channel_id=1, source_target_pairs={{8,0},{9,1},{10,2},{11,3},{12,4},{13,5},{14,6},{15,7}} | collective-permute-start | bytes 786440 | tf_op jit(solution)/shard_map/ppermute | solution.py:106
  151.4 2.6 %collective-permute-start.6 = (f32[2,2,32,1024]{3,2,1,0:T(8,128)S(1)}, f32[2,2,32,1024]{3,2,1,0:T(8,128)S(1)}, u32[]{:S(2)}, u32[]{:S(2)}) collective-permute-start(f32[2,2,32,1024]{3,2,1,0:T(8,128)S(1)} %dynamic-slice_bitcast_fusion.7), channel_id=1, source_target_pairs={{0,1},{1,0},{2,3},{3,2},{4,5},{5,4},{6,7},{7,6},{8,9},{9,8},{10,11... | collective-permute-start | bytes 1572872 | tf_op jit(solution)/shard_map/ppermute | solution.py:93
  154.1 13.9 %collective-permute-start.9 = (f32[2,32,1024]{2,1,0:T(8,128)S(1)}, f32[2,32,1024]{2,1,0:T(8,128)S(1)}, u32[]{:S(2)}, u32[]{:S(2)}) collective-permute-start(f32[2,32,1024]{2,1,0:T(8,128)S(1)} %dynamic-slice_bitcast_fusion.14), channel_id=1, source_target_pairs={{0,4},{1,5},{2,6},{3,7},{4,0},{5,1},{6,2},{7,3},{8,12},{9,13},{10,... | collective-permute-start | bytes 786440 | tf_op jit(solution)/shard_map/ppermute | solution.py:93
  166.0 8.9 %collective-permute-start.11 = (f32[2,2,32,1024]{3,2,1,0:T(8,128)S(1)}, f32[2,2,32,1024]{3,2,1,0:T(8,128)S(1)}, u32[]{:S(2)}, u32[]{:S(2)}) collective-permute-start(f32[2,2,32,1024]{3,2,1,0:T(8,128)S(1)} %dynamic-slice_bitcast_fusion.4), channel_id=1, source_target_pairs={{0,1},{1,0},{2,3},{3,2},{4,5},{5,4},{6,7},{7,6},{8,9},{9,8},{10,11... | collective-permute-start | bytes 1572872 | tf_op jit(solution)/shard_map/ppermute | solution.py:93
  166.2 8.8 %collective-permute-start.8 = (f32[2,32,1024]{2,1,0:T(8,128)S(1)}, f32[2,32,1024]{2,1,0:T(8,128)S(1)}, u32[]{:S(2)}, u32[]{:S(2)}) collective-permute-start(f32[2,32,1024]{2,1,0:T(8,128)S(1)} %dynamic-slice_bitcast_fusion.15), channel_id=1, source_target_pairs={{0,2},{1,3},{2,0},{3,1},{4,6},{5,7},{6,4},{7,5},{8,10},{9,11},{10,... | collective-permute-start | bytes 786440 | tf_op jit(solution)/shard_map/ppermute | solution.py:93
  167.7 7.3 %collective-permute-start.10 = (f32[2,2,32,1024]{3,2,1,0:T(8,128)S(1)}, f32[2,2,32,1024]{3,2,1,0:T(8,128)S(1)}, u32[]{:S(2)}, u32[]{:S(2)}) collective-permute-start(f32[2,2,32,1024]{3,2,1,0:T(8,128)S(1)} %dynamic-slice_bitcast_fusion.5), channel_id=1, source_target_pairs={{0,1},{1,0},{2,3},{3,2},{4,5},{5,4},{6,7},{7,6},{8,9},{9,8},{10,11... | collective-permute-start | bytes 1572872 | tf_op jit(solution)/shard_map/ppermute | solution.py:93
  185.3 12.8 %collective-permute-start.17 = (f32[2,2,32,1024]{3,2,1,0:T(8,128)S(1)}, f32[2,2,32,1024]{3,2,1,0:T(8,128)S(1)}, u32[]{:S(2)}, u32[]{:S(2)}) collective-permute-start(f32[2,2,32,1024]{3,2,1,0:T(8,128)S(1)} %dynamic-slice_bitcast_fusion.2), channel_id=1, source_target_pairs={{0,1},{1,0},{2,3},{3,2},{4,5},{5,4},{6,7},{7,6},{8,9},{9,8},{10,11... | collective-permute-start | bytes 1572872 | tf_op jit(solution)/shard_map/ppermute | solution.py:93
  185.4 12.8 %collective-permute-start.16 = (f32[2,2,32,1024]{3,2,1,0:T(8,128)S(1)}, f32[2,2,32,1024]{3,2,1,0:T(8,128)S(1)}, u32[]{:S(2)}, u32[]{:S(2)}) collective-permute-start(f32[2,2,32,1024]{3,2,1,0:T(8,128)S(1)} %dynamic-slice_bitcast_fusion.3), channel_id=1, source_target_pairs={{0,1},{1,0},{2,3},{3,2},{4,5},{5,4},{6,7},{7,6},{8,9},{9,8},{10,11... | collective-permute-start | bytes 1572872 | tf_op jit(solution)/shard_map/ppermute | solution.py:93
  186.0 12.0 %collective-permute-start.15 = (f32[2,32,1024]{2,1,0:T(8,128)S(1)}, f32[2,32,1024]{2,1,0:T(8,128)S(1)}, u32[]{:S(2)}, u32[]{:S(2)}) collective-permute-start(f32[2,32,1024]{2,1,0:T(8,128)S(1)} %dynamic-slice_bitcast_fusion.12), channel_id=1, source_target_pairs={{0,4},{1,5},{2,6},{3,7},{4,0},{5,1},{6,2},{7,3},{8,12},{9,13},{10,... | collective-permute-start | bytes 786440 | tf_op jit(solution)/shard_map/ppermute | solution.py:93
  186.5 6.5 %collective-permute-start.13 = (f32[32,1024]{1,0:T(8,128)S(1)}, f32[32,1024]{1,0:T(8,128)S(1)}, u32[]{:S(2)}, u32[]{:S(2)}) collective-permute-start(f32[32,1024]{1,0:T(8,128)S(1)} %dynamic-slice_bitcast_fusion.22), channel_id=1, source_target_pairs={{0,2},{1,3},{2,0},{3,1},{4,6},{5,7},{6,4},{7,5},{8,10},{9,11},{10,... | collective-permute-start | bytes 393224 | tf_op jit(solution)/shard_map/ppermute | solution.py:93
  187.8 10.2 %collective-permute-start.14 = (f32[2,32,1024]{2,1,0:T(8,128)S(1)}, f32[2,32,1024]{2,1,0:T(8,128)S(1)}, u32[]{:S(2)}, u32[]{:S(2)}) collective-permute-start(f32[2,32,1024]{2,1,0:T(8,128)S(1)} %dynamic-slice_bitcast_fusion.13), channel_id=1, source_target_pairs={{0,2},{1,3},{2,0},{3,1},{4,6},{5,7},{6,4},{7,5},{8,10},{9,11},{10,... | collective-permute-start | bytes 786440 | tf_op jit(solution)/shard_map/ppermute | solution.py:93
  193.0 5.0 %collective-permute-start.12 = (f32[32,1024]{1,0:T(8,128)S(1)}, f32[32,1024]{1,0:T(8,128)S(1)}, u32[]{:S(2)}, u32[]{:S(2)}) collective-permute-start(f32[32,1024]{1,0:T(8,128)S(1)} %dynamic-slice_bitcast_fusion.23), channel_id=1, source_target_pairs={{0,4},{1,5},{2,6},{3,7},{4,0},{5,1},{6,2},{7,3},{8,12},{9,13},{10,... | collective-permute-start | bytes 393224 | tf_op jit(solution)/shard_map/ppermute | solution.py:93
  198.3 14.6 %collective-permute-start.18 = (f32[32,1024]{1,0:T(8,128)S(1)}, f32[32,1024]{1,0:T(8,128)S(1)}, u32[]{:S(2)}, u32[]{:S(2)}) collective-permute-start(f32[32,1024]{1,0:T(8,128)S(1)} %dynamic-slice_bitcast_fusion.21), channel_id=1, source_target_pairs={{0,4},{1,5},{2,6},{3,7},{4,0},{5,1},{6,2},{7,3},{8,12},{9,13},{10,... | collective-permute-start | bytes 393224 | tf_op jit(solution)/shard_map/ppermute | solution.py:93
  199.9 13.6 %collective-permute-start.19 = (f32[32,1024]{1,0:T(8,128)S(1)}, f32[32,1024]{1,0:T(8,128)S(1)}, u32[]{:S(2)}, u32[]{:S(2)}) collective-permute-start(f32[32,1024]{1,0:T(8,128)S(1)} %dynamic-slice_bitcast_fusion.20), channel_id=1, source_target_pairs={{0,2},{1,3},{2,0},{3,1},{4,6},{5,7},{6,4},{7,5},{8,10},{9,11},{10,... | collective-permute-start | bytes 393224 | tf_op jit(solution)/shard_map/ppermute | solution.py:93
  201.5 12.1 %collective-permute-start.20 = (f32[2,32,1024]{2,1,0:T(8,128)S(1)}, f32[2,32,1024]{2,1,0:T(8,128)S(1)}, u32[]{:S(2)}, u32[]{:S(2)}) collective-permute-start(f32[2,32,1024]{2,1,0:T(8,128)S(1)} %dynamic-slice_bitcast_fusion.11), channel_id=1, source_target_pairs={{0,2},{1,3},{2,0},{3,1},{4,6},{5,7},{6,4},{7,5},{8,10},{9,11},{10,... | collective-permute-start | bytes 786440 | tf_op jit(solution)/shard_map/ppermute | solution.py:93
  202.1 13.2 %collective-permute-start.22 = (f32[2,32,1024]{2,1,0:T(8,128)S(1)}, f32[2,32,1024]{2,1,0:T(8,128)S(1)}, u32[]{:S(2)}, u32[]{:S(2)}) collective-permute-start(f32[2,32,1024]{2,1,0:T(8,128)S(1)} %dynamic-slice_bitcast_fusion.10), channel_id=1, source_target_pairs={{0,4},{1,5},{2,6},{3,7},{4,0},{5,1},{6,2},{7,3},{8,12},{9,13},{10,... | collective-permute-start | bytes 786440 | tf_op jit(solution)/shard_map/ppermute | solution.py:93
  212.8 7.9 %collective-permute-start.24 = (f32[2,2,32,1024]{3,2,1,0:T(8,128)S(1)}, f32[2,2,32,1024]{3,2,1,0:T(8,128)S(1)}, u32[]{:S(2)}, u32[]{:S(2)}) collective-permute-start(f32[2,2,32,1024]{3,2,1,0:T(8,128)S(1)} %dynamic-slice_bitcast_fusion.1), channel_id=1, source_target_pairs={{0,1},{1,0},{2,3},{3,2},{4,5},{5,4},{6,7},{7,6},{8,9},{9,8},{10,11... | collective-permute-start | bytes 1572872 | tf_op jit(solution)/shard_map/ppermute | solution.py:93
  212.9 9.3 %collective-permute-start.27 = (f32[2,2,32,1024]{3,2,1,0:T(8,128)S(1)}, f32[2,2,32,1024]{3,2,1,0:T(8,128)S(1)}, u32[]{:S(2)}, u32[]{:S(2)}) collective-permute-start(f32[2,2,32,1024]{3,2,1,0:T(8,128)S(1)} %dynamic-slice_bitcast_fusion), channel_id=1, source_target_pairs={{0,1},{1,0},{2,3},{3,2},{4,5},{5,4},{6,7},{7,6},{8,9},{9,8},{10,11... | collective-permute-start | bytes 1572872 | tf_op jit(solution)/shard_map/ppermute | solution.py:93
  213.6 5.5 %collective-permute-start.21 = (f32[32,1024]{1,0:T(8,128)S(1)}, f32[32,1024]{1,0:T(8,128)S(1)}, u32[]{:S(2)}, u32[]{:S(2)}) collective-permute-start(f32[32,1024]{1,0:T(8,128)S(1)} %dynamic-slice_bitcast_fusion.19), channel_id=1, source_target_pairs={{0,4},{1,5},{2,6},{3,7},{4,0},{5,1},{6,2},{7,3},{8,12},{9,13},{10,... | collective-permute-start | bytes 393224 | tf_op jit(solution)/shard_map/ppermute | solution.py:93
  215.4 5.2 %collective-permute-start.23 = (f32[32,1024]{1,0:T(8,128)S(1)}, f32[32,1024]{1,0:T(8,128)S(1)}, u32[]{:S(2)}, u32[]{:S(2)}) collective-permute-start(f32[32,1024]{1,0:T(8,128)S(1)} %dynamic-slice_bitcast_fusion.18), channel_id=1, source_target_pairs={{0,2},{1,3},{2,0},{3,1},{4,6},{5,7},{6,4},{7,5},{8,10},{9,11},{10,... | collective-permute-start | bytes 393224 | tf_op jit(solution)/shard_map/ppermute | solution.py:93
  220.8 7.1 %collective-permute-start.25 = (f32[2,32,1024]{2,1,0:T(8,128)S(1)}, f32[2,32,1024]{2,1,0:T(8,128)S(1)}, u32[]{:S(2)}, u32[]{:S(2)}) collective-permute-start(f32[2,32,1024]{2,1,0:T(8,128)S(1)} %dynamic-slice_bitcast_fusion.9), channel_id=1, source_target_pairs={{0,2},{1,3},{2,0},{3,1},{4,6},{5,7},{6,4},{7,5},{8,10},{9,11},{10,... | collective-permute-start | bytes 786440 | tf_op jit(solution)/shard_map/ppermute | solution.py:93
  222.4 7.5 %collective-permute-start.28 = (f32[2,32,1024]{2,1,0:T(8,128)S(1)}, f32[2,32,1024]{2,1,0:T(8,128)S(1)}, u32[]{:S(2)}, u32[]{:S(2)}) collective-permute-start(f32[2,32,1024]{2,1,0:T(8,128)S(1)} %dynamic-slice_bitcast_fusion.8), channel_id=1, source_target_pairs={{0,4},{1,5},{2,6},{3,7},{4,0},{5,1},{6,2},{7,3},{8,12},{9,13},{10,... | collective-permute-start | bytes 786440 | tf_op jit(solution)/shard_map/ppermute | solution.py:93
  228.0 5.0 %collective-permute-start.26 = (f32[32,1024]{1,0:T(8,128)S(1)}, f32[32,1024]{1,0:T(8,128)S(1)}, u32[]{:S(2)}, u32[]{:S(2)}) collective-permute-start(f32[32,1024]{1,0:T(8,128)S(1)} %dynamic-slice_bitcast_fusion.17), channel_id=1, source_target_pairs={{0,4},{1,5},{2,6},{3,7},{4,0},{5,1},{6,2},{7,3},{8,12},{9,13},{10,... | collective-permute-start | bytes 393224 | tf_op jit(solution)/shard_map/ppermute | solution.py:93
  229.9 5.0 %collective-permute-start.29 = (f32[32,1024]{1,0:T(8,128)S(1)}, f32[32,1024]{1,0:T(8,128)S(1)}, u32[]{:S(2)}, u32[]{:S(2)}) collective-permute-start(f32[32,1024]{1,0:T(8,128)S(1)} %dynamic-slice_bitcast_fusion.16), channel_id=1, source_target_pairs={{0,2},{1,3},{2,0},{3,1},{4,6},{5,7},{6,4},{7,5},{8,10},{9,11},{10,... | collective-permute-start | bytes 393224 | tf_op jit(solution)/shard_map/ppermute | solution.py:93
  (11 other events, 379.4 us)
Sparse Core Ops, SparseCore 0:
  8.9 56.7 all-gather.10
  67.2 35.3 all-gather.8
  104.2 31.5 all-gather.6

commit v11 on v4

--- a/solution.py
+++ b/solution.py
@@ -116,7 +116,14 @@
     rep_index = lax.axis_index("rep")
     levels = rep_count.bit_length() - 1
     orders = (list(range(levels)), [0] + list(range(levels - 1, 0, -1)))
-    gathered = [lax.all_gather(local4[:, c], "own", axis=0, tiled=True) for c in range(N_CHUNK)]
+    gathered = [lax.all_gather(local4[:, c], "own", axis=0, tiled=True) for c in range(N_CHUNK - 1)]
+    last = local4[:, N_CHUNK - 1]
+    copies = jnp.broadcast_to(last[None], (own_count,) + last.shape)
+    gathered.append(
+        lax.all_to_all(copies, "own", split_axis=0, concat_axis=0, tiled=True).reshape(
+            (own_count * last.shape[0],) + last.shape[1:]
+        )
+    )
     flows = []
     for chunk in range(N_CHUNK):
         for flow in flows:

time: 201 us -> 209 us (1.040)
  starting transfers between devices: 26.9 us -> 33.6 us
    all_gather x4 -> x3, waiting for transfers between devices: 68.9 us -> 73.3 us  [on_device(): lax.all_gather(local4[:, c], 'own', axis=0, tiled=True)]
    all_to_all x0 -> x1, starting transfers between devices: none -> 4.27 us  [on_device(): lax.all_to_all(copies, 'own', split_axis=0, concat_axis=0, tiled=True)]
    ppermute x24, waiting for transfers between devices: 30.7 us -> 27.4 us  [advance(): self.x = keep + lax.ppermute(send, 'rep', perm=pairs)]
    ppermute x24, starting transfers between devices: 19.5 us -> 21.9 us  [advance(): self.x = keep + lax.ppermute(send, 'rep', perm=pairs)]
  transfers between devices with their start and end apart: 29 -> 29, of which waited for: 16 -> 12; matrix products, arithmetic and copies ran while one was open for 7% -> 7% of each run, Pallas kernels for 17% -> 16%
where the time goes in v11:
time: 209 us
  waiting for transfers between devices  110 us (53%)
  starting transfers between devices  33.6 us (16%)
  Pallas kernels  33.6 us (16%)
  between operations  13.6 us (7%)
  local copies, waits for them, and re-layouts  12.6 us (6%)
  other arithmetic  4.73 us (2%)
    all_gather x3, waiting for transfers between devices, on_device(): lax.all_gather(local4[:, c], 'own', axis=0, tiled=True)  73.3 us
    pallas_call x4, Pallas kernels, _ladder_products(): pl.pallas_call(_ladder_kernel, grid_spec=grid_spec, out_shape=jax.ShapeDt...  33.6 us
    ppermute x24, waiting for transfers between devices, advance(): self.x = keep + lax.ppermute(send, 'rep', perm=pairs)  27.4 us
    ppermute x24, starting transfers between devices, advance(): self.x = keep + lax.ppermute(send, 'rep', perm=pairs)  21.9 us
    all_to_all x1, waiting for transfers between devices, on_device(): lax.all_to_all(integrals, ('own', 'rep'), split_axis=0, concat_axis=0, ti...  8.25 us
    all_to_all x1, starting transfers between devices, on_device(): lax.all_to_all(integrals, ('own', 'rep'), split_axis=0, concat_axis=0, ti...  7.3 us
    slice x4, local copies, waits for them, and re-layouts, on_device(): partial[:, h * half:(h + 1) * half]  6.73 us
    all_to_all x1, starting transfers between devices, on_device(): lax.all_to_all(copies, 'own', split_axis=0, concat_axis=0, tiled=True)  4.27 us
  transfers between devices with their start and end apart: 29, of which 12 were waited for; matrix products, arithmetic and copies ran while one was open for 7% of the time, Pallas kernels for 16%

profile of v11, /device:TPU:0, one launch (start us, length us, event | category | flops | bytes accessed | tf_op | source)
XLA Modules:
  0.0 208.6 jit_solution(15824125813888973572)
XLA Ops:
  6.5 7.3 %all-to-all-start.1 = ((bf16[64,128,128]{2,1,0:T(8,128)(2,1)}), bf16[64,128,128]{2,1,0:T(8,128)(2,1)S(1)}, u32[]{:S(2)}, u32[]{:S(2)}) async-start(bf16[64,128,128]{2,1,0:T(8,128)(2,1)} %param.6), calls=%async_computation.1 | async-start | bytes 4194304 | tf_op jit(solution)/shard_map/all_to_all | solution.py:105
  18.3 52.8 %all-gather.11.cloned.1.call-done = bf16[8,1,32,2048]{3,2,1,0:T(8,128)(2,1)} async-done(((bf16[2,1,32,2048]{3,2,1,0:T(8,128)(2,1)}), bf16[8,1,32,2048]{3,2,1,0:T(8,128)(2,1)}) %all-gather.11.cloned.1.call-update) | async-done | bytes 1048592 | tf_op jit(solution)/shard_map/all_gather | solution.py:119
  71.2 8.2 %all-to-all-done.1.tiles_ref = bf16[64,128,128]{2,1,0:T(8,128)(2,1)S(1)} async-done(((bf16[64,128,128]{2,1,0:T(8,128)(2,1)}), bf16[64,128,128]{2,1,0:T(8,128)(2,1)S(1)}, u32[]{:S(2)}, u32[]{:S(2)}) %all-to-all-start.1) | async-done | bytes 2097184 | tf_op jit(solution)/shard_map/all_to_all | solution.py:105
  79.4 1.4 copy-done
  80.8 8.4 %shard_map.55 = f32[256,2048]{1,0:T(8,128)} custom-call(s32[64]{0:T(128)} %select_reduce_fusion.order_ref, s32[17]{0:T(128)} %convert_reduce_fusion.1.starts_ref, s32[64]{0:T(128)} %copy-done.5, s32[64]{0:T(128)} %reshape.75.cd_ref, bf16[8,32,2048]{2,1,0:T(8,128)(2,1)} %bitcast.132, bf16[64,128,128]{2,1,0:T(8,128)(2,1)} %copy-done), custom_call_target="tpu_custom_call" | custom-call | flops 2147483648 | bytes 5242880 | tf_op jit(solution)/shard_map/pallas_call | solution.py:66
  89.2 1.7 fusion.5
  93.4 4.3 %all-to-all-start = ((bf16[4,2,32,2048]{3,2,1,0:T(8,128)(2,1)}), bf16[4,2,32,2048]{3,2,1,0:T(8,128)(2,1)}, u32[]{:S(2)}, u32[]{:S(2)}) async-start(bf16[4,2,32,2048]{3,2,1,0:T(8,128)(2,1)} %broadcast_in_dim.15), calls=%async_computation | async-start | bytes 2097152 | tf_op jit(solution)/shard_map/all_to_all | solution.py:123
  99.7 1.6 collective-permute-start.3
  101.3 8.4 %shard_map.56 = f32[256,2048]{1,0:T(8,128)} custom-call(s32[64]{0:T(128)} %select_reduce_fusion.order_ref, s32[17]{0:T(128)} %convert_reduce_fusion.1.starts_ref, s32[64]{0:T(128)} %copy-done.5, s32[64]{0:T(128)} %reshape.75.cd_ref, bf16[8,32,2048]{2,1,0:T(8,128)(2,1)} %bitcast.130, bf16[64,128,128]{2,1,0:T(8,128)(2,1)} %copy-done), custom_call_target="tpu_custom_call" | custom-call | flops 2147483648 | bytes 5242880 | tf_op jit(solution)/shard_map/pallas_call | solution.py:66
  109.8 1.7 fusion.4
  111.6 1.6 collective-permute-start.2
  113.5 6.9 %collective-permute-done.2 = f32[2,32,1024]{2,1,0:T(8,128)S(1)} collective-permute-done((f32[2,32,1024]{2,1,0:T(8,128)S(1)}, f32[2,32,1024]{2,1,0:T(8,128)S(1)}, u32[]{:S(2)}, u32[]{:S(2)}) %collective-permute-start.2) | collective-permute-done | bytes 262176 | tf_op jit(solution)/shard_map/ppermute | solution.py:93
  120.6 20.5 %all-gather.7.cloned.1.call-done = bf16[8,1,32,2048]{3,2,1,0:T(8,128)(2,1)} async-done(((bf16[2,1,32,2048]{3,2,1,0:T(8,128)(2,1)}), bf16[8,1,32,2048]{3,2,1,0:T(8,128)(2,1)}) %all-gather.7.cloned.1.call-update) | async-done | bytes 1048592 | tf_op jit(solution)/shard_map/all_gather | solution.py:119
  141.1 8.4 %shard_map.57 = f32[256,2048]{1,0:T(8,128)} custom-call(s32[64]{0:T(128)} %select_reduce_fusion.order_ref, s32[17]{0:T(128)} %convert_reduce_fusion.1.starts_ref, s32[64]{0:T(128)} %copy-done.5, s32[64]{0:T(128)} %reshape.75.cd_ref, bf16[8,32,2048]{2,1,0:T(8,128)(2,1)} %bitcast.131, bf16[64,128,128]{2,1,0:T(8,128)(2,1)} %copy-done), custom_call_target="tpu_custom_call" | custom-call | flops 2147483648 | bytes 5242880 | tf_op jit(solution)/shard_map/pallas_call | solution.py:66
  149.5 1.7 fusion.3
  151.9 1.7 collective-permute-start.9
  153.6 1.6 collective-permute-start.7
  155.8 4.3 %collective-permute-done.7 = f32[32,1024]{1,0:T(8,128)S(1)} collective-permute-done((f32[32,1024]{1,0:T(8,128)S(1)}, f32[32,1024]{1,0:T(8,128)S(1)}, u32[]{:S(2)}, u32[]{:S(2)}) %collective-permute-start.7) | collective-permute-done | bytes 131104 | tf_op jit(solution)/shard_map/ppermute | solution.py:93
  160.5 4.5 %collective-permute-done.6 = f32[32,1024]{1,0:T(8,128)S(1)} collective-permute-done((f32[32,1024]{1,0:T(8,128)S(1)}, f32[32,1024]{1,0:T(8,128)S(1)}, u32[]{:S(2)}, u32[]{:S(2)}) %collective-permute-start.6) | collective-permute-done | bytes 131104 | tf_op jit(solution)/shard_map/ppermute | solution.py:93
  165.9 1.6 collective-permute-start.13
  168.1 1.7 collective-permute-start.16
  169.8 8.4 %shard_map.58 = f32[256,2048]{1,0:T(8,128)} custom-call(s32[64]{0:T(128)} %select_reduce_fusion.order_ref, s32[17]{0:T(128)} %convert_reduce_fusion.1.starts_ref, s32[64]{0:T(128)} %copy-done.5, s32[64]{0:T(128)} %reshape.75.cd_ref, bf16[8,32,2048]{2,1,0:T(8,128)(2,1)} %bitcast.2.amp_ref, bf16[64,128,128]{2,1,0:T(8,128)(2,1)} %copy-done), custom_call_target="tpu_custom_call" | custom-call | flops 2147483648 | bytes 5242880 | tf_op jit(solution)/shard_map/pallas_call | solution.py:66
  178.2 1.7 fusion.2
  181.3 1.6 collective-permute-start.17
  182.9 3.3 %collective-permute-done.15 = f32[32,1024]{1,0:T(8,128)S(1)} collective-permute-done((f32[32,1024]{1,0:T(8,128)S(1)}, f32[32,1024]{1,0:T(8,128)S(1)}, u32[]{:S(2)}, u32[]{:S(2)}) %collective-permute-start.15) | collective-permute-done | bytes 131104 | tf_op jit(solution)/shard_map/ppermute | solution.py:93
  186.7 1.6 collective-permute-start.19
  188.4 1.6 collective-permute-start.22
  190.0 3.9 %collective-permute-done.19 = f32[2,32,1024]{2,1,0:T(8,128)S(1)} collective-permute-done((f32[2,32,1024]{2,1,0:T(8,128)S(1)}, f32[2,32,1024]{2,1,0:T(8,128)S(1)}, u32[]{:S(2)}, u32[]{:S(2)}) %collective-permute-start.19) | collective-permute-done | bytes 262176 | tf_op jit(solution)/shard_map/ppermute | solution.py:93
  193.9 1.6 collective-permute-start.20
  195.9 1.2 collective-permute-start.23
  197.1 1.8 collective-permute-done.20
  199.0 2.0 collective-permute-done.23
  (110 shorter events, 16.2 us)
Async XLA Ops:
  6.5 7.4 %copy-start.1 = (bf16[256,2048]{1,0:T(8,128)(2,1)S(1)}, bf16[256,2048]{1,0:T(8,128)(2,1)}, u32[]{:S(2)}) copy-start(bf16[256,2048]{1,0:T(8,128)(2,1)} %param.5) | copy-start | bytes 3145732
  6.5 72.9 %all-to-all-start.1 = ((bf16[64,128,128]{2,1,0:T(8,128)(2,1)}), bf16[64,128,128]{2,1,0:T(8,128)(2,1)S(1)}, u32[]{:S(2)}, u32[]{:S(2)}) async-start(bf16[64,128,128]{2,1,0:T(8,128)(2,1)} %param.6), calls=%async_computation.1 | async-start | bytes 4194304 | tf_op jit(solution)/shard_map/all_to_all | solution.py:105
  13.9 2.2 %copy-start.3 = (s32[1,32,2]{1,2,0:T(2,128)S(1)}, s32[1,32,2]{1,2,0:T(2,128)}, u32[]{:S(2)}) copy-start(s32[1,32,2]{1,2,0:T(2,128)} %param.8) | copy-start | bytes 772
  13.9 57.3 %all-gather.11.cloned.1.call-start = ((), (), s32[]{:S(2)}) async-start(), calls=%async_computation.4 | async-start | bytes 1310720 | tf_op jit(solution)/shard_map/all_gather | solution.py:119
  14.9 84.8 %all-gather.9.cloned.1.call-start = ((), (), s32[]{:S(2)}) async-start(), calls=%async_computation.3 | async-start | bytes 1310720 | tf_op jit(solution)/shard_map/all_gather | solution.py:119
  15.8 63.6 %copy-start.5 = (s32[64]{0:T(128)}, s32[64]{0:T(128)S(1)}, u32[]{:S(2)}) copy-start(s32[64]{0:T(128)S(1)} %reshape.74.ab_ref) | copy-start | bytes 772
  90.9 7.5 %collective-permute-start.1 = (f32[2,2,32,1024]{3,2,1,0:T(8,128)S(1)}, f32[2,2,32,1024]{3,2,1,0:T(8,128)}, u32[]{:S(2)}, u32[]{:S(2)}) collective-permute-start(f32[2,2,32,1024]{3,2,1,0:T(8,128)S(1)} %dynamic-slice_bitcast_fusion.6), channel_id=1, source_target_pairs={{0,1},{1,0},{2,3},{3,2},{4,5},{5,4},{6,7},{7,6},{8,9},{9,8},{10,11... | collective-permute-start | bytes 1572872 | tf_op jit(solution)/shard_map/ppermute | solution.py:93
  91.9 7.7 %collective-permute-start = (f32[2,2,32,1024]{3,2,1,0:T(8,128)}, f32[2,2,32,1024]{3,2,1,0:T(8,128)S(1)}, u32[]{:S(2)}, u32[]{:S(2)}) collective-permute-start(f32[2,2,32,1024]{3,2,1,0:T(8,128)} %dynamic-slice_bitcast_fusion.7), channel_id=1, source_target_pairs={{0,1},{1,0},{2,3},{3,2},{4,5},{5,4},{6,7},{7,6},{8,9},{9,8},{10,11... | collective-permute-start | bytes 1572872 | tf_op jit(solution)/shard_map/ppermute | solution.py:93
  93.4 71.9 %all-to-all-start = ((bf16[4,2,32,2048]{3,2,1,0:T(8,128)(2,1)}), bf16[4,2,32,2048]{3,2,1,0:T(8,128)(2,1)}, u32[]{:S(2)}, u32[]{:S(2)}) async-start(bf16[4,2,32,2048]{3,2,1,0:T(8,128)(2,1)} %broadcast_in_dim.15), calls=%async_computation | async-start | bytes 2097152 | tf_op jit(solution)/shard_map/all_to_all | solution.py:123
  97.7 43.4 %all-gather.7.cloned.1.call-start = ((), (), s32[]{:S(2)}) async-start(), calls=%async_computation.2 | async-start | bytes 1310720 | tf_op jit(solution)/shard_map/all_gather | solution.py:119
  99.7 13.7 %collective-permute-start.3 = (f32[2,32,1024]{2,1,0:T(8,128)S(1)}, f32[2,32,1024]{2,1,0:T(8,128)S(1)}, u32[]{:S(2)}, u32[]{:S(2)}) collective-permute-start(f32[2,32,1024]{2,1,0:T(8,128)S(1)} %dynamic-slice_bitcast_fusion.14), channel_id=1, source_target_pairs={{0,4},{1,5},{2,6},{3,7},{4,0},{5,1},{6,2},{7,3},{8,12},{9,13},{10,... | collective-permute-start | bytes 786440 | tf_op jit(solution)/shard_map/ppermute | solution.py:93
  111.5 8.9 %collective-permute-start.5 = (f32[2,2,32,1024]{3,2,1,0:T(8,128)S(1)}, f32[2,2,32,1024]{3,2,1,0:T(8,128)S(1)}, u32[]{:S(2)}, u32[]{:S(2)}) collective-permute-start(f32[2,2,32,1024]{3,2,1,0:T(8,128)S(1)} %dynamic-slice_bitcast_fusion.4), channel_id=1, source_target_pairs={{0,1},{1,0},{2,3},{3,2},{4,5},{5,4},{6,7},{7,6},{8,9},{9,8},{10,11... | collective-permute-start | bytes 1572872 | tf_op jit(solution)/shard_map/ppermute | solution.py:93
  111.6 8.8 %collective-permute-start.2 = (f32[2,32,1024]{2,1,0:T(8,128)S(1)}, f32[2,32,1024]{2,1,0:T(8,128)S(1)}, u32[]{:S(2)}, u32[]{:S(2)}) collective-permute-start(f32[2,32,1024]{2,1,0:T(8,128)S(1)} %dynamic-slice_bitcast_fusion.15), channel_id=1, source_target_pairs={{0,2},{1,3},{2,0},{3,1},{4,6},{5,7},{6,4},{7,5},{8,10},{9,11},{10,... | collective-permute-start | bytes 786440 | tf_op jit(solution)/shard_map/ppermute | solution.py:93
  113.2 7.3 %collective-permute-start.4 = (f32[2,2,32,1024]{3,2,1,0:T(8,128)S(1)}, f32[2,2,32,1024]{3,2,1,0:T(8,128)S(1)}, u32[]{:S(2)}, u32[]{:S(2)}) collective-permute-start(f32[2,2,32,1024]{3,2,1,0:T(8,128)S(1)} %dynamic-slice_bitcast_fusion.5), channel_id=1, source_target_pairs={{0,1},{1,0},{2,3},{3,2},{4,5},{5,4},{6,7},{7,6},{8,9},{9,8},{10,11... | collective-permute-start | bytes 1572872 | tf_op jit(solution)/shard_map/ppermute | solution.py:93
  151.2 14.0 %collective-permute-start.11 = (f32[2,2,32,1024]{3,2,1,0:T(8,128)S(1)}, f32[2,2,32,1024]{3,2,1,0:T(8,128)S(1)}, u32[]{:S(2)}, u32[]{:S(2)}) collective-permute-start(f32[2,2,32,1024]{3,2,1,0:T(8,128)S(1)} %dynamic-slice_bitcast_fusion.2), channel_id=1, source_target_pairs={{0,1},{1,0},{2,3},{3,2},{4,5},{5,4},{6,7},{7,6},{8,9},{9,8},{10,11... | collective-permute-start | bytes 1572872 | tf_op jit(solution)/shard_map/ppermute | solution.py:93
  151.4 13.9 %collective-permute-start.10 = (f32[2,2,32,1024]{3,2,1,0:T(8,128)S(1)}, f32[2,2,32,1024]{3,2,1,0:T(8,128)S(1)}, u32[]{:S(2)}, u32[]{:S(2)}) collective-permute-start(f32[2,2,32,1024]{3,2,1,0:T(8,128)S(1)} %dynamic-slice_bitcast_fusion.3), channel_id=1, source_target_pairs={{0,1},{1,0},{2,3},{3,2},{4,5},{5,4},{6,7},{7,6},{8,9},{9,8},{10,11... | collective-permute-start | bytes 1572872 | tf_op jit(solution)/shard_map/ppermute | solution.py:93
  151.9 13.2 %collective-permute-start.9 = (f32[2,32,1024]{2,1,0:T(8,128)S(1)}, f32[2,32,1024]{2,1,0:T(8,128)S(1)}, u32[]{:S(2)}, u32[]{:S(2)}) collective-permute-start(f32[2,32,1024]{2,1,0:T(8,128)S(1)} %dynamic-slice_bitcast_fusion.12), channel_id=1, source_target_pairs={{0,4},{1,5},{2,6},{3,7},{4,0},{5,1},{6,2},{7,3},{8,12},{9,13},{10,... | collective-permute-start | bytes 786440 | tf_op jit(solution)/shard_map/ppermute | solution.py:93
  153.6 6.5 %collective-permute-start.7 = (f32[32,1024]{1,0:T(8,128)S(1)}, f32[32,1024]{1,0:T(8,128)S(1)}, u32[]{:S(2)}, u32[]{:S(2)}) collective-permute-start(f32[32,1024]{1,0:T(8,128)S(1)} %dynamic-slice_bitcast_fusion.22), channel_id=1, source_target_pairs={{0,2},{1,3},{2,0},{3,1},{4,6},{5,7},{6,4},{7,5},{8,10},{9,11},{10,... | collective-permute-start | bytes 393224 | tf_op jit(solution)/shard_map/ppermute | solution.py:93
  155.2 9.9 %collective-permute-start.8 = (f32[2,32,1024]{2,1,0:T(8,128)S(1)}, f32[2,32,1024]{2,1,0:T(8,128)S(1)}, u32[]{:S(2)}, u32[]{:S(2)}) collective-permute-start(f32[2,32,1024]{2,1,0:T(8,128)S(1)} %dynamic-slice_bitcast_fusion.13), channel_id=1, source_target_pairs={{0,2},{1,3},{2,0},{3,1},{4,6},{5,7},{6,4},{7,5},{8,10},{9,11},{10,... | collective-permute-start | bytes 786440 | tf_op jit(solution)/shard_map/ppermute | solution.py:93
  160.1 5.0 %collective-permute-start.6 = (f32[32,1024]{1,0:T(8,128)S(1)}, f32[32,1024]{1,0:T(8,128)S(1)}, u32[]{:S(2)}, u32[]{:S(2)}) collective-permute-start(f32[32,1024]{1,0:T(8,128)S(1)} %dynamic-slice_bitcast_fusion.23), channel_id=1, source_target_pairs={{0,4},{1,5},{2,6},{3,7},{4,0},{5,1},{6,2},{7,3},{8,12},{9,13},{10,... | collective-permute-start | bytes 393224 | tf_op jit(solution)/shard_map/ppermute | solution.py:93
  165.4 14.6 %collective-permute-start.12 = (f32[32,1024]{1,0:T(8,128)S(1)}, f32[32,1024]{1,0:T(8,128)S(1)}, u32[]{:S(2)}, u32[]{:S(2)}) collective-permute-start(f32[32,1024]{1,0:T(8,128)S(1)} %dynamic-slice_bitcast_fusion.21), channel_id=1, source_target_pairs={{0,4},{1,5},{2,6},{3,7},{4,0},{5,1},{6,2},{7,3},{8,12},{9,13},{10,... | collective-permute-start | bytes 393224 | tf_op jit(solution)/shard_map/ppermute | solution.py:93
  165.9 14.7 %collective-permute-start.13 = (f32[32,1024]{1,0:T(8,128)S(1)}, f32[32,1024]{1,0:T(8,128)S(1)}, u32[]{:S(2)}, u32[]{:S(2)}) collective-permute-start(f32[32,1024]{1,0:T(8,128)S(1)} %dynamic-slice_bitcast_fusion.20), channel_id=1, source_target_pairs={{0,2},{1,3},{2,0},{3,1},{4,6},{5,7},{6,4},{7,5},{8,10},{9,11},{10,... | collective-permute-start | bytes 393224 | tf_op jit(solution)/shard_map/ppermute | solution.py:93
  167.5 13.2 %collective-permute-start.14 = (f32[2,32,1024]{2,1,0:T(8,128)S(1)}, f32[2,32,1024]{2,1,0:T(8,128)S(1)}, u32[]{:S(2)}, u32[]{:S(2)}) collective-permute-start(f32[2,32,1024]{2,1,0:T(8,128)S(1)} %dynamic-slice_bitcast_fusion.11), channel_id=1, source_target_pairs={{0,2},{1,3},{2,0},{3,1},{4,6},{5,7},{6,4},{7,5},{8,10},{9,11},{10,... | collective-permute-start | bytes 786440 | tf_op jit(solution)/shard_map/ppermute | solution.py:93
  168.1 13.2 %collective-permute-start.16 = (f32[2,32,1024]{2,1,0:T(8,128)S(1)}, f32[2,32,1024]{2,1,0:T(8,128)S(1)}, u32[]{:S(2)}, u32[]{:S(2)}) collective-permute-start(f32[2,32,1024]{2,1,0:T(8,128)S(1)} %dynamic-slice_bitcast_fusion.10), channel_id=1, source_target_pairs={{0,4},{1,5},{2,6},{3,7},{4,0},{5,1},{6,2},{7,3},{8,12},{9,13},{10,... | collective-permute-start | bytes 786440 | tf_op jit(solution)/shard_map/ppermute | solution.py:93
  179.9 6.7 %collective-permute-start.18 = (f32[2,2,32,1024]{3,2,1,0:T(8,128)S(1)}, f32[2,2,32,1024]{3,2,1,0:T(8,128)S(1)}, u32[]{:S(2)}, u32[]{:S(2)}) collective-permute-start(f32[2,2,32,1024]{3,2,1,0:T(8,128)S(1)} %dynamic-slice_bitcast_fusion.1), channel_id=1, source_target_pairs={{0,1},{1,0},{2,3},{3,2},{4,5},{5,4},{6,7},{7,6},{8,9},{9,8},{10,11... | collective-permute-start | bytes 1572872 | tf_op jit(solution)/shard_map/ppermute | solution.py:93
  180.1 8.2 %collective-permute-start.21 = (f32[2,2,32,1024]{3,2,1,0:T(8,128)S(1)}, f32[2,2,32,1024]{3,2,1,0:T(8,128)S(1)}, u32[]{:S(2)}, u32[]{:S(2)}) collective-permute-start(f32[2,2,32,1024]{3,2,1,0:T(8,128)S(1)} %dynamic-slice_bitcast_fusion), channel_id=1, source_target_pairs={{0,1},{1,0},{2,3},{3,2},{4,5},{5,4},{6,7},{7,6},{8,9},{9,8},{10,11... | collective-permute-start | bytes 1572872 | tf_op jit(solution)/shard_map/ppermute | solution.py:93
  180.7 5.5 %collective-permute-start.15 = (f32[32,1024]{1,0:T(8,128)S(1)}, f32[32,1024]{1,0:T(8,128)S(1)}, u32[]{:S(2)}, u32[]{:S(2)}) collective-permute-start(f32[32,1024]{1,0:T(8,128)S(1)} %dynamic-slice_bitcast_fusion.19), channel_id=1, source_target_pairs={{0,4},{1,5},{2,6},{3,7},{4,0},{5,1},{6,2},{7,3},{8,12},{9,13},{10,... | collective-permute-start | bytes 393224 | tf_op jit(solution)/shard_map/ppermute | solution.py:93
  181.3 5.2 %collective-permute-start.17 = (f32[32,1024]{1,0:T(8,128)S(1)}, f32[32,1024]{1,0:T(8,128)S(1)}, u32[]{:S(2)}, u32[]{:S(2)}) collective-permute-start(f32[32,1024]{1,0:T(8,128)S(1)} %dynamic-slice_bitcast_fusion.18), channel_id=1, source_target_pairs={{0,2},{1,3},{2,0},{3,1},{4,6},{5,7},{6,4},{7,5},{8,10},{9,11},{10,... | collective-permute-start | bytes 393224 | tf_op jit(solution)/shard_map/ppermute | solution.py:93
  186.7 7.2 %collective-permute-start.19 = (f32[2,32,1024]{2,1,0:T(8,128)S(1)}, f32[2,32,1024]{2,1,0:T(8,128)S(1)}, u32[]{:S(2)}, u32[]{:S(2)}) collective-permute-start(f32[2,32,1024]{2,1,0:T(8,128)S(1)} %dynamic-slice_bitcast_fusion.9), channel_id=1, source_target_pairs={{0,2},{1,3},{2,0},{3,1},{4,6},{5,7},{6,4},{7,5},{8,10},{9,11},{10,... | collective-permute-start | bytes 786440 | tf_op jit(solution)/shard_map/ppermute | solution.py:93
  188.4 7.5 %collective-permute-start.22 = (f32[2,32,1024]{2,1,0:T(8,128)S(1)}, f32[2,32,1024]{2,1,0:T(8,128)S(1)}, u32[]{:S(2)}, u32[]{:S(2)}) collective-permute-start(f32[2,32,1024]{2,1,0:T(8,128)S(1)} %dynamic-slice_bitcast_fusion.8), channel_id=1, source_target_pairs={{0,4},{1,5},{2,6},{3,7},{4,0},{5,1},{6,2},{7,3},{8,12},{9,13},{10,... | collective-permute-start | bytes 786440 | tf_op jit(solution)/shard_map/ppermute | solution.py:93
  193.9 5.0 %collective-permute-start.20 = (f32[32,1024]{1,0:T(8,128)S(1)}, f32[32,1024]{1,0:T(8,128)S(1)}, u32[]{:S(2)}, u32[]{:S(2)}) collective-permute-start(f32[32,1024]{1,0:T(8,128)S(1)} %dynamic-slice_bitcast_fusion.17), channel_id=1, source_target_pairs={{0,4},{1,5},{2,6},{3,7},{4,0},{5,1},{6,2},{7,3},{8,12},{9,13},{10,... | collective-permute-start | bytes 393224 | tf_op jit(solution)/shard_map/ppermute | solution.py:93
  195.9 5.0 %collective-permute-start.23 = (f32[32,1024]{1,0:T(8,128)S(1)}, f32[32,1024]{1,0:T(8,128)S(1)}, u32[]{:S(2)}, u32[]{:S(2)}) collective-permute-start(f32[32,1024]{1,0:T(8,128)S(1)} %dynamic-slice_bitcast_fusion.16), channel_id=1, source_target_pairs={{0,2},{1,3},{2,0},{3,1},{4,6},{5,7},{6,4},{7,5},{8,10},{9,11},{10,... | collective-permute-start | bytes 393224 | tf_op jit(solution)/shard_map/ppermute | solution.py:93
  (3 other events, 5.1 us)
Sparse Core Ops, SparseCore 0:
  16.3 54.8 all-gather.10
  72.7 25.6 all-gather.8
  100.1 40.9 all-gather.6

commit v12 on v11

--- a/solution.py
+++ b/solution.py
@@ -124,27 +124,29 @@
             (own_count * last.shape[0],) + last.shape[1:]
         )
     )
-    flows = []
-    for chunk in range(N_CHUNK):
-        for flow in flows:
+    flows = {}
+    sequence = list(range(N_CHUNK - 2)) + [N_CHUNK - 1, N_CHUNK - 2]
+    for chunk in sequence:
+        active = [flow for pair in flows.values() for flow in pair]
+        for flow in active:
             flow.advance(rep_index)
-        if flows:
-            amp3, held = lax.optimization_barrier((gathered[chunk], [f.x for f in flows]))
-            for flow, x in zip(flows, held):
+        if active:
+            amp3, held = lax.optimization_barrier((gathered[chunk], [f.x for f in active]))
+            for flow, x in zip(active, held):
                 flow.x = x
         else:
             amp3 = gathered[chunk]
         partial = _ladder_products(amp3, received, order, starts, ab_ids, cd_ids, AB_DEV)
         half = partial.shape[1] // 2
-        flows.extend(
+        flows[chunk] = [
             _Halving(partial[:, h * half:(h + 1) * half], orders[h], rep_count) for h in range(2)
-        )
-    while any(flow.todo for flow in flows):
-        for flow in flows:
+        ]
+    active = [flow for pair in flows.values() for flow in pair]
+    while any(flow.todo for flow in active):
+        for flow in active:
             flow.advance(rep_index)
     pieces = [
-        jnp.concatenate([flows[2 * c].result(), flows[2 * c + 1].result()], axis=1)
-        for c in range(N_CHUNK)
+        jnp.concatenate([flows[c][0].result(), flows[c][1].result()], axis=1) for c in range(N_CHUNK)
     ]
     return jnp.concatenate(pieces, axis=0)
 

time: 209 us -> 213 us (1.019)
  waiting for transfers between devices: 110 us -> 115 us
    all_gather x3, waiting for transfers between devices: 73.3 us -> 52.9 us  [on_device(): lax.all_gather(local4[:, c], 'own', axis=0, tiled=True)]
    all_to_all x1, waiting for transfers between devices: 0.01 us -> 18.2 us  [on_device(): lax.all_to_all(copies, 'own', split_axis=0, concat_axis=0, tiled=True)]
    ppermute x24, waiting for transfers between devices: 27.4 us -> 34.7 us  [advance(): self.x = keep + lax.ppermute(send, 'rep', perm=pairs)]
  transfers between devices with their start and end apart: 29 -> 29, of which waited for: 12 -> 13; matrix products, arithmetic and copies ran while one was open for 7% -> 7% of each run, Pallas kernels for 16% -> 16%
where the time goes in v12:
time: 213 us; the launch traced here: 212 us
  waiting for transfers between devices  115 us (54%)
  Pallas kernels  33.9 us (16%)
  starting transfers between devices  31.6 us (15%)
  between operations  13.6 us (6%)
  local copies, waits for them, and re-layouts  12.6 us (6%)
  other arithmetic  4.75 us (2%)
    all_gather x3, waiting for transfers between devices, on_device(): lax.all_gather(local4[:, c], 'own', axis=0, tiled=True)  52.9 us
    ppermute x24, waiting for transfers between devices, advance(): self.x = keep + lax.ppermute(send, 'rep', perm=pairs)  34.7 us
    pallas_call x4, Pallas kernels, _ladder_products(): pl.pallas_call(_ladder_kernel, grid_spec=grid_spec, out_shape=jax.ShapeDt...  33.9 us
    ppermute x24, starting transfers between devices, advance(): self.x = keep + lax.ppermute(send, 'rep', perm=pairs)  20 us
    all_to_all x1, waiting for transfers between devices, on_device(): lax.all_to_all(copies, 'own', split_axis=0, concat_axis=0, tiled=True)  18.2 us
    all_to_all x1, waiting for transfers between devices, on_device(): lax.all_to_all(integrals, ('own', 'rep'), split_axis=0, concat_axis=0, ti...  8.25 us
    all_to_all x1, starting transfers between devices, on_device(): lax.all_to_all(integrals, ('own', 'rep'), split_axis=0, concat_axis=0, ti...  7.3 us
    slice x4, local copies, waits for them, and re-layouts, on_device(): partial[:, h * half:(h + 1) * half]  6.73 us
  transfers between devices with their start and end apart: 29, of which 13 were waited for; matrix products, arithmetic and copies ran while one was open for 7% of the time, Pallas kernels for 16%

profile of v12, /device:TPU:0, one launch (start us, length us, event | category | flops | bytes accessed | tf_op | source)
XLA Modules:
  0.0 211.9 jit_solution(9779789604059155151)
XLA Ops:
  6.5 7.3 %all-to-all-start.1 = ((bf16[64,128,128]{2,1,0:T(8,128)(2,1)}), bf16[64,128,128]{2,1,0:T(8,128)(2,1)S(1)}, u32[]{:S(2)}, u32[]{:S(2)}) async-start(bf16[64,128,128]{2,1,0:T(8,128)(2,1)} %param.6), calls=%async_computation.1 | async-start | bytes 4194304 | tf_op jit(solution)/shard_map/all_to_all | solution.py:105
  18.3 52.8 %all-gather.11.cloned.1.call-done = bf16[8,1,32,2048]{3,2,1,0:T(8,128)(2,1)} async-done(((bf16[2,1,32,2048]{3,2,1,0:T(8,128)(2,1)}), bf16[8,1,32,2048]{3,2,1,0:T(8,128)(2,1)}) %all-gather.11.cloned.1.call-update) | async-done | bytes 1048592 | tf_op jit(solution)/shard_map/all_gather | solution.py:119
  71.2 8.2 %all-to-all-done.1.tiles_ref = bf16[64,128,128]{2,1,0:T(8,128)(2,1)S(1)} async-done(((bf16[64,128,128]{2,1,0:T(8,128)(2,1)}), bf16[64,128,128]{2,1,0:T(8,128)(2,1)S(1)}, u32[]{:S(2)}, u32[]{:S(2)}) %all-to-all-start.1) | async-done | bytes 2097184 | tf_op jit(solution)/shard_map/all_to_all | solution.py:105
  79.4 1.4 copy-done
  80.8 8.5 %shard_map.55 = f32[256,2048]{1,0:T(8,128)} custom-call(s32[64]{0:T(128)} %select_reduce_fusion.order_ref, s32[17]{0:T(128)} %convert_reduce_fusion.1.starts_ref, s32[64]{0:T(128)} %copy-done.5, s32[64]{0:T(128)} %reshape.75.cd_ref, bf16[8,32,2048]{2,1,0:T(8,128)(2,1)} %bitcast.132, bf16[64,128,128]{2,1,0:T(8,128)(2,1)} %copy-done), custom_call_target="tpu_custom_call" | custom-call | flops 2147483648 | bytes 5242880 | tf_op jit(solution)/shard_map/pallas_call | solution.py:66
  89.3 1.7 fusion.5
  93.5 4.3 %all-to-all-start = ((bf16[4,2,32,2048]{3,2,1,0:T(8,128)(2,1)}), bf16[4,2,32,2048]{3,2,1,0:T(8,128)(2,1)}, u32[]{:S(2)}, u32[]{:S(2)}) async-start(bf16[4,2,32,2048]{3,2,1,0:T(8,128)(2,1)} %broadcast_in_dim.15), calls=%async_computation | async-start | bytes 2097152 | tf_op jit(solution)/shard_map/all_to_all | solution.py:123
  99.8 1.5 collective-permute-start.3
  101.2 8.5 %shard_map.56 = f32[256,2048]{1,0:T(8,128)} custom-call(s32[64]{0:T(128)} %select_reduce_fusion.order_ref, s32[17]{0:T(128)} %convert_reduce_fusion.1.starts_ref, s32[64]{0:T(128)} %copy-done.5, s32[64]{0:T(128)} %reshape.75.cd_ref, bf16[8,32,2048]{2,1,0:T(8,128)(2,1)} %bitcast.131, bf16[64,128,128]{2,1,0:T(8,128)(2,1)} %copy-done), custom_call_target="tpu_custom_call" | custom-call | flops 2147483648 | bytes 5242880 | tf_op jit(solution)/shard_map/pallas_call | solution.py:66
  109.7 1.7 fusion.4
  111.6 1.4 collective-permute-start.2
  113.4 7.0 %collective-permute-done.2 = f32[2,32,1024]{2,1,0:T(8,128)S(1)} collective-permute-done((f32[2,32,1024]{2,1,0:T(8,128)S(1)}, f32[2,32,1024]{2,1,0:T(8,128)S(1)}, u32[]{:S(2)}, u32[]{:S(2)}) %collective-permute-start.2) | collective-permute-done | bytes 262176 | tf_op jit(solution)/shard_map/ppermute | solution.py:93
  120.6 18.2 %all-to-all-done = bf16[4,2,32,2048]{3,2,1,0:T(8,128)(2,1)} async-done(((bf16[4,2,32,2048]{3,2,1,0:T(8,128)(2,1)}), bf16[4,2,32,2048]{3,2,1,0:T(8,128)(2,1)}, u32[]{:S(2)}, u32[]{:S(2)}) %all-to-all-start) | async-done | bytes 1048608 | tf_op jit(solution)/shard_map/all_to_all | solution.py:123
  138.8 8.5 %shard_map.57 = f32[256,2048]{1,0:T(8,128)} custom-call(s32[64]{0:T(128)} %select_reduce_fusion.order_ref, s32[17]{0:T(128)} %convert_reduce_fusion.1.starts_ref, s32[64]{0:T(128)} %copy-done.5, s32[64]{0:T(128)} %reshape.75.cd_ref, bf16[8,32,2048]{2,1,0:T(8,128)(2,1)} %bitcast.3.amp_ref, bf16[64,128,128]{2,1,0:T(8,128)(2,1)} %copy-done), custom_call_target="tpu_custom_call" | custom-call | flops 2147483648 | bytes 5242880 | tf_op jit(solution)/shard_map/pallas_call | solution.py:66
  147.3 1.7 fusion.3
  149.7 1.3 collective-permute-start.9
  151.1 1.5 collective-permute-start.7
  153.3 4.3 %collective-permute-done.7 = f32[32,1024]{1,0:T(8,128)S(1)} collective-permute-done((f32[32,1024]{1,0:T(8,128)S(1)}, f32[32,1024]{1,0:T(8,128)S(1)}, u32[]{:S(2)}, u32[]{:S(2)}) %collective-permute-start.7) | collective-permute-done | bytes 131104 | tf_op jit(solution)/shard_map/ppermute | solution.py:93
  158.3 4.2 %collective-permute-done.6 = f32[32,1024]{1,0:T(8,128)S(1)} collective-permute-done((f32[32,1024]{1,0:T(8,128)S(1)}, f32[32,1024]{1,0:T(8,128)S(1)}, u32[]{:S(2)}, u32[]{:S(2)}) %collective-permute-start.6) | collective-permute-done | bytes 131104 | tf_op jit(solution)/shard_map/ppermute | solution.py:93
  163.7 1.5 collective-permute-start.13
  165.2 8.5 %shard_map.58 = f32[256,2048]{1,0:T(8,128)} custom-call(s32[64]{0:T(128)} %select_reduce_fusion.order_ref, s32[17]{0:T(128)} %convert_reduce_fusion.1.starts_ref, s32[64]{0:T(128)} %copy-done.5, s32[64]{0:T(128)} %reshape.75.cd_ref, bf16[8,32,2048]{2,1,0:T(8,128)(2,1)} %bitcast.130, bf16[64,128,128]{2,1,0:T(8,128)(2,1)} %copy-done), custom_call_target="tpu_custom_call" | custom-call | flops 2147483648 | bytes 5242880 | tf_op jit(solution)/shard_map/pallas_call | solution.py:66
  173.7 1.7 fusion.2
  176.7 1.3 collective-permute-start.22
  178.1 6.3 %collective-permute-done.20 = f32[2,32,1024]{2,1,0:T(8,128)S(1)} collective-permute-done((f32[2,32,1024]{2,1,0:T(8,128)S(1)}, f32[2,32,1024]{2,1,0:T(8,128)S(1)}, u32[]{:S(2)}, u32[]{:S(2)}) %collective-permute-start.20) | collective-permute-done | bytes 262176 | tf_op jit(solution)/shard_map/ppermute | solution.py:93
  184.5 1.3 collective-permute-start.21
  186.4 3.1 %collective-permute-done.21 = f32[32,1024]{1,0:T(8,128)S(1)} collective-permute-done((f32[32,1024]{1,0:T(8,128)S(1)}, f32[32,1024]{1,0:T(8,128)S(1)}, u32[]{:S(2)}, u32[]{:S(2)}) %collective-permute-start.21) | collective-permute-done | bytes 131104 | tf_op jit(solution)/shard_map/ppermute | solution.py:93
  189.5 1.3 collective-permute-done.23
  191.7 1.2 collective-permute-start.18
  192.9 4.5 %collective-permute-done.15 = f32[2,32,1024]{2,1,0:T(8,128)S(1)} collective-permute-done((f32[2,32,1024]{2,1,0:T(8,128)S(1)}, f32[2,32,1024]{2,1,0:T(8,128)S(1)}, u32[]{:S(2)}, u32[]{:S(2)}) %collective-permute-start.15) | collective-permute-done | bytes 262176 | tf_op jit(solution)/shard_map/ppermute | solution.py:93
  199.3 1.9 collective-permute-start.19
  201.1 1.4 collective-permute-done.16
  202.5 1.8 collective-permute-done.19
  (110 shorter events, 18.8 us)
Async XLA Ops:
  6.5 7.4 %copy-start.1 = (bf16[256,2048]{1,0:T(8,128)(2,1)S(1)}, bf16[256,2048]{1,0:T(8,128)(2,1)}, u32[]{:S(2)}) copy-start(bf16[256,2048]{1,0:T(8,128)(2,1)} %param.5) | copy-start | bytes 3145732
  6.5 72.9 %all-to-all-start.1 = ((bf16[64,128,128]{2,1,0:T(8,128)(2,1)}), bf16[64,128,128]{2,1,0:T(8,128)(2,1)S(1)}, u32[]{:S(2)}, u32[]{:S(2)}) async-start(bf16[64,128,128]{2,1,0:T(8,128)(2,1)} %param.6), calls=%async_computation.1 | async-start | bytes 4194304 | tf_op jit(solution)/shard_map/all_to_all | solution.py:105
  13.9 2.2 %copy-start.3 = (s32[1,32,2]{1,2,0:T(2,128)S(1)}, s32[1,32,2]{1,2,0:T(2,128)}, u32[]{:S(2)}) copy-start(s32[1,32,2]{1,2,0:T(2,128)} %param.8) | copy-start | bytes 772
  13.9 57.3 %all-gather.11.cloned.1.call-start = ((), (), s32[]{:S(2)}) async-start(), calls=%async_computation.4 | async-start | bytes 1310720 | tf_op jit(solution)/shard_map/all_gather | solution.py:119
  14.9 84.9 %all-gather.9.cloned.1.call-start = ((), (), s32[]{:S(2)}) async-start(), calls=%async_computation.3 | async-start | bytes 1310720 | tf_op jit(solution)/shard_map/all_gather | solution.py:119
  15.8 63.6 %copy-start.5 = (s32[64]{0:T(128)}, s32[64]{0:T(128)S(1)}, u32[]{:S(2)}) copy-start(s32[64]{0:T(128)S(1)} %reshape.74.ab_ref) | copy-start | bytes 772
  91.0 7.5 %collective-permute-start.1 = (f32[2,2,32,1024]{3,2,1,0:T(8,128)S(1)}, f32[2,2,32,1024]{3,2,1,0:T(8,128)}, u32[]{:S(2)}, u32[]{:S(2)}) collective-permute-start(f32[2,2,32,1024]{3,2,1,0:T(8,128)S(1)} %dynamic-slice_bitcast_fusion.6), channel_id=1, source_target_pairs={{0,1},{1,0},{2,3},{3,2},{4,5},{5,4},{6,7},{7,6},{8,9},{9,8},{10,11... | collective-permute-start | bytes 1572872 | tf_op jit(solution)/shard_map/ppermute | solution.py:93
  91.9 7.7 %collective-permute-start = (f32[2,2,32,1024]{3,2,1,0:T(8,128)}, f32[2,2,32,1024]{3,2,1,0:T(8,128)S(1)}, u32[]{:S(2)}, u32[]{:S(2)}) collective-permute-start(f32[2,2,32,1024]{3,2,1,0:T(8,128)} %dynamic-slice_bitcast_fusion.7), channel_id=1, source_target_pairs={{0,1},{1,0},{2,3},{3,2},{4,5},{5,4},{6,7},{7,6},{8,9},{9,8},{10,11... | collective-permute-start | bytes 1572872 | tf_op jit(solution)/shard_map/ppermute | solution.py:93
  93.5 45.3 %all-to-all-start = ((bf16[4,2,32,2048]{3,2,1,0:T(8,128)(2,1)}), bf16[4,2,32,2048]{3,2,1,0:T(8,128)(2,1)}, u32[]{:S(2)}, u32[]{:S(2)}) async-start(bf16[4,2,32,2048]{3,2,1,0:T(8,128)(2,1)} %broadcast_in_dim.15), calls=%async_computation | async-start | bytes 2097152 | tf_op jit(solution)/shard_map/all_to_all | solution.py:123
  97.8 65.1 %all-gather.7.cloned.1.call-start = ((), (), s32[]{:S(2)}) async-start(), calls=%async_computation.2 | async-start | bytes 1310720 | tf_op jit(solution)/shard_map/all_gather | solution.py:119
  99.8 13.5 %collective-permute-start.3 = (f32[2,32,1024]{2,1,0:T(8,128)S(1)}, f32[2,32,1024]{2,1,0:T(8,128)S(1)}, u32[]{:S(2)}, u32[]{:S(2)}) collective-permute-start(f32[2,32,1024]{2,1,0:T(8,128)S(1)} %dynamic-slice_bitcast_fusion.14), channel_id=1, source_target_pairs={{0,4},{1,5},{2,6},{3,7},{4,0},{5,1},{6,2},{7,3},{8,12},{9,13},{10,... | collective-permute-start | bytes 786440 | tf_op jit(solution)/shard_map/ppermute | solution.py:93
  111.5 8.9 %collective-permute-start.5 = (f32[2,2,32,1024]{3,2,1,0:T(8,128)S(1)}, f32[2,2,32,1024]{3,2,1,0:T(8,128)S(1)}, u32[]{:S(2)}, u32[]{:S(2)}) collective-permute-start(f32[2,2,32,1024]{3,2,1,0:T(8,128)S(1)} %dynamic-slice_bitcast_fusion.4), channel_id=1, source_target_pairs={{0,1},{1,0},{2,3},{3,2},{4,5},{5,4},{6,7},{7,6},{8,9},{9,8},{10,11... | collective-permute-start | bytes 1572872 | tf_op jit(solution)/shard_map/ppermute | solution.py:93
  111.6 8.8 %collective-permute-start.2 = (f32[2,32,1024]{2,1,0:T(8,128)S(1)}, f32[2,32,1024]{2,1,0:T(8,128)S(1)}, u32[]{:S(2)}, u32[]{:S(2)}) collective-permute-start(f32[2,32,1024]{2,1,0:T(8,128)S(1)} %dynamic-slice_bitcast_fusion.15), channel_id=1, source_target_pairs={{0,2},{1,3},{2,0},{3,1},{4,6},{5,7},{6,4},{7,5},{8,10},{9,11},{10,... | collective-permute-start | bytes 786440 | tf_op jit(solution)/shard_map/ppermute | solution.py:93
  113.1 7.4 %collective-permute-start.4 = (f32[2,2,32,1024]{3,2,1,0:T(8,128)S(1)}, f32[2,2,32,1024]{3,2,1,0:T(8,128)S(1)}, u32[]{:S(2)}, u32[]{:S(2)}) collective-permute-start(f32[2,2,32,1024]{3,2,1,0:T(8,128)S(1)} %dynamic-slice_bitcast_fusion.5), channel_id=1, source_target_pairs={{0,1},{1,0},{2,3},{3,2},{4,5},{5,4},{6,7},{7,6},{8,9},{9,8},{10,11... | collective-permute-start | bytes 1572872 | tf_op jit(solution)/shard_map/ppermute | solution.py:93
  149.0 13.6 %collective-permute-start.11 = (f32[2,2,32,1024]{3,2,1,0:T(8,128)S(1)}, f32[2,2,32,1024]{3,2,1,0:T(8,128)S(1)}, u32[]{:S(2)}, u32[]{:S(2)}) collective-permute-start(f32[2,2,32,1024]{3,2,1,0:T(8,128)S(1)} %dynamic-slice_bitcast_fusion.2), channel_id=1, source_target_pairs={{0,1},{1,0},{2,3},{3,2},{4,5},{5,4},{6,7},{7,6},{8,9},{9,8},{10,11... | collective-permute-start | bytes 1572872 | tf_op jit(solution)/shard_map/ppermute | solution.py:93
  149.1 13.6 %collective-permute-start.10 = (f32[2,2,32,1024]{3,2,1,0:T(8,128)S(1)}, f32[2,2,32,1024]{3,2,1,0:T(8,128)S(1)}, u32[]{:S(2)}, u32[]{:S(2)}) collective-permute-start(f32[2,2,32,1024]{3,2,1,0:T(8,128)S(1)} %dynamic-slice_bitcast_fusion.3), channel_id=1, source_target_pairs={{0,1},{1,0},{2,3},{3,2},{4,5},{5,4},{6,7},{7,6},{8,9},{9,8},{10,11... | collective-permute-start | bytes 1572872 | tf_op jit(solution)/shard_map/ppermute | solution.py:93
  149.7 12.8 %collective-permute-start.9 = (f32[2,32,1024]{2,1,0:T(8,128)S(1)}, f32[2,32,1024]{2,1,0:T(8,128)S(1)}, u32[]{:S(2)}, u32[]{:S(2)}) collective-permute-start(f32[2,32,1024]{2,1,0:T(8,128)S(1)} %dynamic-slice_bitcast_fusion.12), channel_id=1, source_target_pairs={{0,4},{1,5},{2,6},{3,7},{4,0},{5,1},{6,2},{7,3},{8,12},{9,13},{10,... | collective-permute-start | bytes 786440 | tf_op jit(solution)/shard_map/ppermute | solution.py:93
  151.1 6.5 %collective-permute-start.7 = (f32[32,1024]{1,0:T(8,128)S(1)}, f32[32,1024]{1,0:T(8,128)S(1)}, u32[]{:S(2)}, u32[]{:S(2)}) collective-permute-start(f32[32,1024]{1,0:T(8,128)S(1)} %dynamic-slice_bitcast_fusion.22), channel_id=1, source_target_pairs={{0,2},{1,3},{2,0},{3,1},{4,6},{5,7},{6,4},{7,5},{8,10},{9,11},{10,... | collective-permute-start | bytes 393224 | tf_op jit(solution)/shard_map/ppermute | solution.py:93
  152.6 10.0 %collective-permute-start.8 = (f32[2,32,1024]{2,1,0:T(8,128)S(1)}, f32[2,32,1024]{2,1,0:T(8,128)S(1)}, u32[]{:S(2)}, u32[]{:S(2)}) collective-permute-start(f32[2,32,1024]{2,1,0:T(8,128)S(1)} %dynamic-slice_bitcast_fusion.13), channel_id=1, source_target_pairs={{0,2},{1,3},{2,0},{3,1},{4,6},{5,7},{6,4},{7,5},{8,10},{9,11},{10,... | collective-permute-start | bytes 786440 | tf_op jit(solution)/shard_map/ppermute | solution.py:93
  157.5 5.0 %collective-permute-start.6 = (f32[32,1024]{1,0:T(8,128)S(1)}, f32[32,1024]{1,0:T(8,128)S(1)}, u32[]{:S(2)}, u32[]{:S(2)}) collective-permute-start(f32[32,1024]{1,0:T(8,128)S(1)} %dynamic-slice_bitcast_fusion.23), channel_id=1, source_target_pairs={{0,4},{1,5},{2,6},{3,7},{4,0},{5,1},{6,2},{7,3},{8,12},{9,13},{10,... | collective-permute-start | bytes 393224 | tf_op jit(solution)/shard_map/ppermute | solution.py:93
  162.9 13.8 %collective-permute-start.12 = (f32[32,1024]{1,0:T(8,128)S(1)}, f32[32,1024]{1,0:T(8,128)S(1)}, u32[]{:S(2)}, u32[]{:S(2)}) collective-permute-start(f32[32,1024]{1,0:T(8,128)S(1)} %dynamic-slice_bitcast_fusion.21), channel_id=1, source_target_pairs={{0,4},{1,5},{2,6},{3,7},{4,0},{5,1},{6,2},{7,3},{8,12},{9,13},{10,... | collective-permute-start | bytes 393224 | tf_op jit(solution)/shard_map/ppermute | solution.py:93
  163.7 14.3 %collective-permute-start.13 = (f32[32,1024]{1,0:T(8,128)S(1)}, f32[32,1024]{1,0:T(8,128)S(1)}, u32[]{:S(2)}, u32[]{:S(2)}) collective-permute-start(f32[32,1024]{1,0:T(8,128)S(1)} %dynamic-slice_bitcast_fusion.20), channel_id=1, source_target_pairs={{0,2},{1,3},{2,0},{3,1},{4,6},{5,7},{6,4},{7,5},{8,10},{9,11},{10,... | collective-permute-start | bytes 393224 | tf_op jit(solution)/shard_map/ppermute | solution.py:93
  175.4 15.4 %collective-permute-start.14 = (f32[2,2,32,1024]{3,2,1,0:T(8,128)S(1)}, f32[2,2,32,1024]{3,2,1,0:T(8,128)S(1)}, u32[]{:S(2)}, u32[]{:S(2)}) collective-permute-start(f32[2,2,32,1024]{3,2,1,0:T(8,128)S(1)} %dynamic-slice_bitcast_fusion.1), channel_id=1, source_target_pairs={{0,1},{1,0},{2,3},{3,2},{4,5},{5,4},{6,7},{7,6},{8,9},{9,8},{10,11... | collective-permute-start | bytes 1572872 | tf_op jit(solution)/shard_map/ppermute | solution.py:93
  175.5 16.1 %collective-permute-start.17 = (f32[2,2,32,1024]{3,2,1,0:T(8,128)S(1)}, f32[2,2,32,1024]{3,2,1,0:T(8,128)S(1)}, u32[]{:S(2)}, u32[]{:S(2)}) collective-permute-start(f32[2,2,32,1024]{3,2,1,0:T(8,128)S(1)} %dynamic-slice_bitcast_fusion), channel_id=1, source_target_pairs={{0,1},{1,0},{2,3},{3,2},{4,5},{5,4},{6,7},{7,6},{8,9},{9,8},{10,11... | collective-permute-start | bytes 1572872 | tf_op jit(solution)/shard_map/ppermute | solution.py:93
  176.1 8.3 %collective-permute-start.20 = (f32[2,32,1024]{2,1,0:T(8,128)S(1)}, f32[2,32,1024]{2,1,0:T(8,128)S(1)}, u32[]{:S(2)}, u32[]{:S(2)}) collective-permute-start(f32[2,32,1024]{2,1,0:T(8,128)S(1)} %dynamic-slice_bitcast_fusion.9), channel_id=1, source_target_pairs={{0,2},{1,3},{2,0},{3,1},{4,6},{5,7},{6,4},{7,5},{8,10},{9,11},{10,... | collective-permute-start | bytes 786440 | tf_op jit(solution)/shard_map/ppermute | solution.py:93
  176.7 9.0 %collective-permute-start.22 = (f32[2,32,1024]{2,1,0:T(8,128)S(1)}, f32[2,32,1024]{2,1,0:T(8,128)S(1)}, u32[]{:S(2)}, u32[]{:S(2)}) collective-permute-start(f32[2,32,1024]{2,1,0:T(8,128)S(1)} %dynamic-slice_bitcast_fusion.8), channel_id=1, source_target_pairs={{0,4},{1,5},{2,6},{3,7},{4,0},{5,1},{6,2},{7,3},{8,12},{9,13},{10,... | collective-permute-start | bytes 786440 | tf_op jit(solution)/shard_map/ppermute | solution.py:93
  184.5 5.0 %collective-permute-start.21 = (f32[32,1024]{1,0:T(8,128)S(1)}, f32[32,1024]{1,0:T(8,128)S(1)}, u32[]{:S(2)}, u32[]{:S(2)}) collective-permute-start(f32[32,1024]{1,0:T(8,128)S(1)} %dynamic-slice_bitcast_fusion.17), channel_id=1, source_target_pairs={{0,4},{1,5},{2,6},{3,7},{4,0},{5,1},{6,2},{7,3},{8,12},{9,13},{10,... | collective-permute-start | bytes 393224 | tf_op jit(solution)/shard_map/ppermute | solution.py:93
  185.8 5.0 %collective-permute-start.23 = (f32[32,1024]{1,0:T(8,128)S(1)}, f32[32,1024]{1,0:T(8,128)S(1)}, u32[]{:S(2)}, u32[]{:S(2)}) collective-permute-start(f32[32,1024]{1,0:T(8,128)S(1)} %dynamic-slice_bitcast_fusion.16), channel_id=1, source_target_pairs={{0,2},{1,3},{2,0},{3,1},{4,6},{5,7},{6,4},{7,5},{8,10},{9,11},{10,... | collective-permute-start | bytes 393224 | tf_op jit(solution)/shard_map/ppermute | solution.py:93
  191.0 6.4 %collective-permute-start.15 = (f32[2,32,1024]{2,1,0:T(8,128)S(1)}, f32[2,32,1024]{2,1,0:T(8,128)S(1)}, u32[]{:S(2)}, u32[]{:S(2)}) collective-permute-start(f32[2,32,1024]{2,1,0:T(8,128)S(1)} %dynamic-slice_bitcast_fusion.11), channel_id=1, source_target_pairs={{0,2},{1,3},{2,0},{3,1},{4,6},{5,7},{6,4},{7,5},{8,10},{9,11},{10,... | collective-permute-start | bytes 786440 | tf_op jit(solution)/shard_map/ppermute | solution.py:93
  191.7 7.5 %collective-permute-start.18 = (f32[2,32,1024]{2,1,0:T(8,128)S(1)}, f32[2,32,1024]{2,1,0:T(8,128)S(1)}, u32[]{:S(2)}, u32[]{:S(2)}) collective-permute-start(f32[2,32,1024]{2,1,0:T(8,128)S(1)} %dynamic-slice_bitcast_fusion.10), channel_id=1, source_target_pairs={{0,4},{1,5},{2,6},{3,7},{4,0},{5,1},{6,2},{7,3},{8,12},{9,13},{10,... | collective-permute-start | bytes 786440 | tf_op jit(solution)/shard_map/ppermute | solution.py:93
  197.5 5.0 %collective-permute-start.16 = (f32[32,1024]{1,0:T(8,128)S(1)}, f32[32,1024]{1,0:T(8,128)S(1)}, u32[]{:S(2)}, u32[]{:S(2)}) collective-permute-start(f32[32,1024]{1,0:T(8,128)S(1)} %dynamic-slice_bitcast_fusion.19), channel_id=1, source_target_pairs={{0,4},{1,5},{2,6},{3,7},{4,0},{5,1},{6,2},{7,3},{8,12},{9,13},{10,... | collective-permute-start | bytes 393224 | tf_op jit(solution)/shard_map/ppermute | solution.py:93
  199.3 5.0 %collective-permute-start.19 = (f32[32,1024]{1,0:T(8,128)S(1)}, f32[32,1024]{1,0:T(8,128)S(1)}, u32[]{:S(2)}, u32[]{:S(2)}) collective-permute-start(f32[32,1024]{1,0:T(8,128)S(1)} %dynamic-slice_bitcast_fusion.18), channel_id=1, source_target_pairs={{0,2},{1,3},{2,0},{3,1},{4,6},{5,7},{6,4},{7,5},{8,10},{9,11},{10,... | collective-permute-start | bytes 393224 | tf_op jit(solution)/shard_map/ppermute | solution.py:93
  (3 other events, 5.1 us)
Sparse Core Ops, SparseCore 0:
  16.3 54.8 all-gather.10
  72.7 25.6 all-gather.8
  100.2 40.9 all-gather.6

commit v13 on v8

--- a/solution.py
+++ b/solution.py
@@ -8,7 +8,7 @@
 from jax.sharding import PartitionSpec as P
 
 AB_DEV = 16
-CHUNKS = (3, 1)
+CHUNKS = (1, 1, 1, 1)
 
 
 def _slot_order(ab_ids, live_mask, ab_count):

time: 222 us -> 204 us (0.919)
  waiting for transfers between devices: 143 us -> 115 us
  matrix products: 17 us -> 27.2 us
  starting transfers between devices: 18.4 us -> 27.6 us
  local copies, waits for them, and re-layouts: 13.1 us -> 5.98 us
    all_to_all x1, waiting for transfers between devices: 91.4 us -> 60.3 us  [on_device(): lax.all_to_all(integrals, ('own', 'rep'), split_axis=0, concat_axis=0, ti...]
    ppermute x12 -> x24, waiting for transfers between devices: 26.8 us -> 37.7 us  [advance(): self.x = keep + lax.ppermute(send, 'rep', perm=pairs)]
    dot_general x4 -> x8, matrix products: 17 us -> 27.2 us  [on_device(): jnp.dot(lhs, weight[:, h * half:(h + 1) * half], preferred_element_type=j...]
    all_gather x2 -> x4, waiting for transfers between devices: 24.6 us -> 15.1 us  [on_device(): lax.all_gather(local4[:, bounds[c]:bounds[c + 1]], 'own', axis=0, tiled=T...]
    ppermute x12 -> x24, starting transfers between devices: 11.1 us -> 20.1 us  [advance(): self.x = keep + lax.ppermute(send, 'rep', perm=pairs)]
    unnamed x22, local copies, waits for them, and re-layouts: 6.56 us -> 2.72 us
    slice x2 -> x1, local copies, waits for them, and re-layouts: 3.8 us -> 0.97 us  [on_device(): local4[:, bounds[c]:bounds[c + 1]]]
  transfers between devices with their start and end apart: 15 -> 29, of which waited for: 6 -> 17; matrix products, arithmetic and copies ran while one was open for 8% -> 13% of each run, Pallas kernels for 5% -> 5%
where the time goes in v13:
time: 204 us
  waiting for transfers between devices  115 us (56%)
  starting transfers between devices  27.6 us (14%)
  matrix products  27.2 us (13%)
  between operations  13.6 us (7%)
  Pallas kernels  10.1 us (5%)
  local copies, waits for them, and re-layouts  5.98 us (3%)
  other arithmetic  4.72 us (2%)
    all_to_all x1, waiting for transfers between devices, on_device(): lax.all_to_all(integrals, ('own', 'rep'), split_axis=0, concat_axis=0, ti...  60.3 us
    ppermute x24, waiting for transfers between devices, advance(): self.x = keep + lax.ppermute(send, 'rep', perm=pairs)  37.7 us
    dot_general x8, matrix products, on_device(): jnp.dot(lhs, weight[:, h * half:(h + 1) * half], preferred_element_type=j...  27.2 us
    ppermute x24, starting transfers between devices, advance(): self.x = keep + lax.ppermute(send, 'rep', perm=pairs)  20.1 us
    all_gather x4, waiting for transfers between devices, on_device(): lax.all_gather(local4[:, bounds[c]:bounds[c + 1]], 'own', axis=0, tiled=T...  15.1 us
    pallas_call x1, Pallas kernels, _dense_weight(): pl.pallas_call(_weight_kernel, grid_spec=grid_spec, out_shape=jax.ShapeDt...  10.1 us
    all_to_all x1, starting transfers between devices, on_device(): lax.all_to_all(integrals, ('own', 'rep'), split_axis=0, concat_axis=0, ti...  7.3 us
  transfers between devices with their start and end apart: 29, of which 17 were waited for; matrix products, arithmetic and copies ran while one was open for 13% of the time, Pallas kernels for 5%

profile of v13, /device:TPU:0, one launch (start us, length us, event | category | flops | bytes accessed | tf_op | source)
XLA Modules:
  0.0 203.8 jit_solution(11287213748621158747)
XLA Ops:
  6.5 7.3 %all-to-all-start = ((bf16[64,128,128]{2,1,0:T(8,128)(2,1)}), bf16[64,128,128]{2,1,0:T(8,128)(2,1)S(1)}, u32[]{:S(2)}, u32[]{:S(2)}) async-start(bf16[64,128,128]{2,1,0:T(8,128)(2,1)} %param.6), calls=%async_computation | async-start | bytes 4194304 | tf_op jit(solution)/shard_map/all_to_all | solution.py:90
  19.1 60.3 %all-to-all-done.tiles_ref = bf16[64,128,128]{2,1,0:T(8,128)(2,1)S(1)} async-done(((bf16[64,128,128]{2,1,0:T(8,128)(2,1)}), bf16[64,128,128]{2,1,0:T(8,128)(2,1)S(1)}, u32[]{:S(2)}, u32[]{:S(2)}) %all-to-all-start) | async-done | bytes 2097184 | tf_op jit(solution)/shard_map/all_to_all | solution.py:90
  80.8 10.1 %shard_map.55 = bf16[2048,2048]{1,0:T(8,128)(2,1)} custom-call(s32[64]{0:T(128)} %select_reduce_fusion.order_ref, s32[17]{0:T(128)} %convert_reduce_fusion.1.starts_ref, s32[64]{0:T(128)} %reshape.103.cd_ref, bf16[64,128,128]{2,1,0:T(8,128)(2,1)} %copy-done.1), custom_call_target="tpu_custom_call" | custom-call | bytes 10485760 | tf_op jit(solution)/shard_map/pallas_call | solution.py:49
  90.9 3.9 %fusion.15 = f32[1024,256]{0,1:T(8,128)S(1)} fusion(bf16[256,2048]{1,0:T(8,128)(2,1)} %bitcast.175, bf16[2048,2048]{1,0:T(8,128)(2,1)} %shard_map.55), kind=kOutput, calls=%fused_computation.15 | convolution fusion | flops 1073741824 | bytes 6291456 | tf_op jit(solution)/shard_map/dot_general | solution.py:125
  98.4 2.1 %collective-permute-done = f32[2,2,32,1024]{3,2,1,0:T(8,128)} collective-permute-done((f32[2,2,32,1024]{3,2,1,0:T(8,128)}, f32[2,2,32,1024]{3,2,1,0:T(8,128)}, u32[]{:S(2)}, u32[]{:S(2)}) %collective-permute-start) | collective-permute-done | bytes 524320 | tf_op jit(solution)/shard_map/ppermute | solution.py:78
  101.6 3.8 %fusion.4 = f32[2,2,2,32,1024]{4,3,2,1,0:T(8,128)S(1)} fusion(bf16[2,2,2,32,2048]{4,3,2,1,0:T(8,128)(2,1)} %bitcast.173, bf16[2048,2048]{1,0:T(8,128)(2,1)} %shard_map.55), kind=kOutput, calls=%fused_computation.4 | convolution fusion | flops 1073741824 | bytes 6291456 | tf_op jit(solution)/shard_map/dot_general | solution.py:125
  105.5 3.6 %fusion.10 = f32[2,2,2,32,1024]{4,3,2,1,0:T(8,128)S(1)} fusion(bf16[2,2,2,32,2048]{4,3,2,1,0:T(8,128)(2,1)S(1)} %bitcast.174, bf16[2048,2048]{1,0:T(8,128)(2,1)} %shard_map.55), kind=kOutput, calls=%fused_computation.10 | convolution fusion | flops 1073741824 | bytes 6291456 | tf_op jit(solution)/shard_map/dot_general | solution.py:125
  109.1 1.6 collective-permute-start.3
  110.9 1.5 collective-permute-start.2
  112.7 4.8 %collective-permute-done.3 = f32[2,32,1024]{2,1,0:T(8,128)S(1)} collective-permute-done((f32[2,32,1024]{2,1,0:T(8,128)S(1)}, f32[2,32,1024]{2,1,0:T(8,128)S(1)}, u32[]{:S(2)}, u32[]{:S(2)}) %collective-permute-start.3) | collective-permute-done | bytes 262176 | tf_op jit(solution)/shard_map/ppermute | solution.py:78
  117.6 2.1 %collective-permute-done.2 = f32[2,32,1024]{2,1,0:T(8,128)S(1)} collective-permute-done((f32[2,32,1024]{2,1,0:T(8,128)S(1)}, f32[2,32,1024]{2,1,0:T(8,128)S(1)}, u32[]{:S(2)}, u32[]{:S(2)}) %collective-permute-start.2) | collective-permute-done | bytes 262176 | tf_op jit(solution)/shard_map/ppermute | solution.py:78
  119.9 7.6 %all-gather.7.cloned.1.call-done = bf16[8,1,32,2048]{3,2,1,0:T(8,128)(2,1)} async-done(((bf16[2,1,32,2048]{3,2,1,0:T(8,128)(2,1)}), bf16[8,1,32,2048]{3,2,1,0:T(8,128)(2,1)}) %all-gather.7.cloned.1.call-update) | async-done | bytes 1048592 | tf_op jit(solution)/shard_map/all_gather | solution.py:109
  127.4 3.8 %fusion.2 = f32[2,2,2,32,1024]{4,3,2,1,0:T(8,128)S(1)} fusion(bf16[2,2,2,32,2048]{4,3,2,1,0:T(8,128)(2,1)} %bitcast.171, bf16[2048,2048]{1,0:T(8,128)(2,1)} %shard_map.55), kind=kOutput, calls=%fused_computation.2 | convolution fusion | flops 1073741824 | bytes 6291456 | tf_op jit(solution)/shard_map/dot_general | solution.py:125
  131.3 3.5 %fusion.8 = f32[2,2,2,32,1024]{4,3,2,1,0:T(8,128)S(1)} fusion(bf16[2,2,2,32,2048]{4,3,2,1,0:T(8,128)(2,1)S(1)} %bitcast.172, bf16[2048,2048]{1,0:T(8,128)(2,1)} %shard_map.55), kind=kOutput, calls=%fused_computation.8 | convolution fusion | flops 1073741824 | bytes 6291456 | tf_op jit(solution)/shard_map/dot_general | solution.py:125
  135.5 1.5 collective-permute-start.9
  137.1 1.5 collective-permute-start.7
  139.3 4.3 %collective-permute-done.7 = f32[32,1024]{1,0:T(8,128)S(1)} collective-permute-done((f32[32,1024]{1,0:T(8,128)S(1)}, f32[32,1024]{1,0:T(8,128)S(1)}, u32[]{:S(2)}, u32[]{:S(2)}) %collective-permute-start.7) | collective-permute-done | bytes 131104 | tf_op jit(solution)/shard_map/ppermute | solution.py:78
  144.1 4.4 %collective-permute-done.6 = f32[32,1024]{1,0:T(8,128)S(1)} collective-permute-done((f32[32,1024]{1,0:T(8,128)S(1)}, f32[32,1024]{1,0:T(8,128)S(1)}, u32[]{:S(2)}, u32[]{:S(2)}) %collective-permute-start.6) | collective-permute-done | bytes 131104 | tf_op jit(solution)/shard_map/ppermute | solution.py:78
  148.8 7.6 %all-gather.5.cloned.1.call-done = bf16[8,1,32,2048]{3,2,1,0:T(8,128)(2,1)} async-done(((bf16[2,1,32,2048]{3,2,1,0:T(8,128)(2,1)}), bf16[8,1,32,2048]{3,2,1,0:T(8,128)(2,1)}) %all-gather.5.cloned.1.call-update) | async-done | bytes 1048592 | tf_op jit(solution)/shard_map/all_gather | solution.py:109
  156.4 3.8 %fusion.6 = f32[2,2,2,32,1024]{4,3,2,1,0:T(8,128)S(1)} fusion(bf16[2,2,2,32,2048]{4,3,2,1,0:T(8,128)(2,1)} %bitcast.169, bf16[2048,2048]{1,0:T(8,128)(2,1)} %shard_map.55), kind=kOutput, calls=%fused_computation.6 | convolution fusion | flops 1073741824 | bytes 6291456 | tf_op jit(solution)/shard_map/dot_general | solution.py:125
  160.2 3.5 %fusion = f32[2,2,2,32,1024]{4,3,2,1,0:T(8,128)S(1)} fusion(bf16[2,2,2,32,2048]{4,3,2,1,0:T(8,128)(2,1)S(1)} %bitcast.170, bf16[2048,2048]{1,0:T(8,128)(2,1)} %shard_map.55), kind=kOutput, calls=%fused_computation | convolution fusion | flops 1073741824 | bytes 6291456 | tf_op jit(solution)/shard_map/dot_general | solution.py:125
  163.7 1.5 collective-permute-start.12
  165.3 1.5 collective-permute-start.13
  168.9 2.9 %collective-permute-done.13 = f32[32,1024]{1,0:T(8,128)S(1)} collective-permute-done((f32[32,1024]{1,0:T(8,128)S(1)}, f32[32,1024]{1,0:T(8,128)S(1)}, u32[]{:S(2)}, u32[]{:S(2)}) %collective-permute-start.13) | collective-permute-done | bytes 131104 | tf_op jit(solution)/shard_map/ppermute | solution.py:78
  171.8 3.9 %collective-permute-done.14 = f32[2,32,1024]{2,1,0:T(8,128)S(1)} collective-permute-done((f32[2,32,1024]{2,1,0:T(8,128)S(1)}, f32[2,32,1024]{2,1,0:T(8,128)S(1)}, u32[]{:S(2)}, u32[]{:S(2)}) %collective-permute-start.14) | collective-permute-done | bytes 262176 | tf_op jit(solution)/shard_map/ppermute | solution.py:78
  176.5 1.5 collective-permute-start.17
  178.0 2.8 %collective-permute-done.15 = f32[32,1024]{1,0:T(8,128)S(1)} collective-permute-done((f32[32,1024]{1,0:T(8,128)S(1)}, f32[32,1024]{1,0:T(8,128)S(1)}, u32[]{:S(2)}, u32[]{:S(2)}) %collective-permute-start.15) | collective-permute-done | bytes 131104 | tf_op jit(solution)/shard_map/ppermute | solution.py:78
  181.8 1.5 collective-permute-start.19
  183.4 1.4 collective-permute-start.22
  184.8 3.4 %collective-permute-done.19 = f32[2,32,1024]{2,1,0:T(8,128)S(1)} collective-permute-done((f32[2,32,1024]{2,1,0:T(8,128)S(1)}, f32[2,32,1024]{2,1,0:T(8,128)S(1)}, u32[]{:S(2)}, u32[]{:S(2)}) %collective-permute-start.19) | collective-permute-done | bytes 262176 | tf_op jit(solution)/shard_map/ppermute | solution.py:78
  188.3 1.4 collective-permute-start.20
  193.4 2.8 %collective-permute-done.23 = f32[32,1024]{1,0:T(8,128)S(1)} collective-permute-done((f32[32,1024]{1,0:T(8,128)S(1)}, f32[32,1024]{1,0:T(8,128)S(1)}, u32[]{:S(2)}, u32[]{:S(2)}) %collective-permute-start.23) | collective-permute-done | bytes 131104 | tf_op jit(solution)/shard_map/ppermute | solution.py:78
  (119 shorter events, 22.7 us)
Async XLA Ops:
  6.5 9.9 %copy-start.3 = (s32[1,32,2]{1,2,0:T(2,128)S(1)}, s32[1,32,2]{1,2,0:T(2,128)}, u32[]{:S(2)}) copy-start(s32[1,32,2]{1,2,0:T(2,128)} %param.7) | copy-start | bytes 772
  6.5 10.1 %copy-start.5 = (s32[1,32]{1,0:T(1,128)S(1)}, s32[1,32]{1,0:T(1,128)}, u32[]{:S(2)}) copy-start(s32[1,32]{1,0:T(1,128)} %param.9) | copy-start | bytes 388
  6.5 11.1 %copy-start.4 = (s32[1,32,2]{1,2,0:T(2,128)S(1)}, s32[1,32,2]{1,2,0:T(2,128)}, u32[]{:S(2)}) copy-start(s32[1,32,2]{1,2,0:T(2,128)} %param.8) | copy-start | bytes 772
  6.5 72.9 %all-to-all-start = ((bf16[64,128,128]{2,1,0:T(8,128)(2,1)}), bf16[64,128,128]{2,1,0:T(8,128)(2,1)S(1)}, u32[]{:S(2)}, u32[]{:S(2)}) async-start(bf16[64,128,128]{2,1,0:T(8,128)(2,1)} %param.6), calls=%async_computation | async-start | bytes 4194304 | tf_op jit(solution)/shard_map/all_to_all | solution.py:90
  13.8 77.1 %all-gather.11.cloned.1.call-start = ((), (), s32[]{:S(2)}) async-start(), calls=%async_computation.4 | async-start | bytes 1310720 | tf_op jit(solution)/shard_map/all_gather | solution.py:109
  14.9 86.7 %all-gather.9.cloned.1.call-start = ((), (), s32[]{:S(2)}) async-start(), calls=%async_computation.3 | async-start | bytes 1310720 | tf_op jit(solution)/shard_map/all_gather | solution.py:109
  15.7 111.8 %all-gather.7.cloned.1.call-start = ((), (), s32[]{:S(2)}) async-start(), calls=%async_computation.2 | async-start | bytes 1310720 | tf_op jit(solution)/shard_map/all_gather | solution.py:109
  16.4 140.0 %all-gather.5.cloned.1.call-start = ((), (), s32[]{:S(2)}) async-start(), calls=%async_computation.1 | async-start | bytes 1310720 | tf_op jit(solution)/shard_map/all_gather | solution.py:109
  94.9 3.4 %collective-permute-start.1 = (f32[2,2,32,1024]{3,2,1,0:T(8,128)S(1)}, f32[2,2,32,1024]{3,2,1,0:T(8,128)S(1)}, u32[]{:S(2)}, u32[]{:S(2)}) collective-permute-start(f32[2,2,32,1024]{3,2,1,0:T(8,128)S(1)} %dynamic-slice_bitcast_fusion.6), channel_id=1, source_target_pairs={{0,1},{1,0},{2,3},{3,2},{4,5},{5,4},{6,7},{7,6},{8,9},{9,8},{10,11... | collective-permute-start | bytes 1572872 | tf_op jit(solution)/shard_map/ppermute | solution.py:78
  98.2 2.3 %collective-permute-start = (f32[2,2,32,1024]{3,2,1,0:T(8,128)}, f32[2,2,32,1024]{3,2,1,0:T(8,128)}, u32[]{:S(2)}, u32[]{:S(2)}) collective-permute-start(f32[2,2,32,1024]{3,2,1,0:T(8,128)} %dynamic-slice_bitcast_fusion.7), channel_id=1, source_target_pairs={{0,1},{1,0},{2,3},{3,2},{4,5},{5,4},{6,7},{7,6},{8,9},{9,8},{10,11... | collective-permute-start | bytes 1572872 | tf_op jit(solution)/shard_map/ppermute | solution.py:78
  109.1 8.4 %collective-permute-start.3 = (f32[2,32,1024]{2,1,0:T(8,128)S(1)}, f32[2,32,1024]{2,1,0:T(8,128)S(1)}, u32[]{:S(2)}, u32[]{:S(2)}) collective-permute-start(f32[2,32,1024]{2,1,0:T(8,128)S(1)} %dynamic-slice_bitcast_fusion.14), channel_id=1, source_target_pairs={{0,4},{1,5},{2,6},{3,7},{4,0},{5,1},{6,2},{7,3},{8,12},{9,13},{10,... | collective-permute-start | bytes 786440 | tf_op jit(solution)/shard_map/ppermute | solution.py:78
  110.8 8.9 %collective-permute-start.5 = (f32[2,2,32,1024]{3,2,1,0:T(8,128)S(1)}, f32[2,2,32,1024]{3,2,1,0:T(8,128)S(1)}, u32[]{:S(2)}, u32[]{:S(2)}) collective-permute-start(f32[2,2,32,1024]{3,2,1,0:T(8,128)S(1)} %dynamic-slice_bitcast_fusion.4), channel_id=1, source_target_pairs={{0,1},{1,0},{2,3},{3,2},{4,5},{5,4},{6,7},{7,6},{8,9},{9,8},{10,11... | collective-permute-start | bytes 1572872 | tf_op jit(solution)/shard_map/ppermute | solution.py:78
  110.9 8.8 %collective-permute-start.2 = (f32[2,32,1024]{2,1,0:T(8,128)S(1)}, f32[2,32,1024]{2,1,0:T(8,128)S(1)}, u32[]{:S(2)}, u32[]{:S(2)}) collective-permute-start(f32[2,32,1024]{2,1,0:T(8,128)S(1)} %dynamic-slice_bitcast_fusion.15), channel_id=1, source_target_pairs={{0,2},{1,3},{2,0},{3,1},{4,6},{5,7},{6,4},{7,5},{8,10},{9,11},{10,... | collective-permute-start | bytes 786440 | tf_op jit(solution)/shard_map/ppermute | solution.py:78
  112.4 7.3 %collective-permute-start.4 = (f32[2,2,32,1024]{3,2,1,0:T(8,128)S(1)}, f32[2,2,32,1024]{3,2,1,0:T(8,128)S(1)}, u32[]{:S(2)}, u32[]{:S(2)}) collective-permute-start(f32[2,2,32,1024]{3,2,1,0:T(8,128)S(1)} %dynamic-slice_bitcast_fusion.5), channel_id=1, source_target_pairs={{0,1},{1,0},{2,3},{3,2},{4,5},{5,4},{6,7},{7,6},{8,9},{9,8},{10,11... | collective-permute-start | bytes 1572872 | tf_op jit(solution)/shard_map/ppermute | solution.py:78
  134.8 13.8 %collective-permute-start.11 = (f32[2,2,32,1024]{3,2,1,0:T(8,128)S(1)}, f32[2,2,32,1024]{3,2,1,0:T(8,128)S(1)}, u32[]{:S(2)}, u32[]{:S(2)}) collective-permute-start(f32[2,2,32,1024]{3,2,1,0:T(8,128)S(1)} %dynamic-slice_bitcast_fusion.2), channel_id=1, source_target_pairs={{0,1},{1,0},{2,3},{3,2},{4,5},{5,4},{6,7},{7,6},{8,9},{9,8},{10,11... | collective-permute-start | bytes 1572872 | tf_op jit(solution)/shard_map/ppermute | solution.py:78
  134.9 13.8 %collective-permute-start.10 = (f32[2,2,32,1024]{3,2,1,0:T(8,128)S(1)}, f32[2,2,32,1024]{3,2,1,0:T(8,128)S(1)}, u32[]{:S(2)}, u32[]{:S(2)}) collective-permute-start(f32[2,2,32,1024]{3,2,1,0:T(8,128)S(1)} %dynamic-slice_bitcast_fusion.3), channel_id=1, source_target_pairs={{0,1},{1,0},{2,3},{3,2},{4,5},{5,4},{6,7},{7,6},{8,9},{9,8},{10,11... | collective-permute-start | bytes 1572872 | tf_op jit(solution)/shard_map/ppermute | solution.py:78
  135.5 13.0 %collective-permute-start.9 = (f32[2,32,1024]{2,1,0:T(8,128)S(1)}, f32[2,32,1024]{2,1,0:T(8,128)S(1)}, u32[]{:S(2)}, u32[]{:S(2)}) collective-permute-start(f32[2,32,1024]{2,1,0:T(8,128)S(1)} %dynamic-slice_bitcast_fusion.12), channel_id=1, source_target_pairs={{0,4},{1,5},{2,6},{3,7},{4,0},{5,1},{6,2},{7,3},{8,12},{9,13},{10,... | collective-permute-start | bytes 786440 | tf_op jit(solution)/shard_map/ppermute | solution.py:78
  137.1 6.5 %collective-permute-start.7 = (f32[32,1024]{1,0:T(8,128)S(1)}, f32[32,1024]{1,0:T(8,128)S(1)}, u32[]{:S(2)}, u32[]{:S(2)}) collective-permute-start(f32[32,1024]{1,0:T(8,128)S(1)} %dynamic-slice_bitcast_fusion.22), channel_id=1, source_target_pairs={{0,2},{1,3},{2,0},{3,1},{4,6},{5,7},{6,4},{7,5},{8,10},{9,11},{10,... | collective-permute-start | bytes 393224 | tf_op jit(solution)/shard_map/ppermute | solution.py:78
  138.6 10.0 %collective-permute-start.8 = (f32[2,32,1024]{2,1,0:T(8,128)S(1)}, f32[2,32,1024]{2,1,0:T(8,128)S(1)}, u32[]{:S(2)}, u32[]{:S(2)}) collective-permute-start(f32[2,32,1024]{2,1,0:T(8,128)S(1)} %dynamic-slice_bitcast_fusion.13), channel_id=1, source_target_pairs={{0,2},{1,3},{2,0},{3,1},{4,6},{5,7},{6,4},{7,5},{8,10},{9,11},{10,... | collective-permute-start | bytes 786440 | tf_op jit(solution)/shard_map/ppermute | solution.py:78
  143.5 5.0 %collective-permute-start.6 = (f32[32,1024]{1,0:T(8,128)S(1)}, f32[32,1024]{1,0:T(8,128)S(1)}, u32[]{:S(2)}, u32[]{:S(2)}) collective-permute-start(f32[32,1024]{1,0:T(8,128)S(1)} %dynamic-slice_bitcast_fusion.23), channel_id=1, source_target_pairs={{0,4},{1,5},{2,6},{3,7},{4,0},{5,1},{6,2},{7,3},{8,12},{9,13},{10,... | collective-permute-start | bytes 393224 | tf_op jit(solution)/shard_map/ppermute | solution.py:78
  163.7 5.1 %collective-permute-start.12 = (f32[32,1024]{1,0:T(8,128)S(1)}, f32[32,1024]{1,0:T(8,128)S(1)}, u32[]{:S(2)}, u32[]{:S(2)}) collective-permute-start(f32[32,1024]{1,0:T(8,128)S(1)} %dynamic-slice_bitcast_fusion.21), channel_id=1, source_target_pairs={{0,4},{1,5},{2,6},{3,7},{4,0},{5,1},{6,2},{7,3},{8,12},{9,13},{10,... | collective-permute-start | bytes 393224 | tf_op jit(solution)/shard_map/ppermute | solution.py:78
  165.3 6.5 %collective-permute-start.13 = (f32[32,1024]{1,0:T(8,128)S(1)}, f32[32,1024]{1,0:T(8,128)S(1)}, u32[]{:S(2)}, u32[]{:S(2)}) collective-permute-start(f32[32,1024]{1,0:T(8,128)S(1)} %dynamic-slice_bitcast_fusion.20), channel_id=1, source_target_pairs={{0,2},{1,3},{2,0},{3,1},{4,6},{5,7},{6,4},{7,5},{8,10},{9,11},{10,... | collective-permute-start | bytes 393224 | tf_op jit(solution)/shard_map/ppermute | solution.py:78
  166.8 8.9 %collective-permute-start.14 = (f32[2,32,1024]{2,1,0:T(8,128)S(1)}, f32[2,32,1024]{2,1,0:T(8,128)S(1)}, u32[]{:S(2)}, u32[]{:S(2)}) collective-permute-start(f32[2,32,1024]{2,1,0:T(8,128)S(1)} %dynamic-slice_bitcast_fusion.11), channel_id=1, source_target_pairs={{0,2},{1,3},{2,0},{3,1},{4,6},{5,7},{6,4},{7,5},{8,10},{9,11},{10,... | collective-permute-start | bytes 786440 | tf_op jit(solution)/shard_map/ppermute | solution.py:78
  167.5 8.9 %collective-permute-start.16 = (f32[2,32,1024]{2,1,0:T(8,128)S(1)}, f32[2,32,1024]{2,1,0:T(8,128)S(1)}, u32[]{:S(2)}, u32[]{:S(2)}) collective-permute-start(f32[2,32,1024]{2,1,0:T(8,128)S(1)} %dynamic-slice_bitcast_fusion.10), channel_id=1, source_target_pairs={{0,4},{1,5},{2,6},{3,7},{4,0},{5,1},{6,2},{7,3},{8,12},{9,13},{10,... | collective-permute-start | bytes 786440 | tf_op jit(solution)/shard_map/ppermute | solution.py:78
  168.1 13.5 %collective-permute-start.18 = (f32[2,2,32,1024]{3,2,1,0:T(8,128)S(1)}, f32[2,2,32,1024]{3,2,1,0:T(8,128)S(1)}, u32[]{:S(2)}, u32[]{:S(2)}) collective-permute-start(f32[2,2,32,1024]{3,2,1,0:T(8,128)S(1)} %dynamic-slice_bitcast_fusion.1), channel_id=1, source_target_pairs={{0,1},{1,0},{2,3},{3,2},{4,5},{5,4},{6,7},{7,6},{8,9},{9,8},{10,11... | collective-permute-start | bytes 1572872 | tf_op jit(solution)/shard_map/ppermute | solution.py:78
  168.8 14.5 %collective-permute-start.21 = (f32[2,2,32,1024]{3,2,1,0:T(8,128)S(1)}, f32[2,2,32,1024]{3,2,1,0:T(8,128)S(1)}, u32[]{:S(2)}, u32[]{:S(2)}) collective-permute-start(f32[2,2,32,1024]{3,2,1,0:T(8,128)S(1)} %dynamic-slice_bitcast_fusion), channel_id=1, source_target_pairs={{0,1},{1,0},{2,3},{3,2},{4,5},{5,4},{6,7},{7,6},{8,9},{9,8},{10,11... | collective-permute-start | bytes 1572872 | tf_op jit(solution)/shard_map/ppermute | solution.py:78
  175.8 5.0 %collective-permute-start.15 = (f32[32,1024]{1,0:T(8,128)S(1)}, f32[32,1024]{1,0:T(8,128)S(1)}, u32[]{:S(2)}, u32[]{:S(2)}) collective-permute-start(f32[32,1024]{1,0:T(8,128)S(1)} %dynamic-slice_bitcast_fusion.19), channel_id=1, source_target_pairs={{0,4},{1,5},{2,6},{3,7},{4,0},{5,1},{6,2},{7,3},{8,12},{9,13},{10,... | collective-permute-start | bytes 393224 | tf_op jit(solution)/shard_map/ppermute | solution.py:78
  176.5 5.2 %collective-permute-start.17 = (f32[32,1024]{1,0:T(8,128)S(1)}, f32[32,1024]{1,0:T(8,128)S(1)}, u32[]{:S(2)}, u32[]{:S(2)}) collective-permute-start(f32[32,1024]{1,0:T(8,128)S(1)} %dynamic-slice_bitcast_fusion.18), channel_id=1, source_target_pairs={{0,2},{1,3},{2,0},{3,1},{4,6},{5,7},{6,4},{7,5},{8,10},{9,11},{10,... | collective-permute-start | bytes 393224 | tf_op jit(solution)/shard_map/ppermute | solution.py:78
  181.8 6.4 %collective-permute-start.19 = (f32[2,32,1024]{2,1,0:T(8,128)S(1)}, f32[2,32,1024]{2,1,0:T(8,128)S(1)}, u32[]{:S(2)}, u32[]{:S(2)}) collective-permute-start(f32[2,32,1024]{2,1,0:T(8,128)S(1)} %dynamic-slice_bitcast_fusion.9), channel_id=1, source_target_pairs={{0,2},{1,3},{2,0},{3,1},{4,6},{5,7},{6,4},{7,5},{8,10},{9,11},{10,... | collective-permute-start | bytes 786440 | tf_op jit(solution)/shard_map/ppermute | solution.py:78
  183.4 7.6 %collective-permute-start.22 = (f32[2,32,1024]{2,1,0:T(8,128)S(1)}, f32[2,32,1024]{2,1,0:T(8,128)S(1)}, u32[]{:S(2)}, u32[]{:S(2)}) collective-permute-start(f32[2,32,1024]{2,1,0:T(8,128)S(1)} %dynamic-slice_bitcast_fusion.8), channel_id=1, source_target_pairs={{0,4},{1,5},{2,6},{3,7},{4,0},{5,1},{6,2},{7,3},{8,12},{9,13},{10,... | collective-permute-start | bytes 786440 | tf_op jit(solution)/shard_map/ppermute | solution.py:78
  188.3 5.0 %collective-permute-start.20 = (f32[32,1024]{1,0:T(8,128)S(1)}, f32[32,1024]{1,0:T(8,128)S(1)}, u32[]{:S(2)}, u32[]{:S(2)}) collective-permute-start(f32[32,1024]{1,0:T(8,128)S(1)} %dynamic-slice_bitcast_fusion.17), channel_id=1, source_target_pairs={{0,4},{1,5},{2,6},{3,7},{4,0},{5,1},{6,2},{7,3},{8,12},{9,13},{10,... | collective-permute-start | bytes 393224 | tf_op jit(solution)/shard_map/ppermute | solution.py:78
  191.1 5.0 %collective-permute-start.23 = (f32[32,1024]{1,0:T(8,128)S(1)}, f32[32,1024]{1,0:T(8,128)S(1)}, u32[]{:S(2)}, u32[]{:S(2)}) collective-permute-start(f32[32,1024]{1,0:T(8,128)S(1)} %dynamic-slice_bitcast_fusion.16), channel_id=1, source_target_pairs={{0,2},{1,3},{2,0},{3,1},{4,6},{5,7},{6,4},{7,5},{8,10},{9,11},{10,... | collective-permute-start | bytes 393224 | tf_op jit(solution)/shard_map/ppermute | solution.py:78
  (7 other events, 30.5 us)
Sparse Core Ops, SparseCore 0:
  16.3 54.8 all-gather.10
  72.7 25.6 all-gather.8
  100.0 27.4 all-gather.6
  128.8 27.4 all-gather.4

commit v14 on v13

--- a/solution.py
+++ b/solution.py
@@ -112,8 +112,10 @@
     half = weight.shape[1] // 2
     flows = []
     for chunk in range(len(CHUNKS)):
-        for flow in flows:
-            flow.advance(rep_index)
+        rounds = 1 if chunk < len(CHUNKS) - 1 else levels
+        for _ in range(rounds):
+            for flow in flows:
+                flow.advance(rep_index)
         if flows:
             amp4, held = lax.optimization_barrier((gathered[chunk], [f.x for f in flows]))
             for flow, x in zip(flows, held):

time: 204 us -> 201 us (0.985)
  starting transfers between devices: 27.6 us -> 24.5 us
    ppermute x24, waiting for transfers between devices: 37.7 us -> 45.5 us  [advance(): self.x = keep + lax.ppermute(send, 'rep', perm=pairs)]
    all_gather x4, waiting for transfers between devices: 15.1 us -> 7.59 us  [on_device(): lax.all_gather(local4[:, bounds[c]:bounds[c + 1]], 'own', axis=0, tiled=T...]
    ppermute x24, starting transfers between devices: 20.1 us -> 17.1 us  [advance(): self.x = keep + lax.ppermute(send, 'rep', perm=pairs)]
  transfers between devices with their start and end apart: 29 -> 29, of which waited for: 17 -> 17; matrix products, arithmetic and copies ran while one was open for 13% -> 15% of each run, Pallas kernels for 5% -> 5%
where the time goes in v14:
time: 201 us
  waiting for transfers between devices  115 us (57%)
  matrix products  27.2 us (14%)
  starting transfers between devices  24.5 us (12%)
  between operations  13.7 us (7%)
  Pallas kernels  10.2 us (5%)
  local copies, waits for them, and re-layouts  6.02 us (3%)
  other arithmetic  4.68 us (2%)
    all_to_all x1, waiting for transfers between devices, on_device(): lax.all_to_all(integrals, ('own', 'rep'), split_axis=0, concat_axis=0, ti...  60.3 us
    ppermute x24, waiting for transfers between devices, advance(): self.x = keep + lax.ppermute(send, 'rep', perm=pairs)  45.5 us
    dot_general x8, matrix products, on_device(): jnp.dot(lhs, weight[:, h * half:(h + 1) * half], preferred_element_type=j...  27.2 us
    ppermute x24, starting transfers between devices, advance(): self.x = keep + lax.ppermute(send, 'rep', perm=pairs)  17.1 us
    pallas_call x1, Pallas kernels, _dense_weight(): pl.pallas_call(_weight_kernel, grid_spec=grid_spec, out_shape=jax.ShapeDt...  10.2 us
    all_gather x4, waiting for transfers between devices, on_device(): lax.all_gather(local4[:, bounds[c]:bounds[c + 1]], 'own', axis=0, tiled=T...  7.59 us
    all_to_all x1, starting transfers between devices, on_device(): lax.all_to_all(integrals, ('own', 'rep'), split_axis=0, concat_axis=0, ti...  7.3 us
  transfers between devices with their start and end apart: 29, of which 17 were waited for; matrix products, arithmetic and copies ran while one was open for 15% of the time, Pallas kernels for 5%

profile of v14, /device:TPU:0, one launch (start us, length us, event | category | flops | bytes accessed | tf_op | source)
XLA Modules:
  0.0 201.0 jit_solution(14219147349480470749)
XLA Ops:
  6.5 7.3 %all-to-all-start = ((bf16[64,128,128]{2,1,0:T(8,128)(2,1)}), bf16[64,128,128]{2,1,0:T(8,128)(2,1)S(1)}, u32[]{:S(2)}, u32[]{:S(2)}) async-start(bf16[64,128,128]{2,1,0:T(8,128)(2,1)} %param.6), calls=%async_computation | async-start | bytes 4194304 | tf_op jit(solution)/shard_map/all_to_all | solution.py:90
  19.1 60.3 %all-to-all-done.tiles_ref = bf16[64,128,128]{2,1,0:T(8,128)(2,1)S(1)} async-done(((bf16[64,128,128]{2,1,0:T(8,128)(2,1)}), bf16[64,128,128]{2,1,0:T(8,128)(2,1)S(1)}, u32[]{:S(2)}, u32[]{:S(2)}) %all-to-all-start) | async-done | bytes 2097184 | tf_op jit(solution)/shard_map/all_to_all | solution.py:90
  79.4 1.4 copy-done.1
  80.8 10.2 %shard_map.55 = bf16[2048,2048]{1,0:T(8,128)(2,1)} custom-call(s32[64]{0:T(128)} %select_reduce_fusion.order_ref, s32[17]{0:T(128)} %convert_reduce_fusion.1.starts_ref, s32[64]{0:T(128)} %reshape.103.cd_ref, bf16[64,128,128]{2,1,0:T(8,128)(2,1)} %copy-done.1), custom_call_target="tpu_custom_call" | custom-call | bytes 10485760 | tf_op jit(solution)/shard_map/pallas_call | solution.py:49
  91.0 3.9 %fusion.15 = f32[1024,256]{0,1:T(8,128)S(1)} fusion(bf16[256,2048]{1,0:T(8,128)(2,1)} %bitcast.167, bf16[2048,2048]{1,0:T(8,128)(2,1)} %shard_map.55), kind=kOutput, calls=%fused_computation.15 | convolution fusion | flops 1073741824 | bytes 6291456 | tf_op jit(solution)/shard_map/dot_general | solution.py:127
  96.2 1.3 fusion.20
  98.4 2.1 %collective-permute-done = f32[2,2,32,1024]{3,2,1,0:T(8,128)} collective-permute-done((f32[2,2,32,1024]{3,2,1,0:T(8,128)}, f32[2,2,32,1024]{3,2,1,0:T(8,128)}, u32[]{:S(2)}, u32[]{:S(2)}) %collective-permute-start) | collective-permute-done | bytes 524320 | tf_op jit(solution)/shard_map/ppermute | solution.py:78
  101.7 3.8 %fusion.4 = f32[2,2,2,32,1024]{4,3,2,1,0:T(8,128)S(1)} fusion(bf16[2,2,2,32,2048]{4,3,2,1,0:T(8,128)(2,1)} %bitcast.165, bf16[2048,2048]{1,0:T(8,128)(2,1)} %shard_map.55), kind=kOutput, calls=%fused_computation.4 | convolution fusion | flops 1073741824 | bytes 6291456 | tf_op jit(solution)/shard_map/dot_general | solution.py:127
  105.5 3.6 %fusion.10 = f32[2,2,2,32,1024]{4,3,2,1,0:T(8,128)S(1)} fusion(bf16[2,2,2,32,2048]{4,3,2,1,0:T(8,128)(2,1)S(1)} %bitcast.166, bf16[2048,2048]{1,0:T(8,128)(2,1)} %shard_map.55), kind=kOutput, calls=%fused_computation.10 | convolution fusion | flops 1073741824 | bytes 6291456 | tf_op jit(solution)/shard_map/dot_general | solution.py:127
  109.2 1.6 collective-permute-start.3
  110.9 1.5 collective-permute-start.2
  112.7 4.9 %collective-permute-done.3 = f32[2,32,1024]{2,1,0:T(8,128)S(1)} collective-permute-done((f32[2,32,1024]{2,1,0:T(8,128)S(1)}, f32[2,32,1024]{2,1,0:T(8,128)S(1)}, u32[]{:S(2)}, u32[]{:S(2)}) %collective-permute-start.3) | collective-permute-done | bytes 262176 | tf_op jit(solution)/shard_map/ppermute | solution.py:78
  117.6 2.0 %collective-permute-done.2 = f32[2,32,1024]{2,1,0:T(8,128)S(1)} collective-permute-done((f32[2,32,1024]{2,1,0:T(8,128)S(1)}, f32[2,32,1024]{2,1,0:T(8,128)S(1)}, u32[]{:S(2)}, u32[]{:S(2)}) %collective-permute-start.2) | collective-permute-done | bytes 262176 | tf_op jit(solution)/shard_map/ppermute | solution.py:78
  119.9 7.5 %all-gather.7.cloned.1.call-done = bf16[8,1,32,2048]{3,2,1,0:T(8,128)(2,1)} async-done(((bf16[2,1,32,2048]{3,2,1,0:T(8,128)(2,1)}), bf16[8,1,32,2048]{3,2,1,0:T(8,128)(2,1)}) %all-gather.7.cloned.1.call-update) | async-done | bytes 1048592 | tf_op jit(solution)/shard_map/all_gather | solution.py:109
  127.4 3.8 %fusion.2 = f32[2,2,2,32,1024]{4,3,2,1,0:T(8,128)S(1)} fusion(bf16[2,2,2,32,2048]{4,3,2,1,0:T(8,128)(2,1)} %bitcast.163, bf16[2048,2048]{1,0:T(8,128)(2,1)} %shard_map.55), kind=kOutput, calls=%fused_computation.2 | convolution fusion | flops 1073741824 | bytes 6291456 | tf_op jit(solution)/shard_map/dot_general | solution.py:127
  131.3 3.5 %fusion.8 = f32[2,2,2,32,1024]{4,3,2,1,0:T(8,128)S(1)} fusion(bf16[2,2,2,32,2048]{4,3,2,1,0:T(8,128)(2,1)S(1)} %bitcast.164, bf16[2048,2048]{1,0:T(8,128)(2,1)} %shard_map.55), kind=kOutput, calls=%fused_computation.8 | convolution fusion | flops 1073741824 | bytes 6291456 | tf_op jit(solution)/shard_map/dot_general | solution.py:127
  135.5 1.5 collective-permute-start.10
  137.1 1.5 collective-permute-start.7
  139.2 4.3 %collective-permute-done.7 = f32[32,1024]{1,0:T(8,128)S(1)} collective-permute-done((f32[32,1024]{1,0:T(8,128)S(1)}, f32[32,1024]{1,0:T(8,128)S(1)}, u32[]{:S(2)}, u32[]{:S(2)}) %collective-permute-start.7) | collective-permute-done | bytes 131104 | tf_op jit(solution)/shard_map/ppermute | solution.py:78
  144.1 4.4 %collective-permute-done.6 = f32[32,1024]{1,0:T(8,128)S(1)} collective-permute-done((f32[32,1024]{1,0:T(8,128)S(1)}, f32[32,1024]{1,0:T(8,128)S(1)}, u32[]{:S(2)}, u32[]{:S(2)}) %collective-permute-start.6) | collective-permute-done | bytes 131104 | tf_op jit(solution)/shard_map/ppermute | solution.py:78
  148.6 1.5 collective-permute-start.11
  150.8 2.8 %collective-permute-done.11 = f32[32,1024]{1,0:T(8,128)S(1)} collective-permute-done((f32[32,1024]{1,0:T(8,128)S(1)}, f32[32,1024]{1,0:T(8,128)S(1)}, u32[]{:S(2)}, u32[]{:S(2)}) %collective-permute-start.11) | collective-permute-done | bytes 131104 | tf_op jit(solution)/shard_map/ppermute | solution.py:78
  153.6 2.8 %collective-permute-done.9 = f32[32,1024]{1,0:T(8,128)S(1)} collective-permute-done((f32[32,1024]{1,0:T(8,128)S(1)}, f32[32,1024]{1,0:T(8,128)S(1)}, u32[]{:S(2)}, u32[]{:S(2)}) %collective-permute-start.9) | collective-permute-done | bytes 131104 | tf_op jit(solution)/shard_map/ppermute | solution.py:78
  157.0 7.4 %collective-permute-done.16 = f32[2,32,1024]{2,1,0:T(8,128)S(1)} collective-permute-done((f32[2,32,1024]{2,1,0:T(8,128)S(1)}, f32[2,32,1024]{2,1,0:T(8,128)S(1)}, u32[]{:S(2)}, u32[]{:S(2)}) %collective-permute-start.16) | collective-permute-done | bytes 262176 | tf_op jit(solution)/shard_map/ppermute | solution.py:78
  165.5 4.1 %collective-permute-done.17 = f32[32,1024]{1,0:T(8,128)S(1)} collective-permute-done((f32[32,1024]{1,0:T(8,128)S(1)}, f32[32,1024]{1,0:T(8,128)S(1)}, u32[]{:S(2)}, u32[]{:S(2)}) %collective-permute-start.17) | collective-permute-done | bytes 131104 | tf_op jit(solution)/shard_map/ppermute | solution.py:78
  169.8 3.8 %fusion.6 = f32[2,2,2,32,1024]{4,3,2,1,0:T(8,128)S(1)} fusion(bf16[2,2,2,32,2048]{4,3,2,1,0:T(8,128)(2,1)} %bitcast.161, bf16[2048,2048]{1,0:T(8,128)(2,1)} %shard_map.55), kind=kOutput, calls=%fused_computation.6 | convolution fusion | flops 1073741824 | bytes 6291456 | tf_op jit(solution)/shard_map/dot_general | solution.py:127
  173.8 3.5 %fusion = f32[2,2,2,32,1024]{4,3,2,1,0:T(8,128)S(1)} fusion(bf16[2,2,2,32,2048]{4,3,2,1,0:T(8,128)(2,1)S(1)} %bitcast.162, bf16[2048,2048]{1,0:T(8,128)(2,1)} %shard_map.55), kind=kOutput, calls=%fused_computation | convolution fusion | flops 1073741824 | bytes 6291456 | tf_op jit(solution)/shard_map/dot_general | solution.py:127
  178.0 2.0 %collective-permute-start.19 = (f32[2,32,1024]{2,1,0:T(8,128)S(1)}, f32[2,32,1024]{2,1,0:T(8,128)S(1)}, u32[]{:S(2)}, u32[]{:S(2)}) collective-permute-start(f32[2,32,1024]{2,1,0:T(8,128)S(1)} %dynamic-slice_bitcast_fusion.9), channel_id=1, source_target_pairs={{0,2},{1,3},{2,0},{3,1},{4,6},{5,7},{6,4},{7,5},{8,10},{9,11},{10,... | collective-permute-start | bytes 786440 | tf_op jit(solution)/shard_map/ppermute | solution.py:78
  180.3 6.2 %collective-permute-done.19 = f32[2,32,1024]{2,1,0:T(8,128)S(1)} collective-permute-done((f32[2,32,1024]{2,1,0:T(8,128)S(1)}, f32[2,32,1024]{2,1,0:T(8,128)S(1)}, u32[]{:S(2)}, u32[]{:S(2)}) %collective-permute-start.19) | collective-permute-done | bytes 262176 | tf_op jit(solution)/shard_map/ppermute | solution.py:78
  188.2 2.0 %collective-permute-start.23 = (f32[32,1024]{1,0:T(8,128)S(1)}, f32[32,1024]{1,0:T(8,128)S(1)}, u32[]{:S(2)}, u32[]{:S(2)}) collective-permute-start(f32[32,1024]{1,0:T(8,128)S(1)} %dynamic-slice_bitcast_fusion.16), channel_id=1, source_target_pairs={{0,2},{1,3},{2,0},{3,1},{4,6},{5,7},{6,4},{7,5},{8,10},{9,11},{10,... | collective-permute-start | bytes 393224 | tf_op jit(solution)/shard_map/ppermute | solution.py:78
  190.2 1.3 collective-permute-done.20
  191.6 1.9 collective-permute-done.23
  (119 shorter events, 17.6 us)
Async XLA Ops:
  6.5 9.9 %copy-start.3 = (s32[1,32,2]{1,2,0:T(2,128)S(1)}, s32[1,32,2]{1,2,0:T(2,128)}, u32[]{:S(2)}) copy-start(s32[1,32,2]{1,2,0:T(2,128)} %param.7) | copy-start | bytes 772
  6.5 10.1 %copy-start.5 = (s32[1,32]{1,0:T(1,128)S(1)}, s32[1,32]{1,0:T(1,128)}, u32[]{:S(2)}) copy-start(s32[1,32]{1,0:T(1,128)} %param.9) | copy-start | bytes 388
  6.5 11.1 %copy-start.4 = (s32[1,32,2]{1,2,0:T(2,128)S(1)}, s32[1,32,2]{1,2,0:T(2,128)}, u32[]{:S(2)}) copy-start(s32[1,32,2]{1,2,0:T(2,128)} %param.8) | copy-start | bytes 772
  6.5 72.9 %all-to-all-start = ((bf16[64,128,128]{2,1,0:T(8,128)(2,1)}), bf16[64,128,128]{2,1,0:T(8,128)(2,1)S(1)}, u32[]{:S(2)}, u32[]{:S(2)}) async-start(bf16[64,128,128]{2,1,0:T(8,128)(2,1)} %param.6), calls=%async_computation | async-start | bytes 4194304 | tf_op jit(solution)/shard_map/all_to_all | solution.py:90
  13.8 77.1 %all-gather.11.cloned.1.call-start = ((), (), s32[]{:S(2)}) async-start(), calls=%async_computation.4 | async-start | bytes 1310720 | tf_op jit(solution)/shard_map/all_gather | solution.py:109
  14.9 86.8 %all-gather.9.cloned.1.call-start = ((), (), s32[]{:S(2)}) async-start(), calls=%async_computation.3 | async-start | bytes 1310720 | tf_op jit(solution)/shard_map/all_gather | solution.py:109
  15.7 111.8 %all-gather.7.cloned.1.call-start = ((), (), s32[]{:S(2)}) async-start(), calls=%async_computation.2 | async-start | bytes 1310720 | tf_op jit(solution)/shard_map/all_gather | solution.py:109
  16.4 153.4 %all-gather.5.cloned.1.call-start = ((), (), s32[]{:S(2)}) async-start(), calls=%async_computation.1 | async-start | bytes 1310720 | tf_op jit(solution)/shard_map/all_gather | solution.py:109
  95.0 3.4 %collective-permute-start.1 = (f32[2,2,32,1024]{3,2,1,0:T(8,128)S(1)}, f32[2,2,32,1024]{3,2,1,0:T(8,128)S(1)}, u32[]{:S(2)}, u32[]{:S(2)}) collective-permute-start(f32[2,2,32,1024]{3,2,1,0:T(8,128)S(1)} %dynamic-slice_bitcast_fusion.6), channel_id=1, source_target_pairs={{0,1},{1,0},{2,3},{3,2},{4,5},{5,4},{6,7},{7,6},{8,9},{9,8},{10,11... | collective-permute-start | bytes 1572872 | tf_op jit(solution)/shard_map/ppermute | solution.py:78
  98.3 2.3 %collective-permute-start = (f32[2,2,32,1024]{3,2,1,0:T(8,128)}, f32[2,2,32,1024]{3,2,1,0:T(8,128)}, u32[]{:S(2)}, u32[]{:S(2)}) collective-permute-start(f32[2,2,32,1024]{3,2,1,0:T(8,128)} %dynamic-slice_bitcast_fusion.7), channel_id=1, source_target_pairs={{0,1},{1,0},{2,3},{3,2},{4,5},{5,4},{6,7},{7,6},{8,9},{9,8},{10,11... | collective-permute-start | bytes 1572872 | tf_op jit(solution)/shard_map/ppermute | solution.py:78
  109.2 8.4 %collective-permute-start.3 = (f32[2,32,1024]{2,1,0:T(8,128)S(1)}, f32[2,32,1024]{2,1,0:T(8,128)S(1)}, u32[]{:S(2)}, u32[]{:S(2)}) collective-permute-start(f32[2,32,1024]{2,1,0:T(8,128)S(1)} %dynamic-slice_bitcast_fusion.14), channel_id=1, source_target_pairs={{0,4},{1,5},{2,6},{3,7},{4,0},{5,1},{6,2},{7,3},{8,12},{9,13},{10,... | collective-permute-start | bytes 786440 | tf_op jit(solution)/shard_map/ppermute | solution.py:78
  110.8 8.9 %collective-permute-start.5 = (f32[2,2,32,1024]{3,2,1,0:T(8,128)S(1)}, f32[2,2,32,1024]{3,2,1,0:T(8,128)S(1)}, u32[]{:S(2)}, u32[]{:S(2)}) collective-permute-start(f32[2,2,32,1024]{3,2,1,0:T(8,128)S(1)} %dynamic-slice_bitcast_fusion.4), channel_id=1, source_target_pairs={{0,1},{1,0},{2,3},{3,2},{4,5},{5,4},{6,7},{7,6},{8,9},{9,8},{10,11... | collective-permute-start | bytes 1572872 | tf_op jit(solution)/shard_map/ppermute | solution.py:78
  110.9 8.8 %collective-permute-start.2 = (f32[2,32,1024]{2,1,0:T(8,128)S(1)}, f32[2,32,1024]{2,1,0:T(8,128)S(1)}, u32[]{:S(2)}, u32[]{:S(2)}) collective-permute-start(f32[2,32,1024]{2,1,0:T(8,128)S(1)} %dynamic-slice_bitcast_fusion.15), channel_id=1, source_target_pairs={{0,2},{1,3},{2,0},{3,1},{4,6},{5,7},{6,4},{7,5},{8,10},{9,11},{10,... | collective-permute-start | bytes 786440 | tf_op jit(solution)/shard_map/ppermute | solution.py:78
  112.5 7.3 %collective-permute-start.4 = (f32[2,2,32,1024]{3,2,1,0:T(8,128)S(1)}, f32[2,2,32,1024]{3,2,1,0:T(8,128)S(1)}, u32[]{:S(2)}, u32[]{:S(2)}) collective-permute-start(f32[2,2,32,1024]{3,2,1,0:T(8,128)S(1)} %dynamic-slice_bitcast_fusion.5), channel_id=1, source_target_pairs={{0,1},{1,0},{2,3},{3,2},{4,5},{5,4},{6,7},{7,6},{8,9},{9,8},{10,11... | collective-permute-start | bytes 1572872 | tf_op jit(solution)/shard_map/ppermute | solution.py:78
  134.8 21.7 %collective-permute-start.15 = (f32[2,2,32,1024]{3,2,1,0:T(8,128)S(1)}, f32[2,2,32,1024]{3,2,1,0:T(8,128)S(1)}, u32[]{:S(2)}, u32[]{:S(2)}) collective-permute-start(f32[2,2,32,1024]{3,2,1,0:T(8,128)S(1)} %dynamic-slice_bitcast_fusion.2), channel_id=1, source_target_pairs={{0,1},{1,0},{2,3},{3,2},{4,5},{5,4},{6,7},{7,6},{8,9},{9,8},{10,11... | collective-permute-start | bytes 1572872 | tf_op jit(solution)/shard_map/ppermute | solution.py:78
  134.9 21.7 %collective-permute-start.12 = (f32[2,2,32,1024]{3,2,1,0:T(8,128)S(1)}, f32[2,2,32,1024]{3,2,1,0:T(8,128)S(1)}, u32[]{:S(2)}, u32[]{:S(2)}) collective-permute-start(f32[2,2,32,1024]{3,2,1,0:T(8,128)S(1)} %dynamic-slice_bitcast_fusion.3), channel_id=1, source_target_pairs={{0,1},{1,0},{2,3},{3,2},{4,5},{5,4},{6,7},{7,6},{8,9},{9,8},{10,11... | collective-permute-start | bytes 1572872 | tf_op jit(solution)/shard_map/ppermute | solution.py:78
  135.5 13.0 %collective-permute-start.10 = (f32[2,32,1024]{2,1,0:T(8,128)S(1)}, f32[2,32,1024]{2,1,0:T(8,128)S(1)}, u32[]{:S(2)}, u32[]{:S(2)}) collective-permute-start(f32[2,32,1024]{2,1,0:T(8,128)S(1)} %dynamic-slice_bitcast_fusion.12), channel_id=1, source_target_pairs={{0,4},{1,5},{2,6},{3,7},{4,0},{5,1},{6,2},{7,3},{8,12},{9,13},{10,... | collective-permute-start | bytes 786440 | tf_op jit(solution)/shard_map/ppermute | solution.py:78
  137.1 6.5 %collective-permute-start.7 = (f32[32,1024]{1,0:T(8,128)S(1)}, f32[32,1024]{1,0:T(8,128)S(1)}, u32[]{:S(2)}, u32[]{:S(2)}) collective-permute-start(f32[32,1024]{1,0:T(8,128)S(1)} %dynamic-slice_bitcast_fusion.22), channel_id=1, source_target_pairs={{0,2},{1,3},{2,0},{3,1},{4,6},{5,7},{6,4},{7,5},{8,10},{9,11},{10,... | collective-permute-start | bytes 393224 | tf_op jit(solution)/shard_map/ppermute | solution.py:78
  138.6 11.5 %collective-permute-start.8 = (f32[2,32,1024]{2,1,0:T(8,128)S(1)}, f32[2,32,1024]{2,1,0:T(8,128)S(1)}, u32[]{:S(2)}, u32[]{:S(2)}) collective-permute-start(f32[2,32,1024]{2,1,0:T(8,128)S(1)} %dynamic-slice_bitcast_fusion.13), channel_id=1, source_target_pairs={{0,2},{1,3},{2,0},{3,1},{4,6},{5,7},{6,4},{7,5},{8,10},{9,11},{10,... | collective-permute-start | bytes 786440 | tf_op jit(solution)/shard_map/ppermute | solution.py:78
  143.5 5.0 %collective-permute-start.6 = (f32[32,1024]{1,0:T(8,128)S(1)}, f32[32,1024]{1,0:T(8,128)S(1)}, u32[]{:S(2)}, u32[]{:S(2)}) collective-permute-start(f32[32,1024]{1,0:T(8,128)S(1)} %dynamic-slice_bitcast_fusion.23), channel_id=1, source_target_pairs={{0,4},{1,5},{2,6},{3,7},{4,0},{5,1},{6,2},{7,3},{8,12},{9,13},{10,... | collective-permute-start | bytes 393224 | tf_op jit(solution)/shard_map/ppermute | solution.py:78
  148.6 5.0 %collective-permute-start.11 = (f32[32,1024]{1,0:T(8,128)S(1)}, f32[32,1024]{1,0:T(8,128)S(1)}, u32[]{:S(2)}, u32[]{:S(2)}) collective-permute-start(f32[32,1024]{1,0:T(8,128)S(1)} %dynamic-slice_bitcast_fusion.20), channel_id=1, source_target_pairs={{0,2},{1,3},{2,0},{3,1},{4,6},{5,7},{6,4},{7,5},{8,10},{9,11},{10,... | collective-permute-start | bytes 393224 | tf_op jit(solution)/shard_map/ppermute | solution.py:78
  150.2 6.2 %collective-permute-start.9 = (f32[32,1024]{1,0:T(8,128)S(1)}, f32[32,1024]{1,0:T(8,128)S(1)}, u32[]{:S(2)}, u32[]{:S(2)}) collective-permute-start(f32[32,1024]{1,0:T(8,128)S(1)} %dynamic-slice_bitcast_fusion.21), channel_id=1, source_target_pairs={{0,4},{1,5},{2,6},{3,7},{4,0},{5,1},{6,2},{7,3},{8,12},{9,13},{10,... | collective-permute-start | bytes 393224 | tf_op jit(solution)/shard_map/ppermute | solution.py:78
  156.6 7.8 %collective-permute-start.16 = (f32[2,32,1024]{2,1,0:T(8,128)S(1)}, f32[2,32,1024]{2,1,0:T(8,128)S(1)}, u32[]{:S(2)}, u32[]{:S(2)}) collective-permute-start(f32[2,32,1024]{2,1,0:T(8,128)S(1)} %dynamic-slice_bitcast_fusion.10), channel_id=1, source_target_pairs={{0,4},{1,5},{2,6},{3,7},{4,0},{5,1},{6,2},{7,3},{8,12},{9,13},{10,... | collective-permute-start | bytes 786440 | tf_op jit(solution)/shard_map/ppermute | solution.py:78
  156.8 7.8 %collective-permute-start.13 = (f32[2,32,1024]{2,1,0:T(8,128)S(1)}, f32[2,32,1024]{2,1,0:T(8,128)S(1)}, u32[]{:S(2)}, u32[]{:S(2)}) collective-permute-start(f32[2,32,1024]{2,1,0:T(8,128)S(1)} %dynamic-slice_bitcast_fusion.11), channel_id=1, source_target_pairs={{0,2},{1,3},{2,0},{3,1},{4,6},{5,7},{6,4},{7,5},{8,10},{9,11},{10,... | collective-permute-start | bytes 786440 | tf_op jit(solution)/shard_map/ppermute | solution.py:78
  164.5 5.0 %collective-permute-start.17 = (f32[32,1024]{1,0:T(8,128)S(1)}, f32[32,1024]{1,0:T(8,128)S(1)}, u32[]{:S(2)}, u32[]{:S(2)}) collective-permute-start(f32[32,1024]{1,0:T(8,128)S(1)} %dynamic-slice_bitcast_fusion.18), channel_id=1, source_target_pairs={{0,2},{1,3},{2,0},{3,1},{4,6},{5,7},{6,4},{7,5},{8,10},{9,11},{10,... | collective-permute-start | bytes 393224 | tf_op jit(solution)/shard_map/ppermute | solution.py:78
  164.7 5.0 %collective-permute-start.14 = (f32[32,1024]{1,0:T(8,128)S(1)}, f32[32,1024]{1,0:T(8,128)S(1)}, u32[]{:S(2)}, u32[]{:S(2)}) collective-permute-start(f32[32,1024]{1,0:T(8,128)S(1)} %dynamic-slice_bitcast_fusion.19), channel_id=1, source_target_pairs={{0,4},{1,5},{2,6},{3,7},{4,0},{5,1},{6,2},{7,3},{8,12},{9,13},{10,... | collective-permute-start | bytes 393224 | tf_op jit(solution)/shard_map/ppermute | solution.py:78
  173.7 4.2 %collective-permute-start.18 = (f32[2,2,32,1024]{3,2,1,0:T(8,128)S(1)}, f32[2,2,32,1024]{3,2,1,0:T(8,128)S(1)}, u32[]{:S(2)}, u32[]{:S(2)}) collective-permute-start(f32[2,2,32,1024]{3,2,1,0:T(8,128)S(1)} %dynamic-slice_bitcast_fusion.1), channel_id=1, source_target_pairs={{0,1},{1,0},{2,3},{3,2},{4,5},{5,4},{6,7},{7,6},{8,9},{9,8},{10,11... | collective-permute-start | bytes 1572872 | tf_op jit(solution)/shard_map/ppermute | solution.py:78
  177.3 2.7 %collective-permute-start.21 = (f32[2,2,32,1024]{3,2,1,0:T(8,128)S(1)}, f32[2,2,32,1024]{3,2,1,0:T(8,128)S(1)}, u32[]{:S(2)}, u32[]{:S(2)}) collective-permute-start(f32[2,2,32,1024]{3,2,1,0:T(8,128)S(1)} %dynamic-slice_bitcast_fusion), channel_id=1, source_target_pairs={{0,1},{1,0},{2,3},{3,2},{4,5},{5,4},{6,7},{7,6},{8,9},{9,8},{10,11... | collective-permute-start | bytes 1572872 | tf_op jit(solution)/shard_map/ppermute | solution.py:78
  178.0 8.5 %collective-permute-start.19 = (f32[2,32,1024]{2,1,0:T(8,128)S(1)}, f32[2,32,1024]{2,1,0:T(8,128)S(1)}, u32[]{:S(2)}, u32[]{:S(2)}) collective-permute-start(f32[2,32,1024]{2,1,0:T(8,128)S(1)} %dynamic-slice_bitcast_fusion.9), channel_id=1, source_target_pairs={{0,2},{1,3},{2,0},{3,1},{4,6},{5,7},{6,4},{7,5},{8,10},{9,11},{10,... | collective-permute-start | bytes 786440 | tf_op jit(solution)/shard_map/ppermute | solution.py:78
  180.1 8.1 %collective-permute-start.22 = (f32[2,32,1024]{2,1,0:T(8,128)S(1)}, f32[2,32,1024]{2,1,0:T(8,128)S(1)}, u32[]{:S(2)}, u32[]{:S(2)}) collective-permute-start(f32[2,32,1024]{2,1,0:T(8,128)S(1)} %dynamic-slice_bitcast_fusion.8), channel_id=1, source_target_pairs={{0,4},{1,5},{2,6},{3,7},{4,0},{5,1},{6,2},{7,3},{8,12},{9,13},{10,... | collective-permute-start | bytes 786440 | tf_op jit(solution)/shard_map/ppermute | solution.py:78
  186.5 5.0 %collective-permute-start.20 = (f32[32,1024]{1,0:T(8,128)S(1)}, f32[32,1024]{1,0:T(8,128)S(1)}, u32[]{:S(2)}, u32[]{:S(2)}) collective-permute-start(f32[32,1024]{1,0:T(8,128)S(1)} %dynamic-slice_bitcast_fusion.17), channel_id=1, source_target_pairs={{0,4},{1,5},{2,6},{3,7},{4,0},{5,1},{6,2},{7,3},{8,12},{9,13},{10,... | collective-permute-start | bytes 393224 | tf_op jit(solution)/shard_map/ppermute | solution.py:78
  188.2 5.2 %collective-permute-start.23 = (f32[32,1024]{1,0:T(8,128)S(1)}, f32[32,1024]{1,0:T(8,128)S(1)}, u32[]{:S(2)}, u32[]{:S(2)}) collective-permute-start(f32[32,1024]{1,0:T(8,128)S(1)} %dynamic-slice_bitcast_fusion.16), channel_id=1, source_target_pairs={{0,2},{1,3},{2,0},{3,1},{4,6},{5,7},{6,4},{7,5},{8,10},{9,11},{10,... | collective-permute-start | bytes 393224 | tf_op jit(solution)/shard_map/ppermute | solution.py:78
  (7 other events, 30.6 us)
Sparse Core Ops, SparseCore 0:
  16.3 54.8 all-gather.10
  72.7 25.6 all-gather.8
  100.0 27.4 all-gather.6
  128.9 27.4 all-gather.4

commit v15 on v13

--- a/solution.py
+++ b/solution.py
@@ -112,14 +112,14 @@
     half = weight.shape[1] // 2
     flows = []
     for chunk in range(len(CHUNKS)):
-        for flow in flows:
-            flow.advance(rep_index)
         if flows:
             amp4, held = lax.optimization_barrier((gathered[chunk], [f.x for f in flows]))
             for flow, x in zip(flows, held):
                 flow.x = x
         else:
             amp4 = gathered[chunk]
+        for flow in flows:
+            flow.advance(rep_index)
         lhs = amp4.reshape(-1, width)
         for h in range(2):
             partial = jnp.dot(lhs, weight[:, h * half:(h + 1) * half], preferred_element_type=jnp.float32)

time: 204 us -> 217 us (1.064)
  waiting for transfers between devices: 115 us -> 126 us
  matrix products: 27.2 us -> 30.6 us
  starting transfers between devices: 27.6 us -> 25 us
    all_to_all x1, waiting for transfers between devices: 60.3 us -> 71.4 us  [on_device(): lax.all_to_all(integrals, ('own', 'rep'), split_axis=0, concat_axis=0, ti...]
    dot_general x8, matrix products: 27.2 us -> 30.6 us  [on_device(): jnp.dot(lhs, weight[:, h * half:(h + 1) * half], preferred_element_type=j...]
    ppermute x24, starting transfers between devices: 20.1 us -> 17.5 us  [advance(): self.x = keep + lax.ppermute(send, 'rep', perm=pairs)]
where the time goes in v15:
time: 217 us; the launch traced here: 216 us
  waiting for transfers between devices  126 us (58%)
  matrix products  30.6 us (14%)
  starting transfers between devices  25 us (12%)
  between operations  13.6 us (6%)
  Pallas kernels  10.1 us (5%)
  local copies, waits for them, and re-layouts  6.56 us (3%)
  other arithmetic  4.4 us (2%)
    all_to_all x1, waiting for transfers between devices, on_device(): lax.all_to_all(integrals, ('own', 'rep'), split_axis=0, concat_axis=0, ti...  71.4 us
    ppermute x24, waiting for transfers between devices, advance(): self.x = keep + lax.ppermute(send, 'rep', perm=pairs)  37.2 us
    dot_general x8, matrix products, on_device(): jnp.dot(lhs, weight[:, h * half:(h + 1) * half], preferred_element_type=j...  30.6 us
    ppermute x24, starting transfers between devices, advance(): self.x = keep + lax.ppermute(send, 'rep', perm=pairs)  17.5 us
    all_gather x4, waiting for transfers between devices, on_device(): lax.all_gather(local4[:, bounds[c]:bounds[c + 1]], 'own', axis=0, tiled=T...  15.5 us
    pallas_call x1, Pallas kernels, _dense_weight(): pl.pallas_call(_weight_kernel, grid_spec=grid_spec, out_shape=jax.ShapeDt...  10.1 us
    all_to_all x1, starting transfers between devices, on_device(): lax.all_to_all(integrals, ('own', 'rep'), split_axis=0, concat_axis=0, ti...  7.3 us
  transfers between devices with their start and end apart: 29, of which 17 were waited for; matrix products, arithmetic and copies ran while one was open for 13% of the time, Pallas kernels for 5%

profile of v15, /device:TPU:0, one launch (start us, length us, event | category | flops | bytes accessed | tf_op | source)
XLA Modules:
  0.0 216.1 jit_solution(11914965366979104784)
XLA Ops:
  6.5 2.2 %fusion.32 = (bf16[2,1,32,2048]{3,2,1,0:T(8,128)(2,1)}, bf16[2,1,32,2048]{3,2,1,0:T(8,128)(2,1)}, bf16[2,1,32,2048]{3,2,1,0:T(8,128)(2,1)}, bf16[2,1,32,2048]{3,2,1,0:T(8,128)(2,1)}) fusion(bf16[2,4,32,2048]{3,2,1,0:T(8,128)(2,1)} %bitcast.167), kind=kLoop, calls=%fused_computation.89 | loop fusion | bytes 2097152 | tf_op jit(solution)/shard_map/slice | solution.py:109
  8.8 7.3 %all-to-all-start = ((bf16[64,128,128]{2,1,0:T(8,128)(2,1)}), bf16[64,128,128]{2,1,0:T(8,128)(2,1)S(1)}, u32[]{:S(2)}, u32[]{:S(2)}) async-start(bf16[64,128,128]{2,1,0:T(8,128)(2,1)} %param.6), calls=%async_computation | async-start | bytes 4194304 | tf_op jit(solution)/shard_map/all_to_all | solution.py:90
  20.9 71.4 %all-to-all-done.tiles_ref = bf16[64,128,128]{2,1,0:T(8,128)(2,1)S(1)} async-done(((bf16[64,128,128]{2,1,0:T(8,128)(2,1)}), bf16[64,128,128]{2,1,0:T(8,128)(2,1)S(1)}, u32[]{:S(2)}, u32[]{:S(2)}) %all-to-all-start) | async-done | bytes 2097184 | tf_op jit(solution)/shard_map/all_to_all | solution.py:90
  92.2 1.4 copy-done.1
  93.6 10.1 %shard_map.55 = bf16[2048,2048]{1,0:T(8,128)(2,1)} custom-call(s32[64]{0:T(128)} %select_reduce_fusion.order_ref, s32[17]{0:T(128)} %convert_reduce_fusion.1.starts_ref, s32[64]{0:T(128)} %reshape.103.cd_ref, bf16[64,128,128]{2,1,0:T(8,128)(2,1)} %copy-done.1), custom_call_target="tpu_custom_call" | custom-call | bytes 10485760 | tf_op jit(solution)/shard_map/pallas_call | solution.py:49
  103.7 4.0 %fusion.15 = f32[1024,256]{0,1:T(8,128)S(1)} fusion(bf16[256,2048]{1,0:T(8,128)(2,1)} %bitcast.179, bf16[2048,2048]{1,0:T(8,128)(2,1)} %shard_map.55), kind=kOutput, calls=%fused_computation.15 | convolution fusion | flops 1073741824 | bytes 6291456 | tf_op jit(solution)/shard_map/dot_general | solution.py:125
  108.9 2.5 %fusion.20 = f32[1024,256]{0,1:T(8,128)S(1)} fusion(bf16[256,2048]{1,0:T(8,128)(2,1)} %bitcast.180, bf16[2048,2048]{1,0:T(8,128)(2,1)S(1)} %copy-done), kind=kOutput, calls=%fused_computation.20 | convolution fusion | flops 1073741824 | bytes 6291456 | tf_op jit(solution)/shard_map/dot_general | solution.py:125
  112.2 4.8 %fusion.4 = f32[2,2,2,32,1024]{4,3,2,1,0:T(8,128)} fusion(bf16[2,2,2,32,2048]{4,3,2,1,0:T(8,128)(2,1)} %bitcast.177, bf16[2048,2048]{1,0:T(8,128)(2,1)} %shard_map.55), kind=kOutput, calls=%fused_computation.4 | convolution fusion | flops 1073741824 | bytes 6291456 | tf_op jit(solution)/shard_map/dot_general | solution.py:125
  117.1 4.5 %fusion.10 = f32[2,2,2,32,1024]{4,3,2,1,0:T(8,128)} fusion(bf16[2,2,2,32,2048]{4,3,2,1,0:T(8,128)(2,1)S(1)} %bitcast.178, bf16[2048,2048]{1,0:T(8,128)(2,1)} %shard_map.55), kind=kOutput, calls=%fused_computation.10 | convolution fusion | flops 1073741824 | bytes 6291456 | tf_op jit(solution)/shard_map/dot_general | solution.py:125
  121.7 5.4 %all-gather.7.cloned.1.call-done = bf16[8,1,32,2048]{3,2,1,0:T(8,128)(2,1)} async-done(((bf16[2,1,32,2048]{3,2,1,0:T(8,128)(2,1)}), bf16[8,1,32,2048]{3,2,1,0:T(8,128)(2,1)}) %all-gather.7.cloned.1.call-update) | async-done | bytes 1048592 | tf_op jit(solution)/shard_map/all_gather | solution.py:109
  127.1 3.8 %fusion.2 = f32[2,2,2,32,1024]{4,3,2,1,0:T(8,128)S(1)} fusion(bf16[2,2,2,32,2048]{4,3,2,1,0:T(8,128)(2,1)} %bitcast.175, bf16[2048,2048]{1,0:T(8,128)(2,1)} %shard_map.55), kind=kOutput, calls=%fused_computation.2 | convolution fusion | flops 1073741824 | bytes 6291456 | tf_op jit(solution)/shard_map/dot_general | solution.py:125
  131.0 3.6 %fusion.8 = f32[2,2,2,32,1024]{4,3,2,1,0:T(8,128)S(1)} fusion(bf16[2,2,2,32,2048]{4,3,2,1,0:T(8,128)(2,1)S(1)} %bitcast.176, bf16[2048,2048]{1,0:T(8,128)(2,1)} %shard_map.55), kind=kOutput, calls=%fused_computation.8 | convolution fusion | flops 1073741824 | bytes 6291456 | tf_op jit(solution)/shard_map/dot_general | solution.py:125
  134.6 1.5 collective-permute-start.3
  136.3 1.6 collective-permute-start.2
  138.3 4.3 %collective-permute-done.3 = f32[2,32,1024]{2,1,0:T(8,128)S(1)} collective-permute-done((f32[2,32,1024]{2,1,0:T(8,128)S(1)}, f32[2,32,1024]{2,1,0:T(8,128)S(1)}, u32[]{:S(2)}, u32[]{:S(2)}) %collective-permute-start.3) | collective-permute-done | bytes 262176 | tf_op jit(solution)/shard_map/ppermute | solution.py:78
  142.6 2.4 %collective-permute-done.2 = f32[2,32,1024]{2,1,0:T(8,128)S(1)} collective-permute-done((f32[2,32,1024]{2,1,0:T(8,128)S(1)}, f32[2,32,1024]{2,1,0:T(8,128)S(1)}, u32[]{:S(2)}, u32[]{:S(2)}) %collective-permute-start.2) | collective-permute-done | bytes 262176 | tf_op jit(solution)/shard_map/ppermute | solution.py:78
  146.0 10.1 %all-gather.5.cloned.1.call-done = bf16[8,1,32,2048]{3,2,1,0:T(8,128)(2,1)} async-done(((bf16[2,1,32,2048]{3,2,1,0:T(8,128)(2,1)}), bf16[8,1,32,2048]{3,2,1,0:T(8,128)(2,1)}) %all-gather.5.cloned.1.call-update) | async-done | bytes 1048592 | tf_op jit(solution)/shard_map/all_gather | solution.py:109
  156.1 3.8 %fusion.6 = f32[2,2,2,32,1024]{4,3,2,1,0:T(8,128)S(1)} fusion(bf16[2,2,2,32,2048]{4,3,2,1,0:T(8,128)(2,1)} %bitcast.173, bf16[2048,2048]{1,0:T(8,128)(2,1)} %shard_map.55), kind=kOutput, calls=%fused_computation.6 | convolution fusion | flops 1073741824 | bytes 6291456 | tf_op jit(solution)/shard_map/dot_general | solution.py:125
  160.0 3.5 %fusion = f32[2,2,2,32,1024]{4,3,2,1,0:T(8,128)S(1)} fusion(bf16[2,2,2,32,2048]{4,3,2,1,0:T(8,128)(2,1)S(1)} %bitcast.174, bf16[2048,2048]{1,0:T(8,128)(2,1)} %shard_map.55), kind=kOutput, calls=%fused_computation | convolution fusion | flops 1073741824 | bytes 6291456 | tf_op jit(solution)/shard_map/dot_general | solution.py:125
  163.5 1.5 collective-permute-start.6
  165.0 1.5 collective-permute-start.7
  168.7 2.8 %collective-permute-done.7 = f32[32,1024]{1,0:T(8,128)S(1)} collective-permute-done((f32[32,1024]{1,0:T(8,128)S(1)}, f32[32,1024]{1,0:T(8,128)S(1)}, u32[]{:S(2)}, u32[]{:S(2)}) %collective-permute-start.7) | collective-permute-done | bytes 131104 | tf_op jit(solution)/shard_map/ppermute | solution.py:78
  171.6 4.0 %collective-permute-done.8 = f32[2,32,1024]{2,1,0:T(8,128)S(1)} collective-permute-done((f32[2,32,1024]{2,1,0:T(8,128)S(1)}, f32[2,32,1024]{2,1,0:T(8,128)S(1)}, u32[]{:S(2)}, u32[]{:S(2)}) %collective-permute-start.8) | collective-permute-done | bytes 262176 | tf_op jit(solution)/shard_map/ppermute | solution.py:78
  176.3 5.3 %collective-permute-done.9 = f32[32,1024]{1,0:T(8,128)S(1)} collective-permute-done((f32[32,1024]{1,0:T(8,128)S(1)}, f32[32,1024]{1,0:T(8,128)S(1)}, u32[]{:S(2)}, u32[]{:S(2)}) %collective-permute-start.9) | collective-permute-done | bytes 131104 | tf_op jit(solution)/shard_map/ppermute | solution.py:78
  181.6 1.5 collective-permute-start.11
  183.1 3.6 %collective-permute-done.11 = f32[32,1024]{1,0:T(8,128)S(1)} collective-permute-done((f32[32,1024]{1,0:T(8,128)S(1)}, f32[32,1024]{1,0:T(8,128)S(1)}, u32[]{:S(2)}, u32[]{:S(2)}) %collective-permute-start.11) | collective-permute-done | bytes 131104 | tf_op jit(solution)/shard_map/ppermute | solution.py:78
  186.9 1.5 collective-permute-start.13
  190.0 1.6 collective-permute-start.22
  191.6 4.6 %collective-permute-done.13 = f32[2,32,1024]{2,1,0:T(8,128)S(1)} collective-permute-done((f32[2,32,1024]{2,1,0:T(8,128)S(1)}, f32[2,32,1024]{2,1,0:T(8,128)S(1)}, u32[]{:S(2)}, u32[]{:S(2)}) %collective-permute-start.13) | collective-permute-done | bytes 262176 | tf_op jit(solution)/shard_map/ppermute | solution.py:78
  198.6 2.5 %collective-permute-done.19 = f32[2,32,1024]{2,1,0:T(8,128)S(1)} collective-permute-done((f32[2,32,1024]{2,1,0:T(8,128)S(1)}, f32[2,32,1024]{2,1,0:T(8,128)S(1)}, u32[]{:S(2)}, u32[]{:S(2)}) %collective-permute-start.19) | collective-permute-done | bytes 262176 | tf_op jit(solution)/shard_map/ppermute | solution.py:78
  201.7 1.8 collective-permute-done.22
  206.6 1.9 collective-permute-done.23
  (121 shorter events, 20.1 us)
Async XLA Ops:
  6.5 11.6 %copy-start.5 = (s32[1,32,2]{1,2,0:T(2,128)S(1)}, s32[1,32,2]{1,2,0:T(2,128)}, u32[]{:S(2)}) copy-start(s32[1,32,2]{1,2,0:T(2,128)} %param.7) | copy-start | bytes 772
  6.5 11.8 %copy-start.7 = (s32[1,32]{1,0:T(1,128)S(1)}, s32[1,32]{1,0:T(1,128)}, u32[]{:S(2)}) copy-start(s32[1,32]{1,0:T(1,128)} %param.9) | copy-start | bytes 388
  6.5 12.0 %copy-start.6 = (s32[1,32,2]{1,2,0:T(2,128)S(1)}, s32[1,32,2]{1,2,0:T(2,128)}, u32[]{:S(2)}) copy-start(s32[1,32,2]{1,2,0:T(2,128)} %param.8) | copy-start | bytes 772
  6.5 97.2 %all-gather.11.cloned.1.call-start = ((), (), s32[]{:S(2)}) async-start(), calls=%async_computation.4 | async-start | bytes 1310720 | tf_op jit(solution)/shard_map/all_gather | solution.py:109
  8.8 83.5 %all-to-all-start = ((bf16[64,128,128]{2,1,0:T(8,128)(2,1)}), bf16[64,128,128]{2,1,0:T(8,128)(2,1)S(1)}, u32[]{:S(2)}, u32[]{:S(2)}) async-start(bf16[64,128,128]{2,1,0:T(8,128)(2,1)} %param.6), calls=%async_computation | async-start | bytes 4194304 | tf_op jit(solution)/shard_map/all_to_all | solution.py:90
  16.1 95.4 %all-gather.9.cloned.1.call-start = ((), (), s32[]{:S(2)}) async-start(), calls=%async_computation.3 | async-start | bytes 1310720 | tf_op jit(solution)/shard_map/all_gather | solution.py:109
  16.8 110.3 %all-gather.7.cloned.1.call-start = ((), (), s32[]{:S(2)}) async-start(), calls=%async_computation.2 | async-start | bytes 1310720 | tf_op jit(solution)/shard_map/all_gather | solution.py:109
  17.6 138.5 %all-gather.5.cloned.1.call-start = ((), (), s32[]{:S(2)}) async-start(), calls=%async_computation.1 | async-start | bytes 1310720 | tf_op jit(solution)/shard_map/all_gather | solution.py:109
  111.5 10.0 %collective-permute-start.1 = (f32[2,2,32,1024]{3,2,1,0:T(8,128)S(1)}, f32[2,2,32,1024]{3,2,1,0:T(8,128)S(1)}, u32[]{:S(2)}, u32[]{:S(2)}) collective-permute-start(f32[2,2,32,1024]{3,2,1,0:T(8,128)S(1)} %dynamic-slice_bitcast_fusion.6), channel_id=1, source_target_pairs={{0,1},{1,0},{2,3},{3,2},{4,5},{5,4},{6,7},{7,6},{8,9},{9,8},{10,11... | collective-permute-start | bytes 1572872 | tf_op jit(solution)/shard_map/ppermute | solution.py:78
  111.7 9.9 %collective-permute-start = (f32[2,2,32,1024]{3,2,1,0:T(8,128)S(1)}, f32[2,2,32,1024]{3,2,1,0:T(8,128)S(1)}, u32[]{:S(2)}, u32[]{:S(2)}) collective-permute-start(f32[2,2,32,1024]{3,2,1,0:T(8,128)S(1)} %dynamic-slice_bitcast_fusion.7), channel_id=1, source_target_pairs={{0,1},{1,0},{2,3},{3,2},{4,5},{5,4},{6,7},{7,6},{8,9},{9,8},{10,11... | collective-permute-start | bytes 1572872 | tf_op jit(solution)/shard_map/ppermute | solution.py:78
  134.6 8.0 %collective-permute-start.3 = (f32[2,32,1024]{2,1,0:T(8,128)S(1)}, f32[2,32,1024]{2,1,0:T(8,128)S(1)}, u32[]{:S(2)}, u32[]{:S(2)}) collective-permute-start(f32[2,32,1024]{2,1,0:T(8,128)S(1)} %dynamic-slice_bitcast_fusion.14), channel_id=1, source_target_pairs={{0,4},{1,5},{2,6},{3,7},{4,0},{5,1},{6,2},{7,3},{8,12},{9,13},{10,... | collective-permute-start | bytes 786440 | tf_op jit(solution)/shard_map/ppermute | solution.py:78
  136.2 9.6 %collective-permute-start.5 = (f32[2,2,32,1024]{3,2,1,0:T(8,128)S(1)}, f32[2,2,32,1024]{3,2,1,0:T(8,128)S(1)}, u32[]{:S(2)}, u32[]{:S(2)}) collective-permute-start(f32[2,2,32,1024]{3,2,1,0:T(8,128)S(1)} %dynamic-slice_bitcast_fusion.4), channel_id=1, source_target_pairs={{0,1},{1,0},{2,3},{3,2},{4,5},{5,4},{6,7},{7,6},{8,9},{9,8},{10,11... | collective-permute-start | bytes 1572872 | tf_op jit(solution)/shard_map/ppermute | solution.py:78
  136.3 8.8 %collective-permute-start.2 = (f32[2,32,1024]{2,1,0:T(8,128)S(1)}, f32[2,32,1024]{2,1,0:T(8,128)S(1)}, u32[]{:S(2)}, u32[]{:S(2)}) collective-permute-start(f32[2,32,1024]{2,1,0:T(8,128)S(1)} %dynamic-slice_bitcast_fusion.15), channel_id=1, source_target_pairs={{0,2},{1,3},{2,0},{3,1},{4,6},{5,7},{6,4},{7,5},{8,10},{9,11},{10,... | collective-permute-start | bytes 786440 | tf_op jit(solution)/shard_map/ppermute | solution.py:78
  138.0 7.9 %collective-permute-start.4 = (f32[2,2,32,1024]{3,2,1,0:T(8,128)S(1)}, f32[2,2,32,1024]{3,2,1,0:T(8,128)S(1)}, u32[]{:S(2)}, u32[]{:S(2)}) collective-permute-start(f32[2,2,32,1024]{3,2,1,0:T(8,128)S(1)} %dynamic-slice_bitcast_fusion.5), channel_id=1, source_target_pairs={{0,1},{1,0},{2,3},{3,2},{4,5},{5,4},{6,7},{7,6},{8,9},{9,8},{10,11... | collective-permute-start | bytes 1572872 | tf_op jit(solution)/shard_map/ppermute | solution.py:78
  163.5 5.2 %collective-permute-start.6 = (f32[32,1024]{1,0:T(8,128)S(1)}, f32[32,1024]{1,0:T(8,128)S(1)}, u32[]{:S(2)}, u32[]{:S(2)}) collective-permute-start(f32[32,1024]{1,0:T(8,128)S(1)} %dynamic-slice_bitcast_fusion.23), channel_id=1, source_target_pairs={{0,4},{1,5},{2,6},{3,7},{4,0},{5,1},{6,2},{7,3},{8,12},{9,13},{10,... | collective-permute-start | bytes 393224 | tf_op jit(solution)/shard_map/ppermute | solution.py:78
  165.0 6.5 %collective-permute-start.7 = (f32[32,1024]{1,0:T(8,128)S(1)}, f32[32,1024]{1,0:T(8,128)S(1)}, u32[]{:S(2)}, u32[]{:S(2)}) collective-permute-start(f32[32,1024]{1,0:T(8,128)S(1)} %dynamic-slice_bitcast_fusion.22), channel_id=1, source_target_pairs={{0,2},{1,3},{2,0},{3,1},{4,6},{5,7},{6,4},{7,5},{8,10},{9,11},{10,... | collective-permute-start | bytes 393224 | tf_op jit(solution)/shard_map/ppermute | solution.py:78
  166.6 9.0 %collective-permute-start.8 = (f32[2,32,1024]{2,1,0:T(8,128)S(1)}, f32[2,32,1024]{2,1,0:T(8,128)S(1)}, u32[]{:S(2)}, u32[]{:S(2)}) collective-permute-start(f32[2,32,1024]{2,1,0:T(8,128)S(1)} %dynamic-slice_bitcast_fusion.13), channel_id=1, source_target_pairs={{0,2},{1,3},{2,0},{3,1},{4,6},{5,7},{6,4},{7,5},{8,10},{9,11},{10,... | collective-permute-start | bytes 786440 | tf_op jit(solution)/shard_map/ppermute | solution.py:78
  167.2 8.4 %collective-permute-start.10 = (f32[2,32,1024]{2,1,0:T(8,128)S(1)}, f32[2,32,1024]{2,1,0:T(8,128)S(1)}, u32[]{:S(2)}, u32[]{:S(2)}) collective-permute-start(f32[2,32,1024]{2,1,0:T(8,128)S(1)} %dynamic-slice_bitcast_fusion.12), channel_id=1, source_target_pairs={{0,4},{1,5},{2,6},{3,7},{4,0},{5,1},{6,2},{7,3},{8,12},{9,13},{10,... | collective-permute-start | bytes 786440 | tf_op jit(solution)/shard_map/ppermute | solution.py:78
  167.9 18.8 %collective-permute-start.12 = (f32[2,2,32,1024]{3,2,1,0:T(8,128)S(1)}, f32[2,2,32,1024]{3,2,1,0:T(8,128)S(1)}, u32[]{:S(2)}, u32[]{:S(2)}) collective-permute-start(f32[2,2,32,1024]{3,2,1,0:T(8,128)S(1)} %dynamic-slice_bitcast_fusion.3), channel_id=1, source_target_pairs={{0,1},{1,0},{2,3},{3,2},{4,5},{5,4},{6,7},{7,6},{8,9},{9,8},{10,11... | collective-permute-start | bytes 1572872 | tf_op jit(solution)/shard_map/ppermute | solution.py:78
  168.7 19.7 %collective-permute-start.15 = (f32[2,2,32,1024]{3,2,1,0:T(8,128)S(1)}, f32[2,2,32,1024]{3,2,1,0:T(8,128)S(1)}, u32[]{:S(2)}, u32[]{:S(2)}) collective-permute-start(f32[2,2,32,1024]{3,2,1,0:T(8,128)S(1)} %dynamic-slice_bitcast_fusion.2), channel_id=1, source_target_pairs={{0,1},{1,0},{2,3},{3,2},{4,5},{5,4},{6,7},{7,6},{8,9},{9,8},{10,11... | collective-permute-start | bytes 1572872 | tf_op jit(solution)/shard_map/ppermute | solution.py:78
  171.5 17.6 %collective-permute-start.18 = (f32[2,2,32,1024]{3,2,1,0:T(8,128)S(1)}, f32[2,2,32,1024]{3,2,1,0:T(8,128)S(1)}, u32[]{:S(2)}, u32[]{:S(2)}) collective-permute-start(f32[2,2,32,1024]{3,2,1,0:T(8,128)S(1)} %dynamic-slice_bitcast_fusion.1), channel_id=1, source_target_pairs={{0,1},{1,0},{2,3},{3,2},{4,5},{5,4},{6,7},{7,6},{8,9},{9,8},{10,11... | collective-permute-start | bytes 1572872 | tf_op jit(solution)/shard_map/ppermute | solution.py:78
  175.6 14.3 %collective-permute-start.21 = (f32[2,2,32,1024]{3,2,1,0:T(8,128)S(1)}, f32[2,2,32,1024]{3,2,1,0:T(8,128)S(1)}, u32[]{:S(2)}, u32[]{:S(2)}) collective-permute-start(f32[2,2,32,1024]{3,2,1,0:T(8,128)S(1)} %dynamic-slice_bitcast_fusion), channel_id=1, source_target_pairs={{0,1},{1,0},{2,3},{3,2},{4,5},{5,4},{6,7},{7,6},{8,9},{9,8},{10,11... | collective-permute-start | bytes 1572872 | tf_op jit(solution)/shard_map/ppermute | solution.py:78
  175.6 6.0 %collective-permute-start.9 = (f32[32,1024]{1,0:T(8,128)S(1)}, f32[32,1024]{1,0:T(8,128)S(1)}, u32[]{:S(2)}, u32[]{:S(2)}) collective-permute-start(f32[32,1024]{1,0:T(8,128)S(1)} %dynamic-slice_bitcast_fusion.21), channel_id=1, source_target_pairs={{0,4},{1,5},{2,6},{3,7},{4,0},{5,1},{6,2},{7,3},{8,12},{9,13},{10,... | collective-permute-start | bytes 393224 | tf_op jit(solution)/shard_map/ppermute | solution.py:78
  181.6 5.1 %collective-permute-start.11 = (f32[32,1024]{1,0:T(8,128)S(1)}, f32[32,1024]{1,0:T(8,128)S(1)}, u32[]{:S(2)}, u32[]{:S(2)}) collective-permute-start(f32[32,1024]{1,0:T(8,128)S(1)} %dynamic-slice_bitcast_fusion.20), channel_id=1, source_target_pairs={{0,2},{1,3},{2,0},{3,1},{4,6},{5,7},{6,4},{7,5},{8,10},{9,11},{10,... | collective-permute-start | bytes 393224 | tf_op jit(solution)/shard_map/ppermute | solution.py:78
  186.9 9.3 %collective-permute-start.13 = (f32[2,32,1024]{2,1,0:T(8,128)S(1)}, f32[2,32,1024]{2,1,0:T(8,128)S(1)}, u32[]{:S(2)}, u32[]{:S(2)}) collective-permute-start(f32[2,32,1024]{2,1,0:T(8,128)S(1)} %dynamic-slice_bitcast_fusion.11), channel_id=1, source_target_pairs={{0,2},{1,3},{2,0},{3,1},{4,6},{5,7},{6,4},{7,5},{8,10},{9,11},{10,... | collective-permute-start | bytes 786440 | tf_op jit(solution)/shard_map/ppermute | solution.py:78
  188.5 9.3 %collective-permute-start.16 = (f32[2,32,1024]{2,1,0:T(8,128)S(1)}, f32[2,32,1024]{2,1,0:T(8,128)S(1)}, u32[]{:S(2)}, u32[]{:S(2)}) collective-permute-start(f32[2,32,1024]{2,1,0:T(8,128)S(1)} %dynamic-slice_bitcast_fusion.10), channel_id=1, source_target_pairs={{0,4},{1,5},{2,6},{3,7},{4,0},{5,1},{6,2},{7,3},{8,12},{9,13},{10,... | collective-permute-start | bytes 786440 | tf_op jit(solution)/shard_map/ppermute | solution.py:78
  189.3 11.7 %collective-permute-start.19 = (f32[2,32,1024]{2,1,0:T(8,128)S(1)}, f32[2,32,1024]{2,1,0:T(8,128)S(1)}, u32[]{:S(2)}, u32[]{:S(2)}) collective-permute-start(f32[2,32,1024]{2,1,0:T(8,128)S(1)} %dynamic-slice_bitcast_fusion.9), channel_id=1, source_target_pairs={{0,2},{1,3},{2,0},{3,1},{4,6},{5,7},{6,4},{7,5},{8,10},{9,11},{10,... | collective-permute-start | bytes 786440 | tf_op jit(solution)/shard_map/ppermute | solution.py:78
  190.0 13.4 %collective-permute-start.22 = (f32[2,32,1024]{2,1,0:T(8,128)S(1)}, f32[2,32,1024]{2,1,0:T(8,128)S(1)}, u32[]{:S(2)}, u32[]{:S(2)}) collective-permute-start(f32[2,32,1024]{2,1,0:T(8,128)S(1)} %dynamic-slice_bitcast_fusion.8), channel_id=1, source_target_pairs={{0,4},{1,5},{2,6},{3,7},{4,0},{5,1},{6,2},{7,3},{8,12},{9,13},{10,... | collective-permute-start | bytes 786440 | tf_op jit(solution)/shard_map/ppermute | solution.py:78
  196.2 8.9 %collective-permute-start.14 = (f32[32,1024]{1,0:T(8,128)S(1)}, f32[32,1024]{1,0:T(8,128)S(1)}, u32[]{:S(2)}, u32[]{:S(2)}) collective-permute-start(f32[32,1024]{1,0:T(8,128)S(1)} %dynamic-slice_bitcast_fusion.19), channel_id=1, source_target_pairs={{0,4},{1,5},{2,6},{3,7},{4,0},{5,1},{6,2},{7,3},{8,12},{9,13},{10,... | collective-permute-start | bytes 393224 | tf_op jit(solution)/shard_map/ppermute | solution.py:78
  197.9 7.3 %collective-permute-start.17 = (f32[32,1024]{1,0:T(8,128)S(1)}, f32[32,1024]{1,0:T(8,128)S(1)}, u32[]{:S(2)}, u32[]{:S(2)}) collective-permute-start(f32[32,1024]{1,0:T(8,128)S(1)} %dynamic-slice_bitcast_fusion.18), channel_id=1, source_target_pairs={{0,2},{1,3},{2,0},{3,1},{4,6},{5,7},{6,4},{7,5},{8,10},{9,11},{10,... | collective-permute-start | bytes 393224 | tf_op jit(solution)/shard_map/ppermute | solution.py:78
  201.1 5.5 %collective-permute-start.20 = (f32[32,1024]{1,0:T(8,128)S(1)}, f32[32,1024]{1,0:T(8,128)S(1)}, u32[]{:S(2)}, u32[]{:S(2)}) collective-permute-start(f32[32,1024]{1,0:T(8,128)S(1)} %dynamic-slice_bitcast_fusion.17), channel_id=1, source_target_pairs={{0,4},{1,5},{2,6},{3,7},{4,0},{5,1},{6,2},{7,3},{8,12},{9,13},{10,... | collective-permute-start | bytes 393224 | tf_op jit(solution)/shard_map/ppermute | solution.py:78
  203.5 5.0 %collective-permute-start.23 = (f32[32,1024]{1,0:T(8,128)S(1)}, f32[32,1024]{1,0:T(8,128)S(1)}, u32[]{:S(2)}, u32[]{:S(2)}) collective-permute-start(f32[32,1024]{1,0:T(8,128)S(1)} %dynamic-slice_bitcast_fusion.16), channel_id=1, source_target_pairs={{0,2},{1,3},{2,0},{3,1},{4,6},{5,7},{6,4},{7,5},{8,10},{9,11},{10,... | collective-permute-start | bytes 393224 | tf_op jit(solution)/shard_map/ppermute | solution.py:78
  (8 other events, 34.8 us)
Sparse Core Ops, SparseCore 0:
  8.9 57.0 all-gather.10
  67.6 31.2 all-gather.8
  100.5 26.6 all-gather.6
  128.5 27.5 all-gather.4

commit v16 on v4

--- a/solution.py
+++ b/solution.py
@@ -27,7 +27,7 @@
     step = pl.program_id(0)
     tile = tiles_ref.shape[-1]
     groups, part, width = amp_ref.shape
-    per_step = out_ref.shape[1] // tile
+    per_step = out_ref.shape[-1] // tile
     weight_ref[...] = jnp.zeros(weight_ref.shape, weight_ref.dtype)
     first = step * per_step
 
@@ -47,7 +47,8 @@
     groups, part, width = amp3.shape
     rows = groups * part
     n, tile, _ = tiles.shape
-    per_step = 2 if ab_count % 2 == 0 else 1
+    per_step = 4 if ab_count % 8 == 0 else 1
+    steps_per_half = ab_count // (2 * per_step)
     cost = pl.CostEstimate(
         flops=2 * rows * width * ab_count * tile,
         transcendentals=0,
@@ -60,13 +61,15 @@
             pl.BlockSpec((groups, part, width), lambda j, *_: (0, 0, 0)),
             pl.BlockSpec((n, tile, tile), lambda j, *_: (0, 0, 0)),
         ],
-        out_specs=pl.BlockSpec((rows, per_step * tile), lambda j, *_: (0, j)),
+        out_specs=pl.BlockSpec(
+            (None, rows, per_step * tile), lambda j, *_: (j // steps_per_half, 0, j % steps_per_half)
+        ),
         scratch_shapes=[pltpu.VMEM((width, per_step * tile), tiles.dtype)],
     )
     return pl.pallas_call(
         _ladder_kernel,
         grid_spec=grid_spec,
-        out_shape=jax.ShapeDtypeStruct((rows, ab_count * tile), jnp.float32),
+        out_shape=jax.ShapeDtypeStruct((2, rows, ab_count * tile // 2), jnp.float32),
         cost_estimate=cost,
     )(order, starts, ab_ids, cd_ids, amp3, tiles)
 
@@ -128,10 +131,7 @@
         else:
             amp3 = gathered[chunk]
         partial = _ladder_products(amp3, received, order, starts, ab_ids, cd_ids, AB_DEV)
-        half = partial.shape[1] // 2
-        flows.extend(
-            _Halving(partial[:, h * half:(h + 1) * half], orders[h], rep_count) for h in range(2)
-        )
+        flows.extend(_Halving(partial[h], orders[h], rep_count) for h in range(2))
     while any(flow.todo for flow in flows):
         for flow in flows:
             flow.advance(rep_index)

time: 201 us -> 200 us (level)
  Pallas kernels: 34.2 us -> 29.4 us
  waiting for transfers between devices: 109 us -> 113 us
    pallas_call x4, Pallas kernels: 34.2 us -> 29.4 us  [_ladder_products(): pl.pallas_call(_ladder_kernel, grid_spec=grid_spec, out_shape=jax.ShapeDt...]
    all_gather x4, waiting for transfers between devices: 68.9 us -> 72.1 us  [on_device(): lax.all_gather(local4[:, c], 'own', axis=0, tiled=True)]
  transfers between devices with their start and end apart: 29 -> 29, of which waited for: 16 -> 16; matrix products, arithmetic and copies ran while one was open for 7% -> 7% of each run, Pallas kernels for 17% -> 15%
where the time goes in v16:
time: 200 us; the launch traced here: 199 us
  waiting for transfers between devices  113 us (56%)
  Pallas kernels  29.4 us (15%)
  starting transfers between devices  27.4 us (14%)
  between operations  13.6 us (7%)
  local copies, waits for them, and re-layouts  11.7 us (6%)
  other arithmetic  4.69 us (2%)
    all_gather x4, waiting for transfers between devices, on_device(): lax.all_gather(local4[:, c], 'own', axis=0, tiled=True)  72.1 us
    ppermute x24, waiting for transfers between devices, advance(): self.x = keep + lax.ppermute(send, 'rep', perm=pairs)  30.7 us
    pallas_call x4, Pallas kernels, _ladder_products(): pl.pallas_call(_ladder_kernel, grid_spec=grid_spec, out_shape=jax.ShapeDt...  29.4 us
    ppermute x24, starting transfers between devices, advance(): self.x = keep + lax.ppermute(send, 'rep', perm=pairs)  19.9 us
    all_to_all x1, waiting for transfers between devices, on_device(): lax.all_to_all(integrals, ('own', 'rep'), split_axis=0, concat_axis=0, ti...  8.25 us
    all_to_all x1, starting transfers between devices, on_device(): lax.all_to_all(integrals, ('own', 'rep'), split_axis=0, concat_axis=0, ti...  7.3 us
    slice x4, local copies, waits for them, and re-layouts, on_device(): flows.extend((_Halving(partial[h], orders[h], rep_count) for h in range(2)))  6.89 us
  transfers between devices with their start and end apart: 29, of which 16 were waited for; matrix products, arithmetic and copies ran while one was open for 7% of the time, Pallas kernels for 15%

profile of v16, /device:TPU:0, one launch (start us, length us, event | category | flops | bytes accessed | tf_op | source)
XLA Modules:
  0.0 199.4 jit_solution(11198950197592319258)
XLA Ops:
  6.5 7.3 %all-to-all-start = ((bf16[64,128,128]{2,1,0:T(8,128)(2,1)}), bf16[64,128,128]{2,1,0:T(8,128)(2,1)S(1)}, u32[]{:S(2)}, u32[]{:S(2)}) async-start(bf16[64,128,128]{2,1,0:T(8,128)(2,1)} %param.6), calls=%async_computation | async-start | bytes 4194304 | tf_op jit(solution)/shard_map/all_to_all | solution.py:108
  19.2 52.0 %all-gather.15.cloned.1.call-done = bf16[8,1,32,2048]{3,2,1,0:T(8,128)(2,1)} async-done(((bf16[2,1,32,2048]{3,2,1,0:T(8,128)(2,1)}), bf16[8,1,32,2048]{3,2,1,0:T(8,128)(2,1)}) %all-gather.15.cloned.1.call-update) | async-done | bytes 1048592 | tf_op jit(solution)/shard_map/all_gather | solution.py:122
  71.2 8.2 %all-to-all-done.tiles_ref = bf16[64,128,128]{2,1,0:T(8,128)(2,1)S(1)} async-done(((bf16[64,128,128]{2,1,0:T(8,128)(2,1)}), bf16[64,128,128]{2,1,0:T(8,128)(2,1)S(1)}, u32[]{:S(2)}, u32[]{:S(2)}) %all-to-all-start) | async-done | bytes 2097184 | tf_op jit(solution)/shard_map/all_to_all | solution.py:108
  79.4 1.4 copy-done
  80.8 7.4 %shard_map.55 = f32[2,256,1024]{2,1,0:T(8,128)} custom-call(s32[64]{0:T(128)} %select_reduce_fusion.order_ref, s32[17]{0:T(128)} %convert_reduce_fusion.1.starts_ref, s32[64]{0:T(128)} %copy-done.5, s32[64]{0:T(128)} %reshape.46.cd_ref, bf16[8,32,2048]{2,1,0:T(8,128)(2,1)} %bitcast.131, bf16[64,128,128]{2,1,0:T(8,128)(2,1)} %copy-done), custom_call_target="tpu_custom_call" | custom-call | flops 2147483648 | bytes 5242880 | tf_op jit(solution)/shard_map/pallas_call | solution.py:69
  88.1 1.7 fusion.5
  93.2 5.2 %all-gather.13.cloned.1.call-done = bf16[8,1,32,2048]{3,2,1,0:T(8,128)(2,1)} async-done(((bf16[2,1,32,2048]{3,2,1,0:T(8,128)(2,1)}), bf16[8,1,32,2048]{3,2,1,0:T(8,128)(2,1)}) %all-gather.13.cloned.1.call-update) | async-done | bytes 1048592 | tf_op jit(solution)/shard_map/all_gather | solution.py:122
  98.4 7.4 %shard_map.56 = f32[2,256,1024]{2,1,0:T(8,128)} custom-call(s32[64]{0:T(128)} %select_reduce_fusion.order_ref, s32[17]{0:T(128)} %convert_reduce_fusion.1.starts_ref, s32[64]{0:T(128)} %copy-done.5, s32[64]{0:T(128)} %reshape.46.cd_ref, bf16[8,32,2048]{2,1,0:T(8,128)(2,1)} %bitcast.130, bf16[64,128,128]{2,1,0:T(8,128)(2,1)} %copy-done), custom_call_target="tpu_custom_call" | custom-call | flops 2147483648 | bytes 5242880 | tf_op jit(solution)/shard_map/pallas_call | solution.py:69
  105.8 1.8 fusion.4
  107.6 1.5 collective-permute-start.3
  109.3 1.5 collective-permute-start.2
  111.1 4.5 %collective-permute-done.3 = f32[2,32,1024]{2,1,0:T(8,128)S(1)} collective-permute-done((f32[2,32,1024]{2,1,0:T(8,128)S(1)}, f32[2,32,1024]{2,1,0:T(8,128)S(1)}, u32[]{:S(2)}, u32[]{:S(2)}) %collective-permute-start.3) | collective-permute-done | bytes 262176 | tf_op jit(solution)/shard_map/ppermute | solution.py:96
  115.6 2.4 %collective-permute-done.2 = f32[2,32,1024]{2,1,0:T(8,128)S(1)} collective-permute-done((f32[2,32,1024]{2,1,0:T(8,128)S(1)}, f32[2,32,1024]{2,1,0:T(8,128)S(1)}, u32[]{:S(2)}, u32[]{:S(2)}) %collective-permute-start.2) | collective-permute-done | bytes 262176 | tf_op jit(solution)/shard_map/ppermute | solution.py:96
  118.3 9.2 %all-gather.11.cloned.1.call-done = bf16[8,1,32,2048]{3,2,1,0:T(8,128)(2,1)} async-done(((bf16[2,1,32,2048]{3,2,1,0:T(8,128)(2,1)}), bf16[8,1,32,2048]{3,2,1,0:T(8,128)(2,1)}) %all-gather.11.cloned.1.call-update) | async-done | bytes 1048592 | tf_op jit(solution)/shard_map/all_gather | solution.py:122
  127.5 7.4 %shard_map.57 = f32[2,256,1024]{2,1,0:T(8,128)} custom-call(s32[64]{0:T(128)} %select_reduce_fusion.order_ref, s32[17]{0:T(128)} %convert_reduce_fusion.1.starts_ref, s32[64]{0:T(128)} %copy-done.5, s32[64]{0:T(128)} %reshape.46.cd_ref, bf16[8,32,2048]{2,1,0:T(8,128)(2,1)} %bitcast.129, bf16[64,128,128]{2,1,0:T(8,128)(2,1)} %copy-done), custom_call_target="tpu_custom_call" | custom-call | flops 2147483648 | bytes 5242880 | tf_op jit(solution)/shard_map/pallas_call | solution.py:69
  134.8 1.8 fusion.3
  137.3 1.5 collective-permute-start.9
  138.9 1.5 collective-permute-start.7
  141.1 4.3 %collective-permute-done.7 = f32[32,1024]{1,0:T(8,128)S(1)} collective-permute-done((f32[32,1024]{1,0:T(8,128)S(1)}, f32[32,1024]{1,0:T(8,128)S(1)}, u32[]{:S(2)}, u32[]{:S(2)}) %collective-permute-start.7) | collective-permute-done | bytes 131104 | tf_op jit(solution)/shard_map/ppermute | solution.py:96
  145.9 4.4 %collective-permute-done.6 = f32[32,1024]{1,0:T(8,128)S(1)} collective-permute-done((f32[32,1024]{1,0:T(8,128)S(1)}, f32[32,1024]{1,0:T(8,128)S(1)}, u32[]{:S(2)}, u32[]{:S(2)}) %collective-permute-start.6) | collective-permute-done | bytes 131104 | tf_op jit(solution)/shard_map/ppermute | solution.py:96
  150.6 5.7 %all-gather.9.cloned.1.call-done = bf16[8,1,32,2048]{3,2,1,0:T(8,128)(2,1)} async-done(((bf16[2,1,32,2048]{3,2,1,0:T(8,128)(2,1)}), bf16[8,1,32,2048]{3,2,1,0:T(8,128)(2,1)}) %all-gather.9.cloned.1.call-update) | async-done | bytes 1048592 | tf_op jit(solution)/shard_map/all_gather | solution.py:122
  156.4 1.5 collective-permute-start.12
  157.9 1.5 collective-permute-start.13
  160.8 7.4 %shard_map.58 = f32[2,256,1024]{2,1,0:T(8,128)} custom-call(s32[64]{0:T(128)} %select_reduce_fusion.order_ref, s32[17]{0:T(128)} %convert_reduce_fusion.1.starts_ref, s32[64]{0:T(128)} %copy-done.5, s32[64]{0:T(128)} %reshape.46.cd_ref, bf16[8,32,2048]{2,1,0:T(8,128)(2,1)} %bitcast.128, bf16[64,128,128]{2,1,0:T(8,128)(2,1)} %copy-done), custom_call_target="tpu_custom_call" | custom-call | flops 2147483648 | bytes 5242880 | tf_op jit(solution)/shard_map/pallas_call | solution.py:69
  168.1 1.7 fusion.2
  170.7 1.5 collective-permute-start.15
  172.2 1.5 collective-permute-start.17
  173.7 2.4 %collective-permute-done.15 = f32[32,1024]{1,0:T(8,128)S(1)} collective-permute-done((f32[32,1024]{1,0:T(8,128)S(1)}, f32[32,1024]{1,0:T(8,128)S(1)}, u32[]{:S(2)}, u32[]{:S(2)}) %collective-permute-start.15) | collective-permute-done | bytes 131104 | tf_op jit(solution)/shard_map/ppermute | solution.py:96
  177.6 1.5 collective-permute-start.19
  179.9 4.8 %collective-permute-done.19 = f32[2,32,1024]{2,1,0:T(8,128)S(1)} collective-permute-done((f32[2,32,1024]{2,1,0:T(8,128)S(1)}, f32[2,32,1024]{2,1,0:T(8,128)S(1)}, u32[]{:S(2)}, u32[]{:S(2)}) %collective-permute-start.19) | collective-permute-done | bytes 262176 | tf_op jit(solution)/shard_map/ppermute | solution.py:96
  187.1 2.8 %collective-permute-done.20 = f32[32,1024]{1,0:T(8,128)S(1)} collective-permute-done((f32[32,1024]{1,0:T(8,128)S(1)}, f32[32,1024]{1,0:T(8,128)S(1)}, u32[]{:S(2)}, u32[]{:S(2)}) %collective-permute-start.20) | collective-permute-done | bytes 131104 | tf_op jit(solution)/shard_map/ppermute | solution.py:96
  189.9 1.9 collective-permute-done.23
  (110 shorter events, 19.3 us)
Async XLA Ops:
  6.5 7.4 %copy-start.1 = (bf16[256,2048]{1,0:T(8,128)(2,1)S(1)}, bf16[256,2048]{1,0:T(8,128)(2,1)}, u32[]{:S(2)}) copy-start(bf16[256,2048]{1,0:T(8,128)(2,1)} %param.5) | copy-start | bytes 3145732
  6.5 72.9 %all-to-all-start = ((bf16[64,128,128]{2,1,0:T(8,128)(2,1)}), bf16[64,128,128]{2,1,0:T(8,128)(2,1)S(1)}, u32[]{:S(2)}, u32[]{:S(2)}) async-start(bf16[64,128,128]{2,1,0:T(8,128)(2,1)} %param.6), calls=%async_computation | async-start | bytes 4194304 | tf_op jit(solution)/shard_map/all_to_all | solution.py:108
  13.9 3.0 %copy-start.3 = (s32[1,32,2]{1,2,0:T(2,128)S(1)}, s32[1,32,2]{1,2,0:T(2,128)}, u32[]{:S(2)}) copy-start(s32[1,32,2]{1,2,0:T(2,128)} %param.8) | copy-start | bytes 772
  13.9 57.3 %all-gather.15.cloned.1.call-start = ((), (), s32[]{:S(2)}) async-start(), calls=%async_computation.4 | async-start | bytes 1310720 | tf_op jit(solution)/shard_map/all_gather | solution.py:122
  14.9 83.5 %all-gather.13.cloned.1.call-start = ((), (), s32[]{:S(2)}) async-start(), calls=%async_computation.3 | async-start | bytes 1310720 | tf_op jit(solution)/shard_map/all_gather | solution.py:122
  15.7 111.8 %all-gather.11.cloned.1.call-start = ((), (), s32[]{:S(2)}) async-start(), calls=%async_computation.2 | async-start | bytes 1310720 | tf_op jit(solution)/shard_map/all_gather | solution.py:122
  16.4 139.9 %all-gather.9.cloned.1.call-start = ((), (), s32[]{:S(2)}) async-start(), calls=%async_computation.1 | async-start | bytes 1310720 | tf_op jit(solution)/shard_map/all_gather | solution.py:122
  16.7 62.7 %copy-start.5 = (s32[64]{0:T(128)}, s32[64]{0:T(128)S(1)}, u32[]{:S(2)}) copy-start(s32[64]{0:T(128)S(1)} %reshape.45.ab_ref) | copy-start | bytes 772
  89.9 2.1 %collective-permute-start.1 = (f32[2,2,32,1024]{3,2,1,0:T(8,128)S(1)}, f32[2,2,32,1024]{3,2,1,0:T(8,128)}, u32[]{:S(2)}, u32[]{:S(2)}) collective-permute-start(f32[2,2,32,1024]{3,2,1,0:T(8,128)S(1)} %dynamic-slice_bitcast_fusion.6), channel_id=1, source_target_pairs={{0,1},{1,0},{2,3},{3,2},{4,5},{5,4},{6,7},{7,6},{8,9},{9,8},{10,11... | collective-permute-start | bytes 1572872 | tf_op jit(solution)/shard_map/ppermute | solution.py:96
  90.8 2.3 %collective-permute-start = (f32[2,2,32,1024]{3,2,1,0:T(8,128)}, f32[2,2,32,1024]{3,2,1,0:T(8,128)S(1)}, u32[]{:S(2)}, u32[]{:S(2)}) collective-permute-start(f32[2,2,32,1024]{3,2,1,0:T(8,128)} %dynamic-slice_bitcast_fusion.7), channel_id=1, source_target_pairs={{0,1},{1,0},{2,3},{3,2},{4,5},{5,4},{6,7},{7,6},{8,9},{9,8},{10,11... | collective-permute-start | bytes 1572872 | tf_op jit(solution)/shard_map/ppermute | solution.py:96
  107.6 8.0 %collective-permute-start.3 = (f32[2,32,1024]{2,1,0:T(8,128)S(1)}, f32[2,32,1024]{2,1,0:T(8,128)S(1)}, u32[]{:S(2)}, u32[]{:S(2)}) collective-permute-start(f32[2,32,1024]{2,1,0:T(8,128)S(1)} %dynamic-slice_bitcast_fusion.14), channel_id=1, source_target_pairs={{0,4},{1,5},{2,6},{3,7},{4,0},{5,1},{6,2},{7,3},{8,12},{9,13},{10,... | collective-permute-start | bytes 786440 | tf_op jit(solution)/shard_map/ppermute | solution.py:96
  109.2 8.9 %collective-permute-start.5 = (f32[2,2,32,1024]{3,2,1,0:T(8,128)S(1)}, f32[2,2,32,1024]{3,2,1,0:T(8,128)S(1)}, u32[]{:S(2)}, u32[]{:S(2)}) collective-permute-start(f32[2,2,32,1024]{3,2,1,0:T(8,128)S(1)} %dynamic-slice_bitcast_fusion.4), channel_id=1, source_target_pairs={{0,1},{1,0},{2,3},{3,2},{4,5},{5,4},{6,7},{7,6},{8,9},{9,8},{10,11... | collective-permute-start | bytes 1572872 | tf_op jit(solution)/shard_map/ppermute | solution.py:96
  109.3 8.8 %collective-permute-start.2 = (f32[2,32,1024]{2,1,0:T(8,128)S(1)}, f32[2,32,1024]{2,1,0:T(8,128)S(1)}, u32[]{:S(2)}, u32[]{:S(2)}) collective-permute-start(f32[2,32,1024]{2,1,0:T(8,128)S(1)} %dynamic-slice_bitcast_fusion.15), channel_id=1, source_target_pairs={{0,2},{1,3},{2,0},{3,1},{4,6},{5,7},{6,4},{7,5},{8,10},{9,11},{10,... | collective-permute-start | bytes 786440 | tf_op jit(solution)/shard_map/ppermute | solution.py:96
  110.8 7.4 %collective-permute-start.4 = (f32[2,2,32,1024]{3,2,1,0:T(8,128)S(1)}, f32[2,2,32,1024]{3,2,1,0:T(8,128)S(1)}, u32[]{:S(2)}, u32[]{:S(2)}) collective-permute-start(f32[2,2,32,1024]{3,2,1,0:T(8,128)S(1)} %dynamic-slice_bitcast_fusion.5), channel_id=1, source_target_pairs={{0,1},{1,0},{2,3},{3,2},{4,5},{5,4},{6,7},{7,6},{8,9},{9,8},{10,11... | collective-permute-start | bytes 1572872 | tf_op jit(solution)/shard_map/ppermute | solution.py:96
  136.6 13.8 %collective-permute-start.11 = (f32[2,2,32,1024]{3,2,1,0:T(8,128)S(1)}, f32[2,2,32,1024]{3,2,1,0:T(8,128)S(1)}, u32[]{:S(2)}, u32[]{:S(2)}) collective-permute-start(f32[2,2,32,1024]{3,2,1,0:T(8,128)S(1)} %dynamic-slice_bitcast_fusion.2), channel_id=1, source_target_pairs={{0,1},{1,0},{2,3},{3,2},{4,5},{5,4},{6,7},{7,6},{8,9},{9,8},{10,11... | collective-permute-start | bytes 1572872 | tf_op jit(solution)/shard_map/ppermute | solution.py:96
  136.8 13.8 %collective-permute-start.10 = (f32[2,2,32,1024]{3,2,1,0:T(8,128)S(1)}, f32[2,2,32,1024]{3,2,1,0:T(8,128)S(1)}, u32[]{:S(2)}, u32[]{:S(2)}) collective-permute-start(f32[2,2,32,1024]{3,2,1,0:T(8,128)S(1)} %dynamic-slice_bitcast_fusion.3), channel_id=1, source_target_pairs={{0,1},{1,0},{2,3},{3,2},{4,5},{5,4},{6,7},{7,6},{8,9},{9,8},{10,11... | collective-permute-start | bytes 1572872 | tf_op jit(solution)/shard_map/ppermute | solution.py:96
  137.3 13.0 %collective-permute-start.9 = (f32[2,32,1024]{2,1,0:T(8,128)S(1)}, f32[2,32,1024]{2,1,0:T(8,128)S(1)}, u32[]{:S(2)}, u32[]{:S(2)}) collective-permute-start(f32[2,32,1024]{2,1,0:T(8,128)S(1)} %dynamic-slice_bitcast_fusion.12), channel_id=1, source_target_pairs={{0,4},{1,5},{2,6},{3,7},{4,0},{5,1},{6,2},{7,3},{8,12},{9,13},{10,... | collective-permute-start | bytes 786440 | tf_op jit(solution)/shard_map/ppermute | solution.py:96
  138.9 6.5 %collective-permute-start.7 = (f32[32,1024]{1,0:T(8,128)S(1)}, f32[32,1024]{1,0:T(8,128)S(1)}, u32[]{:S(2)}, u32[]{:S(2)}) collective-permute-start(f32[32,1024]{1,0:T(8,128)S(1)} %dynamic-slice_bitcast_fusion.22), channel_id=1, source_target_pairs={{0,2},{1,3},{2,0},{3,1},{4,6},{5,7},{6,4},{7,5},{8,10},{9,11},{10,... | collective-permute-start | bytes 393224 | tf_op jit(solution)/shard_map/ppermute | solution.py:96
  140.4 10.0 %collective-permute-start.8 = (f32[2,32,1024]{2,1,0:T(8,128)S(1)}, f32[2,32,1024]{2,1,0:T(8,128)S(1)}, u32[]{:S(2)}, u32[]{:S(2)}) collective-permute-start(f32[2,32,1024]{2,1,0:T(8,128)S(1)} %dynamic-slice_bitcast_fusion.13), channel_id=1, source_target_pairs={{0,2},{1,3},{2,0},{3,1},{4,6},{5,7},{6,4},{7,5},{8,10},{9,11},{10,... | collective-permute-start | bytes 786440 | tf_op jit(solution)/shard_map/ppermute | solution.py:96
  145.4 5.0 %collective-permute-start.6 = (f32[32,1024]{1,0:T(8,128)S(1)}, f32[32,1024]{1,0:T(8,128)S(1)}, u32[]{:S(2)}, u32[]{:S(2)}) collective-permute-start(f32[32,1024]{1,0:T(8,128)S(1)} %dynamic-slice_bitcast_fusion.23), channel_id=1, source_target_pairs={{0,4},{1,5},{2,6},{3,7},{4,0},{5,1},{6,2},{7,3},{8,12},{9,13},{10,... | collective-permute-start | bytes 393224 | tf_op jit(solution)/shard_map/ppermute | solution.py:96
  156.4 13.6 %collective-permute-start.12 = (f32[32,1024]{1,0:T(8,128)S(1)}, f32[32,1024]{1,0:T(8,128)S(1)}, u32[]{:S(2)}, u32[]{:S(2)}) collective-permute-start(f32[32,1024]{1,0:T(8,128)S(1)} %dynamic-slice_bitcast_fusion.21), channel_id=1, source_target_pairs={{0,4},{1,5},{2,6},{3,7},{4,0},{5,1},{6,2},{7,3},{8,12},{9,13},{10,... | collective-permute-start | bytes 393224 | tf_op jit(solution)/shard_map/ppermute | solution.py:96
  157.9 12.7 %collective-permute-start.13 = (f32[32,1024]{1,0:T(8,128)S(1)}, f32[32,1024]{1,0:T(8,128)S(1)}, u32[]{:S(2)}, u32[]{:S(2)}) collective-permute-start(f32[32,1024]{1,0:T(8,128)S(1)} %dynamic-slice_bitcast_fusion.20), channel_id=1, source_target_pairs={{0,2},{1,3},{2,0},{3,1},{4,6},{5,7},{6,4},{7,5},{8,10},{9,11},{10,... | collective-permute-start | bytes 393224 | tf_op jit(solution)/shard_map/ppermute | solution.py:96
  159.4 11.2 %collective-permute-start.14 = (f32[2,32,1024]{2,1,0:T(8,128)S(1)}, f32[2,32,1024]{2,1,0:T(8,128)S(1)}, u32[]{:S(2)}, u32[]{:S(2)}) collective-permute-start(f32[2,32,1024]{2,1,0:T(8,128)S(1)} %dynamic-slice_bitcast_fusion.11), channel_id=1, source_target_pairs={{0,2},{1,3},{2,0},{3,1},{4,6},{5,7},{6,4},{7,5},{8,10},{9,11},{10,... | collective-permute-start | bytes 786440 | tf_op jit(solution)/shard_map/ppermute | solution.py:96
  160.1 12.1 %collective-permute-start.16 = (f32[2,32,1024]{2,1,0:T(8,128)S(1)}, f32[2,32,1024]{2,1,0:T(8,128)S(1)}, u32[]{:S(2)}, u32[]{:S(2)}) collective-permute-start(f32[2,32,1024]{2,1,0:T(8,128)S(1)} %dynamic-slice_bitcast_fusion.10), channel_id=1, source_target_pairs={{0,4},{1,5},{2,6},{3,7},{4,0},{5,1},{6,2},{7,3},{8,12},{9,13},{10,... | collective-permute-start | bytes 786440 | tf_op jit(solution)/shard_map/ppermute | solution.py:96
  169.8 7.6 %collective-permute-start.18 = (f32[2,2,32,1024]{3,2,1,0:T(8,128)S(1)}, f32[2,2,32,1024]{3,2,1,0:T(8,128)S(1)}, u32[]{:S(2)}, u32[]{:S(2)}) collective-permute-start(f32[2,2,32,1024]{3,2,1,0:T(8,128)S(1)} %dynamic-slice_bitcast_fusion.1), channel_id=1, source_target_pairs={{0,1},{1,0},{2,3},{3,2},{4,5},{5,4},{6,7},{7,6},{8,9},{9,8},{10,11... | collective-permute-start | bytes 1572872 | tf_op jit(solution)/shard_map/ppermute | solution.py:96
  170.0 9.1 %collective-permute-start.21 = (f32[2,2,32,1024]{3,2,1,0:T(8,128)S(1)}, f32[2,2,32,1024]{3,2,1,0:T(8,128)S(1)}, u32[]{:S(2)}, u32[]{:S(2)}) collective-permute-start(f32[2,2,32,1024]{3,2,1,0:T(8,128)S(1)} %dynamic-slice_bitcast_fusion), channel_id=1, source_target_pairs={{0,1},{1,0},{2,3},{3,2},{4,5},{5,4},{6,7},{7,6},{8,9},{9,8},{10,11... | collective-permute-start | bytes 1572872 | tf_op jit(solution)/shard_map/ppermute | solution.py:96
  170.7 5.5 %collective-permute-start.15 = (f32[32,1024]{1,0:T(8,128)S(1)}, f32[32,1024]{1,0:T(8,128)S(1)}, u32[]{:S(2)}, u32[]{:S(2)}) collective-permute-start(f32[32,1024]{1,0:T(8,128)S(1)} %dynamic-slice_bitcast_fusion.19), channel_id=1, source_target_pairs={{0,4},{1,5},{2,6},{3,7},{4,0},{5,1},{6,2},{7,3},{8,12},{9,13},{10,... | collective-permute-start | bytes 393224 | tf_op jit(solution)/shard_map/ppermute | solution.py:96
  172.2 5.2 %collective-permute-start.17 = (f32[32,1024]{1,0:T(8,128)S(1)}, f32[32,1024]{1,0:T(8,128)S(1)}, u32[]{:S(2)}, u32[]{:S(2)}) collective-permute-start(f32[32,1024]{1,0:T(8,128)S(1)} %dynamic-slice_bitcast_fusion.18), channel_id=1, source_target_pairs={{0,2},{1,3},{2,0},{3,1},{4,6},{5,7},{6,4},{7,5},{8,10},{9,11},{10,... | collective-permute-start | bytes 393224 | tf_op jit(solution)/shard_map/ppermute | solution.py:96
  177.6 7.1 %collective-permute-start.19 = (f32[2,32,1024]{2,1,0:T(8,128)S(1)}, f32[2,32,1024]{2,1,0:T(8,128)S(1)}, u32[]{:S(2)}, u32[]{:S(2)}) collective-permute-start(f32[2,32,1024]{2,1,0:T(8,128)S(1)} %dynamic-slice_bitcast_fusion.9), channel_id=1, source_target_pairs={{0,2},{1,3},{2,0},{3,1},{4,6},{5,7},{6,4},{7,5},{8,10},{9,11},{10,... | collective-permute-start | bytes 786440 | tf_op jit(solution)/shard_map/ppermute | solution.py:96
  179.2 7.5 %collective-permute-start.22 = (f32[2,32,1024]{2,1,0:T(8,128)S(1)}, f32[2,32,1024]{2,1,0:T(8,128)S(1)}, u32[]{:S(2)}, u32[]{:S(2)}) collective-permute-start(f32[2,32,1024]{2,1,0:T(8,128)S(1)} %dynamic-slice_bitcast_fusion.8), channel_id=1, source_target_pairs={{0,4},{1,5},{2,6},{3,7},{4,0},{5,1},{6,2},{7,3},{8,12},{9,13},{10,... | collective-permute-start | bytes 786440 | tf_op jit(solution)/shard_map/ppermute | solution.py:96
  184.8 5.0 %collective-permute-start.20 = (f32[32,1024]{1,0:T(8,128)S(1)}, f32[32,1024]{1,0:T(8,128)S(1)}, u32[]{:S(2)}, u32[]{:S(2)}) collective-permute-start(f32[32,1024]{1,0:T(8,128)S(1)} %dynamic-slice_bitcast_fusion.17), channel_id=1, source_target_pairs={{0,4},{1,5},{2,6},{3,7},{4,0},{5,1},{6,2},{7,3},{8,12},{9,13},{10,... | collective-permute-start | bytes 393224 | tf_op jit(solution)/shard_map/ppermute | solution.py:96
  186.7 5.0 %collective-permute-start.23 = (f32[32,1024]{1,0:T(8,128)S(1)}, f32[32,1024]{1,0:T(8,128)S(1)}, u32[]{:S(2)}, u32[]{:S(2)}) collective-permute-start(f32[32,1024]{1,0:T(8,128)S(1)} %dynamic-slice_bitcast_fusion.16), channel_id=1, source_target_pairs={{0,2},{1,3},{2,0},{3,1},{4,6},{5,7},{6,4},{7,5},{8,10},{9,11},{10,... | collective-permute-start | bytes 393224 | tf_op jit(solution)/shard_map/ppermute | solution.py:96
  (3 other events, 6.8 us)
Sparse Core Ops, SparseCore 0:
  16.3 54.8 all-gather.14
  72.7 25.6 all-gather.12
  100.0 27.4 all-gather.10
  128.9 27.4 all-gather.8

commit v17 on v16

--- a/solution.py
+++ b/solution.py
@@ -124,7 +124,7 @@
     for chunk in range(N_CHUNK):
         for flow in flows:
             flow.advance(rep_index)
-        if flows:
+        if flows and chunk < N_CHUNK - 1:
             amp3, held = lax.optimization_barrier((gathered[chunk], [f.x for f in flows]))
             for flow, x in zip(flows, held):
                 flow.x = x

time: 200 us -> 209 us (1.045)
  local copies, waits for them, and re-layouts: 11.7 us -> 16.6 us
  other arithmetic: 4.69 us -> 9.45 us
    all_gather x4, waiting for transfers between devices: 72.1 us -> 51.2 us  [on_device(): lax.all_gather(local4[:, c], 'own', axis=0, tiled=True)]
    all_to_all x1, waiting for transfers between devices: 8.25 us -> 26.2 us  [on_device(): lax.all_to_all(integrals, ('own', 'rep'), split_axis=0, concat_axis=0, ti...]
    add x24, other arithmetic: 2.08 us -> 6.76 us  [advance(): self.x = keep + lax.ppermute(send, 'rep', perm=pairs)]
    squeeze x24, local copies, waits for them, and re-layouts: 1.41 us -> 3.92 us  [advance(): send = lax.dynamic_index_in_dim(self.x, 1 - mine, ax, keepdims=False)]
  transfers between devices with their start and end apart: 29 -> 29, of which waited for: 16 -> 13; matrix products, arithmetic and copies ran while one was open for 7% -> 10% of each run, Pallas kernels for 15% -> 14%
where the time goes in v17:
time: 209 us; the launch traced here: 208 us
  waiting for transfers between devices  111 us (53%)
  Pallas kernels  29.5 us (14%)
  starting transfers between devices  27.2 us (13%)
  local copies, waits for them, and re-layouts  16.6 us (8%)
  between operations  13.6 us (7%)
  other arithmetic  9.45 us (5%)
    all_gather x4, waiting for transfers between devices, on_device(): lax.all_gather(local4[:, c], 'own', axis=0, tiled=True)  51.2 us
    ppermute x24, waiting for transfers between devices, advance(): self.x = keep + lax.ppermute(send, 'rep', perm=pairs)  31.9 us
    pallas_call x4, Pallas kernels, _ladder_products(): pl.pallas_call(_ladder_kernel, grid_spec=grid_spec, out_shape=jax.ShapeDt...  29.5 us
    all_to_all x1, waiting for transfers between devices, on_device(): lax.all_to_all(integrals, ('own', 'rep'), split_axis=0, concat_axis=0, ti...  26.2 us
    ppermute x24, starting transfers between devices, advance(): self.x = keep + lax.ppermute(send, 'rep', perm=pairs)  19.8 us
    all_to_all x1, starting transfers between devices, on_device(): lax.all_to_all(integrals, ('own', 'rep'), split_axis=0, concat_axis=0, ti...  7.3 us
    slice x4, local copies, waits for them, and re-layouts, on_device(): flows.extend((_Halving(partial[h], orders[h], rep_count) for h in range(2)))  6.8 us
    add x24, other arithmetic, advance(): self.x = keep + lax.ppermute(send, 'rep', perm=pairs)  6.76 us
  transfers between devices with their start and end apart: 29, of which 13 were waited for; matrix products, arithmetic and copies ran while one was open for 10% of the time, Pallas kernels for 14%

profile of v17, /device:TPU:0, one launch (start us, length us, event | category | flops | bytes accessed | tf_op | source)
XLA Modules:
  0.0 207.6 jit_solution(402902417508195763)
XLA Ops:
  6.5 2.2 %fusion.6 = (bf16[2,1,32,2048]{3,2,1,0:T(8,128)(2,1)}, bf16[2,1,32,2048]{3,2,1,0:T(8,128)(2,1)}, bf16[2,1,32,2048]{3,2,1,0:T(8,128)(2,1)}, bf16[2,1,32,2048]{3,2,1,0:T(8,128)(2,1)}) fusion(bf16[2,4,32,2048]{3,2,1,0:T(8,128)(2,1)} %bitcast.126), kind=kLoop, calls=%fused_computation.63 | loop fusion | bytes 2097152 | tf_op jit(solution)/shard_map/slice | solution.py:122
  8.8 7.3 %all-to-all-start = ((bf16[64,128,128]{2,1,0:T(8,128)(2,1)}), bf16[64,128,128]{2,1,0:T(8,128)(2,1)S(1)}, u32[]{:S(2)}, u32[]{:S(2)}) async-start(bf16[64,128,128]{2,1,0:T(8,128)(2,1)} %param.6), calls=%async_computation | async-start | bytes 4194304 | tf_op jit(solution)/shard_map/all_to_all | solution.py:108
  20.9 45.1 %all-gather.13.cloned.1.call-done = bf16[8,1,32,2048]{3,2,1,0:T(8,128)(2,1)} async-done(((bf16[2,1,32,2048]{3,2,1,0:T(8,128)(2,1)}), bf16[8,1,32,2048]{3,2,1,0:T(8,128)(2,1)}) %all-gather.13.cloned.1.call-update) | async-done | bytes 1048592 | tf_op jit(solution)/shard_map/all_gather | solution.py:122
  66.0 26.2 %all-to-all-done.tiles_ref = bf16[64,128,128]{2,1,0:T(8,128)(2,1)S(1)} async-done(((bf16[64,128,128]{2,1,0:T(8,128)(2,1)}), bf16[64,128,128]{2,1,0:T(8,128)(2,1)S(1)}, u32[]{:S(2)}, u32[]{:S(2)}) %all-to-all-start) | async-done | bytes 2097184 | tf_op jit(solution)/shard_map/all_to_all | solution.py:108
  92.2 1.4 copy-done.2
  93.6 7.4 %shard_map.55 = f32[2,256,1024]{2,1,0:T(8,128)} custom-call(s32[64]{0:T(128)} %select_reduce_fusion.order_ref, s32[17]{0:T(128)} %convert_reduce_fusion.1.starts_ref, s32[64]{0:T(128)} %copy-done.8, s32[64]{0:T(128)} %reshape.46.cd_ref, bf16[8,32,2048]{2,1,0:T(8,128)(2,1)} %bitcast.131, bf16[64,128,128]{2,1,0:T(8,128)(2,1)} %copy-done.2), custom_call_target="tpu_custom_call" | custom-call | flops 2147483648 | bytes 5242880 | tf_op jit(solution)/shard_map/pallas_call | solution.py:69
  100.9 1.7 fusion.4
  105.8 7.5 %shard_map.58 = f32[2,256,1024]{2,1,0:T(8,128)} custom-call(s32[64]{0:T(128)} %select_reduce_fusion.order_ref, s32[17]{0:T(128)} %convert_reduce_fusion.1.starts_ref, s32[64]{0:T(128)} %copy-done.8, s32[64]{0:T(128)} %reshape.46.cd_ref, bf16[8,32,2048]{2,1,0:T(8,128)(2,1)} %bitcast.130, bf16[64,128,128]{2,1,0:T(8,128)(2,1)} %copy-done.2), custom_call_target="tpu_custom_call" | custom-call | flops 2147483648 | bytes 5242880 | tf_op jit(solution)/shard_map/pallas_call | solution.py:69
  113.3 1.7 fusion.5
  117.2 1.9 bitcast_add_fusion.6
  119.1 1.9 bitcast_add_fusion.7
  121.1 6.0 %all-gather.11.cloned.1.call-done = bf16[8,1,32,2048]{3,2,1,0:T(8,128)(2,1)} async-done(((bf16[2,1,32,2048]{3,2,1,0:T(8,128)(2,1)}), bf16[8,1,32,2048]{3,2,1,0:T(8,128)(2,1)}) %all-gather.11.cloned.1.call-update) | async-done | bytes 1048592 | tf_op jit(solution)/shard_map/all_gather | solution.py:122
  127.1 7.3 %shard_map.56 = f32[2,256,1024]{2,1,0:T(8,128)} custom-call(s32[64]{0:T(128)} %select_reduce_fusion.order_ref, s32[17]{0:T(128)} %convert_reduce_fusion.1.starts_ref, s32[64]{0:T(128)} %copy-done.8, s32[64]{0:T(128)} %reshape.46.cd_ref, bf16[8,32,2048]{2,1,0:T(8,128)(2,1)} %bitcast.129, bf16[64,128,128]{2,1,0:T(8,128)(2,1)} %copy-done.2), custom_call_target="tpu_custom_call" | custom-call | flops 2147483648 | bytes 5242880 | tf_op jit(solution)/shard_map/pallas_call | solution.py:69
  134.4 1.8 fusion.3
  137.3 1.6 collective-permute-start.3
  138.9 1.4 collective-permute-start.2
  140.3 1.1 bitcast_add_fusion.1
  142.2 1.1 bitcast_add_fusion
  143.3 8.9 %collective-permute-done.19 = f32[2,32,1024]{2,1,0:T(8,128)S(1)} collective-permute-done((f32[2,32,1024]{2,1,0:T(8,128)S(1)}, f32[2,32,1024]{2,1,0:T(8,128)S(1)}, u32[]{:S(2)}, u32[]{:S(2)}) %collective-permute-start.19) | collective-permute-done | bytes 262176 | tf_op jit(solution)/shard_map/ppermute | solution.py:96
  152.8 6.3 %collective-permute-done.22 = f32[2,32,1024]{2,1,0:T(8,128)S(1)} collective-permute-done((f32[2,32,1024]{2,1,0:T(8,128)S(1)}, f32[2,32,1024]{2,1,0:T(8,128)S(1)}, u32[]{:S(2)}, u32[]{:S(2)}) %collective-permute-start.22) | collective-permute-done | bytes 262176 | tf_op jit(solution)/shard_map/ppermute | solution.py:96
  159.7 1.7 collective-permute-start.23
  161.5 2.6 %collective-permute-done.20 = f32[32,1024]{1,0:T(8,128)S(1)} collective-permute-done((f32[32,1024]{1,0:T(8,128)S(1)}, f32[32,1024]{1,0:T(8,128)S(1)}, u32[]{:S(2)}, u32[]{:S(2)}) %collective-permute-start.20) | collective-permute-done | bytes 131104 | tf_op jit(solution)/shard_map/ppermute | solution.py:96
  165.0 2.0 collective-permute-start.6
  166.9 1.2 collective-permute-start.7
  169.3 7.4 %shard_map.57 = f32[2,256,1024]{2,1,0:T(8,128)} custom-call(s32[64]{0:T(128)} %select_reduce_fusion.order_ref, s32[17]{0:T(128)} %convert_reduce_fusion.1.starts_ref, s32[64]{0:T(128)} %copy-done.8, s32[64]{0:T(128)} %reshape.46.cd_ref, bf16[8,32,2048]{2,1,0:T(8,128)(2,1)} %bitcast.128, bf16[64,128,128]{2,1,0:T(8,128)(2,1)} %copy-done.2), custom_call_target="tpu_custom_call" | custom-call | flops 2147483648 | bytes 5242880 | tf_op jit(solution)/shard_map/pallas_call | solution.py:69
  176.7 1.7 fusion.2
  179.3 2.0 collective-permute-start.9
  182.4 2.5 %collective-permute-done.9 = f32[32,1024]{1,0:T(8,128)S(1)} collective-permute-done((f32[32,1024]{1,0:T(8,128)S(1)}, f32[32,1024]{1,0:T(8,128)S(1)}, u32[]{:S(2)}, u32[]{:S(2)}) %collective-permute-start.9) | collective-permute-done | bytes 131104 | tf_op jit(solution)/shard_map/ppermute | solution.py:96
  184.9 1.6 collective-permute-done.11
  188.8 5.0 %collective-permute-done.13 = f32[2,32,1024]{2,1,0:T(8,128)S(1)} collective-permute-done((f32[2,32,1024]{2,1,0:T(8,128)S(1)}, f32[2,32,1024]{2,1,0:T(8,128)S(1)}, u32[]{:S(2)}, u32[]{:S(2)}) %collective-permute-start.13) | collective-permute-done | bytes 262176 | tf_op jit(solution)/shard_map/ppermute | solution.py:96
  196.0 2.9 %collective-permute-done.14 = f32[32,1024]{1,0:T(8,128)S(1)} collective-permute-done((f32[32,1024]{1,0:T(8,128)S(1)}, f32[32,1024]{1,0:T(8,128)S(1)}, u32[]{:S(2)}, u32[]{:S(2)}) %collective-permute-start.14) | collective-permute-done | bytes 131104 | tf_op jit(solution)/shard_map/ppermute | solution.py:96
  198.9 1.1 collective-permute-done.17
  (116 shorter events, 22.8 us)
Async XLA Ops:
  6.5 59.5 %all-gather.13.cloned.1.call-start = ((), (), s32[]{:S(2)}) async-start(), calls=%async_computation.3 | async-start | bytes 1310720 | tf_op jit(solution)/shard_map/all_gather | solution.py:122
  8.7 9.6 %copy-start.7 = (s32[1,32]{1,0:T(1,128)S(1)}, s32[1,32]{1,0:T(1,128)}, u32[]{:S(2)}) copy-start(s32[1,32]{1,0:T(1,128)} %param.9) | copy-start | bytes 388
  8.8 9.8 %copy-start.6 = (s32[1,32,2]{1,2,0:T(2,128)S(1)}, s32[1,32,2]{1,2,0:T(2,128)}, u32[]{:S(2)}) copy-start(s32[1,32,2]{1,2,0:T(2,128)} %param.8) | copy-start | bytes 772
  8.8 83.5 %all-to-all-start = ((bf16[64,128,128]{2,1,0:T(8,128)(2,1)}), bf16[64,128,128]{2,1,0:T(8,128)(2,1)S(1)}, u32[]{:S(2)}, u32[]{:S(2)}) async-start(bf16[64,128,128]{2,1,0:T(8,128)(2,1)} %param.6), calls=%async_computation | async-start | bytes 4194304 | tf_op jit(solution)/shard_map/all_to_all | solution.py:108
  16.1 89.8 %all-gather.15.cloned.1.call-start = ((), (), s32[]{:S(2)}) async-start(), calls=%async_computation.4 | async-start | bytes 1310720 | tf_op jit(solution)/shard_map/all_gather | solution.py:122
  16.8 110.3 %all-gather.11.cloned.1.call-start = ((), (), s32[]{:S(2)}) async-start(), calls=%async_computation.2 | async-start | bytes 1310720 | tf_op jit(solution)/shard_map/all_gather | solution.py:122
  17.6 147.4 %all-gather.9.cloned.1.call-start = ((), (), s32[]{:S(2)}) async-start(), calls=%async_computation.1 | async-start | bytes 1310720 | tf_op jit(solution)/shard_map/all_gather | solution.py:122
  18.4 73.9 %copy-start.8 = (s32[64]{0:T(128)}, s32[64]{0:T(128)S(1)}, u32[]{:S(2)}) copy-start(s32[64]{0:T(128)S(1)} %reshape.45.ab_ref) | copy-start | bytes 772
  104.5 12.7 %collective-permute-start.1 = (f32[2,2,32,1024]{3,2,1,0:T(8,128)}, f32[2,2,32,1024]{3,2,1,0:T(8,128)}, u32[]{:S(2)}, u32[]{:S(2)}) collective-permute-start(f32[2,2,32,1024]{3,2,1,0:T(8,128)} %dynamic-slice_bitcast_fusion.6), channel_id=1, source_target_pairs={{0,1},{1,0},{2,3},{3,2},{4,5},{5,4},{6,7},{7,6},{8,9},{9,8},{10,11... | collective-permute-start | bytes 1572872 | tf_op jit(solution)/shard_map/ppermute | solution.py:96
  105.3 13.8 %collective-permute-start = (f32[2,2,32,1024]{3,2,1,0:T(8,128)}, f32[2,2,32,1024]{3,2,1,0:T(8,128)}, u32[]{:S(2)}, u32[]{:S(2)}) collective-permute-start(f32[2,2,32,1024]{3,2,1,0:T(8,128)} %dynamic-slice_bitcast_fusion.7), channel_id=1, source_target_pairs={{0,1},{1,0},{2,3},{3,2},{4,5},{5,4},{6,7},{7,6},{8,9},{9,8},{10,11... | collective-permute-start | bytes 1572872 | tf_op jit(solution)/shard_map/ppermute | solution.py:96
  115.8 23.0 %collective-permute-start.18 = (f32[2,2,32,1024]{3,2,1,0:T(8,128)}, f32[2,2,32,1024]{3,2,1,0:T(8,128)}, u32[]{:S(2)}, u32[]{:S(2)}) collective-permute-start(f32[2,2,32,1024]{3,2,1,0:T(8,128)} %dynamic-slice_bitcast_fusion.1), channel_id=1, source_target_pairs={{0,1},{1,0},{2,3},{3,2},{4,5},{5,4},{6,7},{7,6},{8,9},{9,8},{10,11... | collective-permute-start | bytes 1572872 | tf_op jit(solution)/shard_map/ppermute | solution.py:96
  116.7 24.8 %collective-permute-start.21 = (f32[2,2,32,1024]{3,2,1,0:T(8,128)}, f32[2,2,32,1024]{3,2,1,0:T(8,128)}, u32[]{:S(2)}, u32[]{:S(2)}) collective-permute-start(f32[2,2,32,1024]{3,2,1,0:T(8,128)} %dynamic-slice_bitcast_fusion), channel_id=1, source_target_pairs={{0,1},{1,0},{2,3},{3,2},{4,5},{5,4},{6,7},{7,6},{8,9},{9,8},{10,11... | collective-permute-start | bytes 1572872 | tf_op jit(solution)/shard_map/ppermute | solution.py:96
  136.3 28.5 %collective-permute-start.5 = (f32[2,2,32,1024]{3,2,1,0:T(8,128)S(1)}, f32[2,2,32,1024]{3,2,1,0:T(8,128)S(1)}, u32[]{:S(2)}, u32[]{:S(2)}) collective-permute-start(f32[2,2,32,1024]{3,2,1,0:T(8,128)S(1)} %dynamic-slice_bitcast_fusion.4), channel_id=1, source_target_pairs={{0,1},{1,0},{2,3},{3,2},{4,5},{5,4},{6,7},{7,6},{8,9},{9,8},{10,11... | collective-permute-start | bytes 1572872 | tf_op jit(solution)/shard_map/ppermute | solution.py:96
  136.4 28.4 %collective-permute-start.4 = (f32[2,2,32,1024]{3,2,1,0:T(8,128)S(1)}, f32[2,2,32,1024]{3,2,1,0:T(8,128)S(1)}, u32[]{:S(2)}, u32[]{:S(2)}) collective-permute-start(f32[2,2,32,1024]{3,2,1,0:T(8,128)S(1)} %dynamic-slice_bitcast_fusion.5), channel_id=1, source_target_pairs={{0,1},{1,0},{2,3},{3,2},{4,5},{5,4},{6,7},{7,6},{8,9},{9,8},{10,11... | collective-permute-start | bytes 1572872 | tf_op jit(solution)/shard_map/ppermute | solution.py:96
  137.3 22.4 %collective-permute-start.3 = (f32[2,32,1024]{2,1,0:T(8,128)S(1)}, f32[2,32,1024]{2,1,0:T(8,128)S(1)}, u32[]{:S(2)}, u32[]{:S(2)}) collective-permute-start(f32[2,32,1024]{2,1,0:T(8,128)S(1)} %dynamic-slice_bitcast_fusion.14), channel_id=1, source_target_pairs={{0,4},{1,5},{2,6},{3,7},{4,0},{5,1},{6,2},{7,3},{8,12},{9,13},{10,... | collective-permute-start | bytes 786440 | tf_op jit(solution)/shard_map/ppermute | solution.py:96
  138.9 22.5 %collective-permute-start.2 = (f32[2,32,1024]{2,1,0:T(8,128)S(1)}, f32[2,32,1024]{2,1,0:T(8,128)S(1)}, u32[]{:S(2)}, u32[]{:S(2)}) collective-permute-start(f32[2,32,1024]{2,1,0:T(8,128)S(1)} %dynamic-slice_bitcast_fusion.15), channel_id=1, source_target_pairs={{0,2},{1,3},{2,0},{3,1},{4,6},{5,7},{6,4},{7,5},{8,10},{9,11},{10,... | collective-permute-start | bytes 786440 | tf_op jit(solution)/shard_map/ppermute | solution.py:96
  141.5 10.8 %collective-permute-start.19 = (f32[2,32,1024]{2,1,0:T(8,128)S(1)}, f32[2,32,1024]{2,1,0:T(8,128)S(1)}, u32[]{:S(2)}, u32[]{:S(2)}) collective-permute-start(f32[2,32,1024]{2,1,0:T(8,128)S(1)} %dynamic-slice_bitcast_fusion.9), channel_id=1, source_target_pairs={{0,2},{1,3},{2,0},{3,1},{4,6},{5,7},{6,4},{7,5},{8,10},{9,11},{10,... | collective-permute-start | bytes 786440 | tf_op jit(solution)/shard_map/ppermute | solution.py:96
  152.2 6.9 %collective-permute-start.22 = (f32[2,32,1024]{2,1,0:T(8,128)S(1)}, f32[2,32,1024]{2,1,0:T(8,128)S(1)}, u32[]{:S(2)}, u32[]{:S(2)}) collective-permute-start(f32[2,32,1024]{2,1,0:T(8,128)S(1)} %dynamic-slice_bitcast_fusion.8), channel_id=1, source_target_pairs={{0,4},{1,5},{2,6},{3,7},{4,0},{5,1},{6,2},{7,3},{8,12},{9,13},{10,... | collective-permute-start | bytes 786440 | tf_op jit(solution)/shard_map/ppermute | solution.py:96
  159.1 5.0 %collective-permute-start.20 = (f32[32,1024]{1,0:T(8,128)S(1)}, f32[32,1024]{1,0:T(8,128)S(1)}, u32[]{:S(2)}, u32[]{:S(2)}) collective-permute-start(f32[32,1024]{1,0:T(8,128)S(1)} %dynamic-slice_bitcast_fusion.17), channel_id=1, source_target_pairs={{0,4},{1,5},{2,6},{3,7},{4,0},{5,1},{6,2},{7,3},{8,12},{9,13},{10,... | collective-permute-start | bytes 393224 | tf_op jit(solution)/shard_map/ppermute | solution.py:96
  159.7 5.0 %collective-permute-start.23 = (f32[32,1024]{1,0:T(8,128)S(1)}, f32[32,1024]{1,0:T(8,128)S(1)}, u32[]{:S(2)}, u32[]{:S(2)}) collective-permute-start(f32[32,1024]{1,0:T(8,128)S(1)} %dynamic-slice_bitcast_fusion.16), channel_id=1, source_target_pairs={{0,2},{1,3},{2,0},{3,1},{4,6},{5,7},{6,4},{7,5},{8,10},{9,11},{10,... | collective-permute-start | bytes 393224 | tf_op jit(solution)/shard_map/ppermute | solution.py:96
  165.0 13.6 %collective-permute-start.6 = (f32[32,1024]{1,0:T(8,128)S(1)}, f32[32,1024]{1,0:T(8,128)S(1)}, u32[]{:S(2)}, u32[]{:S(2)}) collective-permute-start(f32[32,1024]{1,0:T(8,128)S(1)} %dynamic-slice_bitcast_fusion.23), channel_id=1, source_target_pairs={{0,4},{1,5},{2,6},{3,7},{4,0},{5,1},{6,2},{7,3},{8,12},{9,13},{10,... | collective-permute-start | bytes 393224 | tf_op jit(solution)/shard_map/ppermute | solution.py:96
  166.9 12.2 %collective-permute-start.7 = (f32[32,1024]{1,0:T(8,128)S(1)}, f32[32,1024]{1,0:T(8,128)S(1)}, u32[]{:S(2)}, u32[]{:S(2)}) collective-permute-start(f32[32,1024]{1,0:T(8,128)S(1)} %dynamic-slice_bitcast_fusion.22), channel_id=1, source_target_pairs={{0,2},{1,3},{2,0},{3,1},{4,6},{5,7},{6,4},{7,5},{8,10},{9,11},{10,... | collective-permute-start | bytes 393224 | tf_op jit(solution)/shard_map/ppermute | solution.py:96
  168.1 11.1 %collective-permute-start.8 = (f32[2,32,1024]{2,1,0:T(8,128)S(1)}, f32[2,32,1024]{2,1,0:T(8,128)S(1)}, u32[]{:S(2)}, u32[]{:S(2)}) collective-permute-start(f32[2,32,1024]{2,1,0:T(8,128)S(1)} %dynamic-slice_bitcast_fusion.13), channel_id=1, source_target_pairs={{0,2},{1,3},{2,0},{3,1},{4,6},{5,7},{6,4},{7,5},{8,10},{9,11},{10,... | collective-permute-start | bytes 786440 | tf_op jit(solution)/shard_map/ppermute | solution.py:96
  169.1 12.1 %collective-permute-start.10 = (f32[2,32,1024]{2,1,0:T(8,128)S(1)}, f32[2,32,1024]{2,1,0:T(8,128)S(1)}, u32[]{:S(2)}, u32[]{:S(2)}) collective-permute-start(f32[2,32,1024]{2,1,0:T(8,128)S(1)} %dynamic-slice_bitcast_fusion.12), channel_id=1, source_target_pairs={{0,4},{1,5},{2,6},{3,7},{4,0},{5,1},{6,2},{7,3},{8,12},{9,13},{10,... | collective-permute-start | bytes 786440 | tf_op jit(solution)/shard_map/ppermute | solution.py:96
  178.4 8.1 %collective-permute-start.12 = (f32[2,2,32,1024]{3,2,1,0:T(8,128)S(1)}, f32[2,2,32,1024]{3,2,1,0:T(8,128)S(1)}, u32[]{:S(2)}, u32[]{:S(2)}) collective-permute-start(f32[2,2,32,1024]{3,2,1,0:T(8,128)S(1)} %dynamic-slice_bitcast_fusion.3), channel_id=1, source_target_pairs={{0,1},{1,0},{2,3},{3,2},{4,5},{5,4},{6,7},{7,6},{8,9},{9,8},{10,11... | collective-permute-start | bytes 1572872 | tf_op jit(solution)/shard_map/ppermute | solution.py:96
  178.6 9.2 %collective-permute-start.15 = (f32[2,2,32,1024]{3,2,1,0:T(8,128)S(1)}, f32[2,2,32,1024]{3,2,1,0:T(8,128)S(1)}, u32[]{:S(2)}, u32[]{:S(2)}) collective-permute-start(f32[2,2,32,1024]{3,2,1,0:T(8,128)S(1)} %dynamic-slice_bitcast_fusion.2), channel_id=1, source_target_pairs={{0,1},{1,0},{2,3},{3,2},{4,5},{5,4},{6,7},{7,6},{8,9},{9,8},{10,11... | collective-permute-start | bytes 1572872 | tf_op jit(solution)/shard_map/ppermute | solution.py:96
  179.3 5.6 %collective-permute-start.9 = (f32[32,1024]{1,0:T(8,128)S(1)}, f32[32,1024]{1,0:T(8,128)S(1)}, u32[]{:S(2)}, u32[]{:S(2)}) collective-permute-start(f32[32,1024]{1,0:T(8,128)S(1)} %dynamic-slice_bitcast_fusion.21), channel_id=1, source_target_pairs={{0,4},{1,5},{2,6},{3,7},{4,0},{5,1},{6,2},{7,3},{8,12},{9,13},{10,... | collective-permute-start | bytes 393224 | tf_op jit(solution)/shard_map/ppermute | solution.py:96
  181.3 5.2 %collective-permute-start.11 = (f32[32,1024]{1,0:T(8,128)S(1)}, f32[32,1024]{1,0:T(8,128)S(1)}, u32[]{:S(2)}, u32[]{:S(2)}) collective-permute-start(f32[32,1024]{1,0:T(8,128)S(1)} %dynamic-slice_bitcast_fusion.20), channel_id=1, source_target_pairs={{0,2},{1,3},{2,0},{3,1},{4,6},{5,7},{6,4},{7,5},{8,10},{9,11},{10,... | collective-permute-start | bytes 393224 | tf_op jit(solution)/shard_map/ppermute | solution.py:96
  186.6 7.1 %collective-permute-start.13 = (f32[2,32,1024]{2,1,0:T(8,128)S(1)}, f32[2,32,1024]{2,1,0:T(8,128)S(1)}, u32[]{:S(2)}, u32[]{:S(2)}) collective-permute-start(f32[2,32,1024]{2,1,0:T(8,128)S(1)} %dynamic-slice_bitcast_fusion.11), channel_id=1, source_target_pairs={{0,2},{1,3},{2,0},{3,1},{4,6},{5,7},{6,4},{7,5},{8,10},{9,11},{10,... | collective-permute-start | bytes 786440 | tf_op jit(solution)/shard_map/ppermute | solution.py:96
  187.9 7.1 %collective-permute-start.16 = (f32[2,32,1024]{2,1,0:T(8,128)S(1)}, f32[2,32,1024]{2,1,0:T(8,128)S(1)}, u32[]{:S(2)}, u32[]{:S(2)}) collective-permute-start(f32[2,32,1024]{2,1,0:T(8,128)S(1)} %dynamic-slice_bitcast_fusion.10), channel_id=1, source_target_pairs={{0,4},{1,5},{2,6},{3,7},{4,0},{5,1},{6,2},{7,3},{8,12},{9,13},{10,... | collective-permute-start | bytes 786440 | tf_op jit(solution)/shard_map/ppermute | solution.py:96
  193.8 5.0 %collective-permute-start.14 = (f32[32,1024]{1,0:T(8,128)S(1)}, f32[32,1024]{1,0:T(8,128)S(1)}, u32[]{:S(2)}, u32[]{:S(2)}) collective-permute-start(f32[32,1024]{1,0:T(8,128)S(1)} %dynamic-slice_bitcast_fusion.19), channel_id=1, source_target_pairs={{0,4},{1,5},{2,6},{3,7},{4,0},{5,1},{6,2},{7,3},{8,12},{9,13},{10,... | collective-permute-start | bytes 393224 | tf_op jit(solution)/shard_map/ppermute | solution.py:96
  195.0 5.0 %collective-permute-start.17 = (f32[32,1024]{1,0:T(8,128)S(1)}, f32[32,1024]{1,0:T(8,128)S(1)}, u32[]{:S(2)}, u32[]{:S(2)}) collective-permute-start(f32[32,1024]{1,0:T(8,128)S(1)} %dynamic-slice_bitcast_fusion.18), channel_id=1, source_target_pairs={{0,2},{1,3},{2,0},{3,1},{4,6},{5,7},{6,4},{7,5},{8,10},{9,11},{10,... | collective-permute-start | bytes 393224 | tf_op jit(solution)/shard_map/ppermute | solution.py:96
  (6 other events, 17.7 us)
Sparse Core Ops, SparseCore 0:
  8.9 57.0 all-gather.12
  67.6 31.2 all-gather.14
  100.4 26.6 all-gather.10
  128.5 27.4 all-gather.8

commit v18 on v16

--- a/solution.py
+++ b/solution.py
@@ -47,7 +47,7 @@
     groups, part, width = amp3.shape
     rows = groups * part
     n, tile, _ = tiles.shape
-    per_step = 4 if ab_count % 8 == 0 else 1
+    per_step = ab_count // 2 if ab_count % 2 == 0 else 1
     steps_per_half = ab_count // (2 * per_step)
     cost = pl.CostEstimate(
         flops=2 * rows * width * ab_count * tile,

time: 200 us -> 200 us (level)
  transfers between devices with their start and end apart: 29 -> 29, of which waited for: 16 -> 16; matrix products, arithmetic and copies ran while one was open for 7% -> 7% of each run, Pallas kernels for 15% -> 14%
where the time goes in v18:
time: 200 us; the launch traced here: 199 us
  waiting for transfers between devices  113 us (56%)
  Pallas kernels  28.5 us (14%)
  starting transfers between devices  27.1 us (14%)
  between operations  13.6 us (7%)
  local copies, waits for them, and re-layouts  11.7 us (6%)
  other arithmetic  4.69 us (2%)
    all_gather x4, waiting for transfers between devices, on_device(): lax.all_gather(local4[:, c], 'own', axis=0, tiled=True)  72.6 us
    ppermute x24, waiting for transfers between devices, advance(): self.x = keep + lax.ppermute(send, 'rep', perm=pairs)  31.1 us
    pallas_call x4, Pallas kernels, _ladder_products(): pl.pallas_call(_ladder_kernel, grid_spec=grid_spec, out_shape=jax.ShapeDt...  28.5 us
    ppermute x24, starting transfers between devices, advance(): self.x = keep + lax.ppermute(send, 'rep', perm=pairs)  19.7 us
    all_to_all x1, waiting for transfers between devices, on_device(): lax.all_to_all(integrals, ('own', 'rep'), split_axis=0, concat_axis=0, ti...  8.25 us
    all_to_all x1, starting transfers between devices, on_device(): lax.all_to_all(integrals, ('own', 'rep'), split_axis=0, concat_axis=0, ti...  7.3 us
    slice x4, local copies, waits for them, and re-layouts, on_device(): flows.extend((_Halving(partial[h], orders[h], rep_count) for h in range(2)))  6.89 us
  transfers between devices with their start and end apart: 29, of which 16 were waited for; matrix products, arithmetic and copies ran while one was open for 7% of the time, Pallas kernels for 14%

profile of v18, /device:TPU:0, one launch (start us, length us, event | category | flops | bytes accessed | tf_op | source)
XLA Modules:
  0.0 199.1 jit_solution(13544718743787139111)
XLA Ops:
  6.5 7.3 %all-to-all-start = ((bf16[64,128,128]{2,1,0:T(8,128)(2,1)}), bf16[64,128,128]{2,1,0:T(8,128)(2,1)S(1)}, u32[]{:S(2)}, u32[]{:S(2)}) async-start(bf16[64,128,128]{2,1,0:T(8,128)(2,1)} %param.6), calls=%async_computation | async-start | bytes 4194304 | tf_op jit(solution)/shard_map/all_to_all | solution.py:108
  19.2 52.0 %all-gather.15.cloned.1.call-done = bf16[8,1,32,2048]{3,2,1,0:T(8,128)(2,1)} async-done(((bf16[2,1,32,2048]{3,2,1,0:T(8,128)(2,1)}), bf16[8,1,32,2048]{3,2,1,0:T(8,128)(2,1)}) %all-gather.15.cloned.1.call-update) | async-done | bytes 1048592 | tf_op jit(solution)/shard_map/all_gather | solution.py:122
  71.2 8.2 %all-to-all-done.tiles_ref = bf16[64,128,128]{2,1,0:T(8,128)(2,1)S(1)} async-done(((bf16[64,128,128]{2,1,0:T(8,128)(2,1)}), bf16[64,128,128]{2,1,0:T(8,128)(2,1)S(1)}, u32[]{:S(2)}, u32[]{:S(2)}) %all-to-all-start) | async-done | bytes 2097184 | tf_op jit(solution)/shard_map/all_to_all | solution.py:108
  80.8 7.1 %shard_map.55 = f32[2,256,1024]{2,1,0:T(8,128)} custom-call(s32[64]{0:T(128)} %select_reduce_fusion.order_ref, s32[17]{0:T(128)} %convert_reduce_fusion.1.starts_ref, s32[64]{0:T(128)} %copy-done.5, s32[64]{0:T(128)} %reshape.46.cd_ref, bf16[8,32,2048]{2,1,0:T(8,128)(2,1)} %bitcast.131, bf16[64,128,128]{2,1,0:T(8,128)(2,1)} %copy-done), custom_call_target="tpu_custom_call" | custom-call | flops 2147483648 | bytes 5242880 | tf_op jit(solution)/shard_map/pallas_call | solution.py:69
  87.9 1.7 fusion.5
  93.0 5.5 %all-gather.13.cloned.1.call-done = bf16[8,1,32,2048]{3,2,1,0:T(8,128)(2,1)} async-done(((bf16[2,1,32,2048]{3,2,1,0:T(8,128)(2,1)}), bf16[8,1,32,2048]{3,2,1,0:T(8,128)(2,1)}) %all-gather.13.cloned.1.call-update) | async-done | bytes 1048592 | tf_op jit(solution)/shard_map/all_gather | solution.py:122
  98.4 7.1 %shard_map.56 = f32[2,256,1024]{2,1,0:T(8,128)} custom-call(s32[64]{0:T(128)} %select_reduce_fusion.order_ref, s32[17]{0:T(128)} %convert_reduce_fusion.1.starts_ref, s32[64]{0:T(128)} %copy-done.5, s32[64]{0:T(128)} %reshape.46.cd_ref, bf16[8,32,2048]{2,1,0:T(8,128)(2,1)} %bitcast.130, bf16[64,128,128]{2,1,0:T(8,128)(2,1)} %copy-done), custom_call_target="tpu_custom_call" | custom-call | flops 2147483648 | bytes 5242880 | tf_op jit(solution)/shard_map/pallas_call | solution.py:69
  105.6 1.8 fusion.4
  107.3 1.6 collective-permute-start.3
  109.1 1.4 collective-permute-start.2
  110.9 4.5 %collective-permute-done.3 = f32[2,32,1024]{2,1,0:T(8,128)S(1)} collective-permute-done((f32[2,32,1024]{2,1,0:T(8,128)S(1)}, f32[2,32,1024]{2,1,0:T(8,128)S(1)}, u32[]{:S(2)}, u32[]{:S(2)}) %collective-permute-start.3) | collective-permute-done | bytes 262176 | tf_op jit(solution)/shard_map/ppermute | solution.py:96
  115.4 2.5 %collective-permute-done.2 = f32[2,32,1024]{2,1,0:T(8,128)S(1)} collective-permute-done((f32[2,32,1024]{2,1,0:T(8,128)S(1)}, f32[2,32,1024]{2,1,0:T(8,128)S(1)}, u32[]{:S(2)}, u32[]{:S(2)}) %collective-permute-start.2) | collective-permute-done | bytes 262176 | tf_op jit(solution)/shard_map/ppermute | solution.py:96
  118.1 9.3 %all-gather.11.cloned.1.call-done = bf16[8,1,32,2048]{3,2,1,0:T(8,128)(2,1)} async-done(((bf16[2,1,32,2048]{3,2,1,0:T(8,128)(2,1)}), bf16[8,1,32,2048]{3,2,1,0:T(8,128)(2,1)}) %all-gather.11.cloned.1.call-update) | async-done | bytes 1048592 | tf_op jit(solution)/shard_map/all_gather | solution.py:122
  127.5 7.1 %shard_map.57 = f32[2,256,1024]{2,1,0:T(8,128)} custom-call(s32[64]{0:T(128)} %select_reduce_fusion.order_ref, s32[17]{0:T(128)} %convert_reduce_fusion.1.starts_ref, s32[64]{0:T(128)} %copy-done.5, s32[64]{0:T(128)} %reshape.46.cd_ref, bf16[8,32,2048]{2,1,0:T(8,128)(2,1)} %bitcast.129, bf16[64,128,128]{2,1,0:T(8,128)(2,1)} %copy-done), custom_call_target="tpu_custom_call" | custom-call | flops 2147483648 | bytes 5242880 | tf_op jit(solution)/shard_map/pallas_call | solution.py:69
  134.6 1.8 fusion.3
  137.1 1.6 collective-permute-start.9
  138.7 1.4 collective-permute-start.7
  140.9 4.3 %collective-permute-done.7 = f32[32,1024]{1,0:T(8,128)S(1)} collective-permute-done((f32[32,1024]{1,0:T(8,128)S(1)}, f32[32,1024]{1,0:T(8,128)S(1)}, u32[]{:S(2)}, u32[]{:S(2)}) %collective-permute-start.7) | collective-permute-done | bytes 131104 | tf_op jit(solution)/shard_map/ppermute | solution.py:96
  145.7 4.5 %collective-permute-done.6 = f32[32,1024]{1,0:T(8,128)S(1)} collective-permute-done((f32[32,1024]{1,0:T(8,128)S(1)}, f32[32,1024]{1,0:T(8,128)S(1)}, u32[]{:S(2)}, u32[]{:S(2)}) %collective-permute-start.6) | collective-permute-done | bytes 131104 | tf_op jit(solution)/shard_map/ppermute | solution.py:96
  150.5 5.9 %all-gather.9.cloned.1.call-done = bf16[8,1,32,2048]{3,2,1,0:T(8,128)(2,1)} async-done(((bf16[2,1,32,2048]{3,2,1,0:T(8,128)(2,1)}), bf16[8,1,32,2048]{3,2,1,0:T(8,128)(2,1)}) %all-gather.9.cloned.1.call-update) | async-done | bytes 1048592 | tf_op jit(solution)/shard_map/all_gather | solution.py:122
  156.4 1.5 collective-permute-start.12
  157.9 1.5 collective-permute-start.13
  160.7 7.1 %shard_map.58 = f32[2,256,1024]{2,1,0:T(8,128)} custom-call(s32[64]{0:T(128)} %select_reduce_fusion.order_ref, s32[17]{0:T(128)} %convert_reduce_fusion.1.starts_ref, s32[64]{0:T(128)} %copy-done.5, s32[64]{0:T(128)} %reshape.46.cd_ref, bf16[8,32,2048]{2,1,0:T(8,128)(2,1)} %bitcast.128, bf16[64,128,128]{2,1,0:T(8,128)(2,1)} %copy-done), custom_call_target="tpu_custom_call" | custom-call | flops 2147483648 | bytes 5242880 | tf_op jit(solution)/shard_map/pallas_call | solution.py:69
  167.9 1.7 fusion.2
  170.4 1.6 collective-permute-start.15
  172.1 1.4 collective-permute-start.17
  173.5 2.4 %collective-permute-done.15 = f32[32,1024]{1,0:T(8,128)S(1)} collective-permute-done((f32[32,1024]{1,0:T(8,128)S(1)}, f32[32,1024]{1,0:T(8,128)S(1)}, u32[]{:S(2)}, u32[]{:S(2)}) %collective-permute-start.15) | collective-permute-done | bytes 131104 | tf_op jit(solution)/shard_map/ppermute | solution.py:96
  175.9 1.4 collective-permute-done.17
  177.5 1.4 collective-permute-start.19
  179.6 5.0 %collective-permute-done.19 = f32[2,32,1024]{2,1,0:T(8,128)S(1)} collective-permute-done((f32[2,32,1024]{2,1,0:T(8,128)S(1)}, f32[2,32,1024]{2,1,0:T(8,128)S(1)}, u32[]{:S(2)}, u32[]{:S(2)}) %collective-permute-start.19) | collective-permute-done | bytes 262176 | tf_op jit(solution)/shard_map/ppermute | solution.py:96
  186.8 2.9 %collective-permute-done.20 = f32[32,1024]{1,0:T(8,128)S(1)} collective-permute-done((f32[32,1024]{1,0:T(8,128)S(1)}, f32[32,1024]{1,0:T(8,128)S(1)}, u32[]{:S(2)}, u32[]{:S(2)}) %collective-permute-start.20) | collective-permute-done | bytes 131104 | tf_op jit(solution)/shard_map/ppermute | solution.py:96
  189.7 1.8 collective-permute-done.23
  (110 shorter events, 19.0 us)
Async XLA Ops:
  6.5 7.4 %copy-start.1 = (bf16[256,2048]{1,0:T(8,128)(2,1)S(1)}, bf16[256,2048]{1,0:T(8,128)(2,1)}, u32[]{:S(2)}) copy-start(bf16[256,2048]{1,0:T(8,128)(2,1)} %param.5) | copy-start | bytes 3145732
  6.5 72.9 %all-to-all-start = ((bf16[64,128,128]{2,1,0:T(8,128)(2,1)}), bf16[64,128,128]{2,1,0:T(8,128)(2,1)S(1)}, u32[]{:S(2)}, u32[]{:S(2)}) async-start(bf16[64,128,128]{2,1,0:T(8,128)(2,1)} %param.6), calls=%async_computation | async-start | bytes 4194304 | tf_op jit(solution)/shard_map/all_to_all | solution.py:108
  13.9 3.0 %copy-start.3 = (s32[1,32,2]{1,2,0:T(2,128)S(1)}, s32[1,32,2]{1,2,0:T(2,128)}, u32[]{:S(2)}) copy-start(s32[1,32,2]{1,2,0:T(2,128)} %param.8) | copy-start | bytes 772
  13.9 57.3 %all-gather.15.cloned.1.call-start = ((), (), s32[]{:S(2)}) async-start(), calls=%async_computation.4 | async-start | bytes 1310720 | tf_op jit(solution)/shard_map/all_gather | solution.py:122
  14.9 83.5 %all-gather.13.cloned.1.call-start = ((), (), s32[]{:S(2)}) async-start(), calls=%async_computation.3 | async-start | bytes 1310720 | tf_op jit(solution)/shard_map/all_gather | solution.py:122
  15.7 111.8 %all-gather.11.cloned.1.call-start = ((), (), s32[]{:S(2)}) async-start(), calls=%async_computation.2 | async-start | bytes 1310720 | tf_op jit(solution)/shard_map/all_gather | solution.py:122
  16.4 139.9 %all-gather.9.cloned.1.call-start = ((), (), s32[]{:S(2)}) async-start(), calls=%async_computation.1 | async-start | bytes 1310720 | tf_op jit(solution)/shard_map/all_gather | solution.py:122
  16.7 62.7 %copy-start.5 = (s32[64]{0:T(128)}, s32[64]{0:T(128)S(1)}, u32[]{:S(2)}) copy-start(s32[64]{0:T(128)S(1)} %reshape.45.ab_ref) | copy-start | bytes 772
  89.7 2.1 %collective-permute-start.1 = (f32[2,2,32,1024]{3,2,1,0:T(8,128)S(1)}, f32[2,2,32,1024]{3,2,1,0:T(8,128)}, u32[]{:S(2)}, u32[]{:S(2)}) collective-permute-start(f32[2,2,32,1024]{3,2,1,0:T(8,128)S(1)} %dynamic-slice_bitcast_fusion.6), channel_id=1, source_target_pairs={{0,1},{1,0},{2,3},{3,2},{4,5},{5,4},{6,7},{7,6},{8,9},{9,8},{10,11... | collective-permute-start | bytes 1572872 | tf_op jit(solution)/shard_map/ppermute | solution.py:96
  90.6 2.3 %collective-permute-start = (f32[2,2,32,1024]{3,2,1,0:T(8,128)}, f32[2,2,32,1024]{3,2,1,0:T(8,128)S(1)}, u32[]{:S(2)}, u32[]{:S(2)}) collective-permute-start(f32[2,2,32,1024]{3,2,1,0:T(8,128)} %dynamic-slice_bitcast_fusion.7), channel_id=1, source_target_pairs={{0,1},{1,0},{2,3},{3,2},{4,5},{5,4},{6,7},{7,6},{8,9},{9,8},{10,11... | collective-permute-start | bytes 1572872 | tf_op jit(solution)/shard_map/ppermute | solution.py:96
  107.3 8.0 %collective-permute-start.3 = (f32[2,32,1024]{2,1,0:T(8,128)S(1)}, f32[2,32,1024]{2,1,0:T(8,128)S(1)}, u32[]{:S(2)}, u32[]{:S(2)}) collective-permute-start(f32[2,32,1024]{2,1,0:T(8,128)S(1)} %dynamic-slice_bitcast_fusion.14), channel_id=1, source_target_pairs={{0,4},{1,5},{2,6},{3,7},{4,0},{5,1},{6,2},{7,3},{8,12},{9,13},{10,... | collective-permute-start | bytes 786440 | tf_op jit(solution)/shard_map/ppermute | solution.py:96
  109.0 8.9 %collective-permute-start.5 = (f32[2,2,32,1024]{3,2,1,0:T(8,128)S(1)}, f32[2,2,32,1024]{3,2,1,0:T(8,128)S(1)}, u32[]{:S(2)}, u32[]{:S(2)}) collective-permute-start(f32[2,2,32,1024]{3,2,1,0:T(8,128)S(1)} %dynamic-slice_bitcast_fusion.4), channel_id=1, source_target_pairs={{0,1},{1,0},{2,3},{3,2},{4,5},{5,4},{6,7},{7,6},{8,9},{9,8},{10,11... | collective-permute-start | bytes 1572872 | tf_op jit(solution)/shard_map/ppermute | solution.py:96
  109.1 8.8 %collective-permute-start.2 = (f32[2,32,1024]{2,1,0:T(8,128)S(1)}, f32[2,32,1024]{2,1,0:T(8,128)S(1)}, u32[]{:S(2)}, u32[]{:S(2)}) collective-permute-start(f32[2,32,1024]{2,1,0:T(8,128)S(1)} %dynamic-slice_bitcast_fusion.15), channel_id=1, source_target_pairs={{0,2},{1,3},{2,0},{3,1},{4,6},{5,7},{6,4},{7,5},{8,10},{9,11},{10,... | collective-permute-start | bytes 786440 | tf_op jit(solution)/shard_map/ppermute | solution.py:96
  110.6 7.4 %collective-permute-start.4 = (f32[2,2,32,1024]{3,2,1,0:T(8,128)S(1)}, f32[2,2,32,1024]{3,2,1,0:T(8,128)S(1)}, u32[]{:S(2)}, u32[]{:S(2)}) collective-permute-start(f32[2,2,32,1024]{3,2,1,0:T(8,128)S(1)} %dynamic-slice_bitcast_fusion.5), channel_id=1, source_target_pairs={{0,1},{1,0},{2,3},{3,2},{4,5},{5,4},{6,7},{7,6},{8,9},{9,8},{10,11... | collective-permute-start | bytes 1572872 | tf_op jit(solution)/shard_map/ppermute | solution.py:96
  136.4 13.9 %collective-permute-start.11 = (f32[2,2,32,1024]{3,2,1,0:T(8,128)S(1)}, f32[2,2,32,1024]{3,2,1,0:T(8,128)S(1)}, u32[]{:S(2)}, u32[]{:S(2)}) collective-permute-start(f32[2,2,32,1024]{3,2,1,0:T(8,128)S(1)} %dynamic-slice_bitcast_fusion.2), channel_id=1, source_target_pairs={{0,1},{1,0},{2,3},{3,2},{4,5},{5,4},{6,7},{7,6},{8,9},{9,8},{10,11... | collective-permute-start | bytes 1572872 | tf_op jit(solution)/shard_map/ppermute | solution.py:96
  136.5 13.9 %collective-permute-start.10 = (f32[2,2,32,1024]{3,2,1,0:T(8,128)S(1)}, f32[2,2,32,1024]{3,2,1,0:T(8,128)S(1)}, u32[]{:S(2)}, u32[]{:S(2)}) collective-permute-start(f32[2,2,32,1024]{3,2,1,0:T(8,128)S(1)} %dynamic-slice_bitcast_fusion.3), channel_id=1, source_target_pairs={{0,1},{1,0},{2,3},{3,2},{4,5},{5,4},{6,7},{7,6},{8,9},{9,8},{10,11... | collective-permute-start | bytes 1572872 | tf_op jit(solution)/shard_map/ppermute | solution.py:96
  137.1 13.1 %collective-permute-start.9 = (f32[2,32,1024]{2,1,0:T(8,128)S(1)}, f32[2,32,1024]{2,1,0:T(8,128)S(1)}, u32[]{:S(2)}, u32[]{:S(2)}) collective-permute-start(f32[2,32,1024]{2,1,0:T(8,128)S(1)} %dynamic-slice_bitcast_fusion.12), channel_id=1, source_target_pairs={{0,4},{1,5},{2,6},{3,7},{4,0},{5,1},{6,2},{7,3},{8,12},{9,13},{10,... | collective-permute-start | bytes 786440 | tf_op jit(solution)/shard_map/ppermute | solution.py:96
  138.7 6.5 %collective-permute-start.7 = (f32[32,1024]{1,0:T(8,128)S(1)}, f32[32,1024]{1,0:T(8,128)S(1)}, u32[]{:S(2)}, u32[]{:S(2)}) collective-permute-start(f32[32,1024]{1,0:T(8,128)S(1)} %dynamic-slice_bitcast_fusion.22), channel_id=1, source_target_pairs={{0,2},{1,3},{2,0},{3,1},{4,6},{5,7},{6,4},{7,5},{8,10},{9,11},{10,... | collective-permute-start | bytes 393224 | tf_op jit(solution)/shard_map/ppermute | solution.py:96
  140.2 10.1 %collective-permute-start.8 = (f32[2,32,1024]{2,1,0:T(8,128)S(1)}, f32[2,32,1024]{2,1,0:T(8,128)S(1)}, u32[]{:S(2)}, u32[]{:S(2)}) collective-permute-start(f32[2,32,1024]{2,1,0:T(8,128)S(1)} %dynamic-slice_bitcast_fusion.13), channel_id=1, source_target_pairs={{0,2},{1,3},{2,0},{3,1},{4,6},{5,7},{6,4},{7,5},{8,10},{9,11},{10,... | collective-permute-start | bytes 786440 | tf_op jit(solution)/shard_map/ppermute | solution.py:96
  145.2 5.0 %collective-permute-start.6 = (f32[32,1024]{1,0:T(8,128)S(1)}, f32[32,1024]{1,0:T(8,128)S(1)}, u32[]{:S(2)}, u32[]{:S(2)}) collective-permute-start(f32[32,1024]{1,0:T(8,128)S(1)} %dynamic-slice_bitcast_fusion.23), channel_id=1, source_target_pairs={{0,4},{1,5},{2,6},{3,7},{4,0},{5,1},{6,2},{7,3},{8,12},{9,13},{10,... | collective-permute-start | bytes 393224 | tf_op jit(solution)/shard_map/ppermute | solution.py:96
  156.4 13.4 %collective-permute-start.12 = (f32[32,1024]{1,0:T(8,128)S(1)}, f32[32,1024]{1,0:T(8,128)S(1)}, u32[]{:S(2)}, u32[]{:S(2)}) collective-permute-start(f32[32,1024]{1,0:T(8,128)S(1)} %dynamic-slice_bitcast_fusion.21), channel_id=1, source_target_pairs={{0,4},{1,5},{2,6},{3,7},{4,0},{5,1},{6,2},{7,3},{8,12},{9,13},{10,... | collective-permute-start | bytes 393224 | tf_op jit(solution)/shard_map/ppermute | solution.py:96
  157.9 12.4 %collective-permute-start.13 = (f32[32,1024]{1,0:T(8,128)S(1)}, f32[32,1024]{1,0:T(8,128)S(1)}, u32[]{:S(2)}, u32[]{:S(2)}) collective-permute-start(f32[32,1024]{1,0:T(8,128)S(1)} %dynamic-slice_bitcast_fusion.20), channel_id=1, source_target_pairs={{0,2},{1,3},{2,0},{3,1},{4,6},{5,7},{6,4},{7,5},{8,10},{9,11},{10,... | collective-permute-start | bytes 393224 | tf_op jit(solution)/shard_map/ppermute | solution.py:96
  159.5 10.9 %collective-permute-start.14 = (f32[2,32,1024]{2,1,0:T(8,128)S(1)}, f32[2,32,1024]{2,1,0:T(8,128)S(1)}, u32[]{:S(2)}, u32[]{:S(2)}) collective-permute-start(f32[2,32,1024]{2,1,0:T(8,128)S(1)} %dynamic-slice_bitcast_fusion.11), channel_id=1, source_target_pairs={{0,2},{1,3},{2,0},{3,1},{4,6},{5,7},{6,4},{7,5},{8,10},{9,11},{10,... | collective-permute-start | bytes 786440 | tf_op jit(solution)/shard_map/ppermute | solution.py:96
  160.1 11.9 %collective-permute-start.16 = (f32[2,32,1024]{2,1,0:T(8,128)S(1)}, f32[2,32,1024]{2,1,0:T(8,128)S(1)}, u32[]{:S(2)}, u32[]{:S(2)}) collective-permute-start(f32[2,32,1024]{2,1,0:T(8,128)S(1)} %dynamic-slice_bitcast_fusion.10), channel_id=1, source_target_pairs={{0,4},{1,5},{2,6},{3,7},{4,0},{5,1},{6,2},{7,3},{8,12},{9,13},{10,... | collective-permute-start | bytes 786440 | tf_op jit(solution)/shard_map/ppermute | solution.py:96
  169.6 7.8 %collective-permute-start.18 = (f32[2,2,32,1024]{3,2,1,0:T(8,128)S(1)}, f32[2,2,32,1024]{3,2,1,0:T(8,128)S(1)}, u32[]{:S(2)}, u32[]{:S(2)}) collective-permute-start(f32[2,2,32,1024]{3,2,1,0:T(8,128)S(1)} %dynamic-slice_bitcast_fusion.1), channel_id=1, source_target_pairs={{0,1},{1,0},{2,3},{3,2},{4,5},{5,4},{6,7},{7,6},{8,9},{9,8},{10,11... | collective-permute-start | bytes 1572872 | tf_op jit(solution)/shard_map/ppermute | solution.py:96
  169.7 9.2 %collective-permute-start.21 = (f32[2,2,32,1024]{3,2,1,0:T(8,128)S(1)}, f32[2,2,32,1024]{3,2,1,0:T(8,128)S(1)}, u32[]{:S(2)}, u32[]{:S(2)}) collective-permute-start(f32[2,2,32,1024]{3,2,1,0:T(8,128)S(1)} %dynamic-slice_bitcast_fusion), channel_id=1, source_target_pairs={{0,1},{1,0},{2,3},{3,2},{4,5},{5,4},{6,7},{7,6},{8,9},{9,8},{10,11... | collective-permute-start | bytes 1572872 | tf_op jit(solution)/shard_map/ppermute | solution.py:96
  170.4 5.5 %collective-permute-start.15 = (f32[32,1024]{1,0:T(8,128)S(1)}, f32[32,1024]{1,0:T(8,128)S(1)}, u32[]{:S(2)}, u32[]{:S(2)}) collective-permute-start(f32[32,1024]{1,0:T(8,128)S(1)} %dynamic-slice_bitcast_fusion.19), channel_id=1, source_target_pairs={{0,4},{1,5},{2,6},{3,7},{4,0},{5,1},{6,2},{7,3},{8,12},{9,13},{10,... | collective-permute-start | bytes 393224 | tf_op jit(solution)/shard_map/ppermute | solution.py:96
  172.1 5.2 %collective-permute-start.17 = (f32[32,1024]{1,0:T(8,128)S(1)}, f32[32,1024]{1,0:T(8,128)S(1)}, u32[]{:S(2)}, u32[]{:S(2)}) collective-permute-start(f32[32,1024]{1,0:T(8,128)S(1)} %dynamic-slice_bitcast_fusion.18), channel_id=1, source_target_pairs={{0,2},{1,3},{2,0},{3,1},{4,6},{5,7},{6,4},{7,5},{8,10},{9,11},{10,... | collective-permute-start | bytes 393224 | tf_op jit(solution)/shard_map/ppermute | solution.py:96
  177.5 7.1 %collective-permute-start.19 = (f32[2,32,1024]{2,1,0:T(8,128)S(1)}, f32[2,32,1024]{2,1,0:T(8,128)S(1)}, u32[]{:S(2)}, u32[]{:S(2)}) collective-permute-start(f32[2,32,1024]{2,1,0:T(8,128)S(1)} %dynamic-slice_bitcast_fusion.9), channel_id=1, source_target_pairs={{0,2},{1,3},{2,0},{3,1},{4,6},{5,7},{6,4},{7,5},{8,10},{9,11},{10,... | collective-permute-start | bytes 786440 | tf_op jit(solution)/shard_map/ppermute | solution.py:96
  179.0 7.4 %collective-permute-start.22 = (f32[2,32,1024]{2,1,0:T(8,128)S(1)}, f32[2,32,1024]{2,1,0:T(8,128)S(1)}, u32[]{:S(2)}, u32[]{:S(2)}) collective-permute-start(f32[2,32,1024]{2,1,0:T(8,128)S(1)} %dynamic-slice_bitcast_fusion.8), channel_id=1, source_target_pairs={{0,4},{1,5},{2,6},{3,7},{4,0},{5,1},{6,2},{7,3},{8,12},{9,13},{10,... | collective-permute-start | bytes 786440 | tf_op jit(solution)/shard_map/ppermute | solution.py:96
  184.7 5.0 %collective-permute-start.20 = (f32[32,1024]{1,0:T(8,128)S(1)}, f32[32,1024]{1,0:T(8,128)S(1)}, u32[]{:S(2)}, u32[]{:S(2)}) collective-permute-start(f32[32,1024]{1,0:T(8,128)S(1)} %dynamic-slice_bitcast_fusion.17), channel_id=1, source_target_pairs={{0,4},{1,5},{2,6},{3,7},{4,0},{5,1},{6,2},{7,3},{8,12},{9,13},{10,... | collective-permute-start | bytes 393224 | tf_op jit(solution)/shard_map/ppermute | solution.py:96
  186.5 5.0 %collective-permute-start.23 = (f32[32,1024]{1,0:T(8,128)S(1)}, f32[32,1024]{1,0:T(8,128)S(1)}, u32[]{:S(2)}, u32[]{:S(2)}) collective-permute-start(f32[32,1024]{1,0:T(8,128)S(1)} %dynamic-slice_bitcast_fusion.16), channel_id=1, source_target_pairs={{0,2},{1,3},{2,0},{3,1},{4,6},{5,7},{6,4},{7,5},{8,10},{9,11},{10,... | collective-permute-start | bytes 393224 | tf_op jit(solution)/shard_map/ppermute | solution.py:96
  (3 other events, 6.8 us)
Sparse Core Ops, SparseCore 0:
  16.3 54.8 all-gather.14
  72.7 25.6 all-gather.12
  100.0 27.4 all-gather.10
  128.9 27.4 all-gather.8

commit v19 on v16

--- a/solution.py
+++ b/solution.py
@@ -105,7 +105,7 @@
     rep_count = lax.axis_size("rep")
     peer_count = own_count * rep_count
     slot_count = integrals.shape[0] // peer_count
-    received = lax.all_to_all(integrals, ("own", "rep"), split_axis=0, concat_axis=0, tiled=True)
+
     ab_ids = ab_list.reshape(-1)
     cd_ids = cd_list.reshape(-1)
     live_mask = (
@@ -120,6 +120,8 @@
     levels = rep_count.bit_length() - 1
     orders = (list(range(levels)), [0] + list(range(levels - 1, 0, -1)))
     gathered = [lax.all_gather(local4[:, c], "own", axis=0, tiled=True) for c in range(N_CHUNK)]
+    _, integrals_in = lax.optimization_barrier((gathered[0], integrals))
+    received = lax.all_to_all(integrals_in, ("own", "rep"), split_axis=0, concat_axis=0, tiled=True)
     flows = []
     for chunk in range(N_CHUNK):
         for flow in flows:

time: 200 us -> 208 us (1.040)
  waiting for transfers between devices: 113 us -> 123 us
  starting transfers between devices: 27.4 us -> 24 us
    all_to_all x1, waiting for transfers between devices: 8.25 us -> 61.3 us  [on_device(): lax.all_to_all(integrals_in, ('own', 'rep'), split_axis=0, concat_axis=0,...]
    all_gather x4, waiting for transfers between devices: 72.1 us -> 30.9 us  [on_device(): lax.all_gather(local4[:, c], 'own', axis=0, tiled=True)]
    all_to_all x1, starting transfers between devices: 7.3 us -> 4.09 us  [on_device(): lax.all_to_all(integrals_in, ('own', 'rep'), split_axis=0, concat_axis=0,...]
  transfers between devices with their start and end apart: 29 -> 29, of which waited for: 16 -> 13; matrix products, arithmetic and copies ran while one was open for 7% -> 6% of each run, Pallas kernels for 15% -> 14%
where the time goes in v19:
time: 208 us; the launch traced here: 207 us
  waiting for transfers between devices  123 us (59%)
  Pallas kernels  29.5 us (14%)
  starting transfers between devices  24 us (12%)
  between operations  13.6 us (7%)
  local copies, waits for them, and re-layouts  12.8 us (6%)
  other arithmetic  4.66 us (2%)
    all_to_all x1, waiting for transfers between devices, on_device(): lax.all_to_all(integrals_in, ('own', 'rep'), split_axis=0, concat_axis=0,...  61.3 us
    all_gather x4, waiting for transfers between devices, on_device(): lax.all_gather(local4[:, c], 'own', axis=0, tiled=True)  30.9 us
    pallas_call x4, Pallas kernels, _ladder_products(): pl.pallas_call(_ladder_kernel, grid_spec=grid_spec, out_shape=jax.ShapeDt...  29.5 us
    ppermute x24, waiting for transfers between devices, advance(): self.x = keep + lax.ppermute(send, 'rep', perm=pairs)  29.1 us
    ppermute x24, starting transfers between devices, advance(): self.x = keep + lax.ppermute(send, 'rep', perm=pairs)  19.8 us
    slice x4, local copies, waits for them, and re-layouts, on_device(): flows.extend((_Halving(partial[h], orders[h], rep_count) for h in range(2)))  6.72 us
  transfers between devices with their start and end apart: 29, of which 13 were waited for; matrix products, arithmetic and copies ran while one was open for 6% of the time, Pallas kernels for 14%

profile of v19, /device:TPU:0, one launch (start us, length us, event | category | flops | bytes accessed | tf_op | source)
XLA Modules:
  0.0 207.4 jit_solution(10711846263661243803)
XLA Ops:
  6.5 2.2 %fusion.6 = (bf16[2,1,32,2048]{3,2,1,0:T(8,128)(2,1)}, bf16[2,1,32,2048]{3,2,1,0:T(8,128)(2,1)}, bf16[2,1,32,2048]{3,2,1,0:T(8,128)(2,1)}, bf16[2,1,32,2048]{3,2,1,0:T(8,128)(2,1)}) fusion(bf16[2,4,32,2048]{3,2,1,0:T(8,128)(2,1)} %bitcast.126), kind=kLoop, calls=%fused_computation.63 | loop fusion | bytes 2097152 | tf_op jit(solution)/shard_map/slice | solution.py:122
  8.7 30.9 %all-gather.15.cloned.1.call-done = bf16[8,1,32,2048]{3,2,1,0:T(8,128)(2,1)} async-done(((bf16[2,1,32,2048]{3,2,1,0:T(8,128)(2,1)}), bf16[8,1,32,2048]{3,2,1,0:T(8,128)(2,1)}) %all-gather.15.cloned.1.call-update) | async-done | bytes 1048592 | tf_op jit(solution)/shard_map/all_gather | solution.py:122
  39.6 4.1 %all-to-all-start = ((bf16[64,128,128]{2,1,0:T(8,128)(2,1)}), bf16[64,128,128]{2,1,0:T(8,128)(2,1)S(1)}, u32[]{:S(2)}, u32[]{:S(2)}) async-start(bf16[64,128,128]{2,1,0:T(8,128)(2,1)} %param.6), calls=%async_computation | async-start | bytes 4194304 | tf_op jit(solution)/shard_map/all_to_all | solution.py:124
  47.9 61.3 %all-to-all-done.tiles_ref = bf16[64,128,128]{2,1,0:T(8,128)(2,1)S(1)} async-done(((bf16[64,128,128]{2,1,0:T(8,128)(2,1)}), bf16[64,128,128]{2,1,0:T(8,128)(2,1)S(1)}, u32[]{:S(2)}, u32[]{:S(2)}) %all-to-all-start) | async-done | bytes 2097184 | tf_op jit(solution)/shard_map/all_to_all | solution.py:124
  109.3 1.4 copy-done
  110.6 7.4 %shard_map.55 = f32[2,256,1024]{2,1,0:T(8,128)} custom-call(s32[64]{0:T(128)} %select_reduce_fusion.order_ref, s32[17]{0:T(128)} %convert_reduce_fusion.1.starts_ref, s32[64]{0:T(128)} %copy-done.4, s32[64]{0:T(128)} %reshape.46.cd_ref, bf16[8,32,2048]{2,1,0:T(8,128)(2,1)} %bitcast.131, bf16[64,128,128]{2,1,0:T(8,128)(2,1)} %copy-done), custom_call_target="tpu_custom_call" | custom-call | flops 2147483648 | bytes 5242880 | tf_op jit(solution)/shard_map/pallas_call | solution.py:69
  118.0 1.7 fusion.5
  121.9 1.1 bitcast_add_fusion.6
  123.1 7.4 %shard_map.56 = f32[2,256,1024]{2,1,0:T(8,128)} custom-call(s32[64]{0:T(128)} %select_reduce_fusion.order_ref, s32[17]{0:T(128)} %convert_reduce_fusion.1.starts_ref, s32[64]{0:T(128)} %copy-done.4, s32[64]{0:T(128)} %reshape.46.cd_ref, bf16[8,32,2048]{2,1,0:T(8,128)(2,1)} %bitcast.130, bf16[64,128,128]{2,1,0:T(8,128)(2,1)} %copy-done), custom_call_target="tpu_custom_call" | custom-call | flops 2147483648 | bytes 5242880 | tf_op jit(solution)/shard_map/pallas_call | solution.py:69
  130.5 1.7 fusion.4
  132.2 1.6 collective-permute-start.3
  133.9 1.3 collective-permute-start.2
  135.5 5.2 %collective-permute-done.3 = f32[2,32,1024]{2,1,0:T(8,128)S(1)} collective-permute-done((f32[2,32,1024]{2,1,0:T(8,128)S(1)}, f32[2,32,1024]{2,1,0:T(8,128)S(1)}, u32[]{:S(2)}, u32[]{:S(2)}) %collective-permute-start.3) | collective-permute-done | bytes 262176 | tf_op jit(solution)/shard_map/ppermute | solution.py:96
  140.7 1.9 collective-permute-done.2
  142.9 7.4 %shard_map.57 = f32[2,256,1024]{2,1,0:T(8,128)} custom-call(s32[64]{0:T(128)} %select_reduce_fusion.order_ref, s32[17]{0:T(128)} %convert_reduce_fusion.1.starts_ref, s32[64]{0:T(128)} %copy-done.4, s32[64]{0:T(128)} %reshape.46.cd_ref, bf16[8,32,2048]{2,1,0:T(8,128)(2,1)} %bitcast.129, bf16[64,128,128]{2,1,0:T(8,128)(2,1)} %copy-done), custom_call_target="tpu_custom_call" | custom-call | flops 2147483648 | bytes 5242880 | tf_op jit(solution)/shard_map/pallas_call | solution.py:69
  150.3 1.7 fusion.3
  153.4 1.4 collective-permute-start.7
  155.6 4.3 %collective-permute-done.7 = f32[32,1024]{1,0:T(8,128)S(1)} collective-permute-done((f32[32,1024]{1,0:T(8,128)S(1)}, f32[32,1024]{1,0:T(8,128)S(1)}, u32[]{:S(2)}, u32[]{:S(2)}) %collective-permute-start.7) | collective-permute-done | bytes 131104 | tf_op jit(solution)/shard_map/ppermute | solution.py:96
  159.8 1.5 collective-permute-start.6
  161.3 3.5 %collective-permute-done.6 = f32[32,1024]{1,0:T(8,128)S(1)} collective-permute-done((f32[32,1024]{1,0:T(8,128)S(1)}, f32[32,1024]{1,0:T(8,128)S(1)}, u32[]{:S(2)}, u32[]{:S(2)}) %collective-permute-start.6) | collective-permute-done | bytes 131104 | tf_op jit(solution)/shard_map/ppermute | solution.py:96
  165.2 1.6 collective-permute-start.12
  166.7 1.2 collective-permute-start.13
  169.5 7.4 %shard_map.58 = f32[2,256,1024]{2,1,0:T(8,128)} custom-call(s32[64]{0:T(128)} %select_reduce_fusion.order_ref, s32[17]{0:T(128)} %convert_reduce_fusion.1.starts_ref, s32[64]{0:T(128)} %copy-done.4, s32[64]{0:T(128)} %reshape.46.cd_ref, bf16[8,32,2048]{2,1,0:T(8,128)(2,1)} %bitcast.128, bf16[64,128,128]{2,1,0:T(8,128)(2,1)} %copy-done), custom_call_target="tpu_custom_call" | custom-call | flops 2147483648 | bytes 5242880 | tf_op jit(solution)/shard_map/pallas_call | solution.py:69
  176.9 1.7 fusion.2
  179.5 1.6 collective-permute-start.15
  181.1 1.1 collective-permute-start.17
  182.2 2.8 %collective-permute-done.15 = f32[32,1024]{1,0:T(8,128)S(1)} collective-permute-done((f32[32,1024]{1,0:T(8,128)S(1)}, f32[32,1024]{1,0:T(8,128)S(1)}, u32[]{:S(2)}, u32[]{:S(2)}) %collective-permute-start.15) | collective-permute-done | bytes 131104 | tf_op jit(solution)/shard_map/ppermute | solution.py:96
  185.0 1.3 collective-permute-done.17
  186.5 1.1 collective-permute-start.19
  188.5 5.1 %collective-permute-done.19 = f32[2,32,1024]{2,1,0:T(8,128)S(1)} collective-permute-done((f32[2,32,1024]{2,1,0:T(8,128)S(1)}, f32[2,32,1024]{2,1,0:T(8,128)S(1)}, u32[]{:S(2)}, u32[]{:S(2)}) %collective-permute-start.19) | collective-permute-done | bytes 262176 | tf_op jit(solution)/shard_map/ppermute | solution.py:96
  194.7 1.1 collective-permute-start.23
  195.9 2.8 %collective-permute-done.20 = f32[32,1024]{1,0:T(8,128)S(1)} collective-permute-done((f32[32,1024]{1,0:T(8,128)S(1)}, f32[32,1024]{1,0:T(8,128)S(1)}, u32[]{:S(2)}, u32[]{:S(2)}) %collective-permute-start.20) | collective-permute-done | bytes 131104 | tf_op jit(solution)/shard_map/ppermute | solution.py:96
  (108 shorter events, 16.3 us)
Async XLA Ops:
  6.5 33.1 %all-gather.15.cloned.1.call-start = ((), (), s32[]{:S(2)}) async-start(), calls=%async_computation.4 | async-start | bytes 1310720 | tf_op jit(solution)/shard_map/all_gather | solution.py:122
  39.6 5.9 %copy-start.3 = (s32[1,32]{1,0:T(1,128)S(1)}, s32[1,32]{1,0:T(1,128)}, u32[]{:S(2)}) copy-start(s32[1,32]{1,0:T(1,128)} %param.9) | copy-start | bytes 388
  39.6 6.1 %copy-start.2 = (s32[1,32,2]{1,2,0:T(2,128)S(1)}, s32[1,32,2]{1,2,0:T(2,128)}, u32[]{:S(2)}) copy-start(s32[1,32,2]{1,2,0:T(2,128)} %param.8) | copy-start | bytes 772
  39.6 69.7 %all-to-all-start = ((bf16[64,128,128]{2,1,0:T(8,128)(2,1)}), bf16[64,128,128]{2,1,0:T(8,128)(2,1)S(1)}, u32[]{:S(2)}, u32[]{:S(2)}) async-start(bf16[64,128,128]{2,1,0:T(8,128)(2,1)} %param.6), calls=%async_computation | async-start | bytes 4194304 | tf_op jit(solution)/shard_map/all_to_all | solution.py:124
  43.7 79.4 %all-gather.13.cloned.1.call-start = ((), (), s32[]{:S(2)}) async-start(), calls=%async_computation.3 | async-start | bytes 1310720 | tf_op jit(solution)/shard_map/all_gather | solution.py:122
  44.4 98.5 %all-gather.11.cloned.1.call-start = ((), (), s32[]{:S(2)}) async-start(), calls=%async_computation.2 | async-start | bytes 1310720 | tf_op jit(solution)/shard_map/all_gather | solution.py:122
  45.2 120.0 %all-gather.9.cloned.1.call-start = ((), (), s32[]{:S(2)}) async-start(), calls=%async_computation.1 | async-start | bytes 1310720 | tf_op jit(solution)/shard_map/all_gather | solution.py:122
  45.4 63.8 %copy-start.4 = (s32[64]{0:T(128)}, s32[64]{0:T(128)S(1)}, u32[]{:S(2)}) copy-start(s32[64]{0:T(128)S(1)} %reshape.45.ab_ref) | copy-start | bytes 772
  119.8 2.1 %collective-permute-start.1 = (f32[2,2,32,1024]{3,2,1,0:T(8,128)S(1)}, f32[2,2,32,1024]{3,2,1,0:T(8,128)}, u32[]{:S(2)}, u32[]{:S(2)}) collective-permute-start(f32[2,2,32,1024]{3,2,1,0:T(8,128)S(1)} %dynamic-slice_bitcast_fusion.6), channel_id=1, source_target_pairs={{0,1},{1,0},{2,3},{3,2},{4,5},{5,4},{6,7},{7,6},{8,9},{9,8},{10,11... | collective-permute-start | bytes 1572872 | tf_op jit(solution)/shard_map/ppermute | solution.py:96
  120.7 2.3 %collective-permute-start = (f32[2,2,32,1024]{3,2,1,0:T(8,128)}, f32[2,2,32,1024]{3,2,1,0:T(8,128)S(1)}, u32[]{:S(2)}, u32[]{:S(2)}) collective-permute-start(f32[2,2,32,1024]{3,2,1,0:T(8,128)} %dynamic-slice_bitcast_fusion.7), channel_id=1, source_target_pairs={{0,1},{1,0},{2,3},{3,2},{4,5},{5,4},{6,7},{7,6},{8,9},{9,8},{10,11... | collective-permute-start | bytes 1572872 | tf_op jit(solution)/shard_map/ppermute | solution.py:96
  132.2 8.5 %collective-permute-start.3 = (f32[2,32,1024]{2,1,0:T(8,128)S(1)}, f32[2,32,1024]{2,1,0:T(8,128)S(1)}, u32[]{:S(2)}, u32[]{:S(2)}) collective-permute-start(f32[2,32,1024]{2,1,0:T(8,128)S(1)} %dynamic-slice_bitcast_fusion.14), channel_id=1, source_target_pairs={{0,4},{1,5},{2,6},{3,7},{4,0},{5,1},{6,2},{7,3},{8,12},{9,13},{10,... | collective-permute-start | bytes 786440 | tf_op jit(solution)/shard_map/ppermute | solution.py:96
  133.8 8.9 %collective-permute-start.5 = (f32[2,2,32,1024]{3,2,1,0:T(8,128)S(1)}, f32[2,2,32,1024]{3,2,1,0:T(8,128)S(1)}, u32[]{:S(2)}, u32[]{:S(2)}) collective-permute-start(f32[2,2,32,1024]{3,2,1,0:T(8,128)S(1)} %dynamic-slice_bitcast_fusion.4), channel_id=1, source_target_pairs={{0,1},{1,0},{2,3},{3,2},{4,5},{5,4},{6,7},{7,6},{8,9},{9,8},{10,11... | collective-permute-start | bytes 1572872 | tf_op jit(solution)/shard_map/ppermute | solution.py:96
  133.9 8.8 %collective-permute-start.2 = (f32[2,32,1024]{2,1,0:T(8,128)S(1)}, f32[2,32,1024]{2,1,0:T(8,128)S(1)}, u32[]{:S(2)}, u32[]{:S(2)}) collective-permute-start(f32[2,32,1024]{2,1,0:T(8,128)S(1)} %dynamic-slice_bitcast_fusion.15), channel_id=1, source_target_pairs={{0,2},{1,3},{2,0},{3,1},{4,6},{5,7},{6,4},{7,5},{8,10},{9,11},{10,... | collective-permute-start | bytes 786440 | tf_op jit(solution)/shard_map/ppermute | solution.py:96
  135.3 7.5 %collective-permute-start.4 = (f32[2,2,32,1024]{3,2,1,0:T(8,128)S(1)}, f32[2,2,32,1024]{3,2,1,0:T(8,128)S(1)}, u32[]{:S(2)}, u32[]{:S(2)}) collective-permute-start(f32[2,2,32,1024]{3,2,1,0:T(8,128)S(1)} %dynamic-slice_bitcast_fusion.5), channel_id=1, source_target_pairs={{0,1},{1,0},{2,3},{3,2},{4,5},{5,4},{6,7},{7,6},{8,9},{9,8},{10,11... | collective-permute-start | bytes 1572872 | tf_op jit(solution)/shard_map/ppermute | solution.py:96
  152.1 12.9 %collective-permute-start.11 = (f32[2,2,32,1024]{3,2,1,0:T(8,128)S(1)}, f32[2,2,32,1024]{3,2,1,0:T(8,128)S(1)}, u32[]{:S(2)}, u32[]{:S(2)}) collective-permute-start(f32[2,2,32,1024]{3,2,1,0:T(8,128)S(1)} %dynamic-slice_bitcast_fusion.2), channel_id=1, source_target_pairs={{0,1},{1,0},{2,3},{3,2},{4,5},{5,4},{6,7},{7,6},{8,9},{9,8},{10,11... | collective-permute-start | bytes 1572872 | tf_op jit(solution)/shard_map/ppermute | solution.py:96
  152.2 12.8 %collective-permute-start.10 = (f32[2,2,32,1024]{3,2,1,0:T(8,128)S(1)}, f32[2,2,32,1024]{3,2,1,0:T(8,128)S(1)}, u32[]{:S(2)}, u32[]{:S(2)}) collective-permute-start(f32[2,2,32,1024]{3,2,1,0:T(8,128)S(1)} %dynamic-slice_bitcast_fusion.3), channel_id=1, source_target_pairs={{0,1},{1,0},{2,3},{3,2},{4,5},{5,4},{6,7},{7,6},{8,9},{9,8},{10,11... | collective-permute-start | bytes 1572872 | tf_op jit(solution)/shard_map/ppermute | solution.py:96
  152.8 12.1 %collective-permute-start.9 = (f32[2,32,1024]{2,1,0:T(8,128)S(1)}, f32[2,32,1024]{2,1,0:T(8,128)S(1)}, u32[]{:S(2)}, u32[]{:S(2)}) collective-permute-start(f32[2,32,1024]{2,1,0:T(8,128)S(1)} %dynamic-slice_bitcast_fusion.12), channel_id=1, source_target_pairs={{0,4},{1,5},{2,6},{3,7},{4,0},{5,1},{6,2},{7,3},{8,12},{9,13},{10,... | collective-permute-start | bytes 786440 | tf_op jit(solution)/shard_map/ppermute | solution.py:96
  153.4 6.5 %collective-permute-start.7 = (f32[32,1024]{1,0:T(8,128)S(1)}, f32[32,1024]{1,0:T(8,128)S(1)}, u32[]{:S(2)}, u32[]{:S(2)}) collective-permute-start(f32[32,1024]{1,0:T(8,128)S(1)} %dynamic-slice_bitcast_fusion.22), channel_id=1, source_target_pairs={{0,2},{1,3},{2,0},{3,1},{4,6},{5,7},{6,4},{7,5},{8,10},{9,11},{10,... | collective-permute-start | bytes 393224 | tf_op jit(solution)/shard_map/ppermute | solution.py:96
  154.8 10.1 %collective-permute-start.8 = (f32[2,32,1024]{2,1,0:T(8,128)S(1)}, f32[2,32,1024]{2,1,0:T(8,128)S(1)}, u32[]{:S(2)}, u32[]{:S(2)}) collective-permute-start(f32[2,32,1024]{2,1,0:T(8,128)S(1)} %dynamic-slice_bitcast_fusion.13), channel_id=1, source_target_pairs={{0,2},{1,3},{2,0},{3,1},{4,6},{5,7},{6,4},{7,5},{8,10},{9,11},{10,... | collective-permute-start | bytes 786440 | tf_op jit(solution)/shard_map/ppermute | solution.py:96
  159.8 5.0 %collective-permute-start.6 = (f32[32,1024]{1,0:T(8,128)S(1)}, f32[32,1024]{1,0:T(8,128)S(1)}, u32[]{:S(2)}, u32[]{:S(2)}) collective-permute-start(f32[32,1024]{1,0:T(8,128)S(1)} %dynamic-slice_bitcast_fusion.23), channel_id=1, source_target_pairs={{0,4},{1,5},{2,6},{3,7},{4,0},{5,1},{6,2},{7,3},{8,12},{9,13},{10,... | collective-permute-start | bytes 393224 | tf_op jit(solution)/shard_map/ppermute | solution.py:96
  165.2 13.6 %collective-permute-start.12 = (f32[32,1024]{1,0:T(8,128)S(1)}, f32[32,1024]{1,0:T(8,128)S(1)}, u32[]{:S(2)}, u32[]{:S(2)}) collective-permute-start(f32[32,1024]{1,0:T(8,128)S(1)} %dynamic-slice_bitcast_fusion.21), channel_id=1, source_target_pairs={{0,4},{1,5},{2,6},{3,7},{4,0},{5,1},{6,2},{7,3},{8,12},{9,13},{10,... | collective-permute-start | bytes 393224 | tf_op jit(solution)/shard_map/ppermute | solution.py:96
  166.7 12.6 %collective-permute-start.13 = (f32[32,1024]{1,0:T(8,128)S(1)}, f32[32,1024]{1,0:T(8,128)S(1)}, u32[]{:S(2)}, u32[]{:S(2)}) collective-permute-start(f32[32,1024]{1,0:T(8,128)S(1)} %dynamic-slice_bitcast_fusion.20), channel_id=1, source_target_pairs={{0,2},{1,3},{2,0},{3,1},{4,6},{5,7},{6,4},{7,5},{8,10},{9,11},{10,... | collective-permute-start | bytes 393224 | tf_op jit(solution)/shard_map/ppermute | solution.py:96
  168.0 11.4 %collective-permute-start.14 = (f32[2,32,1024]{2,1,0:T(8,128)S(1)}, f32[2,32,1024]{2,1,0:T(8,128)S(1)}, u32[]{:S(2)}, u32[]{:S(2)}) collective-permute-start(f32[2,32,1024]{2,1,0:T(8,128)S(1)} %dynamic-slice_bitcast_fusion.11), channel_id=1, source_target_pairs={{0,2},{1,3},{2,0},{3,1},{4,6},{5,7},{6,4},{7,5},{8,10},{9,11},{10,... | collective-permute-start | bytes 786440 | tf_op jit(solution)/shard_map/ppermute | solution.py:96
  168.9 12.1 %collective-permute-start.16 = (f32[2,32,1024]{2,1,0:T(8,128)S(1)}, f32[2,32,1024]{2,1,0:T(8,128)S(1)}, u32[]{:S(2)}, u32[]{:S(2)}) collective-permute-start(f32[2,32,1024]{2,1,0:T(8,128)S(1)} %dynamic-slice_bitcast_fusion.10), channel_id=1, source_target_pairs={{0,4},{1,5},{2,6},{3,7},{4,0},{5,1},{6,2},{7,3},{8,12},{9,13},{10,... | collective-permute-start | bytes 786440 | tf_op jit(solution)/shard_map/ppermute | solution.py:96
  178.7 7.7 %collective-permute-start.18 = (f32[2,2,32,1024]{3,2,1,0:T(8,128)S(1)}, f32[2,2,32,1024]{3,2,1,0:T(8,128)S(1)}, u32[]{:S(2)}, u32[]{:S(2)}) collective-permute-start(f32[2,2,32,1024]{3,2,1,0:T(8,128)S(1)} %dynamic-slice_bitcast_fusion.1), channel_id=1, source_target_pairs={{0,1},{1,0},{2,3},{3,2},{4,5},{5,4},{6,7},{7,6},{8,9},{9,8},{10,11... | collective-permute-start | bytes 1572872 | tf_op jit(solution)/shard_map/ppermute | solution.py:96
  178.8 8.7 %collective-permute-start.21 = (f32[2,2,32,1024]{3,2,1,0:T(8,128)S(1)}, f32[2,2,32,1024]{3,2,1,0:T(8,128)S(1)}, u32[]{:S(2)}, u32[]{:S(2)}) collective-permute-start(f32[2,2,32,1024]{3,2,1,0:T(8,128)S(1)} %dynamic-slice_bitcast_fusion), channel_id=1, source_target_pairs={{0,1},{1,0},{2,3},{3,2},{4,5},{5,4},{6,7},{7,6},{8,9},{9,8},{10,11... | collective-permute-start | bytes 1572872 | tf_op jit(solution)/shard_map/ppermute | solution.py:96
  179.5 5.5 %collective-permute-start.15 = (f32[32,1024]{1,0:T(8,128)S(1)}, f32[32,1024]{1,0:T(8,128)S(1)}, u32[]{:S(2)}, u32[]{:S(2)}) collective-permute-start(f32[32,1024]{1,0:T(8,128)S(1)} %dynamic-slice_bitcast_fusion.19), channel_id=1, source_target_pairs={{0,4},{1,5},{2,6},{3,7},{4,0},{5,1},{6,2},{7,3},{8,12},{9,13},{10,... | collective-permute-start | bytes 393224 | tf_op jit(solution)/shard_map/ppermute | solution.py:96
  181.1 5.2 %collective-permute-start.17 = (f32[32,1024]{1,0:T(8,128)S(1)}, f32[32,1024]{1,0:T(8,128)S(1)}, u32[]{:S(2)}, u32[]{:S(2)}) collective-permute-start(f32[32,1024]{1,0:T(8,128)S(1)} %dynamic-slice_bitcast_fusion.18), channel_id=1, source_target_pairs={{0,2},{1,3},{2,0},{3,1},{4,6},{5,7},{6,4},{7,5},{8,10},{9,11},{10,... | collective-permute-start | bytes 393224 | tf_op jit(solution)/shard_map/ppermute | solution.py:96
  186.5 7.1 %collective-permute-start.19 = (f32[2,32,1024]{2,1,0:T(8,128)S(1)}, f32[2,32,1024]{2,1,0:T(8,128)S(1)}, u32[]{:S(2)}, u32[]{:S(2)}) collective-permute-start(f32[2,32,1024]{2,1,0:T(8,128)S(1)} %dynamic-slice_bitcast_fusion.9), channel_id=1, source_target_pairs={{0,2},{1,3},{2,0},{3,1},{4,6},{5,7},{6,4},{7,5},{8,10},{9,11},{10,... | collective-permute-start | bytes 786440 | tf_op jit(solution)/shard_map/ppermute | solution.py:96
  187.7 7.0 %collective-permute-start.22 = (f32[2,32,1024]{2,1,0:T(8,128)S(1)}, f32[2,32,1024]{2,1,0:T(8,128)S(1)}, u32[]{:S(2)}, u32[]{:S(2)}) collective-permute-start(f32[2,32,1024]{2,1,0:T(8,128)S(1)} %dynamic-slice_bitcast_fusion.8), channel_id=1, source_target_pairs={{0,4},{1,5},{2,6},{3,7},{4,0},{5,1},{6,2},{7,3},{8,12},{9,13},{10,... | collective-permute-start | bytes 786440 | tf_op jit(solution)/shard_map/ppermute | solution.py:96
  193.7 5.0 %collective-permute-start.20 = (f32[32,1024]{1,0:T(8,128)S(1)}, f32[32,1024]{1,0:T(8,128)S(1)}, u32[]{:S(2)}, u32[]{:S(2)}) collective-permute-start(f32[32,1024]{1,0:T(8,128)S(1)} %dynamic-slice_bitcast_fusion.17), channel_id=1, source_target_pairs={{0,4},{1,5},{2,6},{3,7},{4,0},{5,1},{6,2},{7,3},{8,12},{9,13},{10,... | collective-permute-start | bytes 393224 | tf_op jit(solution)/shard_map/ppermute | solution.py:96
  194.7 5.0 %collective-permute-start.23 = (f32[32,1024]{1,0:T(8,128)S(1)}, f32[32,1024]{1,0:T(8,128)S(1)}, u32[]{:S(2)}, u32[]{:S(2)}) collective-permute-start(f32[32,1024]{1,0:T(8,128)S(1)} %dynamic-slice_bitcast_fusion.16), channel_id=1, source_target_pairs={{0,2},{1,3},{2,0},{3,1},{4,6},{5,7},{6,4},{7,5},{8,10},{9,11},{10,... | collective-permute-start | bytes 393224 | tf_op jit(solution)/shard_map/ppermute | solution.py:96
  (2 other events, 7.0 us)
Sparse Core Ops, SparseCore 0:
  8.9 30.6 all-gather.14
  46.1 54.8 all-gather.12
  102.6 25.6 all-gather.10
  129.7 27.4 all-gather.8

commit v20 on v16

--- a/solution.py
+++ b/solution.py
@@ -98,6 +98,58 @@
 
     def result(self):
         return self.x.reshape(self.part, self.width)
+
+
+class _Pair:
+    def __init__(self, partial2, orders, rep_count):
+        self.levels = rep_count.bit_length() - 1
+        self.rep_count = rep_count
+        self.part = partial2.shape[1] // rep_count
+        self.width = partial2.shape[2]
+        self.joint = partial2.reshape((2,) + (2,) * self.levels + (self.part, self.width))
+        self.orders = orders
+        self.halves = None
+
+    @property
+    def todo(self):
+        return self.halves is None or any(h.todo for h in self.halves)
+
+    @property
+    def x(self):
+        return self.joint if self.halves is None else [h.x for h in self.halves]
+
+    @x.setter
+    def x(self, value):
+        if self.halves is None:
+            self.joint = value
+        else:
+            for h, v in zip(self.halves, value):
+                h.x = v
+
+    def advance(self, rep_index):
+        if self.halves is not None:
+            for h in self.halves:
+                h.advance(rep_index)
+            return
+        bit = self.orders[0][0]
+        ax = 1 + (self.levels - 1 - bit)
+        mine = (rep_index >> bit) & 1
+        keep = lax.dynamic_index_in_dim(self.joint, mine, ax, keepdims=False)
+        send = lax.dynamic_index_in_dim(self.joint, 1 - mine, ax, keepdims=False)
+        pairs = [(i, i ^ (1 << bit)) for i in range(self.rep_count)]
+        both = keep + lax.ppermute(send, "rep", perm=pairs)
+        self.halves = []
+        for h in range(2):
+            flow = object.__new__(_Halving)
+            flow.levels, flow.part, flow.width = self.levels, self.part, self.width
+            flow.rep_count = self.rep_count
+            flow.x = both[h]
+            flow.axis_bits = [b for b in range(self.levels - 1, -1, -1) if b != bit]
+            flow.todo = list(self.orders[h][1:])
+            self.halves.append(flow)
+
+    def result(self):
+        return jnp.concatenate([h.result() for h in self.halves], axis=1)
 
 
 def on_device(amplitudes, integrals, ab_list, cd_list, live_count):
@@ -131,14 +183,11 @@
         else:
             amp3 = gathered[chunk]
         partial = _ladder_products(amp3, received, order, starts, ab_ids, cd_ids, AB_DEV)
-        flows.extend(_Halving(partial[h], orders[h], rep_count) for h in range(2))
+        flows.append(_Pair(partial, orders, rep_count))
     while any(flow.todo for flow in flows):
         for flow in flows:
             flow.advance(rep_index)
-    pieces = [
-        jnp.concatenate([flows[2 * c].result(), flows[2 * c + 1].result()], axis=1)
-        for c in range(N_CHUNK)
-    ]
+    pieces = [flow.result() for flow in flows]
     return jnp.concatenate(pieces, axis=0)
 
 

time: 200 us -> 199 us (level)
  waiting for transfers between devices: 113 us -> 107 us
  other arithmetic: 4.69 us -> 7.97 us
    squeeze x0 -> x7, local copies, waits for them, and re-layouts: none -> 6.95 us  [the longest x4 6.64 us: advance(): send = lax.dynamic_index_in_dim(self.joint, 1 - mine, ax, keepdims=False)]
    slice x4 -> x1, local copies, waits for them, and re-layouts: 6.89 us -> 0.07 us  [advance(): flow.x = both[h]]
    ppermute x24 -> x16, waiting for transfers between devices: 30.7 us -> 26.1 us  [advance(): self.x = keep + lax.ppermute(send, 'rep', perm=pairs)]
    add x0 -> x4, other arithmetic: none -> 3.1 us  [advance(): both = keep + lax.ppermute(send, 'rep', perm=pairs)]
    ppermute x0 -> x4, waiting for transfers between devices: none -> 2.71 us  [advance(): both = keep + lax.ppermute(send, 'rep', perm=pairs)]
    all_gather x4, waiting for transfers between devices: 72.1 us -> 69.5 us  [on_device(): lax.all_gather(local4[:, c], 'own', axis=0, tiled=True)]
    ppermute x24 -> x16, starting transfers between devices: 19.9 us -> 20.4 us  [advance(): self.x = keep + lax.ppermute(send, 'rep', perm=pairs)]
  transfers between devices with their start and end apart: 29 -> 25, of which waited for: 16 -> 15; matrix products, arithmetic and copies ran while one was open for 7% -> 9% of each run, Pallas kernels for 15% -> 15%
where the time goes in v20:
time: 199 us; the launch traced here: 198 us
  waiting for transfers between devices  107 us (54%)
  Pallas kernels  30 us (15%)
  starting transfers between devices  28 us (14%)
  between operations  13.6 us (7%)
  local copies, waits for them, and re-layouts  11.5 us (6%)
  other arithmetic  7.97 us (4%)
    all_gather x4, waiting for transfers between devices, on_device(): lax.all_gather(local4[:, c], 'own', axis=0, tiled=True)  69.5 us
    pallas_call x4, Pallas kernels, _ladder_products(): pl.pallas_call(_ladder_kernel, grid_spec=grid_spec, out_shape=jax.ShapeDt...  30 us
    ppermute x16, waiting for transfers between devices, advance(): self.x = keep + lax.ppermute(send, 'rep', perm=pairs)  26.1 us
    ppermute x16, starting transfers between devices, advance(): self.x = keep + lax.ppermute(send, 'rep', perm=pairs)  20.4 us
    all_to_all x1, waiting for transfers between devices, on_device(): lax.all_to_all(integrals, ('own', 'rep'), split_axis=0, concat_axis=0, ti...  8.25 us
    all_to_all x1, starting transfers between devices, on_device(): lax.all_to_all(integrals, ('own', 'rep'), split_axis=0, concat_axis=0, ti...  7.3 us
    squeeze x4, local copies, waits for them, and re-layouts, advance(): send = lax.dynamic_index_in_dim(self.joint, 1 - mine, ax, keepdims=False)  6.64 us
  transfers between devices with their start and end apart: 25, of which 15 were waited for; matrix products, arithmetic and copies ran while one was open for 9% of the time, Pallas kernels for 15%

profile of v20, /device:TPU:0, one launch (start us, length us, event | category | flops | bytes accessed | tf_op | source)
XLA Modules:
  0.0 198.3 jit_solution(4479231111505109114)
XLA Ops:
  6.5 7.3 %all-to-all-start = ((bf16[64,128,128]{2,1,0:T(8,128)(2,1)}), bf16[64,128,128]{2,1,0:T(8,128)(2,1)S(1)}, u32[]{:S(2)}, u32[]{:S(2)}) async-start(bf16[64,128,128]{2,1,0:T(8,128)(2,1)} %param.6), calls=%async_computation | async-start | bytes 4194304 | tf_op jit(solution)/shard_map/all_to_all | solution.py:160
  18.4 52.8 %all-gather.15.cloned.1.call-done = bf16[8,1,32,2048]{3,2,1,0:T(8,128)(2,1)} async-done(((bf16[2,1,32,2048]{3,2,1,0:T(8,128)(2,1)}), bf16[8,1,32,2048]{3,2,1,0:T(8,128)(2,1)}) %all-gather.15.cloned.1.call-update) | async-done | bytes 1048592 | tf_op jit(solution)/shard_map/all_gather | solution.py:174
  71.2 8.2 %all-to-all-done.tiles_ref = bf16[64,128,128]{2,1,0:T(8,128)(2,1)S(1)} async-done(((bf16[64,128,128]{2,1,0:T(8,128)(2,1)}), bf16[64,128,128]{2,1,0:T(8,128)(2,1)S(1)}, u32[]{:S(2)}, u32[]{:S(2)}) %all-to-all-start) | async-done | bytes 2097184 | tf_op jit(solution)/shard_map/all_to_all | solution.py:160
  80.8 7.5 %shard_map.55 = f32[2,256,1024]{2,1,0:T(8,128)} custom-call(s32[64]{0:T(128)} %select_reduce_fusion.order_ref, s32[17]{0:T(128)} %convert_reduce_fusion.1.starts_ref, s32[64]{0:T(128)} %copy-done.9, s32[64]{0:T(128)} %reshape.66.cd_ref, bf16[8,32,2048]{2,1,0:T(8,128)(2,1)} %bitcast.115, bf16[64,128,128]{2,1,0:T(8,128)(2,1)} %copy-done.4), custom_call_target="tpu_custom_call" | custom-call | flops 2147483648 | bytes 5242880 | tf_op jit(solution)/shard_map/pallas_call | solution.py:69
  88.3 1.4 dynamic-slice_bitcast_fusion.3
  89.9 2.7 %collective-permute-done = f32[2,2,2,32,1024]{4,3,2,1,0:T(8,128)} collective-permute-done((f32[2,2,2,32,1024]{4,3,2,1,0:T(8,128)S(1)}, f32[2,2,2,32,1024]{4,3,2,1,0:T(8,128)}, u32[]{:S(2)}, u32[]{:S(2)}) %collective-permute-start) | collective-permute-done | bytes 1048608 | tf_op jit(solution)/shard_map/ppermute | solution.py:140
  94.1 4.4 %all-gather.13.cloned.1.call-done = bf16[8,1,32,2048]{3,2,1,0:T(8,128)(2,1)} async-done(((bf16[2,1,32,2048]{3,2,1,0:T(8,128)(2,1)}), bf16[8,1,32,2048]{3,2,1,0:T(8,128)(2,1)}) %all-gather.13.cloned.1.call-update) | async-done | bytes 1048592 | tf_op jit(solution)/shard_map/all_gather | solution.py:174
  98.4 7.5 %shard_map.56 = f32[2,256,1024]{2,1,0:T(8,128)} custom-call(s32[64]{0:T(128)} %select_reduce_fusion.order_ref, s32[17]{0:T(128)} %convert_reduce_fusion.1.starts_ref, s32[64]{0:T(128)} %copy-done.9, s32[64]{0:T(128)} %reshape.66.cd_ref, bf16[8,32,2048]{2,1,0:T(8,128)(2,1)} %bitcast.114, bf16[64,128,128]{2,1,0:T(8,128)(2,1)} %copy-done.4), custom_call_target="tpu_custom_call" | custom-call | flops 2147483648 | bytes 5242880 | tf_op jit(solution)/shard_map/pallas_call | solution.py:69
  105.9 2.5 %dynamic-slice_bitcast_fusion.2 = f32[2,2,2,32,1024]{4,3,2,1,0:T(8,128)} fusion(f32[2,2,2,2,32,1024]{5,4,3,2,1,0:T(8,128)} %bitcast.102, s32[]{:T(128)S(6)} %select_n.75), kind=kLoop, calls=%fused_computation.7 | loop fusion | bytes 2097156 | tf_op jit(solution)/shard_map/jit(dynamic_index_in_dim)/squeeze | solution.py:138
  108.5 1.5 collective-permute-start.2
  110.6 1.4 collective-permute-start.1
  112.1 5.3 %collective-permute-done.2 = f32[2,32,1024]{2,1,0:T(8,128)} collective-permute-done((f32[2,32,1024]{2,1,0:T(8,128)S(1)}, f32[2,32,1024]{2,1,0:T(8,128)}, u32[]{:S(2)}, u32[]{:S(2)}) %collective-permute-start.2) | collective-permute-done | bytes 262176 | tf_op jit(solution)/shard_map/ppermute | solution.py:96
  121.9 5.6 %all-gather.11.cloned.1.call-done = bf16[8,1,32,2048]{3,2,1,0:T(8,128)(2,1)} async-done(((bf16[2,1,32,2048]{3,2,1,0:T(8,128)(2,1)}), bf16[8,1,32,2048]{3,2,1,0:T(8,128)(2,1)}) %all-gather.11.cloned.1.call-update) | async-done | bytes 1048592 | tf_op jit(solution)/shard_map/all_gather | solution.py:174
  127.4 7.5 %shard_map.57 = f32[2,256,1024]{2,1,0:T(8,128)} custom-call(s32[64]{0:T(128)} %select_reduce_fusion.order_ref, s32[17]{0:T(128)} %convert_reduce_fusion.1.starts_ref, s32[64]{0:T(128)} %copy-done.9, s32[64]{0:T(128)} %reshape.66.cd_ref, bf16[8,32,2048]{2,1,0:T(8,128)(2,1)} %bitcast.113, bf16[64,128,128]{2,1,0:T(8,128)(2,1)} %copy-done.4), custom_call_target="tpu_custom_call" | custom-call | flops 2147483648 | bytes 5242880 | tf_op jit(solution)/shard_map/pallas_call | solution.py:69
  136.4 1.5 collective-permute-start.7
  137.9 1.5 collective-permute-start.5
  140.8 3.5 %collective-permute-done.5 = f32[32,1024]{1,0:T(8,128)S(1)} collective-permute-done((f32[32,1024]{1,0:T(8,128)S(1)}, f32[32,1024]{1,0:T(8,128)S(1)}, u32[]{:S(2)}, u32[]{:S(2)}) %collective-permute-start.5) | collective-permute-done | bytes 131104 | tf_op jit(solution)/shard_map/ppermute | solution.py:96
  144.3 3.7 %collective-permute-done.4 = f32[32,1024]{1,0:T(8,128)S(1)} collective-permute-done((f32[32,1024]{1,0:T(8,128)S(1)}, f32[32,1024]{1,0:T(8,128)S(1)}, u32[]{:S(2)}, u32[]{:S(2)}) %collective-permute-start.4) | collective-permute-done | bytes 131104 | tf_op jit(solution)/shard_map/ppermute | solution.py:96
  149.6 6.8 %all-gather.9.cloned.1.call-done = bf16[8,1,32,2048]{3,2,1,0:T(8,128)(2,1)} async-done(((bf16[2,1,32,2048]{3,2,1,0:T(8,128)(2,1)}), bf16[8,1,32,2048]{3,2,1,0:T(8,128)(2,1)}) %all-gather.9.cloned.1.call-update) | async-done | bytes 1048592 | tf_op jit(solution)/shard_map/all_gather | solution.py:174
  156.4 1.5 collective-permute-start.9
  157.9 1.5 collective-permute-start.10
  160.7 7.5 %shard_map.58 = f32[2,256,1024]{2,1,0:T(8,128)} custom-call(s32[64]{0:T(128)} %select_reduce_fusion.order_ref, s32[17]{0:T(128)} %convert_reduce_fusion.1.starts_ref, s32[64]{0:T(128)} %copy-done.9, s32[64]{0:T(128)} %reshape.66.cd_ref, bf16[8,32,2048]{2,1,0:T(8,128)(2,1)} %bitcast.112, bf16[64,128,128]{2,1,0:T(8,128)(2,1)} %copy-done.4), custom_call_target="tpu_custom_call" | custom-call | flops 2147483648 | bytes 5242880 | tf_op jit(solution)/shard_map/pallas_call | solution.py:69
  169.8 1.5 collective-permute-start.12
  171.3 1.5 collective-permute-start.14
  172.8 2.9 %collective-permute-done.12 = f32[32,1024]{1,0:T(8,128)S(1)} collective-permute-done((f32[32,1024]{1,0:T(8,128)S(1)}, f32[32,1024]{1,0:T(8,128)S(1)}, u32[]{:S(2)}, u32[]{:S(2)}) %collective-permute-start.12) | collective-permute-done | bytes 131104 | tf_op jit(solution)/shard_map/ppermute | solution.py:96
  176.1 1.4 collective-permute-start.16
  177.6 1.5 collective-permute-start.18
  179.1 5.0 %collective-permute-done.16 = f32[2,32,1024]{2,1,0:T(8,128)S(1)} collective-permute-done((f32[2,32,1024]{2,1,0:T(8,128)S(1)}, f32[2,32,1024]{2,1,0:T(8,128)S(1)}, u32[]{:S(2)}, u32[]{:S(2)}) %collective-permute-start.16) | collective-permute-done | bytes 262176 | tf_op jit(solution)/shard_map/ppermute | solution.py:96
  184.1 1.5 collective-permute-start.17
  185.7 1.5 collective-permute-start.19
  187.2 2.0 %collective-permute-done.17 = f32[32,1024]{1,0:T(8,128)S(1)} collective-permute-done((f32[32,1024]{1,0:T(8,128)S(1)}, f32[32,1024]{1,0:T(8,128)S(1)}, u32[]{:S(2)}, u32[]{:S(2)}) %collective-permute-start.17) | collective-permute-done | bytes 131104 | tf_op jit(solution)/shard_map/ppermute | solution.py:96
  189.2 1.5 collective-permute-done.19
  (102 shorter events, 21.4 us)
Async XLA Ops:
  6.5 7.4 %copy-start.5 = (bf16[256,2048]{1,0:T(8,128)(2,1)S(1)}, bf16[256,2048]{1,0:T(8,128)(2,1)}, u32[]{:S(2)}) copy-start(bf16[256,2048]{1,0:T(8,128)(2,1)} %param.5) | copy-start | bytes 3145732
  6.5 72.9 %all-to-all-start = ((bf16[64,128,128]{2,1,0:T(8,128)(2,1)}), bf16[64,128,128]{2,1,0:T(8,128)(2,1)S(1)}, u32[]{:S(2)}, u32[]{:S(2)}) async-start(bf16[64,128,128]{2,1,0:T(8,128)(2,1)} %param.6), calls=%async_computation | async-start | bytes 4194304 | tf_op jit(solution)/shard_map/all_to_all | solution.py:160
  13.9 2.3 %copy-start.7 = (s32[1,32,2]{1,2,0:T(2,128)S(1)}, s32[1,32,2]{1,2,0:T(2,128)}, u32[]{:S(2)}) copy-start(s32[1,32,2]{1,2,0:T(2,128)} %param.8) | copy-start | bytes 772
  13.9 57.3 %all-gather.15.cloned.1.call-start = ((), (), s32[]{:S(2)}) async-start(), calls=%async_computation.4 | async-start | bytes 1310720 | tf_op jit(solution)/shard_map/all_gather | solution.py:174
  14.9 83.5 %all-gather.13.cloned.1.call-start = ((), (), s32[]{:S(2)}) async-start(), calls=%async_computation.3 | async-start | bytes 1310720 | tf_op jit(solution)/shard_map/all_gather | solution.py:174
  15.7 111.8 %all-gather.11.cloned.1.call-start = ((), (), s32[]{:S(2)}) async-start(), calls=%async_computation.2 | async-start | bytes 1310720 | tf_op jit(solution)/shard_map/all_gather | solution.py:174
  15.9 63.5 %copy-start.9 = (s32[64]{0:T(128)}, s32[64]{0:T(128)S(1)}, u32[]{:S(2)}) copy-start(s32[64]{0:T(128)S(1)} %reshape.65.ab_ref) | copy-start | bytes 772
  88.3 4.3 %copy-start.3 = (f32[2,256,1024]{2,1,0:T(8,128)S(1)}, f32[2,256,1024]{2,1,0:T(8,128)}, u32[]{:S(2)}) copy-start(f32[2,256,1024]{2,1,0:T(8,128)} %shard_map.55) | copy-start | bytes 6291460
  89.7 2.9 %collective-permute-start = (f32[2,2,2,32,1024]{4,3,2,1,0:T(8,128)S(1)}, f32[2,2,2,32,1024]{4,3,2,1,0:T(8,128)}, u32[]{:S(2)}, u32[]{:S(2)}) collective-permute-start(f32[2,2,2,32,1024]{4,3,2,1,0:T(8,128)S(1)} %dynamic-slice_bitcast_fusion.3), channel_id=1, source_target_pairs={{0,1},{1,0},{2,3},{3,2},{4,5},{5,4},{6,7},{7,6},{8,9},{9,8},{10,11... | collective-permute-start | bytes 3145736 | tf_op jit(solution)/shard_map/ppermute | solution.py:140
  89.8 66.5 %all-gather.9.cloned.1.call-start = ((), (), s32[]{:S(2)}) async-start(), calls=%async_computation.1 | async-start | bytes 1310720 | tf_op jit(solution)/shard_map/all_gather | solution.py:174
  105.9 14.5 %copy-start = (f32[2,256,1024]{2,1,0:T(8,128)S(1)}, f32[2,256,1024]{2,1,0:T(8,128)}, u32[]{:S(2)}) copy-start(f32[2,256,1024]{2,1,0:T(8,128)} %shard_map.56) | copy-start | bytes 6291460
  108.4 11.9 %collective-permute-start.3 = (f32[2,2,2,32,1024]{4,3,2,1,0:T(8,128)}, f32[2,2,2,32,1024]{4,3,2,1,0:T(8,128)}, u32[]{:S(2)}, u32[]{:S(2)}) collective-permute-start(f32[2,2,2,32,1024]{4,3,2,1,0:T(8,128)} %dynamic-slice_bitcast_fusion.2), channel_id=1, source_target_pairs={{0,1},{1,0},{2,3},{3,2},{4,5},{5,4},{6,7},{7,6},{8,9},{9,8},{10,11... | collective-permute-start | bytes 3145736 | tf_op jit(solution)/shard_map/ppermute | solution.py:140
  108.5 8.9 %collective-permute-start.2 = (f32[2,32,1024]{2,1,0:T(8,128)S(1)}, f32[2,32,1024]{2,1,0:T(8,128)}, u32[]{:S(2)}, u32[]{:S(2)}) collective-permute-start(f32[2,32,1024]{2,1,0:T(8,128)S(1)} %dynamic-slice_bitcast_fusion.10), channel_id=1, source_target_pairs={{0,4},{1,5},{2,6},{3,7},{4,0},{5,1},{6,2},{7,3},{8,12},{9,13},{10,... | collective-permute-start | bytes 786440 | tf_op jit(solution)/shard_map/ppermute | solution.py:96
  110.6 8.8 %collective-permute-start.1 = (f32[2,32,1024]{2,1,0:T(8,128)}, f32[2,32,1024]{2,1,0:T(8,128)}, u32[]{:S(2)}, u32[]{:S(2)}) collective-permute-start(f32[2,32,1024]{2,1,0:T(8,128)} %dynamic-slice_bitcast_fusion.11), channel_id=1, source_target_pairs={{0,2},{1,3},{2,0},{3,1},{4,6},{5,7},{6,4},{7,5},{8,10},{9,11},{10,... | collective-permute-start | bytes 786440 | tf_op jit(solution)/shard_map/ppermute | solution.py:96
  136.3 12.9 %copy-start.2 = (f32[2,256,1024]{2,1,0:T(8,128)S(1)}, f32[2,256,1024]{2,1,0:T(8,128)}, u32[]{:S(2)}) copy-start(f32[2,256,1024]{2,1,0:T(8,128)} %shard_map.57) | copy-start | bytes 6291460
  136.3 12.9 %collective-permute-start.8 = (f32[2,2,2,32,1024]{4,3,2,1,0:T(8,128)S(1)}, f32[2,2,2,32,1024]{4,3,2,1,0:T(8,128)S(1)}, u32[]{:S(2)}, u32[]{:S(2)}) collective-permute-start(f32[2,2,2,32,1024]{4,3,2,1,0:T(8,128)S(1)} %dynamic-slice_bitcast_fusion.1), channel_id=1, source_target_pairs={{0,1},{1,0},{2,3},{3,2},{4,5},{5,4},{6,7},{7,6},{8,9},{9,8},{10,11... | collective-permute-start | bytes 3145736 | tf_op jit(solution)/shard_map/ppermute | solution.py:140
  136.4 11.6 %collective-permute-start.7 = (f32[2,32,1024]{2,1,0:T(8,128)S(1)}, f32[2,32,1024]{2,1,0:T(8,128)S(1)}, u32[]{:S(2)}, u32[]{:S(2)}) collective-permute-start(f32[2,32,1024]{2,1,0:T(8,128)S(1)} %dynamic-slice_bitcast_fusion.8), channel_id=1, source_target_pairs={{0,4},{1,5},{2,6},{3,7},{4,0},{5,1},{6,2},{7,3},{8,12},{9,13},{10,... | collective-permute-start | bytes 786440 | tf_op jit(solution)/shard_map/ppermute | solution.py:96
  137.9 6.4 %collective-permute-start.5 = (f32[32,1024]{1,0:T(8,128)S(1)}, f32[32,1024]{1,0:T(8,128)S(1)}, u32[]{:S(2)}, u32[]{:S(2)}) collective-permute-start(f32[32,1024]{1,0:T(8,128)S(1)} %dynamic-slice_bitcast_fusion.18), channel_id=1, source_target_pairs={{0,2},{1,3},{2,0},{3,1},{4,6},{5,7},{6,4},{7,5},{8,10},{9,11},{10,... | collective-permute-start | bytes 393224 | tf_op jit(solution)/shard_map/ppermute | solution.py:96
  139.4 9.8 %collective-permute-start.6 = (f32[2,32,1024]{2,1,0:T(8,128)S(1)}, f32[2,32,1024]{2,1,0:T(8,128)S(1)}, u32[]{:S(2)}, u32[]{:S(2)}) collective-permute-start(f32[2,32,1024]{2,1,0:T(8,128)S(1)} %dynamic-slice_bitcast_fusion.9), channel_id=1, source_target_pairs={{0,2},{1,3},{2,0},{3,1},{4,6},{5,7},{6,4},{7,5},{8,10},{9,11},{10,... | collective-permute-start | bytes 786440 | tf_op jit(solution)/shard_map/ppermute | solution.py:96
  140.1 7.9 %collective-permute-start.4 = (f32[32,1024]{1,0:T(8,128)S(1)}, f32[32,1024]{1,0:T(8,128)S(1)}, u32[]{:S(2)}, u32[]{:S(2)}) collective-permute-start(f32[32,1024]{1,0:T(8,128)S(1)} %dynamic-slice_bitcast_fusion.19), channel_id=1, source_target_pairs={{0,4},{1,5},{2,6},{3,7},{4,0},{5,1},{6,2},{7,3},{8,12},{9,13},{10,... | collective-permute-start | bytes 393224 | tf_op jit(solution)/shard_map/ppermute | solution.py:96
  156.4 13.3 %collective-permute-start.9 = (f32[32,1024]{1,0:T(8,128)S(1)}, f32[32,1024]{1,0:T(8,128)S(1)}, u32[]{:S(2)}, u32[]{:S(2)}) collective-permute-start(f32[32,1024]{1,0:T(8,128)S(1)} %dynamic-slice_bitcast_fusion.17), channel_id=1, source_target_pairs={{0,4},{1,5},{2,6},{3,7},{4,0},{5,1},{6,2},{7,3},{8,12},{9,13},{10,... | collective-permute-start | bytes 393224 | tf_op jit(solution)/shard_map/ppermute | solution.py:96
  157.9 11.8 %collective-permute-start.10 = (f32[32,1024]{1,0:T(8,128)S(1)}, f32[32,1024]{1,0:T(8,128)S(1)}, u32[]{:S(2)}, u32[]{:S(2)}) collective-permute-start(f32[32,1024]{1,0:T(8,128)S(1)} %dynamic-slice_bitcast_fusion.16), channel_id=1, source_target_pairs={{0,2},{1,3},{2,0},{3,1},{4,6},{5,7},{6,4},{7,5},{8,10},{9,11},{10,... | collective-permute-start | bytes 393224 | tf_op jit(solution)/shard_map/ppermute | solution.py:96
  159.5 10.3 %collective-permute-start.11 = (f32[2,32,1024]{2,1,0:T(8,128)S(1)}, f32[2,32,1024]{2,1,0:T(8,128)S(1)}, u32[]{:S(2)}, u32[]{:S(2)}) collective-permute-start(f32[2,32,1024]{2,1,0:T(8,128)S(1)} %dynamic-slice_bitcast_fusion.7), channel_id=1, source_target_pairs={{0,2},{1,3},{2,0},{3,1},{4,6},{5,7},{6,4},{7,5},{8,10},{9,11},{10,... | collective-permute-start | bytes 786440 | tf_op jit(solution)/shard_map/ppermute | solution.py:96
  160.1 11.2 %collective-permute-start.13 = (f32[2,32,1024]{2,1,0:T(8,128)S(1)}, f32[2,32,1024]{2,1,0:T(8,128)S(1)}, u32[]{:S(2)}, u32[]{:S(2)}) collective-permute-start(f32[2,32,1024]{2,1,0:T(8,128)S(1)} %dynamic-slice_bitcast_fusion.6), channel_id=1, source_target_pairs={{0,4},{1,5},{2,6},{3,7},{4,0},{5,1},{6,2},{7,3},{8,12},{9,13},{10,... | collective-permute-start | bytes 786440 | tf_op jit(solution)/shard_map/ppermute | solution.py:96
  169.6 6.2 %copy-start.1 = (f32[2,256,1024]{2,1,0:T(8,128)S(1)}, f32[2,256,1024]{2,1,0:T(8,128)}, u32[]{:S(2)}) copy-start(f32[2,256,1024]{2,1,0:T(8,128)} %shard_map.58) | copy-start | bytes 6291460
  169.6 6.2 %collective-permute-start.15 = (f32[2,2,2,32,1024]{4,3,2,1,0:T(8,128)S(1)}, f32[2,2,2,32,1024]{4,3,2,1,0:T(8,128)S(1)}, u32[]{:S(2)}, u32[]{:S(2)}) collective-permute-start(f32[2,2,2,32,1024]{4,3,2,1,0:T(8,128)S(1)} %dynamic-slice_bitcast_fusion), channel_id=1, source_target_pairs={{0,1},{1,0},{2,3},{3,2},{4,5},{5,4},{6,7},{7,6},{8,9},{9,8},{10,11... | collective-permute-start | bytes 3145736 | tf_op jit(solution)/shard_map/ppermute | solution.py:140
  169.8 5.9 %collective-permute-start.12 = (f32[32,1024]{1,0:T(8,128)S(1)}, f32[32,1024]{1,0:T(8,128)S(1)}, u32[]{:S(2)}, u32[]{:S(2)}) collective-permute-start(f32[32,1024]{1,0:T(8,128)S(1)} %dynamic-slice_bitcast_fusion.15), channel_id=1, source_target_pairs={{0,4},{1,5},{2,6},{3,7},{4,0},{5,1},{6,2},{7,3},{8,12},{9,13},{10,... | collective-permute-start | bytes 393224 | tf_op jit(solution)/shard_map/ppermute | solution.py:96
  171.3 6.2 %collective-permute-start.14 = (f32[32,1024]{1,0:T(8,128)S(1)}, f32[32,1024]{1,0:T(8,128)S(1)}, u32[]{:S(2)}, u32[]{:S(2)}) collective-permute-start(f32[32,1024]{1,0:T(8,128)S(1)} %dynamic-slice_bitcast_fusion.14), channel_id=1, source_target_pairs={{0,2},{1,3},{2,0},{3,1},{4,6},{5,7},{6,4},{7,5},{8,10},{9,11},{10,... | collective-permute-start | bytes 393224 | tf_op jit(solution)/shard_map/ppermute | solution.py:96
  176.1 8.0 %collective-permute-start.16 = (f32[2,32,1024]{2,1,0:T(8,128)S(1)}, f32[2,32,1024]{2,1,0:T(8,128)S(1)}, u32[]{:S(2)}, u32[]{:S(2)}) collective-permute-start(f32[2,32,1024]{2,1,0:T(8,128)S(1)} %dynamic-slice_bitcast_fusion.5), channel_id=1, source_target_pairs={{0,2},{1,3},{2,0},{3,1},{4,6},{5,7},{6,4},{7,5},{8,10},{9,11},{10,... | collective-permute-start | bytes 786440 | tf_op jit(solution)/shard_map/ppermute | solution.py:96
  177.6 8.0 %collective-permute-start.18 = (f32[2,32,1024]{2,1,0:T(8,128)S(1)}, f32[2,32,1024]{2,1,0:T(8,128)S(1)}, u32[]{:S(2)}, u32[]{:S(2)}) collective-permute-start(f32[2,32,1024]{2,1,0:T(8,128)S(1)} %dynamic-slice_bitcast_fusion.4), channel_id=1, source_target_pairs={{0,4},{1,5},{2,6},{3,7},{4,0},{5,1},{6,2},{7,3},{8,12},{9,13},{10,... | collective-permute-start | bytes 786440 | tf_op jit(solution)/shard_map/ppermute | solution.py:96
  184.1 5.0 %collective-permute-start.17 = (f32[32,1024]{1,0:T(8,128)S(1)}, f32[32,1024]{1,0:T(8,128)S(1)}, u32[]{:S(2)}, u32[]{:S(2)}) collective-permute-start(f32[32,1024]{1,0:T(8,128)S(1)} %dynamic-slice_bitcast_fusion.13), channel_id=1, source_target_pairs={{0,4},{1,5},{2,6},{3,7},{4,0},{5,1},{6,2},{7,3},{8,12},{9,13},{10,... | collective-permute-start | bytes 393224 | tf_op jit(solution)/shard_map/ppermute | solution.py:96
  185.7 5.0 %collective-permute-start.19 = (f32[32,1024]{1,0:T(8,128)S(1)}, f32[32,1024]{1,0:T(8,128)S(1)}, u32[]{:S(2)}, u32[]{:S(2)}) collective-permute-start(f32[32,1024]{1,0:T(8,128)S(1)} %dynamic-slice_bitcast_fusion.12), channel_id=1, source_target_pairs={{0,2},{1,3},{2,0},{3,1},{4,6},{5,7},{6,4},{7,5},{8,10},{9,11},{10,... | collective-permute-start | bytes 393224 | tf_op jit(solution)/shard_map/ppermute | solution.py:96
  (3 other events, 5.4 us)
Sparse Core Ops, SparseCore 0:
  16.3 54.8 all-gather.14
  72.7 25.6 all-gather.12
  100.0 27.4 all-gather.10
  128.9 27.4 all-gather.8

commit v21 on v20

--- a/solution.py
+++ b/solution.py
@@ -47,7 +47,7 @@
     groups, part, width = amp3.shape
     rows = groups * part
     n, tile, _ = tiles.shape
-    per_step = 4 if ab_count % 8 == 0 else 1
+    per_step = ab_count // 2 if ab_count % 2 == 0 else 1
     steps_per_half = ab_count // (2 * per_step)
     cost = pl.CostEstimate(
         flops=2 * rows * width * ab_count * tile,

time: 199 us -> 198 us (level)
  no operation moved by 1% of the time
where the time goes in v21:
time: 198 us
  waiting for transfers between devices  108 us (55%)
  Pallas kernels  28.9 us (15%)
  starting transfers between devices  28.3 us (14%)
  between operations  13.6 us (7%)
  local copies, waits for them, and re-layouts  11.5 us (6%)
  other arithmetic  7.99 us (4%)
    all_gather x4, waiting for transfers between devices, on_device(): lax.all_gather(local4[:, c], 'own', axis=0, tiled=True)  70.3 us
    pallas_call x4, Pallas kernels, _ladder_products(): pl.pallas_call(_ladder_kernel, grid_spec=grid_spec, out_shape=jax.ShapeDt...  28.9 us
    ppermute x16, waiting for transfers between devices, advance(): self.x = keep + lax.ppermute(send, 'rep', perm=pairs)  25.7 us
    ppermute x16, starting transfers between devices, advance(): self.x = keep + lax.ppermute(send, 'rep', perm=pairs)  20.7 us
    all_to_all x1, waiting for transfers between devices, on_device(): lax.all_to_all(integrals, ('own', 'rep'), split_axis=0, concat_axis=0, ti...  8.25 us
    all_to_all x1, starting transfers between devices, on_device(): lax.all_to_all(integrals, ('own', 'rep'), split_axis=0, concat_axis=0, ti...  7.3 us
    squeeze x4, local copies, waits for them, and re-layouts, advance(): send = lax.dynamic_index_in_dim(self.joint, 1 - mine, ax, keepdims=False)  6.64 us
  transfers between devices with their start and end apart: 25, of which 15 were waited for; matrix products, arithmetic and copies ran while one was open for 9% of the time, Pallas kernels for 15%

profile of v21, /device:TPU:0, one launch (start us, length us, event | category | flops | bytes accessed | tf_op | source)
XLA Modules:
  0.0 198.0 jit_solution(5087623076823069273)
XLA Ops:
  6.5 7.3 %all-to-all-start = ((bf16[64,128,128]{2,1,0:T(8,128)(2,1)}), bf16[64,128,128]{2,1,0:T(8,128)(2,1)S(1)}, u32[]{:S(2)}, u32[]{:S(2)}) async-start(bf16[64,128,128]{2,1,0:T(8,128)(2,1)} %param.6), calls=%async_computation | async-start | bytes 4194304 | tf_op jit(solution)/shard_map/all_to_all | solution.py:160
  18.4 52.8 %all-gather.15.cloned.1.call-done = bf16[8,1,32,2048]{3,2,1,0:T(8,128)(2,1)} async-done(((bf16[2,1,32,2048]{3,2,1,0:T(8,128)(2,1)}), bf16[8,1,32,2048]{3,2,1,0:T(8,128)(2,1)}) %all-gather.15.cloned.1.call-update) | async-done | bytes 1048592 | tf_op jit(solution)/shard_map/all_gather | solution.py:174
  71.2 8.2 %all-to-all-done.tiles_ref = bf16[64,128,128]{2,1,0:T(8,128)(2,1)S(1)} async-done(((bf16[64,128,128]{2,1,0:T(8,128)(2,1)}), bf16[64,128,128]{2,1,0:T(8,128)(2,1)S(1)}, u32[]{:S(2)}, u32[]{:S(2)}) %all-to-all-start) | async-done | bytes 2097184 | tf_op jit(solution)/shard_map/all_to_all | solution.py:160
  80.8 7.2 %shard_map.55 = f32[2,256,1024]{2,1,0:T(8,128)} custom-call(s32[64]{0:T(128)} %select_reduce_fusion.order_ref, s32[17]{0:T(128)} %convert_reduce_fusion.1.starts_ref, s32[64]{0:T(128)} %copy-done.9, s32[64]{0:T(128)} %reshape.66.cd_ref, bf16[8,32,2048]{2,1,0:T(8,128)(2,1)} %bitcast.115, bf16[64,128,128]{2,1,0:T(8,128)(2,1)} %copy-done.4), custom_call_target="tpu_custom_call" | custom-call | flops 2147483648 | bytes 5242880 | tf_op jit(solution)/shard_map/pallas_call | solution.py:69
  88.0 1.5 dynamic-slice_bitcast_fusion.3
  89.6 2.7 %collective-permute-done = f32[2,2,2,32,1024]{4,3,2,1,0:T(8,128)} collective-permute-done((f32[2,2,2,32,1024]{4,3,2,1,0:T(8,128)S(1)}, f32[2,2,2,32,1024]{4,3,2,1,0:T(8,128)}, u32[]{:S(2)}, u32[]{:S(2)}) %collective-permute-start) | collective-permute-done | bytes 1048608 | tf_op jit(solution)/shard_map/ppermute | solution.py:140
  93.8 4.6 %all-gather.13.cloned.1.call-done = bf16[8,1,32,2048]{3,2,1,0:T(8,128)(2,1)} async-done(((bf16[2,1,32,2048]{3,2,1,0:T(8,128)(2,1)}), bf16[8,1,32,2048]{3,2,1,0:T(8,128)(2,1)}) %all-gather.13.cloned.1.call-update) | async-done | bytes 1048592 | tf_op jit(solution)/shard_map/all_gather | solution.py:174
  98.4 7.2 %shard_map.56 = f32[2,256,1024]{2,1,0:T(8,128)} custom-call(s32[64]{0:T(128)} %select_reduce_fusion.order_ref, s32[17]{0:T(128)} %convert_reduce_fusion.1.starts_ref, s32[64]{0:T(128)} %copy-done.9, s32[64]{0:T(128)} %reshape.66.cd_ref, bf16[8,32,2048]{2,1,0:T(8,128)(2,1)} %bitcast.114, bf16[64,128,128]{2,1,0:T(8,128)(2,1)} %copy-done.4), custom_call_target="tpu_custom_call" | custom-call | flops 2147483648 | bytes 5242880 | tf_op jit(solution)/shard_map/pallas_call | solution.py:69
  105.6 2.5 %dynamic-slice_bitcast_fusion.2 = f32[2,2,2,32,1024]{4,3,2,1,0:T(8,128)} fusion(f32[2,2,2,2,32,1024]{5,4,3,2,1,0:T(8,128)} %bitcast.102, s32[]{:T(128)S(6)} %select_n.75), kind=kLoop, calls=%fused_computation.7 | loop fusion | bytes 2097156 | tf_op jit(solution)/shard_map/jit(dynamic_index_in_dim)/squeeze | solution.py:138
  108.2 1.4 collective-permute-start.2
  110.3 1.5 collective-permute-start.1
  111.9 5.2 %collective-permute-done.2 = f32[2,32,1024]{2,1,0:T(8,128)} collective-permute-done((f32[2,32,1024]{2,1,0:T(8,128)S(1)}, f32[2,32,1024]{2,1,0:T(8,128)}, u32[]{:S(2)}, u32[]{:S(2)}) %collective-permute-start.2) | collective-permute-done | bytes 262176 | tf_op jit(solution)/shard_map/ppermute | solution.py:96
  121.6 5.9 %all-gather.11.cloned.1.call-done = bf16[8,1,32,2048]{3,2,1,0:T(8,128)(2,1)} async-done(((bf16[2,1,32,2048]{3,2,1,0:T(8,128)(2,1)}), bf16[8,1,32,2048]{3,2,1,0:T(8,128)(2,1)}) %all-gather.11.cloned.1.call-update) | async-done | bytes 1048592 | tf_op jit(solution)/shard_map/all_gather | solution.py:174
  127.5 7.2 %shard_map.57 = f32[2,256,1024]{2,1,0:T(8,128)} custom-call(s32[64]{0:T(128)} %select_reduce_fusion.order_ref, s32[17]{0:T(128)} %convert_reduce_fusion.1.starts_ref, s32[64]{0:T(128)} %copy-done.9, s32[64]{0:T(128)} %reshape.66.cd_ref, bf16[8,32,2048]{2,1,0:T(8,128)(2,1)} %bitcast.113, bf16[64,128,128]{2,1,0:T(8,128)(2,1)} %copy-done.4), custom_call_target="tpu_custom_call" | custom-call | flops 2147483648 | bytes 5242880 | tf_op jit(solution)/shard_map/pallas_call | solution.py:69
  136.2 1.4 collective-permute-start.7
  137.6 1.6 collective-permute-start.5
  140.5 3.5 %collective-permute-done.5 = f32[32,1024]{1,0:T(8,128)S(1)} collective-permute-done((f32[32,1024]{1,0:T(8,128)S(1)}, f32[32,1024]{1,0:T(8,128)S(1)}, u32[]{:S(2)}, u32[]{:S(2)}) %collective-permute-start.5) | collective-permute-done | bytes 131104 | tf_op jit(solution)/shard_map/ppermute | solution.py:96
  144.0 3.7 %collective-permute-done.4 = f32[32,1024]{1,0:T(8,128)S(1)} collective-permute-done((f32[32,1024]{1,0:T(8,128)S(1)}, f32[32,1024]{1,0:T(8,128)S(1)}, u32[]{:S(2)}, u32[]{:S(2)}) %collective-permute-start.4) | collective-permute-done | bytes 131104 | tf_op jit(solution)/shard_map/ppermute | solution.py:96
  149.3 7.1 %all-gather.9.cloned.1.call-done = bf16[8,1,32,2048]{3,2,1,0:T(8,128)(2,1)} async-done(((bf16[2,1,32,2048]{3,2,1,0:T(8,128)(2,1)}), bf16[8,1,32,2048]{3,2,1,0:T(8,128)(2,1)}) %all-gather.9.cloned.1.call-update) | async-done | bytes 1048592 | tf_op jit(solution)/shard_map/all_gather | solution.py:174
  156.4 1.5 collective-permute-start.9
  157.9 1.5 collective-permute-start.10
  160.7 7.2 %shard_map.58 = f32[2,256,1024]{2,1,0:T(8,128)} custom-call(s32[64]{0:T(128)} %select_reduce_fusion.order_ref, s32[17]{0:T(128)} %convert_reduce_fusion.1.starts_ref, s32[64]{0:T(128)} %copy-done.9, s32[64]{0:T(128)} %reshape.66.cd_ref, bf16[8,32,2048]{2,1,0:T(8,128)(2,1)} %bitcast.112, bf16[64,128,128]{2,1,0:T(8,128)(2,1)} %copy-done.4), custom_call_target="tpu_custom_call" | custom-call | flops 2147483648 | bytes 5242880 | tf_op jit(solution)/shard_map/pallas_call | solution.py:69
  169.5 1.4 collective-permute-start.12
  171.0 1.6 collective-permute-start.14
  172.6 2.9 %collective-permute-done.12 = f32[32,1024]{1,0:T(8,128)S(1)} collective-permute-done((f32[32,1024]{1,0:T(8,128)S(1)}, f32[32,1024]{1,0:T(8,128)S(1)}, u32[]{:S(2)}, u32[]{:S(2)}) %collective-permute-start.12) | collective-permute-done | bytes 131104 | tf_op jit(solution)/shard_map/ppermute | solution.py:96
  175.8 1.5 collective-permute-start.16
  177.4 1.5 collective-permute-start.18
  178.9 4.9 %collective-permute-done.16 = f32[2,32,1024]{2,1,0:T(8,128)S(1)} collective-permute-done((f32[2,32,1024]{2,1,0:T(8,128)S(1)}, f32[2,32,1024]{2,1,0:T(8,128)S(1)}, u32[]{:S(2)}, u32[]{:S(2)}) %collective-permute-start.16) | collective-permute-done | bytes 262176 | tf_op jit(solution)/shard_map/ppermute | solution.py:96
  183.8 1.4 collective-permute-start.17
  185.4 1.6 collective-permute-start.19
  186.9 1.9 collective-permute-done.17
  188.9 1.5 collective-permute-done.19
  (102 shorter events, 21.3 us)
Async XLA Ops:
  6.5 7.4 %copy-start.5 = (bf16[256,2048]{1,0:T(8,128)(2,1)S(1)}, bf16[256,2048]{1,0:T(8,128)(2,1)}, u32[]{:S(2)}) copy-start(bf16[256,2048]{1,0:T(8,128)(2,1)} %param.5) | copy-start | bytes 3145732
  6.5 72.9 %all-to-all-start = ((bf16[64,128,128]{2,1,0:T(8,128)(2,1)}), bf16[64,128,128]{2,1,0:T(8,128)(2,1)S(1)}, u32[]{:S(2)}, u32[]{:S(2)}) async-start(bf16[64,128,128]{2,1,0:T(8,128)(2,1)} %param.6), calls=%async_computation | async-start | bytes 4194304 | tf_op jit(solution)/shard_map/all_to_all | solution.py:160
  13.9 2.3 %copy-start.7 = (s32[1,32,2]{1,2,0:T(2,128)S(1)}, s32[1,32,2]{1,2,0:T(2,128)}, u32[]{:S(2)}) copy-start(s32[1,32,2]{1,2,0:T(2,128)} %param.8) | copy-start | bytes 772
  13.9 57.3 %all-gather.15.cloned.1.call-start = ((), (), s32[]{:S(2)}) async-start(), calls=%async_computation.4 | async-start | bytes 1310720 | tf_op jit(solution)/shard_map/all_gather | solution.py:174
  14.9 83.5 %all-gather.13.cloned.1.call-start = ((), (), s32[]{:S(2)}) async-start(), calls=%async_computation.3 | async-start | bytes 1310720 | tf_op jit(solution)/shard_map/all_gather | solution.py:174
  15.7 111.8 %all-gather.11.cloned.1.call-start = ((), (), s32[]{:S(2)}) async-start(), calls=%async_computation.2 | async-start | bytes 1310720 | tf_op jit(solution)/shard_map/all_gather | solution.py:174
  15.9 63.5 %copy-start.9 = (s32[64]{0:T(128)}, s32[64]{0:T(128)S(1)}, u32[]{:S(2)}) copy-start(s32[64]{0:T(128)S(1)} %reshape.65.ab_ref) | copy-start | bytes 772
  88.0 4.3 %copy-start.3 = (f32[2,256,1024]{2,1,0:T(8,128)S(1)}, f32[2,256,1024]{2,1,0:T(8,128)}, u32[]{:S(2)}) copy-start(f32[2,256,1024]{2,1,0:T(8,128)} %shard_map.55) | copy-start | bytes 6291460
  89.5 2.9 %collective-permute-start = (f32[2,2,2,32,1024]{4,3,2,1,0:T(8,128)S(1)}, f32[2,2,2,32,1024]{4,3,2,1,0:T(8,128)}, u32[]{:S(2)}, u32[]{:S(2)}) collective-permute-start(f32[2,2,2,32,1024]{4,3,2,1,0:T(8,128)S(1)} %dynamic-slice_bitcast_fusion.3), channel_id=1, source_target_pairs={{0,1},{1,0},{2,3},{3,2},{4,5},{5,4},{6,7},{7,6},{8,9},{9,8},{10,11... | collective-permute-start | bytes 3145736 | tf_op jit(solution)/shard_map/ppermute | solution.py:140
  89.6 66.8 %all-gather.9.cloned.1.call-start = ((), (), s32[]{:S(2)}) async-start(), calls=%async_computation.1 | async-start | bytes 1310720 | tf_op jit(solution)/shard_map/all_gather | solution.py:174
  105.6 14.4 %copy-start = (f32[2,256,1024]{2,1,0:T(8,128)S(1)}, f32[2,256,1024]{2,1,0:T(8,128)}, u32[]{:S(2)}) copy-start(f32[2,256,1024]{2,1,0:T(8,128)} %shard_map.56) | copy-start | bytes 6291460
  108.1 11.9 %collective-permute-start.3 = (f32[2,2,2,32,1024]{4,3,2,1,0:T(8,128)}, f32[2,2,2,32,1024]{4,3,2,1,0:T(8,128)}, u32[]{:S(2)}, u32[]{:S(2)}) collective-permute-start(f32[2,2,2,32,1024]{4,3,2,1,0:T(8,128)} %dynamic-slice_bitcast_fusion.2), channel_id=1, source_target_pairs={{0,1},{1,0},{2,3},{3,2},{4,5},{5,4},{6,7},{7,6},{8,9},{9,8},{10,11... | collective-permute-start | bytes 3145736 | tf_op jit(solution)/shard_map/ppermute | solution.py:140
  108.2 8.9 %collective-permute-start.2 = (f32[2,32,1024]{2,1,0:T(8,128)S(1)}, f32[2,32,1024]{2,1,0:T(8,128)}, u32[]{:S(2)}, u32[]{:S(2)}) collective-permute-start(f32[2,32,1024]{2,1,0:T(8,128)S(1)} %dynamic-slice_bitcast_fusion.10), channel_id=1, source_target_pairs={{0,4},{1,5},{2,6},{3,7},{4,0},{5,1},{6,2},{7,3},{8,12},{9,13},{10,... | collective-permute-start | bytes 786440 | tf_op jit(solution)/shard_map/ppermute | solution.py:96
  110.3 8.8 %collective-permute-start.1 = (f32[2,32,1024]{2,1,0:T(8,128)}, f32[2,32,1024]{2,1,0:T(8,128)}, u32[]{:S(2)}, u32[]{:S(2)}) collective-permute-start(f32[2,32,1024]{2,1,0:T(8,128)} %dynamic-slice_bitcast_fusion.11), channel_id=1, source_target_pairs={{0,2},{1,3},{2,0},{3,1},{4,6},{5,7},{6,4},{7,5},{8,10},{9,11},{10,... | collective-permute-start | bytes 786440 | tf_op jit(solution)/shard_map/ppermute | solution.py:96
  136.1 12.9 %copy-start.2 = (f32[2,256,1024]{2,1,0:T(8,128)S(1)}, f32[2,256,1024]{2,1,0:T(8,128)}, u32[]{:S(2)}) copy-start(f32[2,256,1024]{2,1,0:T(8,128)} %shard_map.57) | copy-start | bytes 6291460
  136.1 12.9 %collective-permute-start.8 = (f32[2,2,2,32,1024]{4,3,2,1,0:T(8,128)S(1)}, f32[2,2,2,32,1024]{4,3,2,1,0:T(8,128)S(1)}, u32[]{:S(2)}, u32[]{:S(2)}) collective-permute-start(f32[2,2,2,32,1024]{4,3,2,1,0:T(8,128)S(1)} %dynamic-slice_bitcast_fusion.1), channel_id=1, source_target_pairs={{0,1},{1,0},{2,3},{3,2},{4,5},{5,4},{6,7},{7,6},{8,9},{9,8},{10,11... | collective-permute-start | bytes 3145736 | tf_op jit(solution)/shard_map/ppermute | solution.py:140
  136.2 11.6 %collective-permute-start.7 = (f32[2,32,1024]{2,1,0:T(8,128)S(1)}, f32[2,32,1024]{2,1,0:T(8,128)S(1)}, u32[]{:S(2)}, u32[]{:S(2)}) collective-permute-start(f32[2,32,1024]{2,1,0:T(8,128)S(1)} %dynamic-slice_bitcast_fusion.8), channel_id=1, source_target_pairs={{0,4},{1,5},{2,6},{3,7},{4,0},{5,1},{6,2},{7,3},{8,12},{9,13},{10,... | collective-permute-start | bytes 786440 | tf_op jit(solution)/shard_map/ppermute | solution.py:96
  137.6 6.4 %collective-permute-start.5 = (f32[32,1024]{1,0:T(8,128)S(1)}, f32[32,1024]{1,0:T(8,128)S(1)}, u32[]{:S(2)}, u32[]{:S(2)}) collective-permute-start(f32[32,1024]{1,0:T(8,128)S(1)} %dynamic-slice_bitcast_fusion.18), channel_id=1, source_target_pairs={{0,2},{1,3},{2,0},{3,1},{4,6},{5,7},{6,4},{7,5},{8,10},{9,11},{10,... | collective-permute-start | bytes 393224 | tf_op jit(solution)/shard_map/ppermute | solution.py:96
  139.2 9.7 %collective-permute-start.6 = (f32[2,32,1024]{2,1,0:T(8,128)S(1)}, f32[2,32,1024]{2,1,0:T(8,128)S(1)}, u32[]{:S(2)}, u32[]{:S(2)}) collective-permute-start(f32[2,32,1024]{2,1,0:T(8,128)S(1)} %dynamic-slice_bitcast_fusion.9), channel_id=1, source_target_pairs={{0,2},{1,3},{2,0},{3,1},{4,6},{5,7},{6,4},{7,5},{8,10},{9,11},{10,... | collective-permute-start | bytes 786440 | tf_op jit(solution)/shard_map/ppermute | solution.py:96
  139.8 7.9 %collective-permute-start.4 = (f32[32,1024]{1,0:T(8,128)S(1)}, f32[32,1024]{1,0:T(8,128)S(1)}, u32[]{:S(2)}, u32[]{:S(2)}) collective-permute-start(f32[32,1024]{1,0:T(8,128)S(1)} %dynamic-slice_bitcast_fusion.19), channel_id=1, source_target_pairs={{0,4},{1,5},{2,6},{3,7},{4,0},{5,1},{6,2},{7,3},{8,12},{9,13},{10,... | collective-permute-start | bytes 393224 | tf_op jit(solution)/shard_map/ppermute | solution.py:96
  156.4 13.0 %collective-permute-start.9 = (f32[32,1024]{1,0:T(8,128)S(1)}, f32[32,1024]{1,0:T(8,128)S(1)}, u32[]{:S(2)}, u32[]{:S(2)}) collective-permute-start(f32[32,1024]{1,0:T(8,128)S(1)} %dynamic-slice_bitcast_fusion.17), channel_id=1, source_target_pairs={{0,4},{1,5},{2,6},{3,7},{4,0},{5,1},{6,2},{7,3},{8,12},{9,13},{10,... | collective-permute-start | bytes 393224 | tf_op jit(solution)/shard_map/ppermute | solution.py:96
  157.9 11.5 %collective-permute-start.10 = (f32[32,1024]{1,0:T(8,128)S(1)}, f32[32,1024]{1,0:T(8,128)S(1)}, u32[]{:S(2)}, u32[]{:S(2)}) collective-permute-start(f32[32,1024]{1,0:T(8,128)S(1)} %dynamic-slice_bitcast_fusion.16), channel_id=1, source_target_pairs={{0,2},{1,3},{2,0},{3,1},{4,6},{5,7},{6,4},{7,5},{8,10},{9,11},{10,... | collective-permute-start | bytes 393224 | tf_op jit(solution)/shard_map/ppermute | solution.py:96
  159.5 10.0 %collective-permute-start.11 = (f32[2,32,1024]{2,1,0:T(8,128)S(1)}, f32[2,32,1024]{2,1,0:T(8,128)S(1)}, u32[]{:S(2)}, u32[]{:S(2)}) collective-permute-start(f32[2,32,1024]{2,1,0:T(8,128)S(1)} %dynamic-slice_bitcast_fusion.7), channel_id=1, source_target_pairs={{0,2},{1,3},{2,0},{3,1},{4,6},{5,7},{6,4},{7,5},{8,10},{9,11},{10,... | collective-permute-start | bytes 786440 | tf_op jit(solution)/shard_map/ppermute | solution.py:96
  160.1 10.9 %collective-permute-start.13 = (f32[2,32,1024]{2,1,0:T(8,128)S(1)}, f32[2,32,1024]{2,1,0:T(8,128)S(1)}, u32[]{:S(2)}, u32[]{:S(2)}) collective-permute-start(f32[2,32,1024]{2,1,0:T(8,128)S(1)} %dynamic-slice_bitcast_fusion.6), channel_id=1, source_target_pairs={{0,4},{1,5},{2,6},{3,7},{4,0},{5,1},{6,2},{7,3},{8,12},{9,13},{10,... | collective-permute-start | bytes 786440 | tf_op jit(solution)/shard_map/ppermute | solution.py:96
  169.3 6.2 %copy-start.1 = (f32[2,256,1024]{2,1,0:T(8,128)S(1)}, f32[2,256,1024]{2,1,0:T(8,128)}, u32[]{:S(2)}) copy-start(f32[2,256,1024]{2,1,0:T(8,128)} %shard_map.58) | copy-start | bytes 6291460
  169.3 6.2 %collective-permute-start.15 = (f32[2,2,2,32,1024]{4,3,2,1,0:T(8,128)S(1)}, f32[2,2,2,32,1024]{4,3,2,1,0:T(8,128)S(1)}, u32[]{:S(2)}, u32[]{:S(2)}) collective-permute-start(f32[2,2,2,32,1024]{4,3,2,1,0:T(8,128)S(1)} %dynamic-slice_bitcast_fusion), channel_id=1, source_target_pairs={{0,1},{1,0},{2,3},{3,2},{4,5},{5,4},{6,7},{7,6},{8,9},{9,8},{10,11... | collective-permute-start | bytes 3145736 | tf_op jit(solution)/shard_map/ppermute | solution.py:140
  169.5 5.9 %collective-permute-start.12 = (f32[32,1024]{1,0:T(8,128)S(1)}, f32[32,1024]{1,0:T(8,128)S(1)}, u32[]{:S(2)}, u32[]{:S(2)}) collective-permute-start(f32[32,1024]{1,0:T(8,128)S(1)} %dynamic-slice_bitcast_fusion.15), channel_id=1, source_target_pairs={{0,4},{1,5},{2,6},{3,7},{4,0},{5,1},{6,2},{7,3},{8,12},{9,13},{10,... | collective-permute-start | bytes 393224 | tf_op jit(solution)/shard_map/ppermute | solution.py:96
  171.0 6.3 %collective-permute-start.14 = (f32[32,1024]{1,0:T(8,128)S(1)}, f32[32,1024]{1,0:T(8,128)S(1)}, u32[]{:S(2)}, u32[]{:S(2)}) collective-permute-start(f32[32,1024]{1,0:T(8,128)S(1)} %dynamic-slice_bitcast_fusion.14), channel_id=1, source_target_pairs={{0,2},{1,3},{2,0},{3,1},{4,6},{5,7},{6,4},{7,5},{8,10},{9,11},{10,... | collective-permute-start | bytes 393224 | tf_op jit(solution)/shard_map/ppermute | solution.py:96
  175.8 8.0 %collective-permute-start.16 = (f32[2,32,1024]{2,1,0:T(8,128)S(1)}, f32[2,32,1024]{2,1,0:T(8,128)S(1)}, u32[]{:S(2)}, u32[]{:S(2)}) collective-permute-start(f32[2,32,1024]{2,1,0:T(8,128)S(1)} %dynamic-slice_bitcast_fusion.5), channel_id=1, source_target_pairs={{0,2},{1,3},{2,0},{3,1},{4,6},{5,7},{6,4},{7,5},{8,10},{9,11},{10,... | collective-permute-start | bytes 786440 | tf_op jit(solution)/shard_map/ppermute | solution.py:96
  177.4 7.9 %collective-permute-start.18 = (f32[2,32,1024]{2,1,0:T(8,128)S(1)}, f32[2,32,1024]{2,1,0:T(8,128)S(1)}, u32[]{:S(2)}, u32[]{:S(2)}) collective-permute-start(f32[2,32,1024]{2,1,0:T(8,128)S(1)} %dynamic-slice_bitcast_fusion.4), channel_id=1, source_target_pairs={{0,4},{1,5},{2,6},{3,7},{4,0},{5,1},{6,2},{7,3},{8,12},{9,13},{10,... | collective-permute-start | bytes 786440 | tf_op jit(solution)/shard_map/ppermute | solution.py:96
  183.8 5.0 %collective-permute-start.17 = (f32[32,1024]{1,0:T(8,128)S(1)}, f32[32,1024]{1,0:T(8,128)S(1)}, u32[]{:S(2)}, u32[]{:S(2)}) collective-permute-start(f32[32,1024]{1,0:T(8,128)S(1)} %dynamic-slice_bitcast_fusion.13), channel_id=1, source_target_pairs={{0,4},{1,5},{2,6},{3,7},{4,0},{5,1},{6,2},{7,3},{8,12},{9,13},{10,... | collective-permute-start | bytes 393224 | tf_op jit(solution)/shard_map/ppermute | solution.py:96
  185.4 5.0 %collective-permute-start.19 = (f32[32,1024]{1,0:T(8,128)S(1)}, f32[32,1024]{1,0:T(8,128)S(1)}, u32[]{:S(2)}, u32[]{:S(2)}) collective-permute-start(f32[32,1024]{1,0:T(8,128)S(1)} %dynamic-slice_bitcast_fusion.12), channel_id=1, source_target_pairs={{0,2},{1,3},{2,0},{3,1},{4,6},{5,7},{6,4},{7,5},{8,10},{9,11},{10,... | collective-permute-start | bytes 393224 | tf_op jit(solution)/shard_map/ppermute | solution.py:96
  (3 other events, 5.4 us)
Sparse Core Ops, SparseCore 0:
  16.3 54.8 all-gather.14
  72.7 25.6 all-gather.12
  100.0 27.4 all-gather.10
  128.9 27.4 all-gather.8

commit v22 on v21

--- a/solution.py
+++ b/solution.py
@@ -50,7 +50,7 @@
     per_step = ab_count // 2 if ab_count % 2 == 0 else 1
     steps_per_half = ab_count // (2 * per_step)
     cost = pl.CostEstimate(
-        flops=2 * rows * width * ab_count * tile,
+        flops=2 * rows * tile * tile * n,
         transcendentals=0,
         bytes_accessed=rows * width * 2 + tiles.size * 2 + rows * ab_count * tile * 4,
     )

time: 198 us -> 199 us (level)
  no operation moved by 1% of the time
where the time goes in v22:
time: 199 us; the launch traced here: 198 us
  waiting for transfers between devices  107 us (54%)
  starting transfers between devices  28.9 us (15%)
  Pallas kernels  28.7 us (14%)
  between operations  13.6 us (7%)
  local copies, waits for them, and re-layouts  11.5 us (6%)
  other arithmetic  8 us (4%)
    all_gather x4, waiting for transfers between devices, on_device(): lax.all_gather(local4[:, c], 'own', axis=0, tiled=True)  70.4 us
    pallas_call x4, Pallas kernels, _ladder_products(): pl.pallas_call(_ladder_kernel, grid_spec=grid_spec, out_shape=jax.ShapeDt...  28.7 us
    ppermute x16, waiting for transfers between devices, advance(): self.x = keep + lax.ppermute(send, 'rep', perm=pairs)  25.3 us
    ppermute x16, starting transfers between devices, advance(): self.x = keep + lax.ppermute(send, 'rep', perm=pairs)  21.2 us
    all_to_all x1, waiting for transfers between devices, on_device(): lax.all_to_all(integrals, ('own', 'rep'), split_axis=0, concat_axis=0, ti...  8.25 us
    all_to_all x1, starting transfers between devices, on_device(): lax.all_to_all(integrals, ('own', 'rep'), split_axis=0, concat_axis=0, ti...  7.3 us
    squeeze x4, local copies, waits for them, and re-layouts, advance(): send = lax.dynamic_index_in_dim(self.joint, 1 - mine, ax, keepdims=False)  6.65 us
  transfers between devices with their start and end apart: 25, of which 15 were waited for; matrix products, arithmetic and copies ran while one was open for 9% of the time, Pallas kernels for 15%

profile of v22, /device:TPU:0, one launch (start us, length us, event | category | flops | bytes accessed | tf_op | source)
XLA Modules:
  0.0 198.0 jit_solution(10084312769212818988)
XLA Ops:
  6.5 7.3 %all-to-all-start = ((bf16[64,128,128]{2,1,0:T(8,128)(2,1)}), bf16[64,128,128]{2,1,0:T(8,128)(2,1)S(1)}, u32[]{:S(2)}, u32[]{:S(2)}) async-start(bf16[64,128,128]{2,1,0:T(8,128)(2,1)} %param.6), calls=%async_computation | async-start | bytes 4194304 | tf_op jit(solution)/shard_map/all_to_all | solution.py:160
  18.4 52.8 %all-gather.15.cloned.1.call-done = bf16[8,1,32,2048]{3,2,1,0:T(8,128)(2,1)} async-done(((bf16[2,1,32,2048]{3,2,1,0:T(8,128)(2,1)}), bf16[8,1,32,2048]{3,2,1,0:T(8,128)(2,1)}) %all-gather.15.cloned.1.call-update) | async-done | bytes 1048592 | tf_op jit(solution)/shard_map/all_gather | solution.py:174
  71.2 8.2 %all-to-all-done.tiles_ref = bf16[64,128,128]{2,1,0:T(8,128)(2,1)S(1)} async-done(((bf16[64,128,128]{2,1,0:T(8,128)(2,1)}), bf16[64,128,128]{2,1,0:T(8,128)(2,1)S(1)}, u32[]{:S(2)}, u32[]{:S(2)}) %all-to-all-start) | async-done | bytes 2097184 | tf_op jit(solution)/shard_map/all_to_all | solution.py:160
  80.8 7.2 %shard_map.55 = f32[2,256,1024]{2,1,0:T(8,128)} custom-call(s32[64]{0:T(128)} %select_reduce_fusion.order_ref, s32[17]{0:T(128)} %convert_reduce_fusion.1.starts_ref, s32[64]{0:T(128)} %copy-done.6, s32[64]{0:T(128)} %reshape.66.cd_ref, bf16[8,32,2048]{2,1,0:T(8,128)(2,1)} %bitcast.113, bf16[64,128,128]{2,1,0:T(8,128)(2,1)} %copy-done), custom_call_target="tpu_custom_call" | custom-call | flops 536870912 | bytes 5242880 | tf_op jit(solution)/shard_map/pallas_call | solution.py:69
  88.0 1.5 dynamic-slice_bitcast_fusion.3
  89.6 2.7 %collective-permute-done = f32[2,2,2,32,1024]{4,3,2,1,0:T(8,128)} collective-permute-done((f32[2,2,2,32,1024]{4,3,2,1,0:T(8,128)S(1)}, f32[2,2,2,32,1024]{4,3,2,1,0:T(8,128)}, u32[]{:S(2)}, u32[]{:S(2)}) %collective-permute-start) | collective-permute-done | bytes 1048608 | tf_op jit(solution)/shard_map/ppermute | solution.py:140
  93.8 4.7 %all-gather.13.cloned.1.call-done = bf16[8,1,32,2048]{3,2,1,0:T(8,128)(2,1)} async-done(((bf16[2,1,32,2048]{3,2,1,0:T(8,128)(2,1)}), bf16[8,1,32,2048]{3,2,1,0:T(8,128)(2,1)}) %all-gather.13.cloned.1.call-update) | async-done | bytes 1048592 | tf_op jit(solution)/shard_map/all_gather | solution.py:174
  98.5 7.2 %shard_map.56 = f32[2,256,1024]{2,1,0:T(8,128)} custom-call(s32[64]{0:T(128)} %select_reduce_fusion.order_ref, s32[17]{0:T(128)} %convert_reduce_fusion.1.starts_ref, s32[64]{0:T(128)} %copy-done.6, s32[64]{0:T(128)} %reshape.66.cd_ref, bf16[8,32,2048]{2,1,0:T(8,128)(2,1)} %bitcast.112, bf16[64,128,128]{2,1,0:T(8,128)(2,1)} %copy-done), custom_call_target="tpu_custom_call" | custom-call | flops 536870912 | bytes 5242880 | tf_op jit(solution)/shard_map/pallas_call | solution.py:69
  105.7 2.5 %dynamic-slice_bitcast_fusion.2 = f32[2,2,2,32,1024]{4,3,2,1,0:T(8,128)} fusion(f32[2,2,2,2,32,1024]{5,4,3,2,1,0:T(8,128)} %bitcast.102, s32[]{:T(128)S(6)} %select_n.75), kind=kLoop, calls=%fused_computation.7 | loop fusion | bytes 2097156 | tf_op jit(solution)/shard_map/jit(dynamic_index_in_dim)/squeeze | solution.py:138
  108.2 1.5 collective-permute-start.2
  110.4 1.6 collective-permute-start.1
  112.0 5.1 %collective-permute-done.2 = f32[2,32,1024]{2,1,0:T(8,128)} collective-permute-done((f32[2,32,1024]{2,1,0:T(8,128)S(1)}, f32[2,32,1024]{2,1,0:T(8,128)}, u32[]{:S(2)}, u32[]{:S(2)}) %collective-permute-start.2) | collective-permute-done | bytes 262176 | tf_op jit(solution)/shard_map/ppermute | solution.py:96
  121.6 5.9 %all-gather.11.cloned.1.call-done = bf16[8,1,32,2048]{3,2,1,0:T(8,128)(2,1)} async-done(((bf16[2,1,32,2048]{3,2,1,0:T(8,128)(2,1)}), bf16[8,1,32,2048]{3,2,1,0:T(8,128)(2,1)}) %all-gather.11.cloned.1.call-update) | async-done | bytes 1048592 | tf_op jit(solution)/shard_map/all_gather | solution.py:174
  127.5 7.2 %shard_map.57 = f32[2,256,1024]{2,1,0:T(8,128)} custom-call(s32[64]{0:T(128)} %select_reduce_fusion.order_ref, s32[17]{0:T(128)} %convert_reduce_fusion.1.starts_ref, s32[64]{0:T(128)} %copy-done.6, s32[64]{0:T(128)} %reshape.66.cd_ref, bf16[8,32,2048]{2,1,0:T(8,128)(2,1)} %bitcast.111, bf16[64,128,128]{2,1,0:T(8,128)(2,1)} %copy-done), custom_call_target="tpu_custom_call" | custom-call | flops 536870912 | bytes 5242880 | tf_op jit(solution)/shard_map/pallas_call | solution.py:69
  136.2 1.5 collective-permute-start.7
  137.7 1.6 collective-permute-start.5
  140.6 3.5 %collective-permute-done.5 = f32[32,1024]{1,0:T(8,128)S(1)} collective-permute-done((f32[32,1024]{1,0:T(8,128)S(1)}, f32[32,1024]{1,0:T(8,128)S(1)}, u32[]{:S(2)}, u32[]{:S(2)}) %collective-permute-start.5) | collective-permute-done | bytes 131104 | tf_op jit(solution)/shard_map/ppermute | solution.py:96
  144.1 3.7 %collective-permute-done.4 = f32[32,1024]{1,0:T(8,128)S(1)} collective-permute-done((f32[32,1024]{1,0:T(8,128)S(1)}, f32[32,1024]{1,0:T(8,128)S(1)}, u32[]{:S(2)}, u32[]{:S(2)}) %collective-permute-start.4) | collective-permute-done | bytes 131104 | tf_op jit(solution)/shard_map/ppermute | solution.py:96
  149.3 7.0 %all-gather.9.cloned.1.call-done = bf16[8,1,32,2048]{3,2,1,0:T(8,128)(2,1)} async-done(((bf16[2,1,32,2048]{3,2,1,0:T(8,128)(2,1)}), bf16[8,1,32,2048]{3,2,1,0:T(8,128)(2,1)}) %all-gather.9.cloned.1.call-update) | async-done | bytes 1048592 | tf_op jit(solution)/shard_map/all_gather | solution.py:174
  156.4 1.6 collective-permute-start.9
  158.0 1.5 collective-permute-start.10
  160.7 7.2 %shard_map.58 = f32[2,256,1024]{2,1,0:T(8,128)} custom-call(s32[64]{0:T(128)} %select_reduce_fusion.order_ref, s32[17]{0:T(128)} %convert_reduce_fusion.1.starts_ref, s32[64]{0:T(128)} %copy-done.6, s32[64]{0:T(128)} %reshape.66.cd_ref, bf16[8,32,2048]{2,1,0:T(8,128)(2,1)} %bitcast.110, bf16[64,128,128]{2,1,0:T(8,128)(2,1)} %copy-done), custom_call_target="tpu_custom_call" | custom-call | flops 536870912 | bytes 5242880 | tf_op jit(solution)/shard_map/pallas_call | solution.py:69
  169.5 1.5 collective-permute-start.12
  171.1 1.6 collective-permute-start.14
  172.7 2.7 %collective-permute-done.12 = f32[32,1024]{1,0:T(8,128)S(1)} collective-permute-done((f32[32,1024]{1,0:T(8,128)S(1)}, f32[32,1024]{1,0:T(8,128)S(1)}, u32[]{:S(2)}, u32[]{:S(2)}) %collective-permute-start.12) | collective-permute-done | bytes 131104 | tf_op jit(solution)/shard_map/ppermute | solution.py:96
  175.8 1.6 collective-permute-start.16
  177.5 1.6 collective-permute-start.18
  179.0 4.7 %collective-permute-done.16 = f32[2,32,1024]{2,1,0:T(8,128)S(1)} collective-permute-done((f32[2,32,1024]{2,1,0:T(8,128)S(1)}, f32[2,32,1024]{2,1,0:T(8,128)S(1)}, u32[]{:S(2)}, u32[]{:S(2)}) %collective-permute-start.16) | collective-permute-done | bytes 262176 | tf_op jit(solution)/shard_map/ppermute | solution.py:96
  183.8 1.5 collective-permute-start.17
  185.4 1.6 collective-permute-start.19
  187.1 1.8 collective-permute-done.17
  188.9 1.6 collective-permute-done.19
  (102 shorter events, 21.2 us)
Async XLA Ops:
  6.5 7.4 %copy-start.5 = (bf16[256,2048]{1,0:T(8,128)(2,1)S(1)}, bf16[256,2048]{1,0:T(8,128)(2,1)}, u32[]{:S(2)}) copy-start(bf16[256,2048]{1,0:T(8,128)(2,1)} %param.5) | copy-start | bytes 3145732
  6.5 72.9 %all-to-all-start = ((bf16[64,128,128]{2,1,0:T(8,128)(2,1)}), bf16[64,128,128]{2,1,0:T(8,128)(2,1)S(1)}, u32[]{:S(2)}, u32[]{:S(2)}) async-start(bf16[64,128,128]{2,1,0:T(8,128)(2,1)} %param.6), calls=%async_computation | async-start | bytes 4194304 | tf_op jit(solution)/shard_map/all_to_all | solution.py:160
  13.9 2.3 %copy-start.8 = (s32[1,32,2]{1,2,0:T(2,128)S(1)}, s32[1,32,2]{1,2,0:T(2,128)}, u32[]{:S(2)}) copy-start(s32[1,32,2]{1,2,0:T(2,128)} %param.8) | copy-start | bytes 772
  13.9 57.3 %all-gather.15.cloned.1.call-start = ((), (), s32[]{:S(2)}) async-start(), calls=%async_computation.4 | async-start | bytes 1310720 | tf_op jit(solution)/shard_map/all_gather | solution.py:174
  14.9 83.5 %all-gather.13.cloned.1.call-start = ((), (), s32[]{:S(2)}) async-start(), calls=%async_computation.3 | async-start | bytes 1310720 | tf_op jit(solution)/shard_map/all_gather | solution.py:174
  15.7 111.8 %all-gather.11.cloned.1.call-start = ((), (), s32[]{:S(2)}) async-start(), calls=%async_computation.2 | async-start | bytes 1310720 | tf_op jit(solution)/shard_map/all_gather | solution.py:174
  16.0 63.4 %copy-start.6 = (s32[64]{0:T(128)}, s32[64]{0:T(128)S(1)}, u32[]{:S(2)}) copy-start(s32[64]{0:T(128)S(1)} %reshape.65.ab_ref) | copy-start | bytes 772
  87.9 4.3 %copy-start.4 = (f32[2,256,1024]{2,1,0:T(8,128)S(1)}, f32[2,256,1024]{2,1,0:T(8,128)}, u32[]{:S(2)}) copy-start(f32[2,256,1024]{2,1,0:T(8,128)} %shard_map.55) | copy-start | bytes 6291460
  89.4 2.9 %collective-permute-start = (f32[2,2,2,32,1024]{4,3,2,1,0:T(8,128)S(1)}, f32[2,2,2,32,1024]{4,3,2,1,0:T(8,128)}, u32[]{:S(2)}, u32[]{:S(2)}) collective-permute-start(f32[2,2,2,32,1024]{4,3,2,1,0:T(8,128)S(1)} %dynamic-slice_bitcast_fusion.3), channel_id=1, source_target_pairs={{0,1},{1,0},{2,3},{3,2},{4,5},{5,4},{6,7},{7,6},{8,9},{9,8},{10,11... | collective-permute-start | bytes 3145736 | tf_op jit(solution)/shard_map/ppermute | solution.py:140
  89.5 66.8 %all-gather.9.cloned.1.call-start = ((), (), s32[]{:S(2)}) async-start(), calls=%async_computation.1 | async-start | bytes 1310720 | tf_op jit(solution)/shard_map/all_gather | solution.py:174
  105.7 14.5 %copy-start.1 = (f32[2,256,1024]{2,1,0:T(8,128)S(1)}, f32[2,256,1024]{2,1,0:T(8,128)}, u32[]{:S(2)}) copy-start(f32[2,256,1024]{2,1,0:T(8,128)} %shard_map.56) | copy-start | bytes 6291460
  108.2 12.0 %collective-permute-start.3 = (f32[2,2,2,32,1024]{4,3,2,1,0:T(8,128)}, f32[2,2,2,32,1024]{4,3,2,1,0:T(8,128)}, u32[]{:S(2)}, u32[]{:S(2)}) collective-permute-start(f32[2,2,2,32,1024]{4,3,2,1,0:T(8,128)} %dynamic-slice_bitcast_fusion.2), channel_id=1, source_target_pairs={{0,1},{1,0},{2,3},{3,2},{4,5},{5,4},{6,7},{7,6},{8,9},{9,8},{10,11... | collective-permute-start | bytes 3145736 | tf_op jit(solution)/shard_map/ppermute | solution.py:140
  108.2 8.9 %collective-permute-start.2 = (f32[2,32,1024]{2,1,0:T(8,128)S(1)}, f32[2,32,1024]{2,1,0:T(8,128)}, u32[]{:S(2)}, u32[]{:S(2)}) collective-permute-start(f32[2,32,1024]{2,1,0:T(8,128)S(1)} %dynamic-slice_bitcast_fusion.10), channel_id=1, source_target_pairs={{0,4},{1,5},{2,6},{3,7},{4,0},{5,1},{6,2},{7,3},{8,12},{9,13},{10,... | collective-permute-start | bytes 786440 | tf_op jit(solution)/shard_map/ppermute | solution.py:96
  110.4 8.8 %collective-permute-start.1 = (f32[2,32,1024]{2,1,0:T(8,128)}, f32[2,32,1024]{2,1,0:T(8,128)}, u32[]{:S(2)}, u32[]{:S(2)}) collective-permute-start(f32[2,32,1024]{2,1,0:T(8,128)} %dynamic-slice_bitcast_fusion.11), channel_id=1, source_target_pairs={{0,2},{1,3},{2,0},{3,1},{4,6},{5,7},{6,4},{7,5},{8,10},{9,11},{10,... | collective-permute-start | bytes 786440 | tf_op jit(solution)/shard_map/ppermute | solution.py:96
  136.1 12.9 %copy-start.3 = (f32[2,256,1024]{2,1,0:T(8,128)S(1)}, f32[2,256,1024]{2,1,0:T(8,128)}, u32[]{:S(2)}) copy-start(f32[2,256,1024]{2,1,0:T(8,128)} %shard_map.57) | copy-start | bytes 6291460
  136.1 12.9 %collective-permute-start.8 = (f32[2,2,2,32,1024]{4,3,2,1,0:T(8,128)S(1)}, f32[2,2,2,32,1024]{4,3,2,1,0:T(8,128)S(1)}, u32[]{:S(2)}, u32[]{:S(2)}) collective-permute-start(f32[2,2,2,32,1024]{4,3,2,1,0:T(8,128)S(1)} %dynamic-slice_bitcast_fusion.1), channel_id=1, source_target_pairs={{0,1},{1,0},{2,3},{3,2},{4,5},{5,4},{6,7},{7,6},{8,9},{9,8},{10,11... | collective-permute-start | bytes 3145736 | tf_op jit(solution)/shard_map/ppermute | solution.py:140
  136.2 11.6 %collective-permute-start.7 = (f32[2,32,1024]{2,1,0:T(8,128)S(1)}, f32[2,32,1024]{2,1,0:T(8,128)S(1)}, u32[]{:S(2)}, u32[]{:S(2)}) collective-permute-start(f32[2,32,1024]{2,1,0:T(8,128)S(1)} %dynamic-slice_bitcast_fusion.8), channel_id=1, source_target_pairs={{0,4},{1,5},{2,6},{3,7},{4,0},{5,1},{6,2},{7,3},{8,12},{9,13},{10,... | collective-permute-start | bytes 786440 | tf_op jit(solution)/shard_map/ppermute | solution.py:96
  137.7 6.4 %collective-permute-start.5 = (f32[32,1024]{1,0:T(8,128)S(1)}, f32[32,1024]{1,0:T(8,128)S(1)}, u32[]{:S(2)}, u32[]{:S(2)}) collective-permute-start(f32[32,1024]{1,0:T(8,128)S(1)} %dynamic-slice_bitcast_fusion.18), channel_id=1, source_target_pairs={{0,2},{1,3},{2,0},{3,1},{4,6},{5,7},{6,4},{7,5},{8,10},{9,11},{10,... | collective-permute-start | bytes 393224 | tf_op jit(solution)/shard_map/ppermute | solution.py:96
  139.3 9.6 %collective-permute-start.6 = (f32[2,32,1024]{2,1,0:T(8,128)S(1)}, f32[2,32,1024]{2,1,0:T(8,128)S(1)}, u32[]{:S(2)}, u32[]{:S(2)}) collective-permute-start(f32[2,32,1024]{2,1,0:T(8,128)S(1)} %dynamic-slice_bitcast_fusion.9), channel_id=1, source_target_pairs={{0,2},{1,3},{2,0},{3,1},{4,6},{5,7},{6,4},{7,5},{8,10},{9,11},{10,... | collective-permute-start | bytes 786440 | tf_op jit(solution)/shard_map/ppermute | solution.py:96
  139.9 7.9 %collective-permute-start.4 = (f32[32,1024]{1,0:T(8,128)S(1)}, f32[32,1024]{1,0:T(8,128)S(1)}, u32[]{:S(2)}, u32[]{:S(2)}) collective-permute-start(f32[32,1024]{1,0:T(8,128)S(1)} %dynamic-slice_bitcast_fusion.19), channel_id=1, source_target_pairs={{0,4},{1,5},{2,6},{3,7},{4,0},{5,1},{6,2},{7,3},{8,12},{9,13},{10,... | collective-permute-start | bytes 393224 | tf_op jit(solution)/shard_map/ppermute | solution.py:96
  156.4 13.0 %collective-permute-start.9 = (f32[32,1024]{1,0:T(8,128)S(1)}, f32[32,1024]{1,0:T(8,128)S(1)}, u32[]{:S(2)}, u32[]{:S(2)}) collective-permute-start(f32[32,1024]{1,0:T(8,128)S(1)} %dynamic-slice_bitcast_fusion.17), channel_id=1, source_target_pairs={{0,4},{1,5},{2,6},{3,7},{4,0},{5,1},{6,2},{7,3},{8,12},{9,13},{10,... | collective-permute-start | bytes 393224 | tf_op jit(solution)/shard_map/ppermute | solution.py:96
  158.0 11.4 %collective-permute-start.10 = (f32[32,1024]{1,0:T(8,128)S(1)}, f32[32,1024]{1,0:T(8,128)S(1)}, u32[]{:S(2)}, u32[]{:S(2)}) collective-permute-start(f32[32,1024]{1,0:T(8,128)S(1)} %dynamic-slice_bitcast_fusion.16), channel_id=1, source_target_pairs={{0,2},{1,3},{2,0},{3,1},{4,6},{5,7},{6,4},{7,5},{8,10},{9,11},{10,... | collective-permute-start | bytes 393224 | tf_op jit(solution)/shard_map/ppermute | solution.py:96
  159.5 9.9 %collective-permute-start.11 = (f32[2,32,1024]{2,1,0:T(8,128)S(1)}, f32[2,32,1024]{2,1,0:T(8,128)S(1)}, u32[]{:S(2)}, u32[]{:S(2)}) collective-permute-start(f32[2,32,1024]{2,1,0:T(8,128)S(1)} %dynamic-slice_bitcast_fusion.7), channel_id=1, source_target_pairs={{0,2},{1,3},{2,0},{3,1},{4,6},{5,7},{6,4},{7,5},{8,10},{9,11},{10,... | collective-permute-start | bytes 786440 | tf_op jit(solution)/shard_map/ppermute | solution.py:96
  160.2 10.8 %collective-permute-start.13 = (f32[2,32,1024]{2,1,0:T(8,128)S(1)}, f32[2,32,1024]{2,1,0:T(8,128)S(1)}, u32[]{:S(2)}, u32[]{:S(2)}) collective-permute-start(f32[2,32,1024]{2,1,0:T(8,128)S(1)} %dynamic-slice_bitcast_fusion.6), channel_id=1, source_target_pairs={{0,4},{1,5},{2,6},{3,7},{4,0},{5,1},{6,2},{7,3},{8,12},{9,13},{10,... | collective-permute-start | bytes 786440 | tf_op jit(solution)/shard_map/ppermute | solution.py:96
  169.2 6.2 %copy-start.2 = (f32[2,256,1024]{2,1,0:T(8,128)S(1)}, f32[2,256,1024]{2,1,0:T(8,128)}, u32[]{:S(2)}) copy-start(f32[2,256,1024]{2,1,0:T(8,128)} %shard_map.58) | copy-start | bytes 6291460
  169.2 6.2 %collective-permute-start.15 = (f32[2,2,2,32,1024]{4,3,2,1,0:T(8,128)S(1)}, f32[2,2,2,32,1024]{4,3,2,1,0:T(8,128)S(1)}, u32[]{:S(2)}, u32[]{:S(2)}) collective-permute-start(f32[2,2,2,32,1024]{4,3,2,1,0:T(8,128)S(1)} %dynamic-slice_bitcast_fusion), channel_id=1, source_target_pairs={{0,1},{1,0},{2,3},{3,2},{4,5},{5,4},{6,7},{7,6},{8,9},{9,8},{10,11... | collective-permute-start | bytes 3145736 | tf_op jit(solution)/shard_map/ppermute | solution.py:140
  169.5 5.9 %collective-permute-start.12 = (f32[32,1024]{1,0:T(8,128)S(1)}, f32[32,1024]{1,0:T(8,128)S(1)}, u32[]{:S(2)}, u32[]{:S(2)}) collective-permute-start(f32[32,1024]{1,0:T(8,128)S(1)} %dynamic-slice_bitcast_fusion.15), channel_id=1, source_target_pairs={{0,4},{1,5},{2,6},{3,7},{4,0},{5,1},{6,2},{7,3},{8,12},{9,13},{10,... | collective-permute-start | bytes 393224 | tf_op jit(solution)/shard_map/ppermute | solution.py:96
  171.1 6.3 %collective-permute-start.14 = (f32[32,1024]{1,0:T(8,128)S(1)}, f32[32,1024]{1,0:T(8,128)S(1)}, u32[]{:S(2)}, u32[]{:S(2)}) collective-permute-start(f32[32,1024]{1,0:T(8,128)S(1)} %dynamic-slice_bitcast_fusion.14), channel_id=1, source_target_pairs={{0,2},{1,3},{2,0},{3,1},{4,6},{5,7},{6,4},{7,5},{8,10},{9,11},{10,... | collective-permute-start | bytes 393224 | tf_op jit(solution)/shard_map/ppermute | solution.py:96
  175.8 8.0 %collective-permute-start.16 = (f32[2,32,1024]{2,1,0:T(8,128)S(1)}, f32[2,32,1024]{2,1,0:T(8,128)S(1)}, u32[]{:S(2)}, u32[]{:S(2)}) collective-permute-start(f32[2,32,1024]{2,1,0:T(8,128)S(1)} %dynamic-slice_bitcast_fusion.5), channel_id=1, source_target_pairs={{0,2},{1,3},{2,0},{3,1},{4,6},{5,7},{6,4},{7,5},{8,10},{9,11},{10,... | collective-permute-start | bytes 786440 | tf_op jit(solution)/shard_map/ppermute | solution.py:96
  177.5 7.9 %collective-permute-start.18 = (f32[2,32,1024]{2,1,0:T(8,128)S(1)}, f32[2,32,1024]{2,1,0:T(8,128)S(1)}, u32[]{:S(2)}, u32[]{:S(2)}) collective-permute-start(f32[2,32,1024]{2,1,0:T(8,128)S(1)} %dynamic-slice_bitcast_fusion.4), channel_id=1, source_target_pairs={{0,4},{1,5},{2,6},{3,7},{4,0},{5,1},{6,2},{7,3},{8,12},{9,13},{10,... | collective-permute-start | bytes 786440 | tf_op jit(solution)/shard_map/ppermute | solution.py:96
  183.8 5.0 %collective-permute-start.17 = (f32[32,1024]{1,0:T(8,128)S(1)}, f32[32,1024]{1,0:T(8,128)S(1)}, u32[]{:S(2)}, u32[]{:S(2)}) collective-permute-start(f32[32,1024]{1,0:T(8,128)S(1)} %dynamic-slice_bitcast_fusion.13), channel_id=1, source_target_pairs={{0,4},{1,5},{2,6},{3,7},{4,0},{5,1},{6,2},{7,3},{8,12},{9,13},{10,... | collective-permute-start | bytes 393224 | tf_op jit(solution)/shard_map/ppermute | solution.py:96
  185.4 5.0 %collective-permute-start.19 = (f32[32,1024]{1,0:T(8,128)S(1)}, f32[32,1024]{1,0:T(8,128)S(1)}, u32[]{:S(2)}, u32[]{:S(2)}) collective-permute-start(f32[32,1024]{1,0:T(8,128)S(1)} %dynamic-slice_bitcast_fusion.12), channel_id=1, source_target_pairs={{0,2},{1,3},{2,0},{3,1},{4,6},{5,7},{6,4},{7,5},{8,10},{9,11},{10,... | collective-permute-start | bytes 393224 | tf_op jit(solution)/shard_map/ppermute | solution.py:96
  (3 other events, 5.2 us)
Sparse Core Ops, SparseCore 0:
  16.3 54.8 all-gather.14
  72.7 25.7 all-gather.12
  100.1 27.4 all-gather.10
  128.9 27.3 all-gather.8

commit v23 on v21

--- a/solution.py
+++ b/solution.py
@@ -184,11 +184,17 @@
             amp3 = gathered[chunk]
         partial = _ladder_products(amp3, received, order, starts, ab_ids, cd_ids, AB_DEV)
         flows.append(_Pair(partial, orders, rep_count))
+    out = None
     while any(flow.todo for flow in flows):
         for flow in flows:
             flow.advance(rep_index)
-    pieces = [flow.result() for flow in flows]
-    return jnp.concatenate(pieces, axis=0)
+        if out is None:
+            out = jnp.zeros((N_CHUNK * part, width), jnp.float32)
+        for c, flow in enumerate(flows):
+            if not flow.todo and not getattr(flow, "placed", False):
+                flow.placed = True
+                out = lax.dynamic_update_slice(out, flow.result(), (c * part, 0))
+    return out
 
 
 def solution(mesh):

time: 198 us -> 206 us (1.040)
  waiting for transfers between devices: 108 us -> 118 us
  starting transfers between devices: 28.3 us -> 25.8 us
    ppermute x16, waiting for transfers between devices: 25.7 us -> 35.6 us  [advance(): self.x = keep + lax.ppermute(send, 'rep', perm=pairs)]
    ppermute x16, starting transfers between devices: 20.7 us -> 18.2 us  [advance(): self.x = keep + lax.ppermute(send, 'rep', perm=pairs)]
  transfers between devices with their start and end apart: 25 -> 25, of which waited for: 15 -> 18; matrix products, arithmetic and copies ran while one was open for 9% -> 8% of each run, Pallas kernels for 15% -> 11%
where the time goes in v23:
time: 206 us; the launch traced here: 205 us
  waiting for transfers between devices  118 us (57%)
  Pallas kernels  29 us (14%)
  starting transfers between devices  25.8 us (13%)
  between operations  13.6 us (7%)
  local copies, waits for them, and re-layouts  11.5 us (6%)
  other arithmetic  7.86 us (4%)
    all_gather x4, waiting for transfers between devices, on_device(): lax.all_gather(local4[:, c], 'own', axis=0, tiled=True)  70.3 us
    ppermute x16, waiting for transfers between devices, advance(): self.x = keep + lax.ppermute(send, 'rep', perm=pairs)  35.6 us
    pallas_call x4, Pallas kernels, _ladder_products(): pl.pallas_call(_ladder_kernel, grid_spec=grid_spec, out_shape=jax.ShapeDt...  29 us
    ppermute x16, starting transfers between devices, advance(): self.x = keep + lax.ppermute(send, 'rep', perm=pairs)  18.2 us
    all_to_all x1, waiting for transfers between devices, on_device(): lax.all_to_all(integrals, ('own', 'rep'), split_axis=0, concat_axis=0, ti...  8.25 us
    all_to_all x1, starting transfers between devices, on_device(): lax.all_to_all(integrals, ('own', 'rep'), split_axis=0, concat_axis=0, ti...  7.3 us
    squeeze x4, local copies, waits for them, and re-layouts, advance(): send = lax.dynamic_index_in_dim(self.joint, 1 - mine, ax, keepdims=False)  6.65 us
  transfers between devices with their start and end apart: 25, of which 18 were waited for; matrix products, arithmetic and copies ran while one was open for 8% of the time, Pallas kernels for 11%

profile of v23, /device:TPU:0, one launch (start us, length us, event | category | flops | bytes accessed | tf_op | source)
XLA Modules:
  0.0 205.4 jit_solution(7777468899366213308)
XLA Ops:
  6.5 7.3 %all-to-all-start = ((bf16[64,128,128]{2,1,0:T(8,128)(2,1)}), bf16[64,128,128]{2,1,0:T(8,128)(2,1)S(1)}, u32[]{:S(2)}, u32[]{:S(2)}) async-start(bf16[64,128,128]{2,1,0:T(8,128)(2,1)} %param.6), calls=%async_computation | async-start | bytes 4194304 | tf_op jit(solution)/shard_map/all_to_all | solution.py:160
  18.5 52.7 %all-gather.15.cloned.1.call-done = bf16[8,1,32,2048]{3,2,1,0:T(8,128)(2,1)} async-done(((bf16[2,1,32,2048]{3,2,1,0:T(8,128)(2,1)}), bf16[8,1,32,2048]{3,2,1,0:T(8,128)(2,1)}) %all-gather.15.cloned.1.call-update) | async-done | bytes 1048592 | tf_op jit(solution)/shard_map/all_gather | solution.py:174
  71.2 8.2 %all-to-all-done.tiles_ref = bf16[64,128,128]{2,1,0:T(8,128)(2,1)S(1)} async-done(((bf16[64,128,128]{2,1,0:T(8,128)(2,1)}), bf16[64,128,128]{2,1,0:T(8,128)(2,1)S(1)}, u32[]{:S(2)}, u32[]{:S(2)}) %all-to-all-start) | async-done | bytes 2097184 | tf_op jit(solution)/shard_map/all_to_all | solution.py:160
  80.8 7.3 %shard_map.55 = f32[2,256,1024]{2,1,0:T(8,128)} custom-call(s32[64]{0:T(128)} %select_reduce_fusion.order_ref, s32[17]{0:T(128)} %convert_reduce_fusion.1.starts_ref, s32[64]{0:T(128)} %copy-done.10, s32[64]{0:T(128)} %reshape.66.cd_ref, bf16[8,32,2048]{2,1,0:T(8,128)(2,1)} %bitcast.115, bf16[64,128,128]{2,1,0:T(8,128)(2,1)} %copy-done.4), custom_call_target="tpu_custom_call" | custom-call | flops 2147483648 | bytes 5242880 | tf_op jit(solution)/shard_map/pallas_call | solution.py:69
  88.0 1.5 dynamic-slice_bitcast_fusion.3
  89.6 2.7 %collective-permute-done = f32[2,2,2,32,1024]{4,3,2,1,0:T(8,128)} collective-permute-done((f32[2,2,2,32,1024]{4,3,2,1,0:T(8,128)S(1)}, f32[2,2,2,32,1024]{4,3,2,1,0:T(8,128)}, u32[]{:S(2)}, u32[]{:S(2)}) %collective-permute-start) | collective-permute-done | bytes 1048608 | tf_op jit(solution)/shard_map/ppermute | solution.py:140
  92.3 1.4 bitcast_add_fusion.3
  93.8 4.6 %all-gather.13.cloned.1.call-done = bf16[8,1,32,2048]{3,2,1,0:T(8,128)(2,1)} async-done(((bf16[2,1,32,2048]{3,2,1,0:T(8,128)(2,1)}), bf16[8,1,32,2048]{3,2,1,0:T(8,128)(2,1)}) %all-gather.13.cloned.1.call-update) | async-done | bytes 1048592 | tf_op jit(solution)/shard_map/all_gather | solution.py:174
  98.4 7.2 %shard_map.56 = f32[2,256,1024]{2,1,0:T(8,128)} custom-call(s32[64]{0:T(128)} %select_reduce_fusion.order_ref, s32[17]{0:T(128)} %convert_reduce_fusion.1.starts_ref, s32[64]{0:T(128)} %copy-done.10, s32[64]{0:T(128)} %reshape.66.cd_ref, bf16[8,32,2048]{2,1,0:T(8,128)(2,1)} %bitcast.114, bf16[64,128,128]{2,1,0:T(8,128)(2,1)} %copy-done.4), custom_call_target="tpu_custom_call" | custom-call | flops 2147483648 | bytes 5242880 | tf_op jit(solution)/shard_map/pallas_call | solution.py:69
  105.7 2.5 %dynamic-slice_bitcast_fusion.2 = f32[2,2,2,32,1024]{4,3,2,1,0:T(8,128)} fusion(f32[2,2,2,2,32,1024]{5,4,3,2,1,0:T(8,128)} %bitcast.104, s32[]{:T(128)S(6)} %select_n.75), kind=kLoop, calls=%fused_computation.8 | loop fusion | bytes 2097156 | tf_op jit(solution)/shard_map/jit(dynamic_index_in_dim)/squeeze | solution.py:138
  108.2 1.4 collective-permute-start.2
  110.3 1.6 collective-permute-start.1
  111.9 5.1 %collective-permute-done.2 = f32[2,32,1024]{2,1,0:T(8,128)} collective-permute-done((f32[2,32,1024]{2,1,0:T(8,128)S(1)}, f32[2,32,1024]{2,1,0:T(8,128)}, u32[]{:S(2)}, u32[]{:S(2)}) %collective-permute-start.2) | collective-permute-done | bytes 262176 | tf_op jit(solution)/shard_map/ppermute | solution.py:96
  120.1 1.4 bitcast_add_fusion.2
  121.5 5.9 %all-gather.11.cloned.1.call-done = bf16[8,1,32,2048]{3,2,1,0:T(8,128)(2,1)} async-done(((bf16[2,1,32,2048]{3,2,1,0:T(8,128)(2,1)}), bf16[8,1,32,2048]{3,2,1,0:T(8,128)(2,1)}) %all-gather.11.cloned.1.call-update) | async-done | bytes 1048592 | tf_op jit(solution)/shard_map/all_gather | solution.py:174
  127.5 7.2 %shard_map.57 = f32[2,256,1024]{2,1,0:T(8,128)} custom-call(s32[64]{0:T(128)} %select_reduce_fusion.order_ref, s32[17]{0:T(128)} %convert_reduce_fusion.1.starts_ref, s32[64]{0:T(128)} %copy-done.10, s32[64]{0:T(128)} %reshape.66.cd_ref, bf16[8,32,2048]{2,1,0:T(8,128)(2,1)} %bitcast.113, bf16[64,128,128]{2,1,0:T(8,128)(2,1)} %copy-done.4), custom_call_target="tpu_custom_call" | custom-call | flops 2147483648 | bytes 5242880 | tf_op jit(solution)/shard_map/pallas_call | solution.py:69
  136.2 1.4 collective-permute-start.7
  137.6 1.7 collective-permute-start.5
  140.6 3.4 %collective-permute-done.5 = f32[32,1024]{1,0:T(8,128)S(1)} collective-permute-done((f32[32,1024]{1,0:T(8,128)S(1)}, f32[32,1024]{1,0:T(8,128)S(1)}, u32[]{:S(2)}, u32[]{:S(2)}) %collective-permute-start.5) | collective-permute-done | bytes 131104 | tf_op jit(solution)/shard_map/ppermute | solution.py:96
  144.0 3.8 %collective-permute-done.4 = f32[32,1024]{1,0:T(8,128)S(1)} collective-permute-done((f32[32,1024]{1,0:T(8,128)S(1)}, f32[32,1024]{1,0:T(8,128)S(1)}, u32[]{:S(2)}, u32[]{:S(2)}) %collective-permute-start.4) | collective-permute-done | bytes 131104 | tf_op jit(solution)/shard_map/ppermute | solution.py:96
  149.2 7.1 %all-gather.9.cloned.1.call-done = bf16[8,1,32,2048]{3,2,1,0:T(8,128)(2,1)} async-done(((bf16[2,1,32,2048]{3,2,1,0:T(8,128)(2,1)}), bf16[8,1,32,2048]{3,2,1,0:T(8,128)(2,1)}) %all-gather.9.cloned.1.call-update) | async-done | bytes 1048592 | tf_op jit(solution)/shard_map/all_gather | solution.py:174
  156.3 7.2 %shard_map.58 = f32[2,256,1024]{2,1,0:T(8,128)} custom-call(s32[64]{0:T(128)} %select_reduce_fusion.order_ref, s32[17]{0:T(128)} %convert_reduce_fusion.1.starts_ref, s32[64]{0:T(128)} %copy-done.10, s32[64]{0:T(128)} %reshape.66.cd_ref, bf16[8,32,2048]{2,1,0:T(8,128)(2,1)} %bitcast.112, bf16[64,128,128]{2,1,0:T(8,128)(2,1)} %copy-done.4), custom_call_target="tpu_custom_call" | custom-call | flops 2147483648 | bytes 5242880 | tf_op jit(solution)/shard_map/pallas_call | solution.py:69
  165.0 1.6 collective-permute-start.11
  166.6 1.5 collective-permute-start.13
  169.4 8.4 %collective-permute-done.9 = f32[32,1024]{1,0:T(8,128)S(1)} collective-permute-done((f32[32,1024]{1,0:T(8,128)S(1)}, f32[32,1024]{1,0:T(8,128)S(1)}, u32[]{:S(2)}, u32[]{:S(2)}) %collective-permute-start.9) | collective-permute-done | bytes 131104 | tf_op jit(solution)/shard_map/ppermute | solution.py:96
  178.0 1.5 collective-permute-start.12
  180.1 3.0 %collective-permute-done.12 = f32[32,1024]{1,0:T(8,128)S(1)} collective-permute-done((f32[32,1024]{1,0:T(8,128)S(1)}, f32[32,1024]{1,0:T(8,128)S(1)}, u32[]{:S(2)}, u32[]{:S(2)}) %collective-permute-start.12) | collective-permute-done | bytes 131104 | tf_op jit(solution)/shard_map/ppermute | solution.py:96
  183.1 1.6 collective-permute-done.14
  186.3 5.3 %collective-permute-done.16 = f32[2,32,1024]{2,1,0:T(8,128)S(1)} collective-permute-done((f32[2,32,1024]{2,1,0:T(8,128)S(1)}, f32[2,32,1024]{2,1,0:T(8,128)S(1)}, u32[]{:S(2)}, u32[]{:S(2)}) %collective-permute-start.16) | collective-permute-done | bytes 262176 | tf_op jit(solution)/shard_map/ppermute | solution.py:96
  192.4 2.7 %collective-permute-start.19 = (f32[32,1024]{1,0:T(8,128)S(1)}, f32[32,1024]{1,0:T(8,128)S(1)}, u32[]{:S(2)}, u32[]{:S(2)}) collective-permute-start(f32[32,1024]{1,0:T(8,128)S(1)} %dynamic-slice_bitcast_fusion.12), channel_id=1, source_target_pairs={{0,2},{1,3},{2,0},{3,1},{4,6},{5,7},{6,4},{7,5},{8,10},{9,11},{10,... | collective-permute-start | bytes 393224 | tf_op jit(solution)/shard_map/ppermute | solution.py:96
  195.1 1.5 collective-permute-done.17
  196.6 1.4 collective-permute-done.19
  (107 shorter events, 20.7 us)
Async XLA Ops:
  6.5 7.4 %copy-start.6 = (bf16[256,2048]{1,0:T(8,128)(2,1)S(1)}, bf16[256,2048]{1,0:T(8,128)(2,1)}, u32[]{:S(2)}) copy-start(bf16[256,2048]{1,0:T(8,128)(2,1)} %param.5) | copy-start | bytes 3145732
  6.5 72.9 %all-to-all-start = ((bf16[64,128,128]{2,1,0:T(8,128)(2,1)}), bf16[64,128,128]{2,1,0:T(8,128)(2,1)S(1)}, u32[]{:S(2)}, u32[]{:S(2)}) async-start(bf16[64,128,128]{2,1,0:T(8,128)(2,1)} %param.6), calls=%async_computation | async-start | bytes 4194304 | tf_op jit(solution)/shard_map/all_to_all | solution.py:160
  13.9 57.3 %all-gather.15.cloned.1.call-start = ((), (), s32[]{:S(2)}) async-start(), calls=%async_computation.4 | async-start | bytes 1310720 | tf_op jit(solution)/shard_map/all_gather | solution.py:174
  14.9 83.5 %all-gather.13.cloned.1.call-start = ((), (), s32[]{:S(2)}) async-start(), calls=%async_computation.3 | async-start | bytes 1310720 | tf_op jit(solution)/shard_map/all_gather | solution.py:174
  15.7 111.8 %all-gather.11.cloned.1.call-start = ((), (), s32[]{:S(2)}) async-start(), calls=%async_computation.2 | async-start | bytes 1310720 | tf_op jit(solution)/shard_map/all_gather | solution.py:174
  15.9 63.5 %copy-start.10 = (s32[64]{0:T(128)}, s32[64]{0:T(128)S(1)}, u32[]{:S(2)}) copy-start(s32[64]{0:T(128)S(1)} %reshape.65.ab_ref) | copy-start | bytes 772
  88.0 4.3 %copy-start.3 = (f32[2,256,1024]{2,1,0:T(8,128)S(1)}, f32[2,256,1024]{2,1,0:T(8,128)}, u32[]{:S(2)}) copy-start(f32[2,256,1024]{2,1,0:T(8,128)} %shard_map.55) | copy-start | bytes 6291460
  89.5 2.9 %collective-permute-start = (f32[2,2,2,32,1024]{4,3,2,1,0:T(8,128)S(1)}, f32[2,2,2,32,1024]{4,3,2,1,0:T(8,128)}, u32[]{:S(2)}, u32[]{:S(2)}) collective-permute-start(f32[2,2,2,32,1024]{4,3,2,1,0:T(8,128)S(1)} %dynamic-slice_bitcast_fusion.3), channel_id=1, source_target_pairs={{0,1},{1,0},{2,3},{3,2},{4,5},{5,4},{6,7},{7,6},{8,9},{9,8},{10,11... | collective-permute-start | bytes 3145736 | tf_op jit(solution)/shard_map/ppermute | solution.py:140
  89.6 66.7 %all-gather.9.cloned.1.call-start = ((), (), s32[]{:S(2)}) async-start(), calls=%async_computation.1 | async-start | bytes 1310720 | tf_op jit(solution)/shard_map/all_gather | solution.py:174
  105.7 14.4 %copy-start.1 = (f32[2,256,1024]{2,1,0:T(8,128)S(1)}, f32[2,256,1024]{2,1,0:T(8,128)}, u32[]{:S(2)}) copy-start(f32[2,256,1024]{2,1,0:T(8,128)} %shard_map.56) | copy-start | bytes 6291460
  108.2 11.9 %collective-permute-start.3 = (f32[2,2,2,32,1024]{4,3,2,1,0:T(8,128)}, f32[2,2,2,32,1024]{4,3,2,1,0:T(8,128)}, u32[]{:S(2)}, u32[]{:S(2)}) collective-permute-start(f32[2,2,2,32,1024]{4,3,2,1,0:T(8,128)} %dynamic-slice_bitcast_fusion.2), channel_id=1, source_target_pairs={{0,1},{1,0},{2,3},{3,2},{4,5},{5,4},{6,7},{7,6},{8,9},{9,8},{10,11... | collective-permute-start | bytes 3145736 | tf_op jit(solution)/shard_map/ppermute | solution.py:140
  108.2 8.9 %collective-permute-start.2 = (f32[2,32,1024]{2,1,0:T(8,128)S(1)}, f32[2,32,1024]{2,1,0:T(8,128)}, u32[]{:S(2)}, u32[]{:S(2)}) collective-permute-start(f32[2,32,1024]{2,1,0:T(8,128)S(1)} %dynamic-slice_bitcast_fusion.10), channel_id=1, source_target_pairs={{0,4},{1,5},{2,6},{3,7},{4,0},{5,1},{6,2},{7,3},{8,12},{9,13},{10,... | collective-permute-start | bytes 786440 | tf_op jit(solution)/shard_map/ppermute | solution.py:96
  110.3 8.8 %collective-permute-start.1 = (f32[2,32,1024]{2,1,0:T(8,128)}, f32[2,32,1024]{2,1,0:T(8,128)}, u32[]{:S(2)}, u32[]{:S(2)}) collective-permute-start(f32[2,32,1024]{2,1,0:T(8,128)} %dynamic-slice_bitcast_fusion.11), channel_id=1, source_target_pairs={{0,2},{1,3},{2,0},{3,1},{4,6},{5,7},{6,4},{7,5},{8,10},{9,11},{10,... | collective-permute-start | bytes 786440 | tf_op jit(solution)/shard_map/ppermute | solution.py:96
  136.1 12.8 %copy-start.2 = (f32[2,256,1024]{2,1,0:T(8,128)S(1)}, f32[2,256,1024]{2,1,0:T(8,128)}, u32[]{:S(2)}) copy-start(f32[2,256,1024]{2,1,0:T(8,128)} %shard_map.57) | copy-start | bytes 6291460
  136.1 12.8 %collective-permute-start.8 = (f32[2,2,2,32,1024]{4,3,2,1,0:T(8,128)S(1)}, f32[2,2,2,32,1024]{4,3,2,1,0:T(8,128)S(1)}, u32[]{:S(2)}, u32[]{:S(2)}) collective-permute-start(f32[2,2,2,32,1024]{4,3,2,1,0:T(8,128)S(1)} %dynamic-slice_bitcast_fusion.1), channel_id=1, source_target_pairs={{0,1},{1,0},{2,3},{3,2},{4,5},{5,4},{6,7},{7,6},{8,9},{9,8},{10,11... | collective-permute-start | bytes 3145736 | tf_op jit(solution)/shard_map/ppermute | solution.py:140
  136.2 11.6 %collective-permute-start.7 = (f32[2,32,1024]{2,1,0:T(8,128)S(1)}, f32[2,32,1024]{2,1,0:T(8,128)S(1)}, u32[]{:S(2)}, u32[]{:S(2)}) collective-permute-start(f32[2,32,1024]{2,1,0:T(8,128)S(1)} %dynamic-slice_bitcast_fusion.8), channel_id=1, source_target_pairs={{0,4},{1,5},{2,6},{3,7},{4,0},{5,1},{6,2},{7,3},{8,12},{9,13},{10,... | collective-permute-start | bytes 786440 | tf_op jit(solution)/shard_map/ppermute | solution.py:96
  137.6 6.4 %collective-permute-start.5 = (f32[32,1024]{1,0:T(8,128)S(1)}, f32[32,1024]{1,0:T(8,128)S(1)}, u32[]{:S(2)}, u32[]{:S(2)}) collective-permute-start(f32[32,1024]{1,0:T(8,128)S(1)} %dynamic-slice_bitcast_fusion.18), channel_id=1, source_target_pairs={{0,2},{1,3},{2,0},{3,1},{4,6},{5,7},{6,4},{7,5},{8,10},{9,11},{10,... | collective-permute-start | bytes 393224 | tf_op jit(solution)/shard_map/ppermute | solution.py:96
  139.3 9.6 %collective-permute-start.6 = (f32[2,32,1024]{2,1,0:T(8,128)S(1)}, f32[2,32,1024]{2,1,0:T(8,128)S(1)}, u32[]{:S(2)}, u32[]{:S(2)}) collective-permute-start(f32[2,32,1024]{2,1,0:T(8,128)S(1)} %dynamic-slice_bitcast_fusion.9), channel_id=1, source_target_pairs={{0,2},{1,3},{2,0},{3,1},{4,6},{5,7},{6,4},{7,5},{8,10},{9,11},{10,... | collective-permute-start | bytes 786440 | tf_op jit(solution)/shard_map/ppermute | solution.py:96
  139.8 8.0 %collective-permute-start.4 = (f32[32,1024]{1,0:T(8,128)S(1)}, f32[32,1024]{1,0:T(8,128)S(1)}, u32[]{:S(2)}, u32[]{:S(2)}) collective-permute-start(f32[32,1024]{1,0:T(8,128)S(1)} %dynamic-slice_bitcast_fusion.19), channel_id=1, source_target_pairs={{0,4},{1,5},{2,6},{3,7},{4,0},{5,1},{6,2},{7,3},{8,12},{9,13},{10,... | collective-permute-start | bytes 393224 | tf_op jit(solution)/shard_map/ppermute | solution.py:96
  164.9 19.8 %collective-permute-start.15 = (f32[2,2,2,32,1024]{4,3,2,1,0:T(8,128)S(1)}, f32[2,2,2,32,1024]{4,3,2,1,0:T(8,128)S(1)}, u32[]{:S(2)}, u32[]{:S(2)}) collective-permute-start(f32[2,2,2,32,1024]{4,3,2,1,0:T(8,128)S(1)} %dynamic-slice_bitcast_fusion), channel_id=1, source_target_pairs={{0,1},{1,0},{2,3},{3,2},{4,5},{5,4},{6,7},{7,6},{8,9},{9,8},{10,11... | collective-permute-start | bytes 3145736 | tf_op jit(solution)/shard_map/ppermute | solution.py:140
  165.0 13.0 %collective-permute-start.11 = (f32[2,32,1024]{2,1,0:T(8,128)S(1)}, f32[2,32,1024]{2,1,0:T(8,128)S(1)}, u32[]{:S(2)}, u32[]{:S(2)}) collective-permute-start(f32[2,32,1024]{2,1,0:T(8,128)S(1)} %dynamic-slice_bitcast_fusion.7), channel_id=1, source_target_pairs={{0,2},{1,3},{2,0},{3,1},{4,6},{5,7},{6,4},{7,5},{8,10},{9,11},{10,... | collective-permute-start | bytes 786440 | tf_op jit(solution)/shard_map/ppermute | solution.py:96
  166.6 13.0 %collective-permute-start.13 = (f32[2,32,1024]{2,1,0:T(8,128)S(1)}, f32[2,32,1024]{2,1,0:T(8,128)S(1)}, u32[]{:S(2)}, u32[]{:S(2)}) collective-permute-start(f32[2,32,1024]{2,1,0:T(8,128)S(1)} %dynamic-slice_bitcast_fusion.6), channel_id=1, source_target_pairs={{0,4},{1,5},{2,6},{3,7},{4,0},{5,1},{6,2},{7,3},{8,12},{9,13},{10,... | collective-permute-start | bytes 786440 | tf_op jit(solution)/shard_map/ppermute | solution.py:96
  168.1 9.8 %collective-permute-start.9 = (f32[32,1024]{1,0:T(8,128)S(1)}, f32[32,1024]{1,0:T(8,128)S(1)}, u32[]{:S(2)}, u32[]{:S(2)}) collective-permute-start(f32[32,1024]{1,0:T(8,128)S(1)} %dynamic-slice_bitcast_fusion.17), channel_id=1, source_target_pairs={{0,4},{1,5},{2,6},{3,7},{4,0},{5,1},{6,2},{7,3},{8,12},{9,13},{10,... | collective-permute-start | bytes 393224 | tf_op jit(solution)/shard_map/ppermute | solution.py:96
  168.8 9.1 %collective-permute-start.10 = (f32[32,1024]{1,0:T(8,128)S(1)}, f32[32,1024]{1,0:T(8,128)S(1)}, u32[]{:S(2)}, u32[]{:S(2)}) collective-permute-start(f32[32,1024]{1,0:T(8,128)S(1)} %dynamic-slice_bitcast_fusion.16), channel_id=1, source_target_pairs={{0,2},{1,3},{2,0},{3,1},{4,6},{5,7},{6,4},{7,5},{8,10},{9,11},{10,... | collective-permute-start | bytes 393224 | tf_op jit(solution)/shard_map/ppermute | solution.py:96
  169.4 15.3 %copy-start = (f32[2,256,1024]{2,1,0:T(8,128)S(1)}, f32[2,256,1024]{2,1,0:T(8,128)}, u32[]{:S(2)}) copy-start(f32[2,256,1024]{2,1,0:T(8,128)} %shard_map.58) | copy-start | bytes 6291460
  178.0 5.0 %collective-permute-start.12 = (f32[32,1024]{1,0:T(8,128)S(1)}, f32[32,1024]{1,0:T(8,128)S(1)}, u32[]{:S(2)}, u32[]{:S(2)}) collective-permute-start(f32[32,1024]{1,0:T(8,128)S(1)} %dynamic-slice_bitcast_fusion.15), channel_id=1, source_target_pairs={{0,4},{1,5},{2,6},{3,7},{4,0},{5,1},{6,2},{7,3},{8,12},{9,13},{10,... | collective-permute-start | bytes 393224 | tf_op jit(solution)/shard_map/ppermute | solution.py:96
  179.6 5.0 %collective-permute-start.14 = (f32[32,1024]{1,0:T(8,128)S(1)}, f32[32,1024]{1,0:T(8,128)S(1)}, u32[]{:S(2)}, u32[]{:S(2)}) collective-permute-start(f32[32,1024]{1,0:T(8,128)S(1)} %dynamic-slice_bitcast_fusion.14), channel_id=1, source_target_pairs={{0,2},{1,3},{2,0},{3,1},{4,6},{5,7},{6,4},{7,5},{8,10},{9,11},{10,... | collective-permute-start | bytes 393224 | tf_op jit(solution)/shard_map/ppermute | solution.py:96
  185.0 6.5 %collective-permute-start.16 = (f32[2,32,1024]{2,1,0:T(8,128)S(1)}, f32[2,32,1024]{2,1,0:T(8,128)S(1)}, u32[]{:S(2)}, u32[]{:S(2)}) collective-permute-start(f32[2,32,1024]{2,1,0:T(8,128)S(1)} %dynamic-slice_bitcast_fusion.5), channel_id=1, source_target_pairs={{0,2},{1,3},{2,0},{3,1},{4,6},{5,7},{6,4},{7,5},{8,10},{9,11},{10,... | collective-permute-start | bytes 786440 | tf_op jit(solution)/shard_map/ppermute | solution.py:96
  185.5 12.6 %copy-start.5 = (f32[128,2048]{1,0:T(8,128)}, f32[128,2048]{1,0:T(8,128)S(1)}, u32[]{:S(2)}) copy-start(f32[128,2048]{1,0:T(8,128)S(1)} %maximum_dynamic-update-slice_fusion.1) | copy-start | bytes 3145732
  185.6 6.8 %collective-permute-start.18 = (f32[2,32,1024]{2,1,0:T(8,128)S(1)}, f32[2,32,1024]{2,1,0:T(8,128)S(1)}, u32[]{:S(2)}, u32[]{:S(2)}) collective-permute-start(f32[2,32,1024]{2,1,0:T(8,128)S(1)} %dynamic-slice_bitcast_fusion.4), channel_id=1, source_target_pairs={{0,4},{1,5},{2,6},{3,7},{4,0},{5,1},{6,2},{7,3},{8,12},{9,13},{10,... | collective-permute-start | bytes 786440 | tf_op jit(solution)/shard_map/ppermute | solution.py:96
  191.6 5.0 %collective-permute-start.17 = (f32[32,1024]{1,0:T(8,128)S(1)}, f32[32,1024]{1,0:T(8,128)S(1)}, u32[]{:S(2)}, u32[]{:S(2)}) collective-permute-start(f32[32,1024]{1,0:T(8,128)S(1)} %dynamic-slice_bitcast_fusion.13), channel_id=1, source_target_pairs={{0,4},{1,5},{2,6},{3,7},{4,0},{5,1},{6,2},{7,3},{8,12},{9,13},{10,... | collective-permute-start | bytes 393224 | tf_op jit(solution)/shard_map/ppermute | solution.py:96
  192.4 5.7 %collective-permute-start.19 = (f32[32,1024]{1,0:T(8,128)S(1)}, f32[32,1024]{1,0:T(8,128)S(1)}, u32[]{:S(2)}, u32[]{:S(2)}) collective-permute-start(f32[32,1024]{1,0:T(8,128)S(1)} %dynamic-slice_bitcast_fusion.12), channel_id=1, source_target_pairs={{0,2},{1,3},{2,0},{3,1},{4,6},{5,7},{6,4},{7,5},{8,10},{9,11},{10,... | collective-permute-start | bytes 393224 | tf_op jit(solution)/shard_map/ppermute | solution.py:96
  (4 other events, 7.6 us)
Sparse Core Ops, SparseCore 0:
  16.3 54.8 all-gather.14
  72.7 25.6 all-gather.12
  100.0 27.4 all-gather.10
  128.9 27.3 all-gather.8

commit v24 on v21

--- a/solution.py
+++ b/solution.py
@@ -28,19 +28,26 @@
     tile = tiles_ref.shape[-1]
     groups, part, width = amp_ref.shape
     per_step = out_ref.shape[-1] // tile
-    weight_ref[...] = jnp.zeros(weight_ref.shape, weight_ref.dtype)
     first = step * per_step
 
-    def place(t, carry):
+    @pl.when(step == 0)
+    def _():
+        weight_ref[...] = jnp.zeros(weight_ref.shape, weight_ref.dtype)
+
+    def place(t, carry, clear=False):
         i = order_ref[t]
         row = pl.multiple_of(cd_ref[i] * tile, tile)
         col = pl.multiple_of((ab_ref[i] - first) * tile, tile)
-        weight_ref[pl.ds(row, tile), pl.ds(col, tile)] = tiles_ref[i]
+        block = jnp.zeros((tile, tile), weight_ref.dtype) if clear else tiles_ref[i]
+        weight_ref[pl.ds(row, tile), pl.ds(col, tile)] = block
         return carry
 
     lax.fori_loop(starts_ref[first], starts_ref[first + per_step], place, 0)
     lhs = amp_ref[...].reshape(groups * part, width)
     out_ref[...] = jnp.dot(lhs, weight_ref[...], preferred_element_type=jnp.float32)
+    lax.fori_loop(
+        starts_ref[first], starts_ref[first + per_step], lambda t, c: place(t, c, clear=True), 0
+    )
 
 
 def _ladder_products(amp3, tiles, order, starts, ab_ids, cd_ids, ab_count):

time: 198 us -> 199 us (level)
  no operation moved by 1% of the time
where the time goes in v24:
time: 199 us; the launch traced here: 198 us
  waiting for transfers between devices  108 us (54%)
  Pallas kernels  29.3 us (15%)
  starting transfers between devices  28.4 us (14%)
  between operations  13.6 us (7%)
  local copies, waits for them, and re-layouts  11.5 us (6%)
  other arithmetic  7.99 us (4%)
    all_gather x4, waiting for transfers between devices, on_device(): lax.all_gather(local4[:, c], 'own', axis=0, tiled=True)  69.4 us
    pallas_call x4, Pallas kernels, _ladder_products(): pl.pallas_call(_ladder_kernel, grid_spec=grid_spec, out_shape=jax.ShapeDt...  29.3 us
    ppermute x16, waiting for transfers between devices, advance(): self.x = keep + lax.ppermute(send, 'rep', perm=pairs)  26.5 us
    ppermute x16, starting transfers between devices, advance(): self.x = keep + lax.ppermute(send, 'rep', perm=pairs)  20.7 us
    all_to_all x1, waiting for transfers between devices, on_device(): lax.all_to_all(integrals, ('own', 'rep'), split_axis=0, concat_axis=0, ti...  8.25 us
    all_to_all x1, starting transfers between devices, on_device(): lax.all_to_all(integrals, ('own', 'rep'), split_axis=0, concat_axis=0, ti...  7.3 us
    squeeze x4, local copies, waits for them, and re-layouts, advance(): send = lax.dynamic_index_in_dim(self.joint, 1 - mine, ax, keepdims=False)  6.64 us
  transfers between devices with their start and end apart: 25, of which 15 were waited for; matrix products, arithmetic and copies ran while one was open for 9% of the time, Pallas kernels for 15%

profile of v24, /device:TPU:0, one launch (start us, length us, event | category | flops | bytes accessed | tf_op | source)
XLA Modules:
  0.0 198.4 jit_solution(16124596533811641411)
XLA Ops:
  6.5 7.3 %all-to-all-start = ((bf16[64,128,128]{2,1,0:T(8,128)(2,1)}), bf16[64,128,128]{2,1,0:T(8,128)(2,1)S(1)}, u32[]{:S(2)}, u32[]{:S(2)}) async-start(bf16[64,128,128]{2,1,0:T(8,128)(2,1)} %param.6), calls=%async_computation | async-start | bytes 4194304 | tf_op jit(solution)/shard_map/all_to_all | solution.py:167
  18.4 52.8 %all-gather.15.cloned.1.call-done = bf16[8,1,32,2048]{3,2,1,0:T(8,128)(2,1)} async-done(((bf16[2,1,32,2048]{3,2,1,0:T(8,128)(2,1)}), bf16[8,1,32,2048]{3,2,1,0:T(8,128)(2,1)}) %all-gather.15.cloned.1.call-update) | async-done | bytes 1048592 | tf_op jit(solution)/shard_map/all_gather | solution.py:181
  71.2 8.2 %all-to-all-done.tiles_ref = bf16[64,128,128]{2,1,0:T(8,128)(2,1)S(1)} async-done(((bf16[64,128,128]{2,1,0:T(8,128)(2,1)}), bf16[64,128,128]{2,1,0:T(8,128)(2,1)S(1)}, u32[]{:S(2)}, u32[]{:S(2)}) %all-to-all-start) | async-done | bytes 2097184 | tf_op jit(solution)/shard_map/all_to_all | solution.py:167
  80.8 7.3 %shard_map.55 = f32[2,256,1024]{2,1,0:T(8,128)} custom-call(s32[64]{0:T(128)} %select_reduce_fusion.order_ref, s32[17]{0:T(128)} %convert_reduce_fusion.1.starts_ref, s32[64]{0:T(128)} %copy-done.9, s32[64]{0:T(128)} %reshape.66.cd_ref, bf16[8,32,2048]{2,1,0:T(8,128)(2,1)} %bitcast.115, bf16[64,128,128]{2,1,0:T(8,128)(2,1)} %copy-done.4), custom_call_target="tpu_custom_call" | custom-call | flops 2147483648 | bytes 5242880 | tf_op jit(solution)/shard_map/pallas_call | solution.py:76
  88.1 1.4 dynamic-slice_bitcast_fusion.3
  89.7 2.7 %collective-permute-done = f32[2,2,2,32,1024]{4,3,2,1,0:T(8,128)} collective-permute-done((f32[2,2,2,32,1024]{4,3,2,1,0:T(8,128)S(1)}, f32[2,2,2,32,1024]{4,3,2,1,0:T(8,128)}, u32[]{:S(2)}, u32[]{:S(2)}) %collective-permute-start) | collective-permute-done | bytes 1048608 | tf_op jit(solution)/shard_map/ppermute | solution.py:147
  92.4 1.4 bitcast_add_fusion.3
  93.9 4.5 %all-gather.13.cloned.1.call-done = bf16[8,1,32,2048]{3,2,1,0:T(8,128)(2,1)} async-done(((bf16[2,1,32,2048]{3,2,1,0:T(8,128)(2,1)}), bf16[8,1,32,2048]{3,2,1,0:T(8,128)(2,1)}) %all-gather.13.cloned.1.call-update) | async-done | bytes 1048592 | tf_op jit(solution)/shard_map/all_gather | solution.py:181
  98.4 7.3 %shard_map.56 = f32[2,256,1024]{2,1,0:T(8,128)} custom-call(s32[64]{0:T(128)} %select_reduce_fusion.order_ref, s32[17]{0:T(128)} %convert_reduce_fusion.1.starts_ref, s32[64]{0:T(128)} %copy-done.9, s32[64]{0:T(128)} %reshape.66.cd_ref, bf16[8,32,2048]{2,1,0:T(8,128)(2,1)} %bitcast.114, bf16[64,128,128]{2,1,0:T(8,128)(2,1)} %copy-done.4), custom_call_target="tpu_custom_call" | custom-call | flops 2147483648 | bytes 5242880 | tf_op jit(solution)/shard_map/pallas_call | solution.py:76
  105.8 2.5 %dynamic-slice_bitcast_fusion.2 = f32[2,2,2,32,1024]{4,3,2,1,0:T(8,128)} fusion(f32[2,2,2,2,32,1024]{5,4,3,2,1,0:T(8,128)} %bitcast.102, s32[]{:T(128)S(6)} %select_n.75), kind=kLoop, calls=%fused_computation.7 | loop fusion | bytes 2097156 | tf_op jit(solution)/shard_map/jit(dynamic_index_in_dim)/squeeze | solution.py:145
  108.3 1.7 collective-permute-start.2
  112.0 5.2 %collective-permute-done.2 = f32[2,32,1024]{2,1,0:T(8,128)} collective-permute-done((f32[2,32,1024]{2,1,0:T(8,128)S(1)}, f32[2,32,1024]{2,1,0:T(8,128)}, u32[]{:S(2)}, u32[]{:S(2)}) %collective-permute-start.2) | collective-permute-done | bytes 262176 | tf_op jit(solution)/shard_map/ppermute | solution.py:103
  120.5 1.4 bitcast_add_fusion.2
  122.0 5.5 %all-gather.11.cloned.1.call-done = bf16[8,1,32,2048]{3,2,1,0:T(8,128)(2,1)} async-done(((bf16[2,1,32,2048]{3,2,1,0:T(8,128)(2,1)}), bf16[8,1,32,2048]{3,2,1,0:T(8,128)(2,1)}) %all-gather.11.cloned.1.call-update) | async-done | bytes 1048592 | tf_op jit(solution)/shard_map/all_gather | solution.py:181
  127.5 7.3 %shard_map.57 = f32[2,256,1024]{2,1,0:T(8,128)} custom-call(s32[64]{0:T(128)} %select_reduce_fusion.order_ref, s32[17]{0:T(128)} %convert_reduce_fusion.1.starts_ref, s32[64]{0:T(128)} %copy-done.9, s32[64]{0:T(128)} %reshape.66.cd_ref, bf16[8,32,2048]{2,1,0:T(8,128)(2,1)} %bitcast.113, bf16[64,128,128]{2,1,0:T(8,128)(2,1)} %copy-done.4), custom_call_target="tpu_custom_call" | custom-call | flops 2147483648 | bytes 5242880 | tf_op jit(solution)/shard_map/pallas_call | solution.py:76
  134.8 1.4 dynamic-slice_bitcast_fusion.1
  136.3 1.7 collective-permute-start.7
  140.6 3.8 %collective-permute-done.5 = f32[32,1024]{1,0:T(8,128)S(1)} collective-permute-done((f32[32,1024]{1,0:T(8,128)S(1)}, f32[32,1024]{1,0:T(8,128)S(1)}, u32[]{:S(2)}, u32[]{:S(2)}) %collective-permute-start.5) | collective-permute-done | bytes 131104 | tf_op jit(solution)/shard_map/ppermute | solution.py:103
  144.5 3.4 %collective-permute-done.4 = f32[32,1024]{1,0:T(8,128)S(1)} collective-permute-done((f32[32,1024]{1,0:T(8,128)S(1)}, f32[32,1024]{1,0:T(8,128)S(1)}, u32[]{:S(2)}, u32[]{:S(2)}) %collective-permute-start.4) | collective-permute-done | bytes 131104 | tf_op jit(solution)/shard_map/ppermute | solution.py:103
  147.9 1.4 collective-permute-done.6
  149.7 6.7 %all-gather.9.cloned.1.call-done = bf16[8,1,32,2048]{3,2,1,0:T(8,128)(2,1)} async-done(((bf16[2,1,32,2048]{3,2,1,0:T(8,128)(2,1)}), bf16[8,1,32,2048]{3,2,1,0:T(8,128)(2,1)}) %all-gather.9.cloned.1.call-update) | async-done | bytes 1048592 | tf_op jit(solution)/shard_map/all_gather | solution.py:181
  156.4 1.5 collective-permute-start.9
  157.9 1.5 collective-permute-start.10
  160.7 7.3 %shard_map.58 = f32[2,256,1024]{2,1,0:T(8,128)} custom-call(s32[64]{0:T(128)} %select_reduce_fusion.order_ref, s32[17]{0:T(128)} %convert_reduce_fusion.1.starts_ref, s32[64]{0:T(128)} %copy-done.9, s32[64]{0:T(128)} %reshape.66.cd_ref, bf16[8,32,2048]{2,1,0:T(8,128)(2,1)} %bitcast.112, bf16[64,128,128]{2,1,0:T(8,128)(2,1)} %copy-done.4), custom_call_target="tpu_custom_call" | custom-call | flops 2147483648 | bytes 5242880 | tf_op jit(solution)/shard_map/pallas_call | solution.py:76
  169.6 1.7 collective-permute-start.12
  172.7 2.8 %collective-permute-done.12 = f32[32,1024]{1,0:T(8,128)S(1)} collective-permute-done((f32[32,1024]{1,0:T(8,128)S(1)}, f32[32,1024]{1,0:T(8,128)S(1)}, u32[]{:S(2)}, u32[]{:S(2)}) %collective-permute-start.12) | collective-permute-done | bytes 131104 | tf_op jit(solution)/shard_map/ppermute | solution.py:103
  175.9 1.5 collective-permute-start.16
  177.4 1.6 collective-permute-start.18
  179.0 4.9 %collective-permute-done.16 = f32[2,32,1024]{2,1,0:T(8,128)S(1)} collective-permute-done((f32[2,32,1024]{2,1,0:T(8,128)S(1)}, f32[2,32,1024]{2,1,0:T(8,128)S(1)}, u32[]{:S(2)}, u32[]{:S(2)}) %collective-permute-start.16) | collective-permute-done | bytes 262176 | tf_op jit(solution)/shard_map/ppermute | solution.py:103
  184.0 1.7 collective-permute-start.17
  187.1 1.9 collective-permute-done.17
  189.0 1.8 collective-permute-done.19
  (102 shorter events, 21.5 us)
Async XLA Ops:
  6.5 7.4 %copy-start.5 = (bf16[256,2048]{1,0:T(8,128)(2,1)S(1)}, bf16[256,2048]{1,0:T(8,128)(2,1)}, u32[]{:S(2)}) copy-start(bf16[256,2048]{1,0:T(8,128)(2,1)} %param.5) | copy-start | bytes 3145732
  6.5 72.9 %all-to-all-start = ((bf16[64,128,128]{2,1,0:T(8,128)(2,1)}), bf16[64,128,128]{2,1,0:T(8,128)(2,1)S(1)}, u32[]{:S(2)}, u32[]{:S(2)}) async-start(bf16[64,128,128]{2,1,0:T(8,128)(2,1)} %param.6), calls=%async_computation | async-start | bytes 4194304 | tf_op jit(solution)/shard_map/all_to_all | solution.py:167
  13.9 2.3 %copy-start.7 = (s32[1,32,2]{1,2,0:T(2,128)S(1)}, s32[1,32,2]{1,2,0:T(2,128)}, u32[]{:S(2)}) copy-start(s32[1,32,2]{1,2,0:T(2,128)} %param.8) | copy-start | bytes 772
  13.9 57.3 %all-gather.15.cloned.1.call-start = ((), (), s32[]{:S(2)}) async-start(), calls=%async_computation.4 | async-start | bytes 1310720 | tf_op jit(solution)/shard_map/all_gather | solution.py:181
  14.9 83.5 %all-gather.13.cloned.1.call-start = ((), (), s32[]{:S(2)}) async-start(), calls=%async_computation.3 | async-start | bytes 1310720 | tf_op jit(solution)/shard_map/all_gather | solution.py:181
  15.7 111.8 %all-gather.11.cloned.1.call-start = ((), (), s32[]{:S(2)}) async-start(), calls=%async_computation.2 | async-start | bytes 1310720 | tf_op jit(solution)/shard_map/all_gather | solution.py:181
  15.9 63.5 %copy-start.9 = (s32[64]{0:T(128)}, s32[64]{0:T(128)S(1)}, u32[]{:S(2)}) copy-start(s32[64]{0:T(128)S(1)} %reshape.65.ab_ref) | copy-start | bytes 772
  88.1 4.3 %copy-start.3 = (f32[2,256,1024]{2,1,0:T(8,128)S(1)}, f32[2,256,1024]{2,1,0:T(8,128)}, u32[]{:S(2)}) copy-start(f32[2,256,1024]{2,1,0:T(8,128)} %shard_map.55) | copy-start | bytes 6291460
  89.5 2.9 %collective-permute-start = (f32[2,2,2,32,1024]{4,3,2,1,0:T(8,128)S(1)}, f32[2,2,2,32,1024]{4,3,2,1,0:T(8,128)}, u32[]{:S(2)}, u32[]{:S(2)}) collective-permute-start(f32[2,2,2,32,1024]{4,3,2,1,0:T(8,128)S(1)} %dynamic-slice_bitcast_fusion.3), channel_id=1, source_target_pairs={{0,1},{1,0},{2,3},{3,2},{4,5},{5,4},{6,7},{7,6},{8,9},{9,8},{10,11... | collective-permute-start | bytes 3145736 | tf_op jit(solution)/shard_map/ppermute | solution.py:147
  89.7 66.7 %all-gather.9.cloned.1.call-start = ((), (), s32[]{:S(2)}) async-start(), calls=%async_computation.1 | async-start | bytes 1310720 | tf_op jit(solution)/shard_map/all_gather | solution.py:181
  105.8 14.7 %copy-start = (f32[2,256,1024]{2,1,0:T(8,128)S(1)}, f32[2,256,1024]{2,1,0:T(8,128)}, u32[]{:S(2)}) copy-start(f32[2,256,1024]{2,1,0:T(8,128)} %shard_map.56) | copy-start | bytes 6291460
  108.3 12.2 %collective-permute-start.3 = (f32[2,2,2,32,1024]{4,3,2,1,0:T(8,128)}, f32[2,2,2,32,1024]{4,3,2,1,0:T(8,128)}, u32[]{:S(2)}, u32[]{:S(2)}) collective-permute-start(f32[2,2,2,32,1024]{4,3,2,1,0:T(8,128)} %dynamic-slice_bitcast_fusion.2), channel_id=1, source_target_pairs={{0,1},{1,0},{2,3},{3,2},{4,5},{5,4},{6,7},{7,6},{8,9},{9,8},{10,11... | collective-permute-start | bytes 3145736 | tf_op jit(solution)/shard_map/ppermute | solution.py:147
  108.3 8.9 %collective-permute-start.2 = (f32[2,32,1024]{2,1,0:T(8,128)S(1)}, f32[2,32,1024]{2,1,0:T(8,128)}, u32[]{:S(2)}, u32[]{:S(2)}) collective-permute-start(f32[2,32,1024]{2,1,0:T(8,128)S(1)} %dynamic-slice_bitcast_fusion.10), channel_id=1, source_target_pairs={{0,4},{1,5},{2,6},{3,7},{4,0},{5,1},{6,2},{7,3},{8,12},{9,13},{10,... | collective-permute-start | bytes 786440 | tf_op jit(solution)/shard_map/ppermute | solution.py:103
  110.7 8.8 %collective-permute-start.1 = (f32[2,32,1024]{2,1,0:T(8,128)}, f32[2,32,1024]{2,1,0:T(8,128)}, u32[]{:S(2)}, u32[]{:S(2)}) collective-permute-start(f32[2,32,1024]{2,1,0:T(8,128)} %dynamic-slice_bitcast_fusion.11), channel_id=1, source_target_pairs={{0,2},{1,3},{2,0},{3,1},{4,6},{5,7},{6,4},{7,5},{8,10},{9,11},{10,... | collective-permute-start | bytes 786440 | tf_op jit(solution)/shard_map/ppermute | solution.py:103
  136.2 13.2 %copy-start.2 = (f32[2,256,1024]{2,1,0:T(8,128)S(1)}, f32[2,256,1024]{2,1,0:T(8,128)}, u32[]{:S(2)}) copy-start(f32[2,256,1024]{2,1,0:T(8,128)} %shard_map.57) | copy-start | bytes 6291460
  136.2 13.2 %collective-permute-start.8 = (f32[2,2,2,32,1024]{4,3,2,1,0:T(8,128)S(1)}, f32[2,2,2,32,1024]{4,3,2,1,0:T(8,128)S(1)}, u32[]{:S(2)}, u32[]{:S(2)}) collective-permute-start(f32[2,2,2,32,1024]{4,3,2,1,0:T(8,128)S(1)} %dynamic-slice_bitcast_fusion.1), channel_id=1, source_target_pairs={{0,1},{1,0},{2,3},{3,2},{4,5},{5,4},{6,7},{7,6},{8,9},{9,8},{10,11... | collective-permute-start | bytes 3145736 | tf_op jit(solution)/shard_map/ppermute | solution.py:147
  136.3 11.6 %collective-permute-start.7 = (f32[2,32,1024]{2,1,0:T(8,128)S(1)}, f32[2,32,1024]{2,1,0:T(8,128)S(1)}, u32[]{:S(2)}, u32[]{:S(2)}) collective-permute-start(f32[2,32,1024]{2,1,0:T(8,128)S(1)} %dynamic-slice_bitcast_fusion.8), channel_id=1, source_target_pairs={{0,4},{1,5},{2,6},{3,7},{4,0},{5,1},{6,2},{7,3},{8,12},{9,13},{10,... | collective-permute-start | bytes 786440 | tf_op jit(solution)/shard_map/ppermute | solution.py:103
  138.0 6.4 %collective-permute-start.5 = (f32[32,1024]{1,0:T(8,128)S(1)}, f32[32,1024]{1,0:T(8,128)S(1)}, u32[]{:S(2)}, u32[]{:S(2)}) collective-permute-start(f32[32,1024]{1,0:T(8,128)S(1)} %dynamic-slice_bitcast_fusion.18), channel_id=1, source_target_pairs={{0,2},{1,3},{2,0},{3,1},{4,6},{5,7},{6,4},{7,5},{8,10},{9,11},{10,... | collective-permute-start | bytes 393224 | tf_op jit(solution)/shard_map/ppermute | solution.py:103
  139.4 10.0 %collective-permute-start.6 = (f32[2,32,1024]{2,1,0:T(8,128)S(1)}, f32[2,32,1024]{2,1,0:T(8,128)S(1)}, u32[]{:S(2)}, u32[]{:S(2)}) collective-permute-start(f32[2,32,1024]{2,1,0:T(8,128)S(1)} %dynamic-slice_bitcast_fusion.9), channel_id=1, source_target_pairs={{0,2},{1,3},{2,0},{3,1},{4,6},{5,7},{6,4},{7,5},{8,10},{9,11},{10,... | collective-permute-start | bytes 786440 | tf_op jit(solution)/shard_map/ppermute | solution.py:103
  140.2 7.6 %collective-permute-start.4 = (f32[32,1024]{1,0:T(8,128)S(1)}, f32[32,1024]{1,0:T(8,128)S(1)}, u32[]{:S(2)}, u32[]{:S(2)}) collective-permute-start(f32[32,1024]{1,0:T(8,128)S(1)} %dynamic-slice_bitcast_fusion.19), channel_id=1, source_target_pairs={{0,4},{1,5},{2,6},{3,7},{4,0},{5,1},{6,2},{7,3},{8,12},{9,13},{10,... | collective-permute-start | bytes 393224 | tf_op jit(solution)/shard_map/ppermute | solution.py:103
  156.4 13.1 %collective-permute-start.9 = (f32[32,1024]{1,0:T(8,128)S(1)}, f32[32,1024]{1,0:T(8,128)S(1)}, u32[]{:S(2)}, u32[]{:S(2)}) collective-permute-start(f32[32,1024]{1,0:T(8,128)S(1)} %dynamic-slice_bitcast_fusion.17), channel_id=1, source_target_pairs={{0,4},{1,5},{2,6},{3,7},{4,0},{5,1},{6,2},{7,3},{8,12},{9,13},{10,... | collective-permute-start | bytes 393224 | tf_op jit(solution)/shard_map/ppermute | solution.py:103
  157.9 11.6 %collective-permute-start.10 = (f32[32,1024]{1,0:T(8,128)S(1)}, f32[32,1024]{1,0:T(8,128)S(1)}, u32[]{:S(2)}, u32[]{:S(2)}) collective-permute-start(f32[32,1024]{1,0:T(8,128)S(1)} %dynamic-slice_bitcast_fusion.16), channel_id=1, source_target_pairs={{0,2},{1,3},{2,0},{3,1},{4,6},{5,7},{6,4},{7,5},{8,10},{9,11},{10,... | collective-permute-start | bytes 393224 | tf_op jit(solution)/shard_map/ppermute | solution.py:103
  159.5 10.1 %collective-permute-start.11 = (f32[2,32,1024]{2,1,0:T(8,128)S(1)}, f32[2,32,1024]{2,1,0:T(8,128)S(1)}, u32[]{:S(2)}, u32[]{:S(2)}) collective-permute-start(f32[2,32,1024]{2,1,0:T(8,128)S(1)} %dynamic-slice_bitcast_fusion.7), channel_id=1, source_target_pairs={{0,2},{1,3},{2,0},{3,1},{4,6},{5,7},{6,4},{7,5},{8,10},{9,11},{10,... | collective-permute-start | bytes 786440 | tf_op jit(solution)/shard_map/ppermute | solution.py:103
  160.1 11.3 %collective-permute-start.13 = (f32[2,32,1024]{2,1,0:T(8,128)S(1)}, f32[2,32,1024]{2,1,0:T(8,128)S(1)}, u32[]{:S(2)}, u32[]{:S(2)}) collective-permute-start(f32[2,32,1024]{2,1,0:T(8,128)S(1)} %dynamic-slice_bitcast_fusion.6), channel_id=1, source_target_pairs={{0,4},{1,5},{2,6},{3,7},{4,0},{5,1},{6,2},{7,3},{8,12},{9,13},{10,... | collective-permute-start | bytes 786440 | tf_op jit(solution)/shard_map/ppermute | solution.py:103
  169.4 6.2 %copy-start.1 = (f32[2,256,1024]{2,1,0:T(8,128)S(1)}, f32[2,256,1024]{2,1,0:T(8,128)}, u32[]{:S(2)}) copy-start(f32[2,256,1024]{2,1,0:T(8,128)} %shard_map.58) | copy-start | bytes 6291460
  169.4 6.2 %collective-permute-start.15 = (f32[2,2,2,32,1024]{4,3,2,1,0:T(8,128)S(1)}, f32[2,2,2,32,1024]{4,3,2,1,0:T(8,128)S(1)}, u32[]{:S(2)}, u32[]{:S(2)}) collective-permute-start(f32[2,2,2,32,1024]{4,3,2,1,0:T(8,128)S(1)} %dynamic-slice_bitcast_fusion), channel_id=1, source_target_pairs={{0,1},{1,0},{2,3},{3,2},{4,5},{5,4},{6,7},{7,6},{8,9},{9,8},{10,11... | collective-permute-start | bytes 3145736 | tf_op jit(solution)/shard_map/ppermute | solution.py:147
  169.6 5.9 %collective-permute-start.12 = (f32[32,1024]{1,0:T(8,128)S(1)}, f32[32,1024]{1,0:T(8,128)S(1)}, u32[]{:S(2)}, u32[]{:S(2)}) collective-permute-start(f32[32,1024]{1,0:T(8,128)S(1)} %dynamic-slice_bitcast_fusion.15), channel_id=1, source_target_pairs={{0,4},{1,5},{2,6},{3,7},{4,0},{5,1},{6,2},{7,3},{8,12},{9,13},{10,... | collective-permute-start | bytes 393224 | tf_op jit(solution)/shard_map/ppermute | solution.py:103
  171.4 6.0 %collective-permute-start.14 = (f32[32,1024]{1,0:T(8,128)S(1)}, f32[32,1024]{1,0:T(8,128)S(1)}, u32[]{:S(2)}, u32[]{:S(2)}) collective-permute-start(f32[32,1024]{1,0:T(8,128)S(1)} %dynamic-slice_bitcast_fusion.14), channel_id=1, source_target_pairs={{0,2},{1,3},{2,0},{3,1},{4,6},{5,7},{6,4},{7,5},{8,10},{9,11},{10,... | collective-permute-start | bytes 393224 | tf_op jit(solution)/shard_map/ppermute | solution.py:103
  175.9 8.0 %collective-permute-start.16 = (f32[2,32,1024]{2,1,0:T(8,128)S(1)}, f32[2,32,1024]{2,1,0:T(8,128)S(1)}, u32[]{:S(2)}, u32[]{:S(2)}) collective-permute-start(f32[2,32,1024]{2,1,0:T(8,128)S(1)} %dynamic-slice_bitcast_fusion.5), channel_id=1, source_target_pairs={{0,2},{1,3},{2,0},{3,1},{4,6},{5,7},{6,4},{7,5},{8,10},{9,11},{10,... | collective-permute-start | bytes 786440 | tf_op jit(solution)/shard_map/ppermute | solution.py:103
  177.4 8.2 %collective-permute-start.18 = (f32[2,32,1024]{2,1,0:T(8,128)S(1)}, f32[2,32,1024]{2,1,0:T(8,128)S(1)}, u32[]{:S(2)}, u32[]{:S(2)}) collective-permute-start(f32[2,32,1024]{2,1,0:T(8,128)S(1)} %dynamic-slice_bitcast_fusion.4), channel_id=1, source_target_pairs={{0,4},{1,5},{2,6},{3,7},{4,0},{5,1},{6,2},{7,3},{8,12},{9,13},{10,... | collective-permute-start | bytes 786440 | tf_op jit(solution)/shard_map/ppermute | solution.py:103
  184.0 5.0 %collective-permute-start.17 = (f32[32,1024]{1,0:T(8,128)S(1)}, f32[32,1024]{1,0:T(8,128)S(1)}, u32[]{:S(2)}, u32[]{:S(2)}) collective-permute-start(f32[32,1024]{1,0:T(8,128)S(1)} %dynamic-slice_bitcast_fusion.13), channel_id=1, source_target_pairs={{0,4},{1,5},{2,6},{3,7},{4,0},{5,1},{6,2},{7,3},{8,12},{9,13},{10,... | collective-permute-start | bytes 393224 | tf_op jit(solution)/shard_map/ppermute | solution.py:103
  185.8 5.0 %collective-permute-start.19 = (f32[32,1024]{1,0:T(8,128)S(1)}, f32[32,1024]{1,0:T(8,128)S(1)}, u32[]{:S(2)}, u32[]{:S(2)}) collective-permute-start(f32[32,1024]{1,0:T(8,128)S(1)} %dynamic-slice_bitcast_fusion.12), channel_id=1, source_target_pairs={{0,2},{1,3},{2,0},{3,1},{4,6},{5,7},{6,4},{7,5},{8,10},{9,11},{10,... | collective-permute-start | bytes 393224 | tf_op jit(solution)/shard_map/ppermute | solution.py:103
  (3 other events, 5.4 us)
Sparse Core Ops, SparseCore 0:
  16.3 54.8 all-gather.14
  72.7 25.6 all-gather.12
  100.0 27.4 all-gather.10
  128.9 27.4 all-gather.8

commit v25 on v24

--- a/solution.py
+++ b/solution.py
@@ -54,7 +54,7 @@
     groups, part, width = amp3.shape
     rows = groups * part
     n, tile, _ = tiles.shape
-    per_step = ab_count // 2 if ab_count % 2 == 0 else 1
+    per_step = 4 if ab_count % 8 == 0 else 1
     steps_per_half = ab_count // (2 * per_step)
     cost = pl.CostEstimate(
         flops=2 * rows * width * ab_count * tile,

time: 199 us -> 199 us (level)
  waiting for transfers between devices: 108 us -> 106 us
where the time goes in v25:
time: 199 us; the launch traced here: 198 us
  waiting for transfers between devices  106 us (53%)
  Pallas kernels  30.6 us (15%)
  starting transfers between devices  28.6 us (14%)
  between operations  13.6 us (7%)
  local copies, waits for them, and re-layouts  11.5 us (6%)
  other arithmetic  7.97 us (4%)
    all_gather x4, waiting for transfers between devices, on_device(): lax.all_gather(local4[:, c], 'own', axis=0, tiled=True)  69.1 us
    pallas_call x4, Pallas kernels, _ladder_products(): pl.pallas_call(_ladder_kernel, grid_spec=grid_spec, out_shape=jax.ShapeDt...  30.6 us
    ppermute x16, waiting for transfers between devices, advance(): self.x = keep + lax.ppermute(send, 'rep', perm=pairs)  25.4 us
    ppermute x16, starting transfers between devices, advance(): self.x = keep + lax.ppermute(send, 'rep', perm=pairs)  20.9 us
    all_to_all x1, waiting for transfers between devices, on_device(): lax.all_to_all(integrals, ('own', 'rep'), split_axis=0, concat_axis=0, ti...  8.25 us
    all_to_all x1, starting transfers between devices, on_device(): lax.all_to_all(integrals, ('own', 'rep'), split_axis=0, concat_axis=0, ti...  7.3 us
    squeeze x4, local copies, waits for them, and re-layouts, advance(): send = lax.dynamic_index_in_dim(self.joint, 1 - mine, ax, keepdims=False)  6.64 us
  transfers between devices with their start and end apart: 25, of which 15 were waited for; matrix products, arithmetic and copies ran while one was open for 9% of the time, Pallas kernels for 15%

profile of v25, /device:TPU:0, one launch (start us, length us, event | category | flops | bytes accessed | tf_op | source)
XLA Modules:
  0.0 198.4 jit_solution(4076028885926311077)
XLA Ops:
  6.5 7.3 %all-to-all-start = ((bf16[64,128,128]{2,1,0:T(8,128)(2,1)}), bf16[64,128,128]{2,1,0:T(8,128)(2,1)S(1)}, u32[]{:S(2)}, u32[]{:S(2)}) async-start(bf16[64,128,128]{2,1,0:T(8,128)(2,1)} %param.6), calls=%async_computation | async-start | bytes 4194304 | tf_op jit(solution)/shard_map/all_to_all | solution.py:167
  18.4 52.8 %all-gather.15.cloned.1.call-done = bf16[8,1,32,2048]{3,2,1,0:T(8,128)(2,1)} async-done(((bf16[2,1,32,2048]{3,2,1,0:T(8,128)(2,1)}), bf16[8,1,32,2048]{3,2,1,0:T(8,128)(2,1)}) %all-gather.15.cloned.1.call-update) | async-done | bytes 1048592 | tf_op jit(solution)/shard_map/all_gather | solution.py:181
  71.2 8.2 %all-to-all-done.tiles_ref = bf16[64,128,128]{2,1,0:T(8,128)(2,1)S(1)} async-done(((bf16[64,128,128]{2,1,0:T(8,128)(2,1)}), bf16[64,128,128]{2,1,0:T(8,128)(2,1)S(1)}, u32[]{:S(2)}, u32[]{:S(2)}) %all-to-all-start) | async-done | bytes 2097184 | tf_op jit(solution)/shard_map/all_to_all | solution.py:167
  80.8 7.7 %shard_map.55 = f32[2,256,1024]{2,1,0:T(8,128)} custom-call(s32[64]{0:T(128)} %select_reduce_fusion.order_ref, s32[17]{0:T(128)} %convert_reduce_fusion.1.starts_ref, s32[64]{0:T(128)} %copy-done.9, s32[64]{0:T(128)} %reshape.66.cd_ref, bf16[8,32,2048]{2,1,0:T(8,128)(2,1)} %bitcast.115, bf16[64,128,128]{2,1,0:T(8,128)(2,1)} %copy-done.4), custom_call_target="tpu_custom_call" | custom-call | flops 2147483648 | bytes 5242880 | tf_op jit(solution)/shard_map/pallas_call | solution.py:76
  88.4 1.4 dynamic-slice_bitcast_fusion.3
  90.0 2.7 %collective-permute-done = f32[2,2,2,32,1024]{4,3,2,1,0:T(8,128)} collective-permute-done((f32[2,2,2,32,1024]{4,3,2,1,0:T(8,128)S(1)}, f32[2,2,2,32,1024]{4,3,2,1,0:T(8,128)}, u32[]{:S(2)}, u32[]{:S(2)}) %collective-permute-start) | collective-permute-done | bytes 1048608 | tf_op jit(solution)/shard_map/ppermute | solution.py:147
  94.2 4.2 %all-gather.13.cloned.1.call-done = bf16[8,1,32,2048]{3,2,1,0:T(8,128)(2,1)} async-done(((bf16[2,1,32,2048]{3,2,1,0:T(8,128)(2,1)}), bf16[8,1,32,2048]{3,2,1,0:T(8,128)(2,1)}) %all-gather.13.cloned.1.call-update) | async-done | bytes 1048592 | tf_op jit(solution)/shard_map/all_gather | solution.py:181
  98.4 7.6 %shard_map.56 = f32[2,256,1024]{2,1,0:T(8,128)} custom-call(s32[64]{0:T(128)} %select_reduce_fusion.order_ref, s32[17]{0:T(128)} %convert_reduce_fusion.1.starts_ref, s32[64]{0:T(128)} %copy-done.9, s32[64]{0:T(128)} %reshape.66.cd_ref, bf16[8,32,2048]{2,1,0:T(8,128)(2,1)} %bitcast.114, bf16[64,128,128]{2,1,0:T(8,128)(2,1)} %copy-done.4), custom_call_target="tpu_custom_call" | custom-call | flops 2147483648 | bytes 5242880 | tf_op jit(solution)/shard_map/pallas_call | solution.py:76
  106.1 2.5 %dynamic-slice_bitcast_fusion.2 = f32[2,2,2,32,1024]{4,3,2,1,0:T(8,128)} fusion(f32[2,2,2,2,32,1024]{5,4,3,2,1,0:T(8,128)} %bitcast.102, s32[]{:T(128)S(6)} %select_n.75), kind=kLoop, calls=%fused_computation.7 | loop fusion | bytes 2097156 | tf_op jit(solution)/shard_map/jit(dynamic_index_in_dim)/squeeze | solution.py:145
  108.6 1.4 collective-permute-start.2
  110.7 1.6 collective-permute-start.1
  112.4 5.1 %collective-permute-done.2 = f32[2,32,1024]{2,1,0:T(8,128)} collective-permute-done((f32[2,32,1024]{2,1,0:T(8,128)S(1)}, f32[2,32,1024]{2,1,0:T(8,128)}, u32[]{:S(2)}, u32[]{:S(2)}) %collective-permute-start.2) | collective-permute-done | bytes 262176 | tf_op jit(solution)/shard_map/ppermute | solution.py:103
  122.0 5.5 %all-gather.11.cloned.1.call-done = bf16[8,1,32,2048]{3,2,1,0:T(8,128)(2,1)} async-done(((bf16[2,1,32,2048]{3,2,1,0:T(8,128)(2,1)}), bf16[8,1,32,2048]{3,2,1,0:T(8,128)(2,1)}) %all-gather.11.cloned.1.call-update) | async-done | bytes 1048592 | tf_op jit(solution)/shard_map/all_gather | solution.py:181
  127.4 7.6 %shard_map.57 = f32[2,256,1024]{2,1,0:T(8,128)} custom-call(s32[64]{0:T(128)} %select_reduce_fusion.order_ref, s32[17]{0:T(128)} %convert_reduce_fusion.1.starts_ref, s32[64]{0:T(128)} %copy-done.9, s32[64]{0:T(128)} %reshape.66.cd_ref, bf16[8,32,2048]{2,1,0:T(8,128)(2,1)} %bitcast.113, bf16[64,128,128]{2,1,0:T(8,128)(2,1)} %copy-done.4), custom_call_target="tpu_custom_call" | custom-call | flops 2147483648 | bytes 5242880 | tf_op jit(solution)/shard_map/pallas_call | solution.py:76
  136.6 1.5 collective-permute-start.7
  138.1 1.7 collective-permute-start.5
  140.9 3.5 %collective-permute-done.5 = f32[32,1024]{1,0:T(8,128)S(1)} collective-permute-done((f32[32,1024]{1,0:T(8,128)S(1)}, f32[32,1024]{1,0:T(8,128)S(1)}, u32[]{:S(2)}, u32[]{:S(2)}) %collective-permute-start.5) | collective-permute-done | bytes 131104 | tf_op jit(solution)/shard_map/ppermute | solution.py:103
  144.5 3.6 %collective-permute-done.4 = f32[32,1024]{1,0:T(8,128)S(1)} collective-permute-done((f32[32,1024]{1,0:T(8,128)S(1)}, f32[32,1024]{1,0:T(8,128)S(1)}, u32[]{:S(2)}, u32[]{:S(2)}) %collective-permute-start.4) | collective-permute-done | bytes 131104 | tf_op jit(solution)/shard_map/ppermute | solution.py:103
  149.7 6.6 %all-gather.9.cloned.1.call-done = bf16[8,1,32,2048]{3,2,1,0:T(8,128)(2,1)} async-done(((bf16[2,1,32,2048]{3,2,1,0:T(8,128)(2,1)}), bf16[8,1,32,2048]{3,2,1,0:T(8,128)(2,1)}) %all-gather.9.cloned.1.call-update) | async-done | bytes 1048592 | tf_op jit(solution)/shard_map/all_gather | solution.py:181
  156.4 1.5 collective-permute-start.9
  157.9 1.5 collective-permute-start.10
  160.8 7.6 %shard_map.58 = f32[2,256,1024]{2,1,0:T(8,128)} custom-call(s32[64]{0:T(128)} %select_reduce_fusion.order_ref, s32[17]{0:T(128)} %convert_reduce_fusion.1.starts_ref, s32[64]{0:T(128)} %copy-done.9, s32[64]{0:T(128)} %reshape.66.cd_ref, bf16[8,32,2048]{2,1,0:T(8,128)(2,1)} %bitcast.112, bf16[64,128,128]{2,1,0:T(8,128)(2,1)} %copy-done.4), custom_call_target="tpu_custom_call" | custom-call | flops 2147483648 | bytes 5242880 | tf_op jit(solution)/shard_map/pallas_call | solution.py:76
  170.0 1.4 collective-permute-start.12
  171.4 1.7 collective-permute-start.14
  173.1 2.8 %collective-permute-done.12 = f32[32,1024]{1,0:T(8,128)S(1)} collective-permute-done((f32[32,1024]{1,0:T(8,128)S(1)}, f32[32,1024]{1,0:T(8,128)S(1)}, u32[]{:S(2)}, u32[]{:S(2)}) %collective-permute-start.12) | collective-permute-done | bytes 131104 | tf_op jit(solution)/shard_map/ppermute | solution.py:103
  176.3 1.4 collective-permute-start.16
  177.8 1.7 collective-permute-start.18
  179.4 4.8 %collective-permute-done.16 = f32[2,32,1024]{2,1,0:T(8,128)S(1)} collective-permute-done((f32[2,32,1024]{2,1,0:T(8,128)S(1)}, f32[2,32,1024]{2,1,0:T(8,128)S(1)}, u32[]{:S(2)}, u32[]{:S(2)}) %collective-permute-start.16) | collective-permute-done | bytes 262176 | tf_op jit(solution)/shard_map/ppermute | solution.py:103
  184.3 1.4 collective-permute-start.17
  185.8 1.7 collective-permute-start.19
  187.5 1.9 collective-permute-done.17
  189.4 1.4 collective-permute-done.19
  (102 shorter events, 21.2 us)
Async XLA Ops:
  6.5 7.4 %copy-start.5 = (bf16[256,2048]{1,0:T(8,128)(2,1)S(1)}, bf16[256,2048]{1,0:T(8,128)(2,1)}, u32[]{:S(2)}) copy-start(bf16[256,2048]{1,0:T(8,128)(2,1)} %param.5) | copy-start | bytes 3145732
  6.5 72.9 %all-to-all-start = ((bf16[64,128,128]{2,1,0:T(8,128)(2,1)}), bf16[64,128,128]{2,1,0:T(8,128)(2,1)S(1)}, u32[]{:S(2)}, u32[]{:S(2)}) async-start(bf16[64,128,128]{2,1,0:T(8,128)(2,1)} %param.6), calls=%async_computation | async-start | bytes 4194304 | tf_op jit(solution)/shard_map/all_to_all | solution.py:167
  13.9 2.3 %copy-start.7 = (s32[1,32,2]{1,2,0:T(2,128)S(1)}, s32[1,32,2]{1,2,0:T(2,128)}, u32[]{:S(2)}) copy-start(s32[1,32,2]{1,2,0:T(2,128)} %param.8) | copy-start | bytes 772
  13.9 57.3 %all-gather.15.cloned.1.call-start = ((), (), s32[]{:S(2)}) async-start(), calls=%async_computation.4 | async-start | bytes 1310720 | tf_op jit(solution)/shard_map/all_gather | solution.py:181
  14.9 83.5 %all-gather.13.cloned.1.call-start = ((), (), s32[]{:S(2)}) async-start(), calls=%async_computation.3 | async-start | bytes 1310720 | tf_op jit(solution)/shard_map/all_gather | solution.py:181
  15.7 111.7 %all-gather.11.cloned.1.call-start = ((), (), s32[]{:S(2)}) async-start(), calls=%async_computation.2 | async-start | bytes 1310720 | tf_op jit(solution)/shard_map/all_gather | solution.py:181
  15.9 63.5 %copy-start.9 = (s32[64]{0:T(128)}, s32[64]{0:T(128)S(1)}, u32[]{:S(2)}) copy-start(s32[64]{0:T(128)S(1)} %reshape.65.ab_ref) | copy-start | bytes 772
  88.4 4.3 %copy-start.3 = (f32[2,256,1024]{2,1,0:T(8,128)S(1)}, f32[2,256,1024]{2,1,0:T(8,128)}, u32[]{:S(2)}) copy-start(f32[2,256,1024]{2,1,0:T(8,128)} %shard_map.55) | copy-start | bytes 6291460
  89.9 2.9 %collective-permute-start = (f32[2,2,2,32,1024]{4,3,2,1,0:T(8,128)S(1)}, f32[2,2,2,32,1024]{4,3,2,1,0:T(8,128)}, u32[]{:S(2)}, u32[]{:S(2)}) collective-permute-start(f32[2,2,2,32,1024]{4,3,2,1,0:T(8,128)S(1)} %dynamic-slice_bitcast_fusion.3), channel_id=1, source_target_pairs={{0,1},{1,0},{2,3},{3,2},{4,5},{5,4},{6,7},{7,6},{8,9},{9,8},{10,11... | collective-permute-start | bytes 3145736 | tf_op jit(solution)/shard_map/ppermute | solution.py:147
  90.0 66.4 %all-gather.9.cloned.1.call-start = ((), (), s32[]{:S(2)}) async-start(), calls=%async_computation.1 | async-start | bytes 1310720 | tf_op jit(solution)/shard_map/all_gather | solution.py:181
  106.1 14.4 %copy-start = (f32[2,256,1024]{2,1,0:T(8,128)S(1)}, f32[2,256,1024]{2,1,0:T(8,128)}, u32[]{:S(2)}) copy-start(f32[2,256,1024]{2,1,0:T(8,128)} %shard_map.56) | copy-start | bytes 6291460
  108.6 11.9 %collective-permute-start.3 = (f32[2,2,2,32,1024]{4,3,2,1,0:T(8,128)}, f32[2,2,2,32,1024]{4,3,2,1,0:T(8,128)}, u32[]{:S(2)}, u32[]{:S(2)}) collective-permute-start(f32[2,2,2,32,1024]{4,3,2,1,0:T(8,128)} %dynamic-slice_bitcast_fusion.2), channel_id=1, source_target_pairs={{0,1},{1,0},{2,3},{3,2},{4,5},{5,4},{6,7},{7,6},{8,9},{9,8},{10,11... | collective-permute-start | bytes 3145736 | tf_op jit(solution)/shard_map/ppermute | solution.py:147
  108.6 8.9 %collective-permute-start.2 = (f32[2,32,1024]{2,1,0:T(8,128)S(1)}, f32[2,32,1024]{2,1,0:T(8,128)}, u32[]{:S(2)}, u32[]{:S(2)}) collective-permute-start(f32[2,32,1024]{2,1,0:T(8,128)S(1)} %dynamic-slice_bitcast_fusion.10), channel_id=1, source_target_pairs={{0,4},{1,5},{2,6},{3,7},{4,0},{5,1},{6,2},{7,3},{8,12},{9,13},{10,... | collective-permute-start | bytes 786440 | tf_op jit(solution)/shard_map/ppermute | solution.py:103
  110.7 8.8 %collective-permute-start.1 = (f32[2,32,1024]{2,1,0:T(8,128)}, f32[2,32,1024]{2,1,0:T(8,128)}, u32[]{:S(2)}, u32[]{:S(2)}) collective-permute-start(f32[2,32,1024]{2,1,0:T(8,128)} %dynamic-slice_bitcast_fusion.11), channel_id=1, source_target_pairs={{0,2},{1,3},{2,0},{3,1},{4,6},{5,7},{6,4},{7,5},{8,10},{9,11},{10,... | collective-permute-start | bytes 786440 | tf_op jit(solution)/shard_map/ppermute | solution.py:103
  136.5 13.0 %copy-start.2 = (f32[2,256,1024]{2,1,0:T(8,128)S(1)}, f32[2,256,1024]{2,1,0:T(8,128)}, u32[]{:S(2)}) copy-start(f32[2,256,1024]{2,1,0:T(8,128)} %shard_map.57) | copy-start | bytes 6291460
  136.5 12.9 %collective-permute-start.8 = (f32[2,2,2,32,1024]{4,3,2,1,0:T(8,128)S(1)}, f32[2,2,2,32,1024]{4,3,2,1,0:T(8,128)S(1)}, u32[]{:S(2)}, u32[]{:S(2)}) collective-permute-start(f32[2,2,2,32,1024]{4,3,2,1,0:T(8,128)S(1)} %dynamic-slice_bitcast_fusion.1), channel_id=1, source_target_pairs={{0,1},{1,0},{2,3},{3,2},{4,5},{5,4},{6,7},{7,6},{8,9},{9,8},{10,11... | collective-permute-start | bytes 3145736 | tf_op jit(solution)/shard_map/ppermute | solution.py:147
  136.6 11.6 %collective-permute-start.7 = (f32[2,32,1024]{2,1,0:T(8,128)S(1)}, f32[2,32,1024]{2,1,0:T(8,128)S(1)}, u32[]{:S(2)}, u32[]{:S(2)}) collective-permute-start(f32[2,32,1024]{2,1,0:T(8,128)S(1)} %dynamic-slice_bitcast_fusion.8), channel_id=1, source_target_pairs={{0,4},{1,5},{2,6},{3,7},{4,0},{5,1},{6,2},{7,3},{8,12},{9,13},{10,... | collective-permute-start | bytes 786440 | tf_op jit(solution)/shard_map/ppermute | solution.py:103
  138.1 6.4 %collective-permute-start.5 = (f32[32,1024]{1,0:T(8,128)S(1)}, f32[32,1024]{1,0:T(8,128)S(1)}, u32[]{:S(2)}, u32[]{:S(2)}) collective-permute-start(f32[32,1024]{1,0:T(8,128)S(1)} %dynamic-slice_bitcast_fusion.18), channel_id=1, source_target_pairs={{0,2},{1,3},{2,0},{3,1},{4,6},{5,7},{6,4},{7,5},{8,10},{9,11},{10,... | collective-permute-start | bytes 393224 | tf_op jit(solution)/shard_map/ppermute | solution.py:103
  139.8 9.6 %collective-permute-start.6 = (f32[2,32,1024]{2,1,0:T(8,128)S(1)}, f32[2,32,1024]{2,1,0:T(8,128)S(1)}, u32[]{:S(2)}, u32[]{:S(2)}) collective-permute-start(f32[2,32,1024]{2,1,0:T(8,128)S(1)} %dynamic-slice_bitcast_fusion.9), channel_id=1, source_target_pairs={{0,2},{1,3},{2,0},{3,1},{4,6},{5,7},{6,4},{7,5},{8,10},{9,11},{10,... | collective-permute-start | bytes 786440 | tf_op jit(solution)/shard_map/ppermute | solution.py:103
  140.3 7.9 %collective-permute-start.4 = (f32[32,1024]{1,0:T(8,128)S(1)}, f32[32,1024]{1,0:T(8,128)S(1)}, u32[]{:S(2)}, u32[]{:S(2)}) collective-permute-start(f32[32,1024]{1,0:T(8,128)S(1)} %dynamic-slice_bitcast_fusion.19), channel_id=1, source_target_pairs={{0,4},{1,5},{2,6},{3,7},{4,0},{5,1},{6,2},{7,3},{8,12},{9,13},{10,... | collective-permute-start | bytes 393224 | tf_op jit(solution)/shard_map/ppermute | solution.py:103
  156.4 13.4 %collective-permute-start.9 = (f32[32,1024]{1,0:T(8,128)S(1)}, f32[32,1024]{1,0:T(8,128)S(1)}, u32[]{:S(2)}, u32[]{:S(2)}) collective-permute-start(f32[32,1024]{1,0:T(8,128)S(1)} %dynamic-slice_bitcast_fusion.17), channel_id=1, source_target_pairs={{0,4},{1,5},{2,6},{3,7},{4,0},{5,1},{6,2},{7,3},{8,12},{9,13},{10,... | collective-permute-start | bytes 393224 | tf_op jit(solution)/shard_map/ppermute | solution.py:103
  157.9 11.9 %collective-permute-start.10 = (f32[32,1024]{1,0:T(8,128)S(1)}, f32[32,1024]{1,0:T(8,128)S(1)}, u32[]{:S(2)}, u32[]{:S(2)}) collective-permute-start(f32[32,1024]{1,0:T(8,128)S(1)} %dynamic-slice_bitcast_fusion.16), channel_id=1, source_target_pairs={{0,2},{1,3},{2,0},{3,1},{4,6},{5,7},{6,4},{7,5},{8,10},{9,11},{10,... | collective-permute-start | bytes 393224 | tf_op jit(solution)/shard_map/ppermute | solution.py:103
  159.5 10.4 %collective-permute-start.11 = (f32[2,32,1024]{2,1,0:T(8,128)S(1)}, f32[2,32,1024]{2,1,0:T(8,128)S(1)}, u32[]{:S(2)}, u32[]{:S(2)}) collective-permute-start(f32[2,32,1024]{2,1,0:T(8,128)S(1)} %dynamic-slice_bitcast_fusion.7), channel_id=1, source_target_pairs={{0,2},{1,3},{2,0},{3,1},{4,6},{5,7},{6,4},{7,5},{8,10},{9,11},{10,... | collective-permute-start | bytes 786440 | tf_op jit(solution)/shard_map/ppermute | solution.py:103
  160.1 11.2 %collective-permute-start.13 = (f32[2,32,1024]{2,1,0:T(8,128)S(1)}, f32[2,32,1024]{2,1,0:T(8,128)S(1)}, u32[]{:S(2)}, u32[]{:S(2)}) collective-permute-start(f32[2,32,1024]{2,1,0:T(8,128)S(1)} %dynamic-slice_bitcast_fusion.6), channel_id=1, source_target_pairs={{0,4},{1,5},{2,6},{3,7},{4,0},{5,1},{6,2},{7,3},{8,12},{9,13},{10,... | collective-permute-start | bytes 786440 | tf_op jit(solution)/shard_map/ppermute | solution.py:103
  169.7 6.2 %copy-start.1 = (f32[2,256,1024]{2,1,0:T(8,128)S(1)}, f32[2,256,1024]{2,1,0:T(8,128)}, u32[]{:S(2)}) copy-start(f32[2,256,1024]{2,1,0:T(8,128)} %shard_map.58) | copy-start | bytes 6291460
  169.7 6.2 %collective-permute-start.15 = (f32[2,2,2,32,1024]{4,3,2,1,0:T(8,128)S(1)}, f32[2,2,2,32,1024]{4,3,2,1,0:T(8,128)S(1)}, u32[]{:S(2)}, u32[]{:S(2)}) collective-permute-start(f32[2,2,2,32,1024]{4,3,2,1,0:T(8,128)S(1)} %dynamic-slice_bitcast_fusion), channel_id=1, source_target_pairs={{0,1},{1,0},{2,3},{3,2},{4,5},{5,4},{6,7},{7,6},{8,9},{9,8},{10,11... | collective-permute-start | bytes 3145736 | tf_op jit(solution)/shard_map/ppermute | solution.py:147
  170.0 5.9 %collective-permute-start.12 = (f32[32,1024]{1,0:T(8,128)S(1)}, f32[32,1024]{1,0:T(8,128)S(1)}, u32[]{:S(2)}, u32[]{:S(2)}) collective-permute-start(f32[32,1024]{1,0:T(8,128)S(1)} %dynamic-slice_bitcast_fusion.15), channel_id=1, source_target_pairs={{0,4},{1,5},{2,6},{3,7},{4,0},{5,1},{6,2},{7,3},{8,12},{9,13},{10,... | collective-permute-start | bytes 393224 | tf_op jit(solution)/shard_map/ppermute | solution.py:103
  171.4 6.3 %collective-permute-start.14 = (f32[32,1024]{1,0:T(8,128)S(1)}, f32[32,1024]{1,0:T(8,128)S(1)}, u32[]{:S(2)}, u32[]{:S(2)}) collective-permute-start(f32[32,1024]{1,0:T(8,128)S(1)} %dynamic-slice_bitcast_fusion.14), channel_id=1, source_target_pairs={{0,2},{1,3},{2,0},{3,1},{4,6},{5,7},{6,4},{7,5},{8,10},{9,11},{10,... | collective-permute-start | bytes 393224 | tf_op jit(solution)/shard_map/ppermute | solution.py:103
  176.3 8.0 %collective-permute-start.16 = (f32[2,32,1024]{2,1,0:T(8,128)S(1)}, f32[2,32,1024]{2,1,0:T(8,128)S(1)}, u32[]{:S(2)}, u32[]{:S(2)}) collective-permute-start(f32[2,32,1024]{2,1,0:T(8,128)S(1)} %dynamic-slice_bitcast_fusion.5), channel_id=1, source_target_pairs={{0,2},{1,3},{2,0},{3,1},{4,6},{5,7},{6,4},{7,5},{8,10},{9,11},{10,... | collective-permute-start | bytes 786440 | tf_op jit(solution)/shard_map/ppermute | solution.py:103
  177.8 8.0 %collective-permute-start.18 = (f32[2,32,1024]{2,1,0:T(8,128)S(1)}, f32[2,32,1024]{2,1,0:T(8,128)S(1)}, u32[]{:S(2)}, u32[]{:S(2)}) collective-permute-start(f32[2,32,1024]{2,1,0:T(8,128)S(1)} %dynamic-slice_bitcast_fusion.4), channel_id=1, source_target_pairs={{0,4},{1,5},{2,6},{3,7},{4,0},{5,1},{6,2},{7,3},{8,12},{9,13},{10,... | collective-permute-start | bytes 786440 | tf_op jit(solution)/shard_map/ppermute | solution.py:103
  184.3 5.0 %collective-permute-start.17 = (f32[32,1024]{1,0:T(8,128)S(1)}, f32[32,1024]{1,0:T(8,128)S(1)}, u32[]{:S(2)}, u32[]{:S(2)}) collective-permute-start(f32[32,1024]{1,0:T(8,128)S(1)} %dynamic-slice_bitcast_fusion.13), channel_id=1, source_target_pairs={{0,4},{1,5},{2,6},{3,7},{4,0},{5,1},{6,2},{7,3},{8,12},{9,13},{10,... | collective-permute-start | bytes 393224 | tf_op jit(solution)/shard_map/ppermute | solution.py:103
  185.8 5.0 %collective-permute-start.19 = (f32[32,1024]{1,0:T(8,128)S(1)}, f32[32,1024]{1,0:T(8,128)S(1)}, u32[]{:S(2)}, u32[]{:S(2)}) collective-permute-start(f32[32,1024]{1,0:T(8,128)S(1)} %dynamic-slice_bitcast_fusion.12), channel_id=1, source_target_pairs={{0,2},{1,3},{2,0},{3,1},{4,6},{5,7},{6,4},{7,5},{8,10},{9,11},{10,... | collective-permute-start | bytes 393224 | tf_op jit(solution)/shard_map/ppermute | solution.py:103
  (3 other events, 5.4 us)
Sparse Core Ops, SparseCore 0:
  16.3 54.8 all-gather.14
  72.7 25.6 all-gather.12
  100.0 27.3 all-gather.10
  128.9 27.4 all-gather.8
